TPU v7x, 32 devices: a whole 2x2x4 slice. The times are simulated.
32 devices in a mesh: groups: 2 (over x), seq: 8 (over z, y), chan: 2 (over core).
Axes of the slice: x: 2, y: 2, z: 4, core: 2. Of those that a mesh axis runs over, the one named last changes fastest.
Arguments:
- cached_input: bfloat16 [2048, 4096], P(('groups', 'seq'), 'chan'), parts along dimension 0, may hold values from -6 to 6
- cached_gate: bfloat16 [2048, 4096], P(('groups', 'seq'), 'chan'), parts along dimension 0, may hold values from -6 to 6
- out_grad: bfloat16 [2048, 4096], P(('groups', 'seq'), 'chan'), parts along dimension 0, may hold values from -1.75 to 1.75
- filter_taps: bfloat16 [1024, 32], P('seq', 'chan'), may hold values from -6 to 6
- skip_gain: float32 [4096], P('chan'), may hold values from -1 to 1
Outputs:
- input_grad: bfloat16 [2048, 4096], P(('groups', 'seq'), 'chan'), parts along dimension 0
- filter_grad: float32 [2048, 32], P(('groups', 'seq'), 'chan'), parts along dimension 0
There are 2 independent parts, one for each index of `groups`. A program takes and returns all parts, laid end to end along the dimension named above; an argument that names none is the same for every part. Nothing has to cross between parts.
All inputs are finite; a program needn't handle non-finite values.
Results may differ from a plain program's by a relative error of at most 0.005.
Values may be sent and summed in bfloat16 or wider, within the bound.
No kernel may reach another device: no remote copies, remote signals or barrier semaphores. Data moves between devices by JAX's collectives and lax.ppermute only.
A program may use at most 64 MiB of HBM per device.

v0:
```python
import math

import jax
import jax.numpy as jnp
from jax import lax
from jax.sharding import PartitionSpec as P

lag_group = 4


def toeplitz_blocks(windows, block_rows):
    flipped = windows[..., ::-1]
    tiled = jnp.tile(flipped, (1, 1, block_rows))
    trimmed = tiled[..., : block_rows * (2 * block_rows - 1)]
    shaped = trimmed.reshape(windows.shape[0], windows.shape[1], block_rows, 2 * block_rows - 1)
    return shaped[..., block_rows - 1 : 2 * block_rows - 1]


def diagonal_sums(products, block_rows):
    flipped = products[..., ::-1]
    padded = jnp.pad(flipped, ((0, 0), (0, 0), (0, 0), (0, block_rows)))
    flattened = padded.reshape(products.shape[0], products.shape[1], 2 * block_rows * block_rows)
    trimmed = flattened[..., : block_rows * (2 * block_rows - 1)]
    shaped = trimmed.reshape(products.shape[0], products.shape[1], block_rows, 2 * block_rows - 1)
    diag_sums = jnp.sum(shaped, axis=2)
    return jnp.pad(diag_sums, ((0, 0), (0, 0), (1, 0)))


def fold_windows(window_grads, block_rows):
    front_half = jnp.pad(window_grads[..., :block_rows], ((0, 1), (0, 0), (0, 0)))
    back_half = jnp.pad(window_grads[..., block_rows:], ((1, 0), (0, 0), (0, 0)))
    joined = front_half + back_half
    return jnp.transpose(joined, (1, 0, 2)).reshape(window_grads.shape[1], -1)


def lag_table(taps_all, block_rows):
    return jnp.pad(jnp.transpose(taps_all), ((0, 0), (block_rows, lag_group * block_rows)))


def lag_sweep(
    blocks, base_block, block_count, sources, tap_table, block_rows, trip_count, seq_count
):
    filters = sources.shape[2]
    group_width = sources.shape[3]

    def advance(lag_step, state_pair):
        input_acc, lag_acc = state_pair
        lag_start = lag_step * lag_group
        stacked = jnp.stack(
            [
                lax.dynamic_slice_in_dim(blocks, base_block + lag_start + offset, block_count, 0)
                for offset in range(lag_group)
            ],
            axis=1,
        )
        lag_span = lax.dynamic_slice_in_dim(
            tap_table, lag_start * block_rows, (lag_group + 1) * block_rows, 1
        )
        windows = jnp.stack(
            [
                lag_span[:, offset * block_rows : (offset + 2) * block_rows]
                for offset in range(lag_group)
            ],
            axis=0,
        )
        toeplitz = toeplitz_blocks(windows, block_rows)
        input_acc = input_acc + jnp.einsum(
            "kfts,iktfg->isfg", toeplitz, stacked, preferred_element_type=jnp.float32
        )
        products = jnp.einsum(
            "iktfg,isfg->kfts", stacked, sources, preferred_element_type=jnp.float32
        )
        folded = fold_windows(diagonal_sums(products, block_rows), block_rows)
        previous = lax.dynamic_slice_in_dim(
            lag_acc, lag_start * block_rows, (lag_group + 1) * block_rows, 1
        )
        lag_acc = lax.dynamic_update_slice_in_dim(
            lag_acc, previous + folded, lag_start * block_rows, 1
        )
        return (input_acc, lag_acc)

    initial = (
        jnp.zeros((block_count, block_rows, filters, group_width), jnp.float32),
        jnp.zeros((filters, (seq_count + 1 + lag_group) * block_rows), jnp.float32),
    )
    return lax.fori_loop(0, trip_count, advance, initial)


def per_device(cached_input, cached_gate, out_grad, filter_taps, skip_gain):
    block_rows = cached_input.shape[0]
    chan_width = cached_input.shape[1]
    filters = filter_taps.shape[1]
    group_width = chan_width // filters
    seq_count = lax.axis_size("seq")
    seq_index = lax.axis_index("seq")
    length = block_rows * seq_count
    taps_scale = 1.0 / math.sqrt(length)
    gated_grad = (out_grad.astype(jnp.float32) * cached_gate.astype(jnp.float32)).astype(
        jnp.bfloat16
    )
    stretch_width = chan_width // seq_count
    moved_grad, moved_input = (
        lax.all_to_all(gated_grad, "seq", split_axis=1, concat_axis=0, tiled=True),
        lax.all_to_all(cached_input, "seq", split_axis=1, concat_axis=0, tiled=True),
    )
    taps_all = lax.all_gather(filter_taps, "seq", axis=0, tiled=True)
    stretch_filters = max(1, stretch_width // group_width)
    stretch_group = stretch_width // stretch_filters
    first_filter = seq_index * stretch_width // group_width
    stretch_taps = lax.dynamic_slice_in_dim(taps_all, first_filter, stretch_filters, 1)
    shaped_grad = moved_grad.reshape(seq_count, block_rows, stretch_filters, stretch_group)
    blocks = jnp.pad(shaped_grad, ((0, seq_count - 1 + lag_group), (0, 0), (0, 0), (0, 0)))
    sources = moved_input.reshape(seq_count, block_rows, stretch_filters, stretch_group)
    trip_count = (seq_count + lag_group - 1) // lag_group
    input_acc, lag_acc = lag_sweep(
        blocks,
        0,
        seq_count,
        sources,
        lag_table(stretch_taps, block_rows),
        block_rows,
        trip_count,
        seq_count,
    )
    stretch_gain = lax.dynamic_slice_in_dim(skip_gain, seq_index * stretch_width, stretch_width, 0)
    conv_grad = input_acc.reshape(length, stretch_width) * taps_scale
    local_grad = (conv_grad + stretch_gain[None, :] * moved_grad.astype(jnp.float32)).astype(
        jnp.bfloat16
    )
    input_grad = lax.all_to_all(local_grad, "seq", split_axis=0, concat_axis=1, tiled=True)
    stretch_term = jnp.transpose(lag_acc[:, block_rows : block_rows + length]) * taps_scale
    lag_term = lax.dynamic_update_slice_in_dim(
        jnp.zeros((length, filters), jnp.float32), stretch_term, first_filter, 1
    )
    filter_grad = lax.psum_scatter(lag_term, "seq", scatter_dimension=0, tiled=True)
    return (input_grad, filter_grad)


def solution(mesh):
    return jax.shard_map(
        per_device,
        mesh=mesh,
        in_specs=(
            P(("groups", "seq"), "chan"),
            P(("groups", "seq"), "chan"),
            P(("groups", "seq"), "chan"),
            P("seq", "chan"),
            P("chan"),
        ),
        out_specs=(P(("groups", "seq"), "chan"), P(("groups", "seq"), "chan")),
        check_vma=False,
    )
```

profile of v0, /device:TPU:0, one launch (start us, length us, event | category | flops | bytes accessed | tf_op | source)
XLA Modules:
  0.0 169.5 jit_solution(654285990207121783)
XLA Ops:
  7.2 1.3 multiply_convert_fusion
  8.5 1.0 copy.21
  9.5 7.3 %all-to-all-start = ((bf16[128,8,256]{0,2,1:T(8,128)(2,1)}), bf16[128,8,256]{0,2,1:T(8,128)(2,1)S(1)}, u32[]{:S(2)}, u32[]{:S(2)}) async-start(bf16[128,8,256]{0,2,1:T(8,128)(2,1)} %bitcast), calls=%async_computation | async-start | bytes 1048576 | tf_op jit(solution)/shard_map/all_to_all | solution.py:103
  16.8 1.0 copy.22
  17.8 13.4 %all-to-all-done = bf16[128,8,256]{0,2,1:T(8,128)(2,1)S(1)} async-done(((bf16[128,8,256]{0,2,1:T(8,128)(2,1)}), bf16[128,8,256]{0,2,1:T(8,128)(2,1)S(1)}, u32[]{:S(2)}, u32[]{:S(2)}) %all-to-all-start) | async-done | bytes 524320 | tf_op jit(solution)/shard_map/all_to_all | solution.py:103
  31.3 3.6 %all-to-all-start.1 = ((bf16[128,8,256]{0,2,1:T(8,128)(2,1)}), bf16[128,8,256]{0,2,1:T(8,128)(2,1)S(1)}, u32[]{:S(2)}, u32[]{:S(2)}) async-start(bf16[128,8,256]{0,2,1:T(8,128)(2,1)} %bitcast.4), calls=%async_computation.1 | async-start | bytes 1048576 | tf_op jit(solution)/shard_map/all_to_all | solution.py:104
  34.9 33.2 %all_gather.3 = bf16[1024,16]{0,1:T(8,128)(2,1)S(1)} all-gather(bf16[128,16]{0,1:T(8,128)(2,1)S(1)} %copy-done.7), channel_id=1, replica_groups=mesh['groups'=2,'seq'=8,'chan'=2] {'seq'}, dimensions={0}, use_global_device_ids=true | all-gather | bytes 36864 | tf_op jit(solution)/shard_map/all_gather | solution.py:106
  68.2 0.8 dynamic_slice.67
  69.0 0.2 pad.52.clone
  69.2 1.0 copy.24
  70.2 26.8 %while.18 = (s32[]{:T(128)}, f32[8,128,2,128]{1,3,0,2:T(8,128)}, f32[2,1664]{1,0:T(2,128)S(1)}, bf16[19,128,2,128]{1,3,0,2:T(8,128)(2,1)S(1)}, bf16[2,1664]{1,0:...) while((s32[]{:T(128)}, f32[8,128,2,128]{1,3,0,2:T(8,128)}, ...), condition=%wide.region_2.3_spmd.clone, body=%wide.region_0.2_spmd.clone.sunk | while | flops 543954432 | bytes 31783416 | solution.py:86
  70.2 1.2 dynamic-slice_bitcast_fusion.6
  71.4 0.2 rev.24
  71.7 0.1 tile.29
  71.8 0.4 slice.122
  72.2 1.6 reshape.89
  73.8 3.1 %fusion.19 = f32[8,128,2,128]{1,3,0,2:T(8,128)} fusion(f32[8,128,2,128]{1,3,0,2:T(8,128)} %get-tuple-element.301, pred[]{:T(512)S(6)} %compare.11, bf16[8,1,128,2,128]{2,4,1,0,3:T(8,128)(2,1)S(1)} %get-tuple-element.269, bf16[8,1,128,2,128]{2,4,1,0,3:T(8,128)(2,1)} %get-tuple-element.270, bf16[8,1,128,2,128]{2,4,1,0,3:T(8,128)(2,1)} %get-tuple-element.271, ...), kind=kOutput, calls=%fused_computation.2.clone.1 | convolution fusion | flops 272105472 | bytes 4456449 | tf_op jit(solution)/shard_map/while/body/eval_jaxpr/kfts,iktfg->isfg/dot_general | solution.py:67
  76.9 1.1 convolution_bitcast_fusion.3
  78.0 0.7 rev.25
  78.7 0.1 pad.116
  78.8 0.5 reshape.90
  79.4 1.1 slice.123
  80.4 2.8 %reshape.91 = f32[4,2,128,255]{3,2,0,1:T(8,128)S(1)} reshape(f32[4,2,32640]{2,0,1:T(4,128)} %slice.123) | data formatting | bytes 2088960 | tf_op jit(solution)/shard_map/while/body/eval_jaxpr/reshape | solution.py:24
  83.2 0.1 reduce_sum.18
  83.4 0.1 pad_slice_fusion.2
  83.5 1.2 dynamic-slice_bitcast_fusion.6
  84.7 0.2 rev.24
  85.0 0.1 tile.29
  85.1 0.4 slice.122
  85.5 1.6 reshape.89
  87.1 3.4 %fusion.19 = f32[8,128,2,128]{1,3,0,2:T(8,128)} fusion(f32[8,128,2,128]{1,3,0,2:T(8,128)} %get-tuple-element.301, pred[]{:T(512)S(6)} %compare.11, bf16[8,1,128,2,128]{2,4,1,0,3:T(8,128)(2,1)S(1)} %get-tuple-element.269, bf16[8,1,128,2,128]{2,4,1,0,3:T(8,128)(2,1)} %get-tuple-element.270, bf16[8,1,128,2,128]{2,4,1,0,3:T(8,128)(2,1)} %get-tuple-element.271, ...), kind=kOutput, calls=%fused_computation.2.clone.1 | convolution fusion | flops 272105472 | bytes 4456449 | tf_op jit(solution)/shard_map/while/body/eval_jaxpr/kfts,iktfg->isfg/dot_general | solution.py:67
  90.5 1.1 convolution_bitcast_fusion.3
  91.6 0.7 rev.25
  92.3 0.1 pad.116
  92.5 0.5 reshape.90
  93.0 1.1 slice.123
  94.0 2.8 %reshape.91 = f32[4,2,128,255]{3,2,0,1:T(8,128)S(1)} reshape(f32[4,2,32640]{2,0,1:T(4,128)} %slice.123) | data formatting | bytes 2088960 | tf_op jit(solution)/shard_map/while/body/eval_jaxpr/reshape | solution.py:24
  96.9 0.1 reduce_sum.18
  97.0 0.1 pad_slice_fusion.2
  97.1 1.4 copy_multiply_fusion
  98.5 1.0 fusion.9
  99.5 3.5 %all-to-all-start.2 = ((bf16[8,128,256]{1,2,0:T(8,128)(2,1)}), bf16[8,128,256]{1,2,0:T(8,128)(2,1)S(1)}, u32[]{:S(2)}, u32[]{:S(2)}) async-start(bf16[8,128,256]{1,2,0:T(8,128)(2,1)} %fusion.9), calls=%async_computation.2 | async-start | bytes 1048576 | tf_op jit(solution)/shard_map/all_to_all | solution.py:130
  103.0 0.0 reduce-scatter.2.cloned.1.call-start
  103.0 0.3 dynamic_update_slice.13
  103.4 0.6 copy-done.6
  104.0 9.2 %all-to-all-done.2 = bf16[8,128,256]{1,2,0:T(8,128)(2,1)S(1)} async-done(((bf16[8,128,256]{1,2,0:T(8,128)(2,1)}), bf16[8,128,256]{1,2,0:T(8,128)(2,1)S(1)}, u32[]{:S(2)}, u32[]{:S(2)}) %all-to-all-start.2) | async-done | bytes 524320 | tf_op jit(solution)/shard_map/all_to_all | solution.py:130
  113.2 1.0 copy.26
  114.2 48.4 %reduce-scatter.2.cloned.1.call-done = f32[128,16]{0,1:T(8,128)} async-done(((f32[1024,16]{0,1:T(8,128)}), f32[128,16]{0,1:T(8,128)}) %reduce-scatter.2.cloned.1.call-update) | async-done | bytes 8208 | tf_op jit(solution)/shard_map/reduce_scatter | solution.py:135
  (40 shorter events, 0.3 us)
Async XLA Ops:
  8.5 8.3 %copy-start.4 = (bf16[128,2048]{1,0:T(8,128)(2,1)S(1)}, bf16[128,2048]{1,0:T(8,128)(2,1)}, u32[]{:S(2)}) copy-start(bf16[128,2048]{1,0:T(8,128)(2,1)} %param.7) | copy-start | bytes 1572868
  9.5 21.8 %all-to-all-start = ((bf16[128,8,256]{0,2,1:T(8,128)(2,1)}), bf16[128,8,256]{0,2,1:T(8,128)(2,1)S(1)}, u32[]{:S(2)}, u32[]{:S(2)}) async-start(bf16[128,8,256]{0,2,1:T(8,128)(2,1)} %bitcast), calls=%async_computation | async-start | bytes 1048576 | tf_op jit(solution)/shard_map/all_to_all | solution.py:103
  16.8 18.1 %copy-start.7 = (bf16[128,16]{0,1:T(8,128)(2,1)S(1)}, bf16[128,16]{0,1:T(8,128)(2,1)}, u32[]{:S(2)}) copy-start(bf16[128,16]{0,1:T(8,128)(2,1)} %param.10) | copy-start | bytes 12292
  31.3 37.6 %copy-start.2 = (bf16[128,8,256]{0,2,1:T(8,128)(2,1)}, bf16[128,8,256]{0,2,1:T(8,128)(2,1)S(1)}, u32[]{:S(2)}) copy-start(bf16[128,8,256]{0,2,1:T(8,128)(2,1)S(1)} %all-to-all-done) | copy-start | bytes 1572868
  31.3 37.9 %all-to-all-start.1 = ((bf16[128,8,256]{0,2,1:T(8,128)(2,1)}), bf16[128,8,256]{0,2,1:T(8,128)(2,1)S(1)}, u32[]{:S(2)}, u32[]{:S(2)}) async-start(bf16[128,8,256]{0,2,1:T(8,128)(2,1)} %bitcast.4), calls=%async_computation.1 | async-start | bytes 1048576 | tf_op jit(solution)/shard_map/all_to_all | solution.py:104
  73.7 3.1 %copy-start = (bf16[8,1,128,2,128]{2,4,1,0,3:T(8,128)(2,1)S(1)}, bf16[8,1,128,2,128]{2,4,1,0,3:T(8,128)(2,1)}, u32[]{:S(2)}) copy-start(bf16[8,1,128,2,128]{2,4,1,0,3:T(8,128)(2,1)} %get-tuple-element.270) | copy-start | bytes 1572868 | tf_op jit(solution)/shard_map/while
  73.8 3.1 %copy-start.1 = (bf16[8,1,128,2,128]{2,4,1,0,3:T(8,128)(2,1)S(1)}, bf16[8,1,128,2,128]{2,4,1,0,3:T(8,128)(2,1)}, u32[]{:S(2)}) copy-start(bf16[8,1,128,2,128]{2,4,1,0,3:T(8,128)(2,1)} %get-tuple-element.271) | copy-start | bytes 1572868 | tf_op jit(solution)/shard_map/while
  73.8 3.1 %copy-start.5 = (bf16[8,128,2,128]{3,1,0,2:T(8,128)(2,1)S(1)}, bf16[8,128,2,128]{3,1,0,2:T(8,128)(2,1)}, u32[]{:S(2)}) copy-start(bf16[8,128,2,128]{3,1,0,2:T(8,128)(2,1)} %get-tuple-element.326) | copy-start | bytes 1572868 | tf_op jit(solution)/shard_map/while
  87.0 3.5 %copy-start = (bf16[8,1,128,2,128]{2,4,1,0,3:T(8,128)(2,1)S(1)}, bf16[8,1,128,2,128]{2,4,1,0,3:T(8,128)(2,1)}, u32[]{:S(2)}) copy-start(bf16[8,1,128,2,128]{2,4,1,0,3:T(8,128)(2,1)} %get-tuple-element.270) | copy-start | bytes 1572868 | tf_op jit(solution)/shard_map/while
  87.0 3.5 %copy-start.1 = (bf16[8,1,128,2,128]{2,4,1,0,3:T(8,128)(2,1)S(1)}, bf16[8,1,128,2,128]{2,4,1,0,3:T(8,128)(2,1)}, u32[]{:S(2)}) copy-start(bf16[8,1,128,2,128]{2,4,1,0,3:T(8,128)(2,1)} %get-tuple-element.271) | copy-start | bytes 1572868 | tf_op jit(solution)/shard_map/while
  87.0 3.5 %copy-start.5 = (bf16[8,128,2,128]{3,1,0,2:T(8,128)(2,1)S(1)}, bf16[8,128,2,128]{3,1,0,2:T(8,128)(2,1)}, u32[]{:S(2)}) copy-start(bf16[8,128,2,128]{3,1,0,2:T(8,128)(2,1)} %get-tuple-element.326) | copy-start | bytes 1572868 | tf_op jit(solution)/shard_map/while
  97.1 1.4 copy-start.3
  99.5 13.8 %all-to-all-start.2 = ((bf16[8,128,256]{1,2,0:T(8,128)(2,1)}), bf16[8,128,256]{1,2,0:T(8,128)(2,1)S(1)}, u32[]{:S(2)}, u32[]{:S(2)}) async-start(bf16[8,128,256]{1,2,0:T(8,128)(2,1)} %fusion.9), calls=%async_computation.2 | async-start | bytes 1048576 | tf_op jit(solution)/shard_map/all_to_all | solution.py:130
  103.0 59.7 %reduce-scatter.2.cloned.1.call-start = ((), (), s32[]{:S(2)}) async-start(), calls=%async_computation.4 | async-start | bytes 73728 | tf_op jit(solution)/shard_map/reduce_scatter | solution.py:135
  103.3 0.6 copy-start.6
Sparse Core Ops, SparseCore 0:
  107.5 55.0 reduce-scatter.1
where the time goes:
time: 170 us; the launch traced here: 169 us
  waiting for transfers between devices  71.1 us (42%)
  blocking collectives  33.2 us (20%)
  local copies, waits for them, and re-layouts  23.6 us (14%)
  starting transfers between devices  14.5 us (9%)
  between operations  14.2 us (8%)
  matrix products  8.75 us (5%)
  other arithmetic  3.94 us (2%)
    reduce_scatter x1, waiting for transfers between devices, per_device(): lax.psum_scatter(lag_term, 'seq', scatter_dimension=0, tiled=True)  48.4 us
    all_gather x1, blocking collectives, per_device(): taps_all = lax.all_gather(filter_taps, 'seq', axis=0, tiled=True)  33.2 us
    all_to_all x1, waiting for transfers between devices, per_device(): lax.all_to_all(gated_grad, 'seq', split_axis=1, concat_axis=0, tiled=True)  13.4 us
    all_to_all x1, waiting for transfers between devices, per_device(): lax.all_to_all(local_grad, 'seq', split_axis=0, concat_axis=1, tiled=True)  9.23 us
    all_to_all x1, starting transfers between devices, per_device(): lax.all_to_all(gated_grad, 'seq', split_axis=1, concat_axis=0, tiled=True)  7.28 us
    dot_general x2, matrix products, advance(): jnp.einsum('kfts,iktfg->isfg', toeplitz, stacked, preferred_element_type=...  6.53 us
    reshape x2, local copies, waits for them, and re-layouts, diagonal_sums(): trimmed.reshape(products.shape[0], products.shape[1], block_rows, 2 * blo...  5.62 us
    unnamed x14, local copies, waits for them, and re-layouts  3.72 us
  transfers between devices with their start and end apart: 4, of which 3 were waited for; matrix products, arithmetic and copies ran while one was open for 2% of the time, Pallas kernels for 0%

commit v1 on v0

--- a/solution.py
+++ b/solution.py
@@ -1,6 +1,7 @@
 import math
 
 import jax
+import numpy as np
 import jax.numpy as jnp
 from jax import lax
 from jax.sharding import PartitionSpec as P
@@ -99,15 +100,30 @@
         jnp.bfloat16
     )
     stretch_width = chan_width // seq_count
-    moved_grad, moved_input = (
-        lax.all_to_all(gated_grad, "seq", split_axis=1, concat_axis=0, tiled=True),
-        lax.all_to_all(cached_input, "seq", split_axis=1, concat_axis=0, tiled=True),
-    )
-    taps_all = lax.all_gather(filter_taps, "seq", axis=0, tiled=True)
     stretch_filters = max(1, stretch_width // group_width)
     stretch_group = stretch_width // stretch_filters
     first_filter = seq_index * stretch_width // group_width
-    stretch_taps = lax.dynamic_slice_in_dim(taps_all, first_filter, stretch_filters, 1)
+    tap_columns = np.array(
+        [
+            (target * stretch_width) // group_width + offset
+            for target in range(seq_count)
+            for offset in range(stretch_filters)
+        ]
+    )
+    routed_taps = filter_taps[:, tap_columns].reshape(block_rows, seq_count, stretch_filters)
+    packed = jnp.concatenate(
+        [
+            gated_grad.reshape(block_rows, seq_count, stretch_width),
+            cached_input.reshape(block_rows, seq_count, stretch_width),
+            routed_taps,
+        ],
+        axis=2,
+    )
+    moved = lax.all_to_all(packed, "seq", split_axis=1, concat_axis=0, tiled=True)
+    moved = moved.reshape(length, 2 * stretch_width + stretch_filters)
+    moved_grad = moved[:, :stretch_width]
+    moved_input = moved[:, stretch_width : 2 * stretch_width]
+    stretch_taps = moved[:, 2 * stretch_width :]
     shaped_grad = moved_grad.reshape(seq_count, block_rows, stretch_filters, stretch_group)
     blocks = jnp.pad(shaped_grad, ((0, seq_count - 1 + lag_group), (0, 0), (0, 0), (0, 0)))
     sources = moved_input.reshape(seq_count, block_rows, stretch_filters, stretch_group)
@@ -129,10 +145,19 @@
     )
     input_grad = lax.all_to_all(local_grad, "seq", split_axis=0, concat_axis=1, tiled=True)
     stretch_term = jnp.transpose(lag_acc[:, block_rows : block_rows + length]) * taps_scale
-    lag_term = lax.dynamic_update_slice_in_dim(
-        jnp.zeros((length, filters), jnp.float32), stretch_term, first_filter, 1
+    lag_parts = lax.all_to_all(
+        stretch_term.reshape(seq_count, block_rows, stretch_filters),
+        "seq",
+        split_axis=0,
+        concat_axis=0,
+        tiled=True,
     )
-    filter_grad = lax.psum_scatter(lag_term, "seq", scatter_dimension=0, tiled=True)
+    sharers = seq_count * stretch_filters // filters
+    filter_grad = (
+        jnp.transpose(lag_parts, (1, 0, 2))
+        .reshape(block_rows, filters, sharers)
+        .sum(axis=2)
+    )
     return (input_grad, filter_grad)
 
 

time: 170 us -> 99.2 us (0.58)
  blocking collectives: 33.2 us -> 0 us
  waiting for transfers between devices: 71.1 us -> 43.2 us
  between operations: 14.2 us -> 0.83 us
  local copies, waits for them, and re-layouts: 23.6 us -> 25.7 us
    reduce_scatter x1 -> x0, waiting for transfers between devices: 48.4 us -> none  [per_device(): lax.psum_scatter(lag_term, 'seq', scatter_dimension=0, tiled=True)]
    all_gather x1 -> x0, blocking collectives: 33.2 us -> none  [per_device(): taps_all = lax.all_gather(filter_taps, 'seq', axis=0, tiled=True)]
    all_to_all x2, waiting for transfers between devices: 13.4 us -> 29.7 us  [the longest x1 25.4 us: per_device(): lax.all_to_all(packed, 'seq', split_axis=1, concat_axis=0, tiled=True)]
    all_to_all x1, waiting for transfers between devices: 9.23 us -> 13.4 us  [per_device(): lax.all_to_all(local_grad, 'seq', split_axis=0, concat_axis=1, tiled=True)]
    all_to_all x0 -> x1, other arithmetic: none -> 2.14 us  [per_device(): lax.all_to_all(local_grad, 'seq', split_axis=0, concat_axis=1, tiled=True)]
    unnamed x14 -> x17, local copies, waits for them, and re-layouts: 3.72 us -> 5.54 us
  transfers between devices with their start and end apart: 4 -> 3, of which waited for: 3 -> 3; matrix products, arithmetic and copies ran while one was open for 2% -> 3% of each run, Pallas kernels for 0% -> 0%
where the time goes in v1:
time: 99.2 us; the launch traced here: 98.7 us
  waiting for transfers between devices  43.2 us (44%)
  local copies, waits for them, and re-layouts  25.7 us (26%)
  starting transfers between devices  14.4 us (15%)
  matrix products  8.83 us (9%)
  other arithmetic  5.49 us (6%)
    all_to_all x1, waiting for transfers between devices, per_device(): lax.all_to_all(packed, 'seq', split_axis=1, concat_axis=0, tiled=True)  25.4 us
    all_to_all x1, waiting for transfers between devices, per_device(): lax.all_to_all(local_grad, 'seq', split_axis=0, concat_axis=1, tiled=True)  13.4 us
    all_to_all x1, starting transfers between devices, per_device(): lax.all_to_all(packed, 'seq', split_axis=1, concat_axis=0, tiled=True)  7.28 us
    dot_general x2, matrix products, advance(): jnp.einsum('kfts,iktfg->isfg', toeplitz, stacked, preferred_element_type=...  6.6 us
    reshape x2, local copies, waits for them, and re-layouts, diagonal_sums(): trimmed.reshape(products.shape[0], products.shape[1], block_rows, 2 * blo...  5.62 us
    unnamed x17, local copies, waits for them, and re-layouts  5.54 us
    all_to_all x1, waiting for transfers between devices, per_device(): lax.all_to_all(stretch_term.reshape(seq_count, block_rows, stretch_filter...  4.37 us
    all_to_all x1, starting transfers between devices, per_device(): lax.all_to_all(stretch_term.reshape(seq_count, block_rows, stretch_filter...  3.59 us
  transfers between devices with their start and end apart: 3, of which 3 were waited for; matrix products, arithmetic and copies ran while one was open for 3% of the time, Pallas kernels for 0%

profile of v1, /device:TPU:0, one launch (start us, length us, event | category | flops | bytes accessed | tf_op | source)
XLA Modules:
  0.0 98.7 jit_solution(5453652676311803673)
XLA Ops:
  0.7 1.4 %copy.32 = bf16[128,2048]{0,1:T(8,128)(2,1)S(1)} copy(bf16[128,2048]{1,0:T(8,128)(2,1)} %param.9) | data formatting | bytes 1048576 | tf_op args[0]
  2.1 0.1 multiply_convert_fusion
  2.2 0.3 copy.31
  2.5 0.6 gather_fusion
  3.1 1.1 %pad_maximum_fusion.4 = bf16[128,8,514]{0,2,1:T(8,128)(2,1)} fusion(bf16[128,8,2]{0,2,1:T(2,128)(2,1)S(1)} %bitcast.138, bf16[128,8,256]{0,2,1:T(8,128)(2,1)S(1)} %bitcast.136, bf16[128,8,256]{0,2,1:T(8,128)(2,1)S(1)} %bitcast.137), kind=kLoop, calls=%fused_computation.25 | loop fusion | flops 3158016 | bytes 2105344 | tf_op jit(solution)/shard_map/concatenate | solution.py:114
  4.2 7.3 %all-to-all-start = ((bf16[128,8,514]{0,2,1:T(8,128)(2,1)}), bf16[128,8,514]{0,2,1:T(8,128)(2,1)S(1)}, u32[]{:S(2)}, u32[]{:S(2)}) async-start(bf16[128,8,514]{0,2,1:T(8,128)(2,1)} %pad_maximum_fusion.4), calls=%async_computation | async-start | bytes 2129920 | tf_op jit(solution)/shard_map/all_to_all | solution.py:122
  11.4 0.8 dynamic_slice.63
  12.2 25.4 %all-to-all-done = bf16[128,8,514]{0,2,1:T(8,128)(2,1)S(1)} async-done(((bf16[128,8,514]{0,2,1:T(8,128)(2,1)}), bf16[128,8,514]{0,2,1:T(8,128)(2,1)S(1)}, u32[]{:S(2)}, u32[]{:S(2)}) %all-to-all-start) | async-done | bytes 1052704 | tf_op jit(solution)/shard_map/all_to_all | solution.py:122
  37.6 0.1 copy.63
  37.8 0.3 copy.51
  38.3 0.8 copy-done.3
  39.2 0.2 pad.52
  39.5 1.1 %copy.35 = bf16[8,128,2,128]{3,1,0,2:T(8,128)(2,1)} copy(bf16[8,128,2,128]{1,0,3,2:T(8,128)(2,1)S(1)} %bitcast.135) | data formatting | bytes 1048576
  40.6 26.8 %while.18 = (s32[]{:T(128)}, f32[8,128,2,128]{1,3,0,2:T(8,128)}, f32[2,1664]{1,0:T(2,128)S(1)}, bf16[19,128,2,128]{1,3,0,2:T(8,128)(2,1)S(1)}, bf16[2,1664]{1,0:...) while((s32[]{:T(128)}, f32[8,128,2,128]{1,3,0,2:T(8,128)}, ...), condition=%wide.region_2.3_spmd.clone, body=%wide.region_0.2_spmd.clone.sunk | while | flops 543954432 | bytes 31783416 | solution.py:87
  40.6 1.2 %dynamic-slice_bitcast_fusion.5 = (bf16[8,1,128,2,128]{2,4,1,0,3:T(8,128)(2,1)S(1)}, bf16[8,1,128,2,128]{2,4,1,0,3:T(8,128)(2,1)S(1)}, bf16[8,1,128,2,128]{2,4,1,0,3:T(8,128)(2,1)}, bf16[8,1,128,2,128]{2,4,1,0,3:T(8,128)(2,1)}) fusion(bf16[19,128,2,128]{1,3,0,2:T(8,128)(2,1)S(1)} %get-tuple-element.324, s32[]{:T(128)S(6)} %select_n.70, ...), kind=kLoop, calls=%fused_computation.9.clone.1 | loop fusion | bytes 4194320 | tf_op jit(solution)/shard_map/while/body/eval_jaxpr/stack | solution.py:50
  41.8 0.2 rev.24
  42.1 0.1 tile.29
  42.2 0.4 slice.144
  42.6 1.6 %reshape.107 = bf16[4,2,128,255]{3,2,1,0:T(8,128)(2,1)S(1)} reshape(bf16[4,2,32640]{2,1,0:T(2,128)(2,1)S(1)} %slice.144) | data formatting | bytes 1044480 | tf_op jit(solution)/shard_map/while/body/eval_jaxpr/reshape | solution.py:16
  44.2 3.1 %fusion.21 = f32[8,128,2,128]{1,3,0,2:T(8,128)} fusion(f32[8,128,2,128]{1,3,0,2:T(8,128)} %get-tuple-element.301, pred[]{:T(512)S(6)} %compare.9, bf16[8,1,128,2,128]{2,4,1,0,3:T(8,128)(2,1)S(1)} %get-tuple-element.269, bf16[8,1,128,2,128]{2,4,1,0,3:T(8,128)(2,1)} %get-tuple-element.270, bf16[8,1,128,2,128]{2,4,1,0,3:T(8,128)(2,1)} %get-tuple-element.271, ...), kind=kOutput, calls=%fused_computation.3.clone.1 | convolution fusion | flops 272105472 | bytes 4456449 | tf_op jit(solution)/shard_map/while/body/eval_jaxpr/kfts,iktfg->isfg/dot_general | solution.py:68
  47.3 1.1 %convolution_bitcast_fusion.3 = f32[4,2,128,128]{3,2,0,1:T(8,128)S(1)} fusion(bf16[8,128,2,128]{3,1,0,2:T(8,128)(2,1)S(1)} %copy-done.6, bf16[8,1,128,2,128]{2,4,1,0,3:T(8,128)(2,1)S(1)} %get-tuple-element.269, bf16[8,1,128,2,128]{2,4,1,0,3:T(8,128)(2,1)S(1)} %copy-done.1, bf16[8,1,128,2,128]{2,4,1,0,3:T(8,128)(2,1)S(1)} %copy-done.2, ...), kind=kOutput, calls=%fused_computation.4.clone.1 | convolution fusion | flops 271581184 | bytes 3145728 | tf_op jit(solution)/shard_map/while/body/eval_jaxpr/iktfg,isfg->kfts/dot_general | solution.py:71
  48.4 0.7 rev.25
  49.1 0.1 pad.125
  49.3 0.5 reshape.108
  49.8 1.0 %slice.145 = f32[4,2,32640]{2,0,1:T(4,128)} slice(f32[4,2,32768]{2,0,1:T(4,128)S(1)} %reshape.108), slice={[0:4], [0:2], [0:32640]} | slice | bytes 2088960 | tf_op jit(solution)/shard_map/while/body/eval_jaxpr/slice | solution.py:24
  50.8 2.8 %reshape.109 = f32[4,2,128,255]{3,2,0,1:T(8,128)S(1)} reshape(f32[4,2,32640]{2,0,1:T(4,128)} %slice.145) | data formatting | bytes 2088960 | tf_op jit(solution)/shard_map/while/body/eval_jaxpr/reshape | solution.py:25
  53.9 1.2 %dynamic-slice_bitcast_fusion.5 = (bf16[8,1,128,2,128]{2,4,1,0,3:T(8,128)(2,1)S(1)}, bf16[8,1,128,2,128]{2,4,1,0,3:T(8,128)(2,1)S(1)}, bf16[8,1,128,2,128]{2,4,1,0,3:T(8,128)(2,1)}, bf16[8,1,128,2,128]{2,4,1,0,3:T(8,128)(2,1)}) fusion(bf16[19,128,2,128]{1,3,0,2:T(8,128)(2,1)S(1)} %get-tuple-element.324, s32[]{:T(128)S(6)} %select_n.70, ...), kind=kLoop, calls=%fused_computation.9.clone.1 | loop fusion | bytes 4194320 | tf_op jit(solution)/shard_map/while/body/eval_jaxpr/stack | solution.py:50
  55.1 0.2 rev.24
  55.3 0.1 tile.29
  55.5 0.4 slice.144
  55.8 1.6 %reshape.107 = bf16[4,2,128,255]{3,2,1,0:T(8,128)(2,1)S(1)} reshape(bf16[4,2,32640]{2,1,0:T(2,128)(2,1)S(1)} %slice.144) | data formatting | bytes 1044480 | tf_op jit(solution)/shard_map/while/body/eval_jaxpr/reshape | solution.py:16
  57.4 3.5 %fusion.21 = f32[8,128,2,128]{1,3,0,2:T(8,128)} fusion(f32[8,128,2,128]{1,3,0,2:T(8,128)} %get-tuple-element.301, pred[]{:T(512)S(6)} %compare.9, bf16[8,1,128,2,128]{2,4,1,0,3:T(8,128)(2,1)S(1)} %get-tuple-element.269, bf16[8,1,128,2,128]{2,4,1,0,3:T(8,128)(2,1)} %get-tuple-element.270, bf16[8,1,128,2,128]{2,4,1,0,3:T(8,128)(2,1)} %get-tuple-element.271, ...), kind=kOutput, calls=%fused_computation.3.clone.1 | convolution fusion | flops 272105472 | bytes 4456449 | tf_op jit(solution)/shard_map/while/body/eval_jaxpr/kfts,iktfg->isfg/dot_general | solution.py:68
  60.9 1.1 %convolution_bitcast_fusion.3 = f32[4,2,128,128]{3,2,0,1:T(8,128)S(1)} fusion(bf16[8,128,2,128]{3,1,0,2:T(8,128)(2,1)S(1)} %copy-done.6, bf16[8,1,128,2,128]{2,4,1,0,3:T(8,128)(2,1)S(1)} %get-tuple-element.269, bf16[8,1,128,2,128]{2,4,1,0,3:T(8,128)(2,1)S(1)} %copy-done.1, bf16[8,1,128,2,128]{2,4,1,0,3:T(8,128)(2,1)S(1)} %copy-done.2, ...), kind=kOutput, calls=%fused_computation.4.clone.1 | convolution fusion | flops 271581184 | bytes 3145728 | tf_op jit(solution)/shard_map/while/body/eval_jaxpr/iktfg,isfg->kfts/dot_general | solution.py:71
  62.0 0.7 rev.25
  62.8 0.1 pad.125
  62.9 0.5 reshape.108
  63.4 1.0 %slice.145 = f32[4,2,32640]{2,0,1:T(4,128)} slice(f32[4,2,32768]{2,0,1:T(4,128)S(1)} %reshape.108), slice={[0:4], [0:2], [0:32640]} | slice | bytes 2088960 | tf_op jit(solution)/shard_map/while/body/eval_jaxpr/slice | solution.py:24
  64.4 2.8 %reshape.109 = f32[4,2,128,255]{3,2,0,1:T(8,128)S(1)} reshape(f32[4,2,32640]{2,0,1:T(4,128)} %slice.145) | data formatting | bytes 2088960 | tf_op jit(solution)/shard_map/while/body/eval_jaxpr/reshape | solution.py:25
  67.5 1.3 %broadcast_multiply_fusion = f32[8,128,2,128]{1,3,0,2:T(8,128)S(1)} fusion(f32[8,128,2,128]{1,3,0,2:T(8,128)} %get-tuple-element.161), kind=kLoop, calls=%fused_computation.33 | loop fusion | flops 262144 | bytes 2097152 | tf_op jit(solution)/shard_map/mul | solution.py:142
  68.8 0.6 copy.36
  69.4 0.6 multiply_bitcast_fusion
  70.0 3.6 %all-to-all-start.2 = ((f32[8,128,2]{1,2,0:T(2,128)}), f32[8,128,2]{1,2,0:T(2,128)S(1)}, u32[]{:S(2)}, u32[]{:S(2)}) async-start(f32[8,128,2]{1,2,0:T(2,128)} %multiply_bitcast_fusion), calls=%async_computation.2 | async-start | bytes 16384 | tf_op jit(solution)/shard_map/all_to_all | solution.py:148
  73.6 2.1 %copy_bitcast_fusion.3 = bf16[8,128,256]{1,2,0:T(8,128)(2,1)} fusion(f32[32,8,8,128]{3,2,1,0:T(8,128)S(1)} %bitcast.132, f32[256]{0:T(256)S(1)} %dynamic_slice.63, bf16[1024,514]{0,1:T(8,128)(2,1)} %bitcast.128), kind=kLoop, calls=%fused_computation.31 | loop fusion | flops 1048576 | bytes 2098176 | tf_op jit(solution)/shard_map/all_to_all | solution.py:146
  75.7 4.4 %all-to-all-done.2 = f32[8,128,2]{1,2,0:T(2,128)S(1)} async-done(((f32[8,128,2]{1,2,0:T(2,128)}), f32[8,128,2]{1,2,0:T(2,128)S(1)}, u32[]{:S(2)}, u32[]{:S(2)}) %all-to-all-start.2) | async-done | bytes 8224 | tf_op jit(solution)/shard_map/all_to_all | solution.py:148
  80.1 3.5 %all-to-all-start.1 = ((bf16[8,128,256]{1,2,0:T(8,128)(2,1)}), bf16[8,128,256]{1,2,0:T(8,128)(2,1)S(1)}, u32[]{:S(2)}, u32[]{:S(2)}) async-start(bf16[8,128,256]{1,2,0:T(8,128)(2,1)} %copy_bitcast_fusion.3), calls=%async_computation.1 | async-start | bytes 1048576 | tf_op jit(solution)/shard_map/all_to_all | solution.py:146
  83.6 13.4 %all-to-all-done.1 = bf16[8,128,256]{1,2,0:T(8,128)(2,1)S(1)} async-done(((bf16[8,128,256]{1,2,0:T(8,128)(2,1)}), bf16[8,128,256]{1,2,0:T(8,128)(2,1)S(1)}, u32[]{:S(2)}, u32[]{:S(2)}) %all-to-all-start.1) | async-done | bytes 524320 | tf_op jit(solution)/shard_map/all_to_all | solution.py:146
  97.1 1.0 %copy.39 = bf16[128,2048]{1,0:T(8,128)(2,1)} copy(bf16[128,2048]{0,1:T(8,128)(2,1)S(1)} %bitcast.133) | data formatting | bytes 1048576
  98.1 0.6 copy.79
  (44 shorter events, 1.0 us)
Async XLA Ops:
  0.6 1.9 %copy-start = (bf16[128,16]{0,1:T(8,128)(2,1)S(1)}, bf16[128,16]{0,1:T(8,128)(2,1)}, u32[]{:S(2)}) copy-start(bf16[128,16]{0,1:T(8,128)(2,1)} %param.12) | copy-start | bytes 12292
  0.6 1.4 %copy-start.4 = (bf16[128,2048]{1,0:T(8,128)(2,1)S(1)}, bf16[128,2048]{1,0:T(8,128)(2,1)}, u32[]{:S(2)}) copy-start(bf16[128,2048]{1,0:T(8,128)(2,1)} %param.10) | copy-start | bytes 1572868
  0.7 1.4 %copy-start.5 = (bf16[128,2048]{1,0:T(8,128)(2,1)S(1)}, bf16[128,2048]{1,0:T(8,128)(2,1)}, u32[]{:S(2)}) copy-start(bf16[128,2048]{1,0:T(8,128)(2,1)} %param.11) | copy-start | bytes 1572868
  4.2 33.4 %all-to-all-start = ((bf16[128,8,514]{0,2,1:T(8,128)(2,1)}), bf16[128,8,514]{0,2,1:T(8,128)(2,1)S(1)}, u32[]{:S(2)}, u32[]{:S(2)}) async-start(bf16[128,8,514]{0,2,1:T(8,128)(2,1)} %pad_maximum_fusion.4), calls=%async_computation | async-start | bytes 2129920 | tf_op jit(solution)/shard_map/all_to_all | solution.py:122
  38.1 1.0 copy-start.3
  44.1 3.2 %copy-start.1 = (bf16[8,1,128,2,128]{2,4,1,0,3:T(8,128)(2,1)S(1)}, bf16[8,1,128,2,128]{2,4,1,0,3:T(8,128)(2,1)}, u32[]{:S(2)}) copy-start(bf16[8,1,128,2,128]{2,4,1,0,3:T(8,128)(2,1)} %get-tuple-element.270) | copy-start | bytes 1572868 | tf_op jit(solution)/shard_map/while
  44.1 3.2 %copy-start.2 = (bf16[8,1,128,2,128]{2,4,1,0,3:T(8,128)(2,1)S(1)}, bf16[8,1,128,2,128]{2,4,1,0,3:T(8,128)(2,1)}, u32[]{:S(2)}) copy-start(bf16[8,1,128,2,128]{2,4,1,0,3:T(8,128)(2,1)} %get-tuple-element.271) | copy-start | bytes 1572868 | tf_op jit(solution)/shard_map/while
  44.2 3.1 %copy-start.6 = (bf16[8,128,2,128]{3,1,0,2:T(8,128)(2,1)S(1)}, bf16[8,128,2,128]{3,1,0,2:T(8,128)(2,1)}, u32[]{:S(2)}) copy-start(bf16[8,128,2,128]{3,1,0,2:T(8,128)(2,1)} %get-tuple-element.326) | copy-start | bytes 1572868 | tf_op jit(solution)/shard_map/while
  57.4 3.5 %copy-start.1 = (bf16[8,1,128,2,128]{2,4,1,0,3:T(8,128)(2,1)S(1)}, bf16[8,1,128,2,128]{2,4,1,0,3:T(8,128)(2,1)}, u32[]{:S(2)}) copy-start(bf16[8,1,128,2,128]{2,4,1,0,3:T(8,128)(2,1)} %get-tuple-element.270) | copy-start | bytes 1572868 | tf_op jit(solution)/shard_map/while
  57.4 3.5 %copy-start.2 = (bf16[8,1,128,2,128]{2,4,1,0,3:T(8,128)(2,1)S(1)}, bf16[8,1,128,2,128]{2,4,1,0,3:T(8,128)(2,1)}, u32[]{:S(2)}) copy-start(bf16[8,1,128,2,128]{2,4,1,0,3:T(8,128)(2,1)} %get-tuple-element.271) | copy-start | bytes 1572868 | tf_op jit(solution)/shard_map/while
  57.4 3.5 %copy-start.6 = (bf16[8,128,2,128]{3,1,0,2:T(8,128)(2,1)S(1)}, bf16[8,128,2,128]{3,1,0,2:T(8,128)(2,1)}, u32[]{:S(2)}) copy-start(bf16[8,128,2,128]{3,1,0,2:T(8,128)(2,1)} %get-tuple-element.326) | copy-start | bytes 1572868 | tf_op jit(solution)/shard_map/while
  70.0 10.1 %all-to-all-start.2 = ((f32[8,128,2]{1,2,0:T(2,128)}), f32[8,128,2]{1,2,0:T(2,128)S(1)}, u32[]{:S(2)}, u32[]{:S(2)}) async-start(f32[8,128,2]{1,2,0:T(2,128)} %multiply_bitcast_fusion), calls=%async_computation.2 | async-start | bytes 16384 | tf_op jit(solution)/shard_map/all_to_all | solution.py:148
  80.1 16.9 %all-to-all-start.1 = ((bf16[8,128,256]{1,2,0:T(8,128)(2,1)}), bf16[8,128,256]{1,2,0:T(8,128)(2,1)S(1)}, u32[]{:S(2)}, u32[]{:S(2)}) async-start(bf16[8,128,256]{1,2,0:T(8,128)(2,1)} %copy_bitcast_fusion.3), calls=%async_computation.1 | async-start | bytes 1048576 | tf_op jit(solution)/shard_map/all_to_all | solution.py:146

commit v2 on v1

v2 whole, which is shorter than its diff:
```python
import functools
import math

import jax
import jax.numpy as jnp
import numpy as np
from jax import lax
from jax.experimental import pallas as pl
from jax.experimental.pallas import tpu as pltpu
from jax.sharding import PartitionSpec as P


def local_kernel(g_ref, x_ref, v_ref, gain_ref, out_ref, diag_ref, *, nb, br, scale):
    n = nb * br
    width = n + br
    taps_row = jnp.broadcast_to(v_ref[...], (br, width))
    toeplitz = pltpu.roll(taps_row, width - br, 1, stride=1, stride_axis=0)
    toeplitz = toeplitz[:, :n].astype(jnp.bfloat16)
    gain = gain_ref[...]
    for i in range(nb):
        conv = jnp.dot(
            toeplitz[:, : n - i * br], g_ref[i * br :, :], preferred_element_type=jnp.float32
        )
        own = g_ref[i * br : (i + 1) * br, :].astype(jnp.float32)
        out_ref[i * br : (i + 1) * br, :] = (conv * scale + gain * own).astype(out_ref.dtype)
    sums = [None] * nb
    for j in range(nb):
        row = lax.dot_general(
            g_ref[j * br : (j + 1) * br, :],
            x_ref[: (j + 1) * br, :],
            (((1,), (1,)), ((), ())),
            preferred_element_type=jnp.float32,
        )
        for i in range(j + 1):
            piece = row[:, i * br : (i + 1) * br]
            sums[j - i] = piece if sums[j - i] is None else sums[j - i] + piece
    zeros = jnp.zeros((br, br), jnp.float32)
    for k in range(nb):
        padded = jnp.concatenate([sums[k], zeros], axis=1)
        skewed = pltpu.roll(padded, 0, 1, stride=1, stride_axis=0)
        diag_ref[k : k + 1, :] = jnp.sum(skewed, axis=0, keepdims=True)


def local_grads(moved_grad, moved_input, stretch_taps, stretch_gain, nb, br, sf, sg, scale):
    n = nb * br
    width = n + br
    taps_rows = jnp.pad(jnp.transpose(stretch_taps).astype(jnp.float32), ((0, 0), (br, 0)))
    return pl.pallas_call(
        functools.partial(local_kernel, nb=nb, br=br, scale=scale),
        grid=(sf,),
        in_specs=[
            pl.BlockSpec((n, sg), lambda f: (0, f)),
            pl.BlockSpec((n, sg), lambda f: (0, f)),
            pl.BlockSpec((None, 1, width), lambda f: (f, 0, 0)),
            pl.BlockSpec((None, 1, sg), lambda f: (f, 0, 0)),
        ],
        out_specs=[
            pl.BlockSpec((n, sg), lambda f: (0, f)),
            pl.BlockSpec((None, nb, 2 * br), lambda f: (f, 0, 0)),
        ],
        out_shape=[
            jax.ShapeDtypeStruct((n, sf * sg), jnp.bfloat16),
            jax.ShapeDtypeStruct((sf, nb, 2 * br), jnp.float32),
        ],
    )(moved_grad, moved_input, taps_rows[:, None, :], stretch_gain.reshape(sf, 1, sg))


def per_device(cached_input, cached_gate, out_grad, filter_taps, skip_gain):
    block_rows = cached_input.shape[0]
    chan_width = cached_input.shape[1]
    filters = filter_taps.shape[1]
    group_width = chan_width // filters
    seq_count = lax.axis_size("seq")
    seq_index = lax.axis_index("seq")
    length = block_rows * seq_count
    taps_scale = 1.0 / math.sqrt(length)
    gated_grad = (out_grad.astype(jnp.float32) * cached_gate.astype(jnp.float32)).astype(
        jnp.bfloat16
    )
    stretch_width = chan_width // seq_count
    stretch_filters = max(1, stretch_width // group_width)
    stretch_group = stretch_width // stretch_filters
    tap_columns = np.array(
        [
            (target * stretch_width) // group_width + offset
            for target in range(seq_count)
            for offset in range(stretch_filters)
        ]
    )
    routed_taps = filter_taps[:, tap_columns].reshape(block_rows, seq_count, stretch_filters)
    packed = jnp.concatenate(
        [
            gated_grad.reshape(block_rows, seq_count, stretch_width),
            cached_input[::-1].reshape(block_rows, seq_count, stretch_width),
            routed_taps,
        ],
        axis=2,
    )
    moved = lax.all_to_all(packed, "seq", split_axis=1, concat_axis=0, tiled=True)
    moved = moved.reshape(length, 2 * stretch_width + stretch_filters)
    moved_grad = moved[:, :stretch_width]
    moved_input = moved[:, stretch_width : 2 * stretch_width]
    stretch_taps = moved[:, 2 * stretch_width :]
    stretch_gain = lax.dynamic_slice_in_dim(skip_gain, seq_index * stretch_width, stretch_width, 0)
    local_grad, diag = local_grads(
        moved_grad,
        moved_input,
        stretch_taps,
        stretch_gain,
        seq_count,
        block_rows,
        stretch_filters,
        stretch_group,
        taps_scale,
    )
    input_grad = lax.all_to_all(local_grad, "seq", split_axis=0, concat_axis=1, tiled=True)
    front = jnp.pad(diag[:, :, :block_rows], ((0, 0), (0, 1), (0, 0)))
    back = jnp.pad(diag[:, :, block_rows:], ((0, 0), (1, 0), (0, 0)))
    lag_sums = (front + back).reshape(stretch_filters, (seq_count + 1) * block_rows)
    stretch_term = (
        jnp.transpose(lag_sums[:, block_rows - 1 : block_rows - 1 + length]) * taps_scale
    )
    lag_parts = lax.all_to_all(
        stretch_term.reshape(seq_count, block_rows, stretch_filters),
        "seq",
        split_axis=0,
        concat_axis=0,
        tiled=True,
    )
    sharers = seq_count * stretch_filters // filters
    filter_grad = (
        jnp.transpose(lag_parts, (1, 0, 2))
        .reshape(block_rows, filters, sharers)
        .sum(axis=2)
    )
    return (input_grad, filter_grad)


def solution(mesh):
    return jax.shard_map(
        per_device,
        mesh=mesh,
        in_specs=(
            P(("groups", "seq"), "chan"),
            P(("groups", "seq"), "chan"),
            P(("groups", "seq"), "chan"),
            P("seq", "chan"),
            P("chan"),
        ),
        out_specs=(P(("groups", "seq"), "chan"), P(("groups", "seq"), "chan")),
        check_vma=False,
    )
```

time: 99.2 us -> 79.8 us (0.80)
  local copies, waits for them, and re-layouts: 25.7 us -> 14.2 us
  blocking collectives: 0 us -> 9.9 us
  matrix products: 8.83 us -> 0 us
  waiting for transfers between devices: 43.2 us -> 38.2 us
  other arithmetic: 5.49 us -> 1.27 us
  Pallas kernels: 0 us -> 3.8 us
  starting transfers between devices: 14.4 us -> 10.8 us
    all_to_all x0 -> x1, blocking collectives: none -> 9.9 us  [per_device(): lax.all_to_all(stretch_term.reshape(seq_count, block_rows, stretch_filter...]
    reshape x7 -> x0, local copies, waits for them, and re-layouts: 9.89 us -> none  [the longest x2 5.62 us: diagonal_sums(): trimmed.reshape(products.shape[0], products.shape[1], block_rows, 2 * blo...]
    dot_general x4 -> x0, matrix products: 8.83 us -> none  [the longest x2 6.6 us: advance(): jnp.einsum('kfts,iktfg->isfg', toeplitz, stacked, preferred_element_type=...]
    rev x4 -> x2, local copies, waits for them, and re-layouts: 1.86 us -> 6.67 us  [per_device(): cached_input[::-1].reshape(block_rows, seq_count, stretch_width)]
    unnamed x17 -> x10, local copies, waits for them, and re-layouts: 5.54 us -> 0.97 us
    all_to_all x1 -> x0, waiting for transfers between devices: 4.37 us -> none  [per_device(): lax.all_to_all(stretch_term.reshape(seq_count, block_rows, stretch_filter...]
    pallas_call x0 -> x1, Pallas kernels: none -> 3.8 us  [local_grads(): pl.pallas_call(functools.partial(local_kernel, nb=nb, br=br, scale=scale)...]
    all_to_all x1 -> x0, starting transfers between devices: 3.59 us -> none  [per_device(): lax.all_to_all(stretch_term.reshape(seq_count, block_rows, stretch_filter...]
  transfers between devices with their start and end apart: 3 -> 2, of which waited for: 3 -> 2; matrix products, arithmetic and copies ran while one was open for 3% -> 2% of each run, Pallas kernels for 0% -> 0%
where the time goes in v2:
time: 79.8 us; the launch traced here: 78.9 us
  waiting for transfers between devices  38.2 us (48%)
  local copies, waits for them, and re-layouts  14.2 us (18%)
  starting transfers between devices  10.8 us (14%)
  blocking collectives  9.9 us (12%)
  Pallas kernels  3.8 us (5%)
  other arithmetic  1.27 us (2%)
    all_to_all x1, waiting for transfers between devices, per_device(): lax.all_to_all(packed, 'seq', split_axis=1, concat_axis=0, tiled=True)  24.8 us
    all_to_all x1, waiting for transfers between devices, per_device(): lax.all_to_all(local_grad, 'seq', split_axis=0, concat_axis=1, tiled=True)  13.4 us
    all_to_all x1, blocking collectives, per_device(): lax.all_to_all(stretch_term.reshape(seq_count, block_rows, stretch_filter...  9.9 us
    all_to_all x1, starting transfers between devices, per_device(): lax.all_to_all(packed, 'seq', split_axis=1, concat_axis=0, tiled=True)  7.28 us
    rev x2, local copies, waits for them, and re-layouts, per_device(): cached_input[::-1].reshape(block_rows, seq_count, stretch_width)  6.67 us
    pallas_call x1, Pallas kernels, local_grads(): pl.pallas_call(functools.partial(local_kernel, nb=nb, br=br, scale=scale)...  3.8 us
    all_to_all x1, starting transfers between devices, per_device(): lax.all_to_all(local_grad, 'seq', split_axis=0, concat_axis=1, tiled=True)  3.49 us
  transfers between devices with their start and end apart: 2, of which 2 were waited for; matrix products, arithmetic and copies ran while one was open for 2% of the time, Pallas kernels for 0%

profile of v2, /device:TPU:0, one launch (start us, length us, event | category | flops | bytes accessed | tf_op | source)
XLA Modules:
  0.0 78.9 jit_solution(17042155005901986760)
XLA Ops:
  0.6 0.0 copy-start
  0.6 0.0 copy-start.2
  0.7 0.0 copy-start.1
  0.7 6.4 %rev.3 = bf16[128,2048]{1,0:T(8,128)(2,1)S(1)} reverse(bf16[128,2048]{1,0:T(8,128)(2,1)} %param.7), dimensions={0} | reverse | bytes 1048576 | tf_op jit(solution)/shard_map/rev | solution.py:94
  7.1 0.3 copy.24
  7.4 0.0 copy-done.2
  7.4 0.0 copy-done.1
  7.4 0.1 multiply_convert_fusion
  7.5 0.3 copy.23
  7.8 0.0 copy-done
  7.8 0.6 gather_fusion
  8.4 1.1 %pad_maximum_fusion = bf16[128,8,514]{0,2,1:T(8,128)(2,1)} fusion(bf16[128,8,2]{0,2,1:T(2,128)(2,1)S(1)} %bitcast.45, bf16[128,8,256]{0,2,1:T(8,128)(2,1)S(1)} %bitcast.41, bf16[128,8,256]{0,2,1:T(8,128)(2,1)S(1)} %bitcast.42), kind=kLoop, calls=%fused_computation.1 | loop fusion | flops 3158016 | bytes 2105344 | tf_op jit(solution)/shard_map/concatenate | solution.py:91
  9.4 7.3 %all-to-all-start = ((bf16[128,8,514]{0,2,1:T(8,128)(2,1)}), bf16[128,8,514]{0,2,1:T(8,128)(2,1)S(1)}, u32[]{:S(2)}, u32[]{:S(2)}) async-start(bf16[128,8,514]{0,2,1:T(8,128)(2,1)} %pad_maximum_fusion), calls=%async_computation | async-start | bytes 2129920 | tf_op jit(solution)/shard_map/all_to_all | solution.py:99
  16.7 1.3 %dynamic_slice.3 = f32[256]{0:T(256)} dynamic-slice(f32[2048]{0:T(1024)} %param.11, s32[]{:T(128)S(6)} %select_n.7), dynamic_slice_sizes={256} | dynamic-slice | bytes 2052 | tf_op jit(solution)/shard_map/dynamic_slice | solution.py:104
  18.1 24.8 %all-to-all-done = bf16[128,8,514]{0,2,1:T(8,128)(2,1)S(1)} async-done(((bf16[128,8,514]{0,2,1:T(8,128)(2,1)}), bf16[128,8,514]{0,2,1:T(8,128)(2,1)S(1)}, u32[]{:S(2)}, u32[]{:S(2)}) %all-to-all-start) | async-done | bytes 1052704 | tf_op jit(solution)/shard_map/all_to_all | solution.py:99
  42.9 0.1 copy.35
  43.0 0.1 pad.20
  43.1 0.3 copy.31
  43.4 0.1 fusion.1
  43.4 1.0 %copy.27.x_ref = bf16[1024,256]{1,0:T(8,128)(2,1)} copy(bf16[1024,256]{0,1:T(8,128)(2,1)S(1)} %get-tuple-element.6) | data formatting | bytes 1048576 | tf_op jit(solution)/shard_map/slice | solution.py:102
  44.5 0.6 reshape.39.v_ref
  45.1 1.0 %copy.26.g_ref = bf16[1024,256]{1,0:T(8,128)(2,1)} copy(bf16[1024,256]{0,1:T(8,128)(2,1)S(1)} %get-tuple-element.7) | data formatting | bytes 1048576 | tf_op jit(solution)/shard_map/slice | solution.py:101
  46.1 3.8 %shard_map.86 = (bf16[1024,256]{1,0:T(8,128)(2,1)}, f32[2,8,256]{2,1,0:T(8,128)}) custom-call(bf16[1024,256]{1,0:T(8,128)(2,1)} %copy.26.g_ref, bf16[1024,256]{1,0:T(8,128)(2,1)} %copy.27.x_ref, f32[2,1,1152]{2,1,0:T(1,128)} %reshape.39.v_ref, f32[2,1,128]{2,1,0:T(1,128)} %bitcast.48), custom_call_target="tpu_custom_call" | custom-call | tf_op jit(solution)/shard_map/pallas_call | solution.py:48
  49.9 0.7 fusion.2
  50.6 0.1 fusion
  50.7 9.9 %all_to_all.39 = f32[8,128,2]{1,2,0:T(2,128)S(1)} all-to-all(f32[8,128,2]{1,2,0:T(2,128)S(1)} %fusion), channel_id=1, replica_groups=mesh['groups'=2,'seq'=8,'chan'=2] {'seq'}, dimensions={0} | all-to-all | bytes 16384 | tf_op jit(solution)/shard_map/all_to_all | solution.py:123
  60.6 3.5 %all-to-all-start.1 = ((bf16[8,128,256]{2,1,0:T(8,128)(2,1)}), bf16[8,128,256]{2,1,0:T(8,128)(2,1)S(1)}, u32[]{:S(2)}, u32[]{:S(2)}) async-start(bf16[8,128,256]{2,1,0:T(8,128)(2,1)} %bitcast.43), calls=%async_computation.1 | async-start | bytes 1048576 | tf_op jit(solution)/shard_map/all_to_all | solution.py:116
  64.1 13.4 %all-to-all-done.1 = bf16[8,128,256]{2,1,0:T(8,128)(2,1)S(1)} async-done(((bf16[8,128,256]{2,1,0:T(8,128)(2,1)}), bf16[8,128,256]{2,1,0:T(8,128)(2,1)S(1)}, u32[]{:S(2)}, u32[]{:S(2)}) %all-to-all-start.1) | async-done | bytes 524320 | tf_op jit(solution)/shard_map/all_to_all | solution.py:116
  77.5 0.8 %copy.30 = bf16[8,16,8,256]{3,2,0,1:T(8,128)(2,1)} copy(bf16[8,16,8,256]{3,2,1,0:T(8,128)(2,1)S(1)} %bitcast.40) | data formatting | bytes 1048576 | tf_op jit(solution)/shard_map/all_to_all | solution.py:116
  78.3 0.6 copy.38
  (6 shorter events, 0.0 us)
Async XLA Ops:
  0.6 7.2 %copy-start = (bf16[128,16]{0,1:T(8,128)(2,1)S(1)}, bf16[128,16]{0,1:T(8,128)(2,1)}, u32[]{:S(2)}) copy-start(bf16[128,16]{0,1:T(8,128)(2,1)} %param.10) | copy-start | bytes 12292
  0.6 6.7 %copy-start.2 = (bf16[128,2048]{1,0:T(8,128)(2,1)S(1)}, bf16[128,2048]{1,0:T(8,128)(2,1)}, u32[]{:S(2)}) copy-start(bf16[128,2048]{1,0:T(8,128)(2,1)} %param.9) | copy-start | bytes 1572868
  0.7 6.7 %copy-start.1 = (bf16[128,2048]{1,0:T(8,128)(2,1)S(1)}, bf16[128,2048]{1,0:T(8,128)(2,1)}, u32[]{:S(2)}) copy-start(bf16[128,2048]{1,0:T(8,128)(2,1)} %param.8) | copy-start | bytes 1572868
  9.4 33.4 %all-to-all-start = ((bf16[128,8,514]{0,2,1:T(8,128)(2,1)}), bf16[128,8,514]{0,2,1:T(8,128)(2,1)S(1)}, u32[]{:S(2)}, u32[]{:S(2)}) async-start(bf16[128,8,514]{0,2,1:T(8,128)(2,1)} %pad_maximum_fusion), calls=%async_computation | async-start | bytes 2129920 | tf_op jit(solution)/shard_map/all_to_all | solution.py:99
  60.6 16.9 %all-to-all-start.1 = ((bf16[8,128,256]{2,1,0:T(8,128)(2,1)}), bf16[8,128,256]{2,1,0:T(8,128)(2,1)S(1)}, u32[]{:S(2)}, u32[]{:S(2)}) async-start(bf16[8,128,256]{2,1,0:T(8,128)(2,1)} %bitcast.43), calls=%async_computation.1 | async-start | bytes 1048576 | tf_op jit(solution)/shard_map/all_to_all | solution.py:116

commit v3 on v2

--- a/solution.py
+++ b/solution.py
@@ -10,7 +10,7 @@
 from jax.sharding import PartitionSpec as P
 
 
-def local_kernel(g_ref, x_ref, v_ref, gain_ref, out_ref, diag_ref, *, nb, br, scale):
+def local_kernel(g_ref, x_ref, v_ref, gain_ref, out_ref, diag_ref, xrev_ref, *, nb, br, scale):
     n = nb * br
     width = n + br
     taps_row = jnp.broadcast_to(v_ref[...], (br, width))
@@ -23,11 +23,18 @@
         )
         own = g_ref[i * br : (i + 1) * br, :].astype(jnp.float32)
         out_ref[i * br : (i + 1) * br, :] = (conv * scale + gain * own).astype(out_ref.dtype)
+    rows = lax.broadcasted_iota(jnp.int32, (br, br), 0)
+    cols = lax.broadcasted_iota(jnp.int32, (br, br), 1)
+    flip = (rows + cols == br - 1).astype(jnp.bfloat16)
+    for i in range(nb):
+        xrev_ref[i * br : (i + 1) * br, :] = jnp.dot(
+            flip, x_ref[i * br : (i + 1) * br, :], preferred_element_type=jnp.float32
+        ).astype(xrev_ref.dtype)
     sums = [None] * nb
     for j in range(nb):
         row = lax.dot_general(
             g_ref[j * br : (j + 1) * br, :],
-            x_ref[: (j + 1) * br, :],
+            xrev_ref[: (j + 1) * br, :],
             (((1,), (1,)), ((), ())),
             preferred_element_type=jnp.float32,
         )
@@ -62,6 +69,7 @@
             jax.ShapeDtypeStruct((n, sf * sg), jnp.bfloat16),
             jax.ShapeDtypeStruct((sf, nb, 2 * br), jnp.float32),
         ],
+        scratch_shapes=[pltpu.VMEM((n, sg), jnp.bfloat16)],
     )(moved_grad, moved_input, taps_rows[:, None, :], stretch_gain.reshape(sf, 1, sg))
 
 
@@ -91,7 +99,7 @@
     packed = jnp.concatenate(
         [
             gated_grad.reshape(block_rows, seq_count, stretch_width),
-            cached_input[::-1].reshape(block_rows, seq_count, stretch_width),
+            cached_input.reshape(block_rows, seq_count, stretch_width),
             routed_taps,
         ],
         axis=2,
@@ -113,26 +121,31 @@
         stretch_group,
         taps_scale,
     )
-    input_grad = lax.all_to_all(local_grad, "seq", split_axis=0, concat_axis=1, tiled=True)
     front = jnp.pad(diag[:, :, :block_rows], ((0, 0), (0, 1), (0, 0)))
     back = jnp.pad(diag[:, :, block_rows:], ((0, 0), (1, 0), (0, 0)))
     lag_sums = (front + back).reshape(stretch_filters, (seq_count + 1) * block_rows)
     stretch_term = (
         jnp.transpose(lag_sums[:, block_rows - 1 : block_rows - 1 + length]) * taps_scale
     )
-    lag_parts = lax.all_to_all(
-        stretch_term.reshape(seq_count, block_rows, stretch_filters),
-        "seq",
-        split_axis=0,
-        concat_axis=0,
-        tiled=True,
+    high = lax.reduce_precision(stretch_term, exponent_bits=8, mantissa_bits=7)
+    rest = stretch_term - high
+    middle = lax.reduce_precision(rest, exponent_bits=8, mantissa_bits=7)
+    low = rest - middle
+    outgoing = jnp.concatenate(
+        [local_grad, high.astype(jnp.bfloat16), middle.astype(jnp.bfloat16), low.astype(jnp.bfloat16)],
+        axis=1,
+    )
+    returned = lax.all_to_all(outgoing, "seq", split_axis=0, concat_axis=1, tiled=True)
+    returned = returned.reshape(block_rows, seq_count, stretch_width + 3 * stretch_filters)
+    input_grad = returned[:, :, :stretch_width].reshape(block_rows, chan_width)
+    parts = returned[:, :, stretch_width:].astype(jnp.float32)
+    lag_parts = (
+        parts[:, :, :stretch_filters]
+        + parts[:, :, stretch_filters : 2 * stretch_filters]
+        + parts[:, :, 2 * stretch_filters :]
     )
     sharers = seq_count * stretch_filters // filters
-    filter_grad = (
-        jnp.transpose(lag_parts, (1, 0, 2))
-        .reshape(block_rows, filters, sharers)
-        .sum(axis=2)
-    )
+    filter_grad = lag_parts.reshape(block_rows, filters, sharers).sum(axis=2)
     return (input_grad, filter_grad)
 
 

time: 79.8 us -> 68.1 us (0.85)
  waiting for transfers between devices: 38.2 us -> 24.8 us
  blocking collectives: 9.9 us -> 19.2 us
  local copies, waits for them, and re-layouts: 14.2 us -> 9.26 us
  starting transfers between devices: 10.8 us -> 7.28 us
  other arithmetic: 1.27 us -> 2.25 us
    all_to_all x1 -> x0, waiting for transfers between devices: 13.4 us -> none  [per_device(): lax.all_to_all(local_grad, 'seq', split_axis=0, concat_axis=1, tiled=True)]
    all_to_all x1, blocking collectives: 9.9 us -> 19.2 us  [per_device(): lax.all_to_all(outgoing, 'seq', split_axis=0, concat_axis=1, tiled=True)]
    rev x2 -> x0, local copies, waits for them, and re-layouts: 6.67 us -> none  [per_device(): cached_input[::-1].reshape(block_rows, seq_count, stretch_width)]
    all_to_all x1 -> x0, starting transfers between devices: 3.49 us -> none  [per_device(): lax.all_to_all(local_grad, 'seq', split_axis=0, concat_axis=1, tiled=True)]
    unnamed x10 -> x12, local copies, waits for them, and re-layouts: 0.97 us -> 2.79 us
  transfers between devices with their start and end apart: 2 -> 1, of which waited for: 2 -> 1; matrix products, arithmetic and copies ran while one was open for 2% -> 2% of each run, Pallas kernels for 0% -> 0%
where the time goes in v3:
time: 68.1 us; the launch traced here: 67.8 us
  waiting for transfers between devices  24.8 us (36%)
  blocking collectives  19.2 us (28%)
  local copies, waits for them, and re-layouts  9.26 us (14%)
  starting transfers between devices  7.28 us (11%)
  Pallas kernels  4.12 us (6%)
  other arithmetic  2.25 us (3%)
  between operations  0.8 us (1%)
    all_to_all x1, waiting for transfers between devices, per_device(): lax.all_to_all(packed, 'seq', split_axis=1, concat_axis=0, tiled=True)  24.8 us
    all_to_all x1, blocking collectives, per_device(): lax.all_to_all(outgoing, 'seq', split_axis=0, concat_axis=1, tiled=True)  19.2 us
    all_to_all x1, starting transfers between devices, per_device(): lax.all_to_all(packed, 'seq', split_axis=1, concat_axis=0, tiled=True)  7.28 us
    pallas_call x1, Pallas kernels, local_grads(): pl.pallas_call(functools.partial(local_kernel, nb=nb, br=br, scale=scale)...  4.12 us
    unnamed x12, local copies, waits for them, and re-layouts  2.79 us
  transfers between devices with their start and end apart: 1, of which 1 were waited for; matrix products, arithmetic and copies ran while one was open for 2% of the time, Pallas kernels for 0%

profile of v3, /device:TPU:0, one launch (start us, length us, event | category | flops | bytes accessed | tf_op | source)
XLA Modules:
  0.0 67.8 jit_solution(15563736549481232504)
XLA Ops:
  0.6 0.0 copy-start
  0.6 0.0 copy-start.2
  0.7 0.0 copy-start.1
  0.7 1.4 %copy.34 = bf16[128,2048]{0,1:T(8,128)(2,1)S(1)} copy(bf16[128,2048]{1,0:T(8,128)(2,1)} %param.7) | data formatting | bytes 1048576 | tf_op args[0]
  2.1 0.0 copy-done.2
  2.1 0.0 copy-done.1
  2.1 0.1 multiply_convert_fusion
  2.3 0.3 copy.33
  2.6 0.0 copy-done
  2.6 0.6 gather_fusion
  3.1 1.1 %pad_maximum_fusion = bf16[128,8,514]{0,2,1:T(8,128)(2,1)} fusion(bf16[128,8,2]{0,2,1:T(2,128)(2,1)S(1)} %bitcast.46, bf16[128,8,256]{0,2,1:T(8,128)(2,1)S(1)} %bitcast.44, bf16[128,8,256]{0,2,1:T(8,128)(2,1)S(1)} %bitcast.45), kind=kLoop, calls=%fused_computation.1 | loop fusion | flops 3158016 | bytes 2105344 | tf_op jit(solution)/shard_map/concatenate | solution.py:99
  4.2 7.3 %all-to-all-start = ((bf16[128,8,514]{0,2,1:T(8,128)(2,1)}), bf16[128,8,514]{0,2,1:T(8,128)(2,1)S(1)}, u32[]{:S(2)}, u32[]{:S(2)}) async-start(bf16[128,8,514]{0,2,1:T(8,128)(2,1)} %pad_maximum_fusion), calls=%async_computation | async-start | bytes 2129920 | tf_op jit(solution)/shard_map/all_to_all | solution.py:107
  11.5 1.3 %dynamic_slice.3 = f32[256]{0:T(256)} dynamic-slice(f32[2048]{0:T(1024)} %param.11, s32[]{:T(128)S(6)} %select_n.7), dynamic_slice_sizes={256} | dynamic-slice | bytes 2052 | tf_op jit(solution)/shard_map/dynamic_slice | solution.py:112
  12.8 24.8 %all-to-all-done = bf16[128,8,514]{0,2,1:T(8,128)(2,1)S(1)} async-done(((bf16[128,8,514]{0,2,1:T(8,128)(2,1)}), bf16[128,8,514]{0,2,1:T(8,128)(2,1)S(1)}, u32[]{:S(2)}, u32[]{:S(2)}) %all-to-all-start) | async-done | bytes 1052704 | tf_op jit(solution)/shard_map/all_to_all | solution.py:107
  37.6 0.1 copy.44
  37.7 0.1 pad.24
  37.8 0.3 copy.42
  38.1 0.1 fusion.2
  38.2 1.0 %copy.37.x_ref = bf16[1024,256]{1,0:T(8,128)(2,1)} copy(bf16[1024,256]{0,1:T(8,128)(2,1)S(1)} %get-tuple-element.10) | data formatting | bytes 1048576 | tf_op jit(solution)/shard_map/slice | solution.py:110
  39.2 0.6 reshape.41.v_ref
  39.8 1.0 %copy.36.g_ref = bf16[1024,256]{1,0:T(8,128)(2,1)} copy(bf16[1024,256]{0,1:T(8,128)(2,1)S(1)} %get-tuple-element.11) | data formatting | bytes 1048576 | tf_op jit(solution)/shard_map/slice | solution.py:109
  40.8 4.1 %shard_map.86 = (bf16[1024,256]{1,0:T(8,128)(2,1)}, f32[2,8,256]{2,1,0:T(8,128)}) custom-call(bf16[1024,256]{1,0:T(8,128)(2,1)} %copy.36.g_ref, bf16[1024,256]{1,0:T(8,128)(2,1)} %copy.37.x_ref, f32[2,1,1152]{2,1,0:T(1,128)} %reshape.41.v_ref, f32[2,1,128]{2,1,0:T(1,128)} %bitcast.48), custom_call_target="tpu_custom_call" | custom-call | tf_op jit(solution)/shard_map/pallas_call | solution.py:55
  44.9 0.0 copy-start.3
  44.9 0.8 %fusion.3 = (f32[2,8,128]{2,1,0:T(8,128)S(1)}, f32[2,8,128]{2,1,0:T(8,128)S(1)}) fusion(f32[2,8,256]{2,1,0:T(8,128)} %get-tuple-element.5), kind=kLoop, calls=%fused_computation.20 | loop fusion | bytes 32768 | tf_op jit(solution)/shard_map/slice | solution.py:124
  45.7 0.2 copy.41
  46.0 0.2 reduce-precision_convert_fusion.1
  46.2 0.0 copy-done.3
  46.2 0.3 pad_maximum_fusion.1
  46.4 0.4 copy.39
  46.8 19.2 %all_to_all.31 = bf16[8,128,262]{1,2,0:T(8,128)(2,1)S(1)} all-to-all(bf16[8,128,262]{1,2,0:T(8,128)(2,1)S(1)} %copy.39), channel_id=1, replica_groups=mesh['groups'=2,'seq'=8,'chan'=2] {'seq'}, dimensions={0} | all-to-all | bytes 1073152 | tf_op jit(solution)/shard_map/all_to_all | solution.py:138
  66.1 0.6 slice_add_fusion
  66.7 1.0 %copy.40 = bf16[128,2048]{1,0:T(8,128)(2,1)} copy(bf16[128,2048]{0,1:T(8,128)(2,1)S(1)} %bitcast.43) | data formatting | bytes 1048576
  (7 shorter events, 0.1 us)
Async XLA Ops:
  0.6 1.9 %copy-start = (bf16[128,16]{0,1:T(8,128)(2,1)S(1)}, bf16[128,16]{0,1:T(8,128)(2,1)}, u32[]{:S(2)}) copy-start(bf16[128,16]{0,1:T(8,128)(2,1)} %param.10) | copy-start | bytes 12292
  0.6 1.5 %copy-start.2 = (bf16[128,2048]{1,0:T(8,128)(2,1)S(1)}, bf16[128,2048]{1,0:T(8,128)(2,1)}, u32[]{:S(2)}) copy-start(bf16[128,2048]{1,0:T(8,128)(2,1)} %param.9) | copy-start | bytes 1572868
  0.7 1.5 %copy-start.1 = (bf16[128,2048]{1,0:T(8,128)(2,1)S(1)}, bf16[128,2048]{1,0:T(8,128)(2,1)}, u32[]{:S(2)}) copy-start(bf16[128,2048]{1,0:T(8,128)(2,1)} %param.8) | copy-start | bytes 1572868
  4.2 33.4 %all-to-all-start = ((bf16[128,8,514]{0,2,1:T(8,128)(2,1)}), bf16[128,8,514]{0,2,1:T(8,128)(2,1)S(1)}, u32[]{:S(2)}, u32[]{:S(2)}) async-start(bf16[128,8,514]{0,2,1:T(8,128)(2,1)} %pad_maximum_fusion), calls=%async_computation | async-start | bytes 2129920 | tf_op jit(solution)/shard_map/all_to_all | solution.py:107
  44.9 1.2 %copy-start.3 = (bf16[1024,256]{1,0:T(8,128)(2,1)S(1)}, bf16[1024,256]{1,0:T(8,128)(2,1)}, u32[]{:S(2)}) copy-start(bf16[1024,256]{1,0:T(8,128)(2,1)} %get-tuple-element.4) | copy-start | bytes 1572868

commit v4 on v3

--- a/solution.py
+++ b/solution.py
@@ -48,16 +48,21 @@
         diag_ref[k : k + 1, :] = jnp.sum(skewed, axis=0, keepdims=True)
 
 
-def local_grads(moved_grad, moved_input, stretch_taps, stretch_gain, nb, br, sf, sg, scale):
+def local_grads(moved, stretch_taps, stretch_gain, nb, br, sf, sg, scale):
     n = nb * br
     width = n + br
+    sw = sf * sg
+    if sg % 128 == 0:
+        grad_in, input_in, input_base = moved, moved, sf
+    else:
+        grad_in, input_in, input_base = moved[:, :sw], moved[:, sw : 2 * sw], 0
     taps_rows = jnp.pad(jnp.transpose(stretch_taps).astype(jnp.float32), ((0, 0), (br, 0)))
     return pl.pallas_call(
         functools.partial(local_kernel, nb=nb, br=br, scale=scale),
         grid=(sf,),
         in_specs=[
             pl.BlockSpec((n, sg), lambda f: (0, f)),
-            pl.BlockSpec((n, sg), lambda f: (0, f)),
+            pl.BlockSpec((n, sg), lambda f: (0, input_base + f)),
             pl.BlockSpec((None, 1, width), lambda f: (f, 0, 0)),
             pl.BlockSpec((None, 1, sg), lambda f: (f, 0, 0)),
         ],
@@ -66,11 +71,11 @@
             pl.BlockSpec((None, nb, 2 * br), lambda f: (f, 0, 0)),
         ],
         out_shape=[
-            jax.ShapeDtypeStruct((n, sf * sg), jnp.bfloat16),
+            jax.ShapeDtypeStruct((n, sw), jnp.bfloat16),
             jax.ShapeDtypeStruct((sf, nb, 2 * br), jnp.float32),
         ],
         scratch_shapes=[pltpu.VMEM((n, sg), jnp.bfloat16)],
-    )(moved_grad, moved_input, taps_rows[:, None, :], stretch_gain.reshape(sf, 1, sg))
+    )(grad_in, input_in, taps_rows[:, None, :], stretch_gain.reshape(sf, 1, sg))
 
 
 def per_device(cached_input, cached_gate, out_grad, filter_taps, skip_gain):
@@ -104,15 +109,13 @@
         ],
         axis=2,
     )
-    moved = lax.all_to_all(packed, "seq", split_axis=1, concat_axis=0, tiled=True)
+    packed = jnp.transpose(packed, (1, 0, 2))
+    moved = lax.all_to_all(packed, "seq", split_axis=0, concat_axis=0, tiled=True)
     moved = moved.reshape(length, 2 * stretch_width + stretch_filters)
-    moved_grad = moved[:, :stretch_width]
-    moved_input = moved[:, stretch_width : 2 * stretch_width]
     stretch_taps = moved[:, 2 * stretch_width :]
     stretch_gain = lax.dynamic_slice_in_dim(skip_gain, seq_index * stretch_width, stretch_width, 0)
     local_grad, diag = local_grads(
-        moved_grad,
-        moved_input,
+        moved,
         stretch_taps,
         stretch_gain,
         seq_count,
@@ -135,8 +138,14 @@
         [local_grad, high.astype(jnp.bfloat16), middle.astype(jnp.bfloat16), low.astype(jnp.bfloat16)],
         axis=1,
     )
-    returned = lax.all_to_all(outgoing, "seq", split_axis=0, concat_axis=1, tiled=True)
-    returned = returned.reshape(block_rows, seq_count, stretch_width + 3 * stretch_filters)
+    returned = lax.all_to_all(
+        outgoing.reshape(seq_count, block_rows, stretch_width + 3 * stretch_filters),
+        "seq",
+        split_axis=0,
+        concat_axis=0,
+        tiled=True,
+    )
+    returned = jnp.transpose(returned, (1, 0, 2))
     input_grad = returned[:, :, :stretch_width].reshape(block_rows, chan_width)
     parts = returned[:, :, stretch_width:].astype(jnp.float32)
     lag_parts = (

time: 68.1 us -> 67.4 us (0.990)
    slice x3 -> x0, local copies, waits for them, and re-layouts: 2.07 us -> none  [the longest x2 1.08 us: per_device(): moved_input = moved[:, stretch_width:2 * stretch_width]]
    reshape x0 -> x2, local copies, waits for them, and re-layouts: none -> 1.84 us  [the longest x1 1.44 us: per_device(): moved = moved.reshape(length, 2 * stretch_width + stretch_filters)]
    concatenate x1 -> x0, other arithmetic: 1.05 us -> none  [per_device(): jnp.concatenate([gated_grad.reshape(block_rows, seq_count, stretch_width)...]
    transpose x0 -> x1, other arithmetic: none -> 1.04 us  [per_device(): packed = jnp.transpose(packed, (1, 0, 2))]
where the time goes in v4:
time: 67.4 us; the launch traced here: 67.1 us
  waiting for transfers between devices  24.8 us (37%)
  blocking collectives  19.2 us (28%)
  local copies, waits for them, and re-layouts  8.63 us (13%)
  starting transfers between devices  7.28 us (11%)
  Pallas kernels  4.14 us (6%)
  other arithmetic  2.24 us (3%)
  between operations  0.79 us (1%)
    all_to_all x1, waiting for transfers between devices, per_device(): lax.all_to_all(packed, 'seq', split_axis=0, concat_axis=0, tiled=True)  24.8 us
    all_to_all x1, blocking collectives, per_device(): lax.all_to_all(outgoing.reshape(seq_count, block_rows, stretch_width + 3...  19.2 us
    all_to_all x1, starting transfers between devices, per_device(): lax.all_to_all(packed, 'seq', split_axis=0, concat_axis=0, tiled=True)  7.28 us
    pallas_call x1, Pallas kernels, local_grads(): pl.pallas_call(functools.partial(local_kernel, nb=nb, br=br, scale=scale)...  4.14 us
    unnamed x12, local copies, waits for them, and re-layouts  2.79 us
    reshape x1, local copies, waits for them, and re-layouts, per_device(): moved = moved.reshape(length, 2 * stretch_width + stretch_filters)  1.44 us
  transfers between devices with their start and end apart: 1, of which 1 were waited for; matrix products, arithmetic and copies ran while one was open for 2% of the time, Pallas kernels for 0%

profile of v4, /device:TPU:0, one launch (start us, length us, event | category | flops | bytes accessed | tf_op | source)
XLA Modules:
  0.0 67.1 jit_solution(13613938334676646236)
XLA Ops:
  0.6 0.0 copy-start
  0.6 0.0 copy-start.1
  0.7 0.0 copy-start.2
  0.7 1.4 %copy.34 = bf16[128,2048]{0,1:T(8,128)(2,1)S(1)} copy(bf16[128,2048]{1,0:T(8,128)(2,1)} %param.7) | data formatting | bytes 1048576 | tf_op args[0]
  2.1 0.0 copy-done.1
  2.1 0.0 copy-done.2
  2.1 0.1 multiply_convert_fusion
  2.3 0.3 copy.33
  2.6 0.0 copy-done
  2.6 0.6 gather_fusion
  3.1 1.0 %maximum_bitcast_fusion = bf16[8,128,514]{1,2,0:T(8,128)(2,1)} fusion(bf16[128,8,2]{0,2,1:T(2,128)(2,1)S(1)} %bitcast.43, bf16[128,8,256]{0,2,1:T(8,128)(2,1)S(1)} %bitcast.41, bf16[128,8,256]{0,2,1:T(8,128)(2,1)S(1)} %bitcast.42), kind=kLoop, calls=%fused_computation.1 | loop fusion | flops 3158016 | bytes 2105344 | tf_op jit(solution)/shard_map/transpose | solution.py:112
  4.2 7.3 %all-to-all-start = ((bf16[8,128,514]{1,2,0:T(8,128)(2,1)}), bf16[8,128,514]{1,2,0:T(8,128)(2,1)S(1)}, u32[]{:S(2)}, u32[]{:S(2)}) async-start(bf16[8,128,514]{1,2,0:T(8,128)(2,1)} %maximum_bitcast_fusion), calls=%async_computation | async-start | bytes 2129920 | tf_op jit(solution)/shard_map/all_to_all | solution.py:113
  11.5 1.3 %dynamic_slice.3 = f32[256]{0:T(256)} dynamic-slice(f32[2048]{0:T(1024)} %param.11, s32[]{:T(128)S(6)} %select_n.7), dynamic_slice_sizes={256} | dynamic-slice | bytes 2052 | tf_op jit(solution)/shard_map/dynamic_slice | solution.py:116
  12.8 24.8 %all-to-all-done = bf16[8,128,514]{1,2,0:T(8,128)(2,1)S(1)} async-done(((bf16[8,128,514]{1,2,0:T(8,128)(2,1)}), bf16[8,128,514]{1,2,0:T(8,128)(2,1)S(1)}, u32[]{:S(2)}, u32[]{:S(2)}) %all-to-all-start) | async-done | bytes 1052704 | tf_op jit(solution)/shard_map/all_to_all | solution.py:113
  37.6 0.1 copy.44
  37.7 0.1 pad.24
  37.8 0.3 copy.42
  38.1 1.4 %copy.36.g_ref.x_ref = bf16[1024,514]{1,0:T(8,128)(2,1)} copy(bf16[1024,514]{0,1:T(8,128)(2,1)S(1)} %bitcast.32) | data formatting | bytes 2105344 | tf_op jit(solution)/shard_map/reshape | solution.py:114
  39.5 0.6 reshape.39.v_ref
  40.1 4.1 %shard_map.86 = (bf16[1024,256]{1,0:T(8,128)(2,1)}, f32[2,8,256]{2,1,0:T(8,128)}) custom-call(bf16[1024,514]{1,0:T(8,128)(2,1)} %copy.36.g_ref.x_ref, bf16[1024,514]{1,0:T(8,128)(2,1)} %copy.36.g_ref.x_ref, f32[2,1,1152]{2,1,0:T(1,128)} %reshape.39.v_ref, f32[2,1,128]{2,1,0:T(1,128)} %bitcast.45), custom_call_target="tpu_custom_call" | custom-call | tf_op jit(solution)/shard_map/pallas_call | solution.py:60
  44.3 0.0 copy-start.3
  44.3 0.8 %fusion.2 = (f32[2,8,128]{2,1,0:T(8,128)S(1)}, f32[2,8,128]{2,1,0:T(8,128)S(1)}) fusion(f32[2,8,256]{2,1,0:T(8,128)} %get-tuple-element.5), kind=kLoop, calls=%fused_computation.19 | loop fusion | bytes 32768 | tf_op jit(solution)/shard_map/slice | solution.py:127
  45.1 0.2 copy.41
  45.3 0.2 reduce-precision_convert_fusion.1
  45.5 0.0 copy-done.3
  45.5 0.3 pad_maximum_fusion
  45.8 0.4 copy.39
  46.2 19.2 %all_to_all.10 = bf16[8,128,262]{1,2,0:T(8,128)(2,1)S(1)} all-to-all(bf16[8,128,262]{1,2,0:T(8,128)(2,1)S(1)} %copy.39), channel_id=1, replica_groups=mesh['groups'=2,'seq'=8,'chan'=2] {'seq'}, dimensions={0} | all-to-all | bytes 1073152 | tf_op jit(solution)/shard_map/all_to_all | solution.py:141
  65.5 1.0 %copy.40 = bf16[128,2048]{1,0:T(8,128)(2,1)} copy(bf16[128,2048]{0,1:T(8,128)(2,1)S(1)} %bitcast.40) | data formatting | bytes 1048576
  66.5 0.6 slice_add_fusion
  (7 shorter events, 0.1 us)
Async XLA Ops:
  0.6 1.9 %copy-start = (bf16[128,16]{0,1:T(8,128)(2,1)S(1)}, bf16[128,16]{0,1:T(8,128)(2,1)}, u32[]{:S(2)}) copy-start(bf16[128,16]{0,1:T(8,128)(2,1)} %param.10) | copy-start | bytes 12292
  0.6 1.5 %copy-start.1 = (bf16[128,2048]{1,0:T(8,128)(2,1)S(1)}, bf16[128,2048]{1,0:T(8,128)(2,1)}, u32[]{:S(2)}) copy-start(bf16[128,2048]{1,0:T(8,128)(2,1)} %param.8) | copy-start | bytes 1572868
  0.7 1.5 %copy-start.2 = (bf16[128,2048]{1,0:T(8,128)(2,1)S(1)}, bf16[128,2048]{1,0:T(8,128)(2,1)}, u32[]{:S(2)}) copy-start(bf16[128,2048]{1,0:T(8,128)(2,1)} %param.9) | copy-start | bytes 1572868
  4.2 33.4 %all-to-all-start = ((bf16[8,128,514]{1,2,0:T(8,128)(2,1)}), bf16[8,128,514]{1,2,0:T(8,128)(2,1)S(1)}, u32[]{:S(2)}, u32[]{:S(2)}) async-start(bf16[8,128,514]{1,2,0:T(8,128)(2,1)} %maximum_bitcast_fusion), calls=%async_computation | async-start | bytes 2129920 | tf_op jit(solution)/shard_map/all_to_all | solution.py:113
  44.3 1.2 %copy-start.3 = (bf16[1024,256]{1,0:T(8,128)(2,1)S(1)}, bf16[1024,256]{1,0:T(8,128)(2,1)}, u32[]{:S(2)}) copy-start(bf16[1024,256]{1,0:T(8,128)(2,1)} %get-tuple-element.4) | copy-start | bytes 1572868

commit v5 on v4

v5 whole, which is shorter than its diff:
```python
import functools
import math

import jax
import jax.numpy as jnp
import numpy as np
from jax import lax
from jax.experimental import pallas as pl
from jax.experimental.pallas import tpu as pltpu
from jax.sharding import PartitionSpec as P


def local_kernel(g_ref, x_ref, t_ref, gain_ref, out_ref, diag_ref, g_scr, xrev_ref, *, nb, br, scale):
    f = pl.program_id(0)
    n = nb * br
    width = n + br
    pick = lax.broadcasted_iota(jnp.int32, (8, 128), 0) == f
    taps = jnp.concatenate(
        [jnp.zeros((1, br), jnp.float32)]
        + [
            jnp.sum(
                jnp.where(pick, t_ref[j].astype(jnp.float32), 0.0), axis=0, keepdims=True
            )
            for j in range(nb)
        ],
        axis=1,
    )
    taps_row = jnp.broadcast_to(taps, (br, width))
    toeplitz = pltpu.roll(taps_row, width - br, 1, stride=1, stride_axis=0)
    toeplitz = toeplitz[:, :n].astype(jnp.bfloat16)
    rows = lax.broadcasted_iota(jnp.int32, (br, br), 0)
    cols = lax.broadcasted_iota(jnp.int32, (br, br), 1)
    flip = (rows + cols == br - 1).astype(jnp.bfloat16)
    for i in range(nb):
        g_scr[i * br : (i + 1) * br, :] = g_ref[i]
        xrev_ref[i * br : (i + 1) * br, :] = jnp.dot(
            flip, x_ref[i], preferred_element_type=jnp.float32
        ).astype(xrev_ref.dtype)
    gain = gain_ref[...]
    for i in range(nb):
        conv = jnp.dot(
            toeplitz[:, : n - i * br], g_scr[i * br :, :], preferred_element_type=jnp.float32
        )
        own = g_ref[i].astype(jnp.float32)
        out_ref[i] = (conv * scale + gain * own).astype(out_ref.dtype)
    sums = [None] * nb
    for j in range(nb):
        row = lax.dot_general(
            g_ref[j],
            xrev_ref[: (j + 1) * br, :],
            (((1,), (1,)), ((), ())),
            preferred_element_type=jnp.float32,
        )
        for i in range(j + 1):
            piece = row[:, i * br : (i + 1) * br]
            sums[j - i] = piece if sums[j - i] is None else sums[j - i] + piece
    zeros = jnp.zeros((br, br), jnp.float32)
    for k in range(nb):
        padded = jnp.concatenate([sums[k], zeros], axis=1)
        skewed = pltpu.roll(padded, 0, 1, stride=1, stride_axis=0)
        diag_ref[k : k + 1, :] = jnp.sum(skewed, axis=0, keepdims=True)


def local_grads(moved, stretch_gain, nb, br, sf, sg, scale):
    sw = sf * sg
    if sg % 128 == 0:
        grad_in, input_in, input_base = moved, moved, sf
    else:
        grad_in = moved[:, :br, :sw]
        input_in = moved[:, :br, sw : 2 * sw]
        input_base = 0
    tap_in = moved[:, br : br + 8, :128]
    return pl.pallas_call(
        functools.partial(local_kernel, nb=nb, br=br, scale=scale),
        grid=(sf,),
        in_specs=[
            pl.BlockSpec((nb, br, sg), lambda f: (0, 0, f)),
            pl.BlockSpec((nb, br, sg), lambda f: (0, 0, input_base + f)),
            pl.BlockSpec((nb, 8, 128), lambda f: (0, 0, 0)),
            pl.BlockSpec((None, 1, sg), lambda f: (f, 0, 0)),
        ],
        out_specs=[
            pl.BlockSpec((nb, br, sg), lambda f: (0, 0, f)),
            pl.BlockSpec((None, nb, 2 * br), lambda f: (f, 0, 0)),
        ],
        out_shape=[
            jax.ShapeDtypeStruct((nb, br, sw), jnp.bfloat16),
            jax.ShapeDtypeStruct((sf, nb, 2 * br), jnp.float32),
        ],
        scratch_shapes=[
            pltpu.VMEM((nb * br, sg), jnp.bfloat16),
            pltpu.VMEM((nb * br, sg), jnp.bfloat16),
        ],
    )(grad_in, input_in, tap_in, stretch_gain.reshape(sf, 1, sg))


def per_device(cached_input, cached_gate, out_grad, filter_taps, skip_gain):
    block_rows = cached_input.shape[0]
    chan_width = cached_input.shape[1]
    filters = filter_taps.shape[1]
    group_width = chan_width // filters
    seq_count = lax.axis_size("seq")
    seq_index = lax.axis_index("seq")
    length = block_rows * seq_count
    taps_scale = 1.0 / math.sqrt(length)
    gated_grad = (out_grad.astype(jnp.float32) * cached_gate.astype(jnp.float32)).astype(
        jnp.bfloat16
    )
    stretch_width = chan_width // seq_count
    stretch_filters = max(1, stretch_width // group_width)
    stretch_group = stretch_width // stretch_filters
    tap_columns = np.array(
        [
            (target * stretch_width) // group_width + offset
            for target in range(seq_count)
            for offset in range(stretch_filters)
        ]
    )
    routed_taps = jnp.transpose(filter_taps[:, tap_columns]).reshape(
        seq_count, stretch_filters, block_rows
    )
    tap_rows = jnp.pad(
        routed_taps,
        ((0, 0), (0, 8 - stretch_filters), (0, 2 * stretch_width - block_rows)),
    )
    body = jnp.concatenate(
        [
            jnp.transpose(gated_grad.reshape(block_rows, seq_count, stretch_width), (1, 0, 2)),
            jnp.transpose(cached_input.reshape(block_rows, seq_count, stretch_width), (1, 0, 2)),
        ],
        axis=2,
    )
    packed = jnp.concatenate([body, tap_rows], axis=1)
    moved = lax.all_to_all(packed, "seq", split_axis=0, concat_axis=0, tiled=True)
    stretch_gain = lax.dynamic_slice_in_dim(skip_gain, seq_index * stretch_width, stretch_width, 0)
    local_grad, diag = local_grads(
        moved,
        stretch_gain,
        seq_count,
        block_rows,
        stretch_filters,
        stretch_group,
        taps_scale,
    )
    front = jnp.pad(diag[:, :, :block_rows], ((0, 0), (0, 1), (0, 0)))
    back = jnp.pad(diag[:, :, block_rows:], ((0, 0), (1, 0), (0, 0)))
    lag_sums = (front + back).reshape(stretch_filters, (seq_count + 1) * block_rows)
    stretch_term = lag_sums[:, block_rows - 1 : block_rows - 1 + length] * taps_scale
    high = lax.reduce_precision(stretch_term, exponent_bits=8, mantissa_bits=7)
    rest = stretch_term - high
    middle = lax.reduce_precision(rest, exponent_bits=8, mantissa_bits=7)
    low = rest - middle
    split = jnp.stack([high, middle, low], axis=0).astype(jnp.bfloat16)
    split = jnp.transpose(split.reshape(3, stretch_filters, seq_count, block_rows), (2, 0, 1, 3))
    used_rows = 3 * stretch_filters * block_rows // stretch_width
    extra_rows = -(-used_rows // 8) * 8
    split = split.reshape(seq_count, used_rows, stretch_width)
    split = jnp.pad(split, ((0, 0), (0, extra_rows - used_rows), (0, 0)))
    outgoing = jnp.concatenate([local_grad, split], axis=1)
    returned = lax.all_to_all(outgoing, "seq", split_axis=0, concat_axis=0, tiled=True)
    input_grad = jnp.transpose(returned[:, :block_rows, :], (1, 0, 2)).reshape(
        block_rows, chan_width
    )
    parts = returned[:, block_rows : block_rows + used_rows, :].astype(jnp.float32)
    parts = parts.reshape(seq_count, 3, stretch_filters, block_rows).sum(axis=1)
    sharers = seq_count * stretch_filters // filters
    filter_grad = jnp.transpose(
        parts.reshape(filters, sharers, block_rows).sum(axis=1)
    )
    return (input_grad, filter_grad)


def solution(mesh):
    return jax.shard_map(
        per_device,
        mesh=mesh,
        in_specs=(
            P(("groups", "seq"), "chan"),
            P(("groups", "seq"), "chan"),
            P(("groups", "seq"), "chan"),
            P("seq", "chan"),
            P("chan"),
        ),
        out_specs=(P(("groups", "seq"), "chan"), P(("groups", "seq"), "chan")),
        check_vma=False,
    )
```

time: 67.4 us -> 68.8 us (1.021)
  waiting for transfers between devices: 24.8 us -> 25.9 us
    concatenate x1 -> x2, other arithmetic: 0.26 us -> 2.19 us  [the longest x1 1.1 us: per_device(): packed = jnp.concatenate([body, tap_rows], axis=1)]
    reshape x3 -> x4, local copies, waits for them, and re-layouts: 2.09 us -> 0.46 us  [the longest x1 0.22 us: per_device(): cached_input.reshape(block_rows, seq_count, stretch_width)]
    unnamed x12 -> x13, local copies, waits for them, and re-layouts: 2.79 us -> 3.85 us
    all_to_all x1, waiting for transfers between devices: 24.8 us -> 25.9 us  [per_device(): lax.all_to_all(packed, 'seq', split_axis=0, concat_axis=0, tiled=True)]
    transpose x1, other arithmetic: 1.04 us -> 0.02 us  [per_device(): jnp.transpose(split.reshape(3, stretch_filters, seq_count, block_rows), (...]
where the time goes in v5:
time: 68.8 us; the launch traced here: 68.3 us
  waiting for transfers between devices  25.9 us (38%)
  blocking collectives  19.6 us (28%)
  local copies, waits for them, and re-layouts  8.51 us (12%)
  starting transfers between devices  7.28 us (11%)
  Pallas kernels  3.88 us (6%)
  other arithmetic  2.47 us (4%)
  between operations  0.78 us (1%)
    all_to_all x1, waiting for transfers between devices, per_device(): lax.all_to_all(packed, 'seq', split_axis=0, concat_axis=0, tiled=True)  25.9 us
    all_to_all x1, blocking collectives, per_device(): lax.all_to_all(outgoing, 'seq', split_axis=0, concat_axis=0, tiled=True)  19.6 us
    all_to_all x1, starting transfers between devices, per_device(): lax.all_to_all(packed, 'seq', split_axis=0, concat_axis=0, tiled=True)  7.28 us
    pallas_call x1, Pallas kernels, local_grads(): pl.pallas_call(functools.partial(local_kernel, nb=nb, br=br, scale=scale)...  3.88 us
    unnamed x13, local copies, waits for them, and re-layouts  3.85 us
  transfers between devices with their start and end apart: 1, of which 1 were waited for; matrix products, arithmetic and copies ran while one was open for 2% of the time, Pallas kernels for 0%

profile of v5, /device:TPU:0, one launch (start us, length us, event | category | flops | bytes accessed | tf_op | source)
XLA Modules:
  0.0 68.3 jit_solution(2679366672049518332)
XLA Ops:
  0.6 0.0 copy-start
  0.6 0.0 copy-start.2
  0.7 1.4 %copy.15 = bf16[128,2048]{0,1:T(8,128)(2,1)S(1)} copy(bf16[128,2048]{1,0:T(8,128)(2,1)} %param.7) | data formatting | bytes 1048576 | tf_op args[0]
  2.1 0.0 copy-start.3
  2.1 0.2 copy.16
  2.3 0.0 copy-done.2
  2.3 0.3 copy.13
  2.6 0.5 copy-done.3
  3.1 0.3 copy.12
  3.4 0.1 multiply_convert_fusion
  3.6 0.2 copy.14
  3.8 0.0 copy-done
  3.8 0.6 gather_fusion
  4.4 1.1 %fusion.1 = bf16[8,136,512]{2,1,0:T(8,128)(2,1)} fusion(bf16[8,2,128]{2,1,0:T(2,128)(2,1)S(1)} %bitcast.30, bf16[8,128,256]{2,1,0:T(8,128)(2,1)S(1)} %bitcast.28, bf16[8,128,256]{2,1,0:T(8,128)(2,1)S(1)} %bitcast.29), kind=kLoop, calls=%fused_computation.3 | loop fusion | flops 4456448 | bytes 2166784 | tf_op jit(solution)/shard_map/concatenate | solution.py:133
  5.5 7.3 %all-to-all-start = ((bf16[8,136,512]{2,1,0:T(8,128)(2,1)}), bf16[8,136,512]{2,1,0:T(8,128)(2,1)S(1)}, u32[]{:S(2)}, u32[]{:S(2)}) async-start(bf16[8,136,512]{2,1,0:T(8,128)(2,1)} %fusion.1), calls=%async_computation | async-start | bytes 2228224 | tf_op jit(solution)/shard_map/all_to_all | solution.py:134
  12.8 1.3 %dynamic_slice.3 = f32[256]{0:T(256)} dynamic-slice(f32[2048]{0:T(1024)} %param.11, s32[]{:T(128)S(6)} %select_n.7), dynamic_slice_sizes={256} | dynamic-slice | bytes 2052 | tf_op jit(solution)/shard_map/dynamic_slice | solution.py:135
  14.1 25.9 %all-to-all-done.g_ref.x_ref = bf16[8,136,512]{2,1,0:T(8,128)(2,1)S(1)} async-done(((bf16[8,136,512]{2,1,0:T(8,128)(2,1)}), bf16[8,136,512]{2,1,0:T(8,128)(2,1)S(1)}, u32[]{:S(2)}, u32[]{:S(2)}) %all-to-all-start) | async-done | bytes 1114144 | tf_op jit(solution)/shard_map/all_to_all | solution.py:134
  39.9 0.0 copy-start.1
  39.9 0.7 slice.26.t_ref
  40.6 0.3 copy-done.1
  40.9 3.9 %shard_map.86 = (bf16[8,128,256]{2,1,0:T(8,128)(2,1)}, f32[2,8,256]{2,1,0:T(8,128)}) custom-call(bf16[8,136,512]{2,1,0:T(8,128)(2,1)} %copy-done.1, bf16[8,136,512]{2,1,0:T(8,128)(2,1)} %copy-done.1, bf16[8,8,128]{2,1,0:T(8,128)(2,1)} %slice.26.t_ref, f32[2,1,128]{2,1,0:T(1,128)} %bitcast.33), custom_call_target="tpu_custom_call" | custom-call | tf_op jit(solution)/shard_map/pallas_call | solution.py:73
  44.8 0.7 %fusion.8 = (f32[2,8,128]{2,1,0:T(8,128)S(1)}, f32[2,8,128]{2,1,0:T(8,128)S(1)}) fusion(f32[2,8,256]{2,1,0:T(8,128)} %get-tuple-element.5), kind=kLoop, calls=%fused_computation.23 | loop fusion | bytes 32768 | tf_op jit(solution)/shard_map/slice | solution.py:145
  45.5 0.1 fusion.7
  45.7 1.1 %fusion.3 = bf16[8,136,256]{2,1,0:T(8,128)(2,1)S(1)} fusion(bf16[8,3,256]{2,1,0:T(4,128)(2,1)S(1)} %copy.20, bf16[8,128,256]{2,1,0:T(8,128)(2,1)} %get-tuple-element.4), kind=kLoop, calls=%fused_computation.7 | loop fusion | flops 1671168 | bytes 1093632 | tf_op jit(solution)/shard_map/concatenate | solution.py:159
  46.8 19.6 %all_to_all.10 = bf16[8,136,256]{2,1,0:T(8,128)(2,1)S(1)} all-to-all(bf16[8,136,256]{2,1,0:T(8,128)(2,1)S(1)} %fusion.3), channel_id=1, replica_groups=mesh['groups'=2,'seq'=8,'chan'=2] {'seq'}, dimensions={0} | all-to-all | bytes 1114112 | tf_op jit(solution)/shard_map/all_to_all | solution.py:160
  66.4 0.3 copy.21
  66.7 1.0 %copy.22 = bf16[128,2048]{1,0:T(8,128)(2,1)} copy(bf16[128,2048]{0,1:T(8,128)(2,1)S(1)} %bitcast.26) | data formatting | bytes 1048576
  67.7 0.6 reduce_sum.16
  (9 shorter events, 0.1 us)
Async XLA Ops:
  0.6 3.2 %copy-start = (bf16[128,16]{0,1:T(8,128)(2,1)S(1)}, bf16[128,16]{0,1:T(8,128)(2,1)}, u32[]{:S(2)}) copy-start(bf16[128,16]{0,1:T(8,128)(2,1)} %param.10) | copy-start | bytes 12292
  0.6 1.7 %copy-start.2 = (bf16[128,2048]{1,0:T(8,128)(2,1)S(1)}, bf16[128,2048]{1,0:T(8,128)(2,1)}, u32[]{:S(2)}) copy-start(bf16[128,2048]{1,0:T(8,128)(2,1)} %param.8) | copy-start | bytes 1572868
  2.1 1.0 %copy-start.3 = (bf16[128,2048]{1,0:T(8,128)(2,1)S(1)}, bf16[128,2048]{1,0:T(8,128)(2,1)}, u32[]{:S(2)}) copy-start(bf16[128,2048]{1,0:T(8,128)(2,1)} %param.9) | copy-start | bytes 1572868
  5.5 34.5 %all-to-all-start = ((bf16[8,136,512]{2,1,0:T(8,128)(2,1)}), bf16[8,136,512]{2,1,0:T(8,128)(2,1)S(1)}, u32[]{:S(2)}, u32[]{:S(2)}) async-start(bf16[8,136,512]{2,1,0:T(8,128)(2,1)} %fusion.1), calls=%async_computation | async-start | bytes 2228224 | tf_op jit(solution)/shard_map/all_to_all | solution.py:134
  39.9 1.0 %copy-start.1 = (bf16[8,136,512]{2,1,0:T(8,128)(2,1)}, bf16[8,136,512]{2,1,0:T(8,128)(2,1)S(1)}, u32[]{:S(2)}) copy-start(bf16[8,136,512]{2,1,0:T(8,128)(2,1)S(1)} %all-to-all-done.g_ref.x_ref) | copy-start | bytes 3342340

commit v6 on v5

--- a/solution.py
+++ b/solution.py
@@ -61,7 +61,21 @@
         diag_ref[k : k + 1, :] = jnp.sum(skewed, axis=0, keepdims=True)
 
 
-def local_grads(moved, stretch_gain, nb, br, sf, sg, scale):
+def pack_kernel(og_ref, gate_ref, x_ref, taps_ref, out_ref, *, nb, br, sw):
+    for j in range(nb):
+        cols = slice(j * sw, (j + 1) * sw)
+        gated = og_ref[:, cols].astype(jnp.float32) * gate_ref[:, cols].astype(jnp.float32)
+        out_ref[j, :br, :sw] = gated.astype(out_ref.dtype)
+        out_ref[j, :br, sw:] = x_ref[:, cols]
+        out_ref[j, br:, :] = taps_ref[j]
+
+
+def unpack_kernel(in_ref, out_ref, *, nb, br, sw):
+    for j in range(nb):
+        out_ref[:, j * sw : (j + 1) * sw] = in_ref[j, :br, :]
+
+
+def local_grads(moved, stretch_gain, nb, br, sf, sg, scale, out_rows):
     sw = sf * sg
     if sg % 128 == 0:
         grad_in, input_in, input_base = moved, moved, sf
@@ -84,7 +98,7 @@
             pl.BlockSpec((None, nb, 2 * br), lambda f: (f, 0, 0)),
         ],
         out_shape=[
-            jax.ShapeDtypeStruct((nb, br, sw), jnp.bfloat16),
+            jax.ShapeDtypeStruct((nb, out_rows, sw), jnp.bfloat16),
             jax.ShapeDtypeStruct((sf, nb, 2 * br), jnp.float32),
         ],
         scratch_shapes=[
@@ -103,9 +117,6 @@
     seq_index = lax.axis_index("seq")
     length = block_rows * seq_count
     taps_scale = 1.0 / math.sqrt(length)
-    gated_grad = (out_grad.astype(jnp.float32) * cached_gate.astype(jnp.float32)).astype(
-        jnp.bfloat16
-    )
     stretch_width = chan_width // seq_count
     stretch_filters = max(1, stretch_width // group_width)
     stretch_group = stretch_width // stretch_filters
@@ -123,16 +134,30 @@
         routed_taps,
         ((0, 0), (0, 8 - stretch_filters), (0, 2 * stretch_width - block_rows)),
     )
-    body = jnp.concatenate(
-        [
-            jnp.transpose(gated_grad.reshape(block_rows, seq_count, stretch_width), (1, 0, 2)),
-            jnp.transpose(cached_input.reshape(block_rows, seq_count, stretch_width), (1, 0, 2)),
-        ],
-        axis=2,
-    )
-    packed = jnp.concatenate([body, tap_rows], axis=1)
+    def gated_grad():
+        product = out_grad.astype(jnp.float32) * cached_gate.astype(jnp.float32)
+        return product.astype(jnp.bfloat16)
+
+    if stretch_width % 128 == 0:
+        packed = pl.pallas_call(
+            functools.partial(pack_kernel, nb=seq_count, br=block_rows, sw=stretch_width),
+            out_shape=jax.ShapeDtypeStruct(
+                (seq_count, block_rows + 8, 2 * stretch_width), jnp.bfloat16
+            ),
+        )(out_grad, cached_gate, cached_input, tap_rows)
+    else:
+        body = jnp.concatenate(
+            [
+                jnp.transpose(gated_grad().reshape(block_rows, seq_count, stretch_width), (1, 0, 2)),
+                jnp.transpose(cached_input.reshape(block_rows, seq_count, stretch_width), (1, 0, 2)),
+            ],
+            axis=2,
+        )
+        packed = jnp.concatenate([body, tap_rows], axis=1)
     moved = lax.all_to_all(packed, "seq", split_axis=0, concat_axis=0, tiled=True)
     stretch_gain = lax.dynamic_slice_in_dim(skip_gain, seq_index * stretch_width, stretch_width, 0)
+    used_rows = 3 * stretch_filters * block_rows // stretch_width
+    extra_rows = -(-used_rows // 8) * 8
     local_grad, diag = local_grads(
         moved,
         stretch_gain,
@@ -141,6 +166,7 @@
         stretch_filters,
         stretch_group,
         taps_scale,
+        block_rows + extra_rows,
     )
     front = jnp.pad(diag[:, :, :block_rows], ((0, 0), (0, 1), (0, 0)))
     back = jnp.pad(diag[:, :, block_rows:], ((0, 0), (1, 0), (0, 0)))
@@ -152,15 +178,19 @@
     low = rest - middle
     split = jnp.stack([high, middle, low], axis=0).astype(jnp.bfloat16)
     split = jnp.transpose(split.reshape(3, stretch_filters, seq_count, block_rows), (2, 0, 1, 3))
-    used_rows = 3 * stretch_filters * block_rows // stretch_width
-    extra_rows = -(-used_rows // 8) * 8
     split = split.reshape(seq_count, used_rows, stretch_width)
     split = jnp.pad(split, ((0, 0), (0, extra_rows - used_rows), (0, 0)))
-    outgoing = jnp.concatenate([local_grad, split], axis=1)
+    outgoing = lax.dynamic_update_slice_in_dim(local_grad, split, block_rows, 1)
     returned = lax.all_to_all(outgoing, "seq", split_axis=0, concat_axis=0, tiled=True)
-    input_grad = jnp.transpose(returned[:, :block_rows, :], (1, 0, 2)).reshape(
-        block_rows, chan_width
-    )
+    if stretch_width % 128 == 0:
+        input_grad = pl.pallas_call(
+            functools.partial(unpack_kernel, nb=seq_count, br=block_rows, sw=stretch_width),
+            out_shape=jax.ShapeDtypeStruct((block_rows, chan_width), jnp.bfloat16),
+        )(returned)
+    else:
+        input_grad = jnp.transpose(returned[:, :block_rows, :], (1, 0, 2)).reshape(
+            block_rows, chan_width
+        )
     parts = returned[:, block_rows : block_rows + used_rows, :].astype(jnp.float32)
     parts = parts.reshape(seq_count, 3, stretch_filters, block_rows).sum(axis=1)
     sharers = seq_count * stretch_filters // filters

time: 68.8 us -> 68.9 us (level)
  Pallas kernels: 3.88 us -> 8.4 us
  other arithmetic: 2.47 us -> 0.14 us
  local copies, waits for them, and re-layouts: 8.51 us -> 6.33 us
    pallas_call x0 -> x2, Pallas kernels: none -> 4.38 us  [the longest x1 2.48 us: per_device(): pl.pallas_call(functools.partial(pack_kernel, nb=seq_count, br=block_rows...]
    unnamed x13 -> x7, local copies, waits for them, and re-layouts: 3.85 us -> 1.12 us
    concatenate x2 -> x0, other arithmetic: 2.19 us -> none  [the longest x1 1.1 us: per_device(): packed = jnp.concatenate([body, tap_rows], axis=1)]
where the time goes in v6:
time: 68.9 us; the launch traced here: 68.5 us
  waiting for transfers between devices  25.9 us (38%)
  blocking collectives  19.8 us (29%)
  Pallas kernels  8.4 us (12%)
  starting transfers between devices  7.28 us (11%)
  local copies, waits for them, and re-layouts  6.33 us (9%)
  between operations  0.69 us (1%)
    all_to_all x1, waiting for transfers between devices, per_device(): lax.all_to_all(packed, 'seq', split_axis=0, concat_axis=0, tiled=True)  25.9 us
    all_to_all x1, blocking collectives, per_device(): lax.all_to_all(outgoing, 'seq', split_axis=0, concat_axis=0, tiled=True)  19.8 us
    all_to_all x1, starting transfers between devices, per_device(): lax.all_to_all(packed, 'seq', split_axis=0, concat_axis=0, tiled=True)  7.28 us
    pallas_call x1, Pallas kernels, local_grads(): pl.pallas_call(functools.partial(local_kernel, nb=nb, br=br, scale=scale)...  4.02 us
    pallas_call x1, Pallas kernels, per_device(): pl.pallas_call(functools.partial(pack_kernel, nb=seq_count, br=block_rows...  2.48 us
    pallas_call x1, Pallas kernels, per_device(): pl.pallas_call(functools.partial(unpack_kernel, nb=seq_count, br=block_ro...  1.9 us
  transfers between devices with their start and end apart: 1, of which 1 were waited for; matrix products, arithmetic and copies ran while one was open for 2% of the time, Pallas kernels for 0%

profile of v6, /device:TPU:0, one launch (start us, length us, event | category | flops | bytes accessed | tf_op | source)
XLA Modules:
  0.0 68.5 jit_solution(1031750929583116205)
XLA Ops:
  0.6 0.0 copy-start
  0.7 0.7 copy-done
  1.3 0.6 gather_fusion
  1.9 0.6 pad.16.taps_ref
  2.5 2.5 %shard_map.86 = bf16[8,136,512]{2,1,0:T(8,128)(2,1)} custom-call(bf16[128,2048]{1,0:T(8,128)(2,1)} %og_ref.1, bf16[128,2048]{1,0:T(8,128)(2,1)} %gate_ref.1, bf16[128,2048]{1,0:T(8,128)(2,1)} %x_ref.1, bf16[8,8,512]{2,1,0:T(8,128)(2,1)} %pad.16.taps_ref), custom_call_target="tpu_custom_call" | custom-call | tf_op jit(solution)/shard_map/pallas_call | solution.py:142
  5.0 7.3 %all-to-all-start = ((bf16[8,136,512]{2,1,0:T(8,128)(2,1)}), bf16[8,136,512]{2,1,0:T(8,128)(2,1)S(1)}, u32[]{:S(2)}, u32[]{:S(2)}) async-start(bf16[8,136,512]{2,1,0:T(8,128)(2,1)} %shard_map.86), calls=%async_computation | async-start | bytes 2228224 | tf_op jit(solution)/shard_map/all_to_all | solution.py:157
  12.3 1.3 %dynamic_slice.3 = f32[256]{0:T(256)} dynamic-slice(f32[2048]{0:T(1024)} %param.11, s32[]{:T(128)S(6)} %select_n.7), dynamic_slice_sizes={256} | dynamic-slice | bytes 2052 | tf_op jit(solution)/shard_map/dynamic_slice | solution.py:158
  13.6 25.9 %all-to-all-done.g_ref.x_ref = bf16[8,136,512]{2,1,0:T(8,128)(2,1)S(1)} async-done(((bf16[8,136,512]{2,1,0:T(8,128)(2,1)}), bf16[8,136,512]{2,1,0:T(8,128)(2,1)S(1)}, u32[]{:S(2)}, u32[]{:S(2)}) %all-to-all-start) | async-done | bytes 1114144 | tf_op jit(solution)/shard_map/all_to_all | solution.py:157
  39.5 0.0 copy-start.1
  39.5 0.7 slice.22.t_ref
  40.1 0.3 copy-done.1
  40.5 4.0 %shard_map.87 = (bf16[8,136,256]{2,1,0:T(8,128)(2,1)}, f32[2,8,256]{2,1,0:T(8,128)}) custom-call(bf16[8,136,512]{2,1,0:T(8,128)(2,1)} %copy-done.1, bf16[8,136,512]{2,1,0:T(8,128)(2,1)} %copy-done.1, bf16[8,8,128]{2,1,0:T(8,128)(2,1)} %slice.22.t_ref, f32[2,1,128]{2,1,0:T(1,128)} %bitcast.21), custom_call_target="tpu_custom_call" | custom-call | tf_op jit(solution)/shard_map/pallas_call | solution.py:87
  44.5 0.7 %fusion.4 = (f32[2,8,128]{2,1,0:T(8,128)S(1)}, f32[2,8,128]{2,1,0:T(8,128)S(1)}) fusion(f32[2,8,256]{2,1,0:T(8,128)} %get-tuple-element.5), kind=kLoop, calls=%fused_computation.16 | loop fusion | bytes 32768 | tf_op jit(solution)/shard_map/slice | solution.py:171
  45.2 0.1 fusion.3
  45.4 0.6 pad_dynamic-update-slice_fusion
  46.0 19.8 %all_to_all.10.in_ref = bf16[8,136,256]{2,1,0:T(8,128)(2,1)S(1)} all-to-all(bf16[8,136,256]{2,1,0:T(8,128)(2,1)} %pad_dynamic-update-slice_fusion), channel_id=1, replica_groups=mesh['groups'=2,'seq'=8,'chan'=2] {'seq'}, dimensions={0} | all-to-all | bytes 1114112 | tf_op jit(solution)/shard_map/all_to_all | solution.py:184
  65.8 0.0 copy-start.2
  65.8 0.7 reduce_sum.16
  66.5 0.1 copy-done.2
  66.6 1.9 %shard_map.88 = bf16[128,2048]{1,0:T(8,128)(2,1)} custom-call(bf16[8,136,256]{2,1,0:T(8,128)(2,1)} %copy-done.2), custom_call_target="tpu_custom_call" | custom-call | tf_op jit(solution)/shard_map/pallas_call | solution.py:186
  (8 shorter events, 0.1 us)
Async XLA Ops:
  0.6 0.7 %copy-start = (bf16[128,16]{0,1:T(8,128)(2,1)S(1)}, bf16[128,16]{0,1:T(8,128)(2,1)}, u32[]{:S(2)}) copy-start(bf16[128,16]{0,1:T(8,128)(2,1)} %param.10) | copy-start | bytes 12292
  5.0 34.5 %all-to-all-start = ((bf16[8,136,512]{2,1,0:T(8,128)(2,1)}), bf16[8,136,512]{2,1,0:T(8,128)(2,1)S(1)}, u32[]{:S(2)}, u32[]{:S(2)}) async-start(bf16[8,136,512]{2,1,0:T(8,128)(2,1)} %shard_map.86), calls=%async_computation | async-start | bytes 2228224 | tf_op jit(solution)/shard_map/all_to_all | solution.py:157
  39.5 1.0 %copy-start.1 = (bf16[8,136,512]{2,1,0:T(8,128)(2,1)}, bf16[8,136,512]{2,1,0:T(8,128)(2,1)S(1)}, u32[]{:S(2)}) copy-start(bf16[8,136,512]{2,1,0:T(8,128)(2,1)S(1)} %all-to-all-done.g_ref.x_ref) | copy-start | bytes 3342340
  65.8 0.8 %copy-start.2 = (bf16[8,136,256]{2,1,0:T(8,128)(2,1)}, bf16[8,136,256]{2,1,0:T(8,128)(2,1)S(1)}, u32[]{:S(2)}) copy-start(bf16[8,136,256]{2,1,0:T(8,128)(2,1)S(1)} %all_to_all.10.in_ref) | copy-start | bytes 1671172

commit v7 on v6

--- a/solution.py
+++ b/solution.py
@@ -61,18 +61,24 @@
         diag_ref[k : k + 1, :] = jnp.sum(skewed, axis=0, keepdims=True)
 
 
-def pack_kernel(og_ref, gate_ref, x_ref, taps_ref, out_ref, *, nb, br, sw):
-    for j in range(nb):
-        cols = slice(j * sw, (j + 1) * sw)
-        gated = og_ref[:, cols].astype(jnp.float32) * gate_ref[:, cols].astype(jnp.float32)
-        out_ref[j, :br, :sw] = gated.astype(out_ref.dtype)
-        out_ref[j, :br, sw:] = x_ref[:, cols]
-        out_ref[j, br:, :] = taps_ref[j]
-
-
-def unpack_kernel(in_ref, out_ref, *, nb, br, sw):
-    for j in range(nb):
-        out_ref[:, j * sw : (j + 1) * sw] = in_ref[j, :br, :]
+def pack_kernel(og_ref, gate_ref, x_ref, taps_ref, out_ref, *, br, sw, sf, gw):
+    j = pl.program_id(0)
+    gated = og_ref[...].astype(jnp.float32) * gate_ref[...].astype(jnp.float32)
+    out_ref[:br, :sw] = gated.astype(out_ref.dtype)
+    out_ref[:br, sw:] = x_ref[...]
+    filters = taps_ref.shape[1]
+    rows = lax.broadcasted_iota(jnp.int32, (8, filters), 0)
+    cols = lax.broadcasted_iota(jnp.int32, (8, filters), 1)
+    pick = ((cols == (j * sw) // gw + rows) & (rows < sf)).astype(jnp.bfloat16)
+    tap_rows = lax.dot_general(
+        pick, taps_ref[...], (((1,), (1,)), ((), ())), preferred_element_type=jnp.float32
+    )
+    out_ref[br:, :br] = tap_rows.astype(out_ref.dtype)
+    out_ref[br:, br:] = jnp.zeros((8, 2 * sw - br), out_ref.dtype)
+
+
+def unpack_kernel(in_ref, out_ref, *, br):
+    out_ref[...] = in_ref[:br, :]
 
 
 def local_grads(moved, stretch_gain, nb, br, sf, sg, scale, out_rows):
@@ -83,14 +89,17 @@
         grad_in = moved[:, :br, :sw]
         input_in = moved[:, :br, sw : 2 * sw]
         input_base = 0
-    tap_in = moved[:, br : br + 8, :128]
+    if sg % 128 == 0:
+        tap_in, tap_base = moved, br // 8
+    else:
+        tap_in, tap_base = moved[:, br : br + 8, :128], 0
     return pl.pallas_call(
         functools.partial(local_kernel, nb=nb, br=br, scale=scale),
         grid=(sf,),
         in_specs=[
             pl.BlockSpec((nb, br, sg), lambda f: (0, 0, f)),
             pl.BlockSpec((nb, br, sg), lambda f: (0, 0, input_base + f)),
-            pl.BlockSpec((nb, 8, 128), lambda f: (0, 0, 0)),
+            pl.BlockSpec((nb, 8, 128), lambda f: (0, tap_base, 0)),
             pl.BlockSpec((None, 1, sg), lambda f: (f, 0, 0)),
         ],
         out_specs=[
@@ -127,25 +136,42 @@
             for offset in range(stretch_filters)
         ]
     )
-    routed_taps = jnp.transpose(filter_taps[:, tap_columns]).reshape(
-        seq_count, stretch_filters, block_rows
-    )
-    tap_rows = jnp.pad(
-        routed_taps,
-        ((0, 0), (0, 8 - stretch_filters), (0, 2 * stretch_width - block_rows)),
-    )
     def gated_grad():
         product = out_grad.astype(jnp.float32) * cached_gate.astype(jnp.float32)
         return product.astype(jnp.bfloat16)
 
     if stretch_width % 128 == 0:
+        column_block = pl.BlockSpec((block_rows, stretch_width), lambda j: (0, j))
         packed = pl.pallas_call(
-            functools.partial(pack_kernel, nb=seq_count, br=block_rows, sw=stretch_width),
+            functools.partial(
+                pack_kernel,
+                br=block_rows,
+                sw=stretch_width,
+                sf=stretch_filters,
+                gw=group_width,
+            ),
+            grid=(seq_count,),
+            in_specs=[
+                column_block,
+                column_block,
+                column_block,
+                pl.BlockSpec((block_rows, filters), lambda j: (0, 0)),
+            ],
+            out_specs=pl.BlockSpec(
+                (None, block_rows + 8, 2 * stretch_width), lambda j: (j, 0, 0)
+            ),
             out_shape=jax.ShapeDtypeStruct(
                 (seq_count, block_rows + 8, 2 * stretch_width), jnp.bfloat16
             ),
-        )(out_grad, cached_gate, cached_input, tap_rows)
-    else:
+        )(out_grad, cached_gate, cached_input, filter_taps)
+    else:
+        routed_taps = jnp.transpose(filter_taps[:, tap_columns]).reshape(
+            seq_count, stretch_filters, block_rows
+        )
+        tap_rows = jnp.pad(
+            routed_taps,
+            ((0, 0), (0, 8 - stretch_filters), (0, 2 * stretch_width - block_rows)),
+        )
         body = jnp.concatenate(
             [
                 jnp.transpose(gated_grad().reshape(block_rows, seq_count, stretch_width), (1, 0, 2)),
@@ -184,7 +210,12 @@
     returned = lax.all_to_all(outgoing, "seq", split_axis=0, concat_axis=0, tiled=True)
     if stretch_width % 128 == 0:
         input_grad = pl.pallas_call(
-            functools.partial(unpack_kernel, nb=seq_count, br=block_rows, sw=stretch_width),
+            functools.partial(unpack_kernel, br=block_rows),
+            grid=(seq_count,),
+            in_specs=[
+                pl.BlockSpec((None, block_rows + extra_rows, stretch_width), lambda j: (j, 0, 0))
+            ],
+            out_specs=pl.BlockSpec((block_rows, stretch_width), lambda j: (0, j)),
             out_shape=jax.ShapeDtypeStruct((block_rows, chan_width), jnp.bfloat16),
         )(returned)
     else:

time: 68.9 us -> 75.2 us (1.091)
  Pallas kernels: 8.4 us -> 14.6 us
    pallas_call x2, Pallas kernels: 4.38 us -> 10.6 us  [the longest x1 5.71 us: per_device(): pl.pallas_call(functools.partial(pack_kernel, br=block_rows, sw=stretch_w...]
    unnamed x7 -> x6, local copies, waits for them, and re-layouts: 1.12 us -> 2.51 us
where the time goes in v7:
time: 75.2 us; the launch traced here: 74.2 us
  waiting for transfers between devices  25.9 us (34%)
  blocking collectives  19.8 us (26%)
  Pallas kernels  14.6 us (19%)
  starting transfers between devices  7.28 us (10%)
  local copies, waits for them, and re-layouts  5.86 us (8%)
    all_to_all x1, waiting for transfers between devices, per_device(): lax.all_to_all(packed, 'seq', split_axis=0, concat_axis=0, tiled=True)  25.9 us
    all_to_all x1, blocking collectives, per_device(): lax.all_to_all(outgoing, 'seq', split_axis=0, concat_axis=0, tiled=True)  19.8 us
    all_to_all x1, starting transfers between devices, per_device(): lax.all_to_all(packed, 'seq', split_axis=0, concat_axis=0, tiled=True)  7.28 us
    pallas_call x1, Pallas kernels, per_device(): pl.pallas_call(functools.partial(pack_kernel, br=block_rows, sw=stretch_w...  5.71 us
    pallas_call x1, Pallas kernels, per_device(): pl.pallas_call(functools.partial(unpack_kernel, br=block_rows), grid=(seq...  4.91 us
    pallas_call x1, Pallas kernels, local_grads(): pl.pallas_call(functools.partial(local_kernel, nb=nb, br=br, scale=scale)...  4.02 us
    unnamed x6, local copies, waits for them, and re-layouts  2.51 us
  transfers between devices with their start and end apart: 1, of which 1 were waited for; matrix products, arithmetic and copies ran while one was open for 2% of the time, Pallas kernels for 0%

profile of v7, /device:TPU:0, one launch (start us, length us, event | category | flops | bytes accessed | tf_op | source)
XLA Modules:
  0.0 74.2 jit_solution(12707993948199982281)
XLA Ops:
  0.6 1.4 %copy.8.taps_ref = bf16[128,16]{1,0:T(8,128)(2,1)} copy(bf16[128,16]{0,1:T(8,128)(2,1)} %param.8) | data formatting | bytes 8192 | tf_op args[3]
  2.0 5.7 %shard_map.68 = bf16[8,136,512]{2,1,0:T(8,128)(2,1)} custom-call(bf16[128,2048]{1,0:T(8,128)(2,1)} %og_ref.1, bf16[128,2048]{1,0:T(8,128)(2,1)} %gate_ref.1, bf16[128,2048]{1,0:T(8,128)(2,1)} %x_ref.1, bf16[128,16]{1,0:T(8,128)(2,1)} %copy.8.taps_ref), custom_call_target="tpu_custom_call" | custom-call | tf_op jit(solution)/shard_map/pallas_call | solution.py:145
  7.7 7.3 %all-to-all-start = ((bf16[8,136,512]{2,1,0:T(8,128)(2,1)}), bf16[8,136,512]{2,1,0:T(8,128)(2,1)S(1)}, u32[]{:S(2)}, u32[]{:S(2)}) async-start(bf16[8,136,512]{2,1,0:T(8,128)(2,1)} %shard_map.68), calls=%async_computation | async-start | bytes 2228224 | tf_op jit(solution)/shard_map/all_to_all | solution.py:183
  15.0 1.3 %dynamic_slice.3 = f32[256]{0:T(256)} dynamic-slice(f32[2048]{0:T(1024)} %param.9, s32[]{:T(128)S(6)} %select_n.3), dynamic_slice_sizes={256} | dynamic-slice | bytes 2052 | tf_op jit(solution)/shard_map/dynamic_slice | solution.py:184
  16.3 25.9 %all-to-all-done.g_ref.x_ref.t_ref = bf16[8,136,512]{2,1,0:T(8,128)(2,1)S(1)} async-done(((bf16[8,136,512]{2,1,0:T(8,128)(2,1)}), bf16[8,136,512]{2,1,0:T(8,128)(2,1)S(1)}, u32[]{:S(2)}, u32[]{:S(2)}) %all-to-all-start) | async-done | bytes 1114144 | tf_op jit(solution)/shard_map/all_to_all | solution.py:183
  42.2 0.0 copy-start
  42.2 1.0 %copy-done = bf16[8,136,512]{2,1,0:T(8,128)(2,1)} copy-done((bf16[8,136,512]{2,1,0:T(8,128)(2,1)}, bf16[8,136,512]{2,1,0:T(8,128)(2,1)S(1)}, u32[]{:S(2)}) %copy-start) | copy-done | bytes 1114136
  43.2 4.0 %shard_map.69 = (bf16[8,136,256]{2,1,0:T(8,128)(2,1)}, f32[2,8,256]{2,1,0:T(8,128)}) custom-call(bf16[8,136,512]{2,1,0:T(8,128)(2,1)} %copy-done, bf16[8,136,512]{2,1,0:T(8,128)(2,1)} %copy-done, bf16[8,136,512]{2,1,0:T(8,128)(2,1)} %copy-done, f32[2,1,128]{2,1,0:T(1,128)} %bitcast.19), custom_call_target="tpu_custom_call" | custom-call | tf_op jit(solution)/shard_map/pallas_call | solution.py:96
  47.2 0.7 fusion.4
  47.9 0.1 fusion.3
  48.1 0.6 pad_dynamic-update-slice_fusion
  48.7 19.8 %all_to_all.10.in_ref = bf16[8,136,256]{2,1,0:T(8,128)(2,1)S(1)} all-to-all(bf16[8,136,256]{2,1,0:T(8,128)(2,1)} %pad_dynamic-update-slice_fusion), channel_id=1, replica_groups=mesh['groups'=2,'seq'=8,'chan'=2] {'seq'}, dimensions={0} | all-to-all | bytes 1114112 | tf_op jit(solution)/shard_map/all_to_all | solution.py:210
  68.5 0.0 copy-start.1
  68.5 0.7 reduce_sum.16
  69.2 0.1 copy-done.1
  69.3 4.9 %shard_map.70 = bf16[128,2048]{1,0:T(8,128)(2,1)} custom-call(bf16[8,136,256]{2,1,0:T(8,128)(2,1)} %copy-done.1), custom_call_target="tpu_custom_call" | custom-call | tf_op jit(solution)/shard_map/pallas_call | solution.py:212
  (6 shorter events, 0.1 us)
Async XLA Ops:
  7.7 34.5 %all-to-all-start = ((bf16[8,136,512]{2,1,0:T(8,128)(2,1)}), bf16[8,136,512]{2,1,0:T(8,128)(2,1)S(1)}, u32[]{:S(2)}, u32[]{:S(2)}) async-start(bf16[8,136,512]{2,1,0:T(8,128)(2,1)} %shard_map.68), calls=%async_computation | async-start | bytes 2228224 | tf_op jit(solution)/shard_map/all_to_all | solution.py:183
  42.2 1.0 %copy-start = (bf16[8,136,512]{2,1,0:T(8,128)(2,1)}, bf16[8,136,512]{2,1,0:T(8,128)(2,1)S(1)}, u32[]{:S(2)}) copy-start(bf16[8,136,512]{2,1,0:T(8,128)(2,1)S(1)} %all-to-all-done.g_ref.x_ref.t_ref) | copy-start | bytes 3342340
  68.5 0.8 %copy-start.1 = (bf16[8,136,256]{2,1,0:T(8,128)(2,1)}, bf16[8,136,256]{2,1,0:T(8,128)(2,1)S(1)}, u32[]{:S(2)}) copy-start(bf16[8,136,256]{2,1,0:T(8,128)(2,1)S(1)} %all_to_all.10.in_ref) | copy-start | bytes 1671172

commit v8 on v7

--- a/solution.py
+++ b/solution.py
@@ -61,24 +61,20 @@
         diag_ref[k : k + 1, :] = jnp.sum(skewed, axis=0, keepdims=True)
 
 
-def pack_kernel(og_ref, gate_ref, x_ref, taps_ref, out_ref, *, br, sw, sf, gw):
-    j = pl.program_id(0)
-    gated = og_ref[...].astype(jnp.float32) * gate_ref[...].astype(jnp.float32)
-    out_ref[:br, :sw] = gated.astype(out_ref.dtype)
-    out_ref[:br, sw:] = x_ref[...]
-    filters = taps_ref.shape[1]
+def pack_kernel(og_ref, gate_ref, x_ref, taps_ref, out_ref, *, br, sw, sf, gw, per_step):
+    filters = taps_ref.shape[0]
     rows = lax.broadcasted_iota(jnp.int32, (8, filters), 0)
     cols = lax.broadcasted_iota(jnp.int32, (8, filters), 1)
-    pick = ((cols == (j * sw) // gw + rows) & (rows < sf)).astype(jnp.bfloat16)
-    tap_rows = lax.dot_general(
-        pick, taps_ref[...], (((1,), (1,)), ((), ())), preferred_element_type=jnp.float32
-    )
-    out_ref[br:, :br] = tap_rows.astype(out_ref.dtype)
-    out_ref[br:, br:] = jnp.zeros((8, 2 * sw - br), out_ref.dtype)
-
-
-def unpack_kernel(in_ref, out_ref, *, br):
-    out_ref[...] = in_ref[:br, :]
+    for d in range(per_step):
+        j = pl.program_id(0) * per_step + d
+        span = slice(d * sw, (d + 1) * sw)
+        gated = og_ref[:, span].astype(jnp.float32) * gate_ref[:, span].astype(jnp.float32)
+        out_ref[d, :br, :sw] = gated.astype(out_ref.dtype)
+        out_ref[d, :br, sw:] = x_ref[:, span]
+        pick = ((cols == (j * sw) // gw + rows) & (rows < sf)).astype(jnp.bfloat16)
+        tap_rows = jnp.dot(pick, taps_ref[...], preferred_element_type=jnp.float32)
+        out_ref[d, br:, :br] = tap_rows.astype(out_ref.dtype)
+        out_ref[d, br:, br:] = jnp.zeros((8, 2 * sw - br), out_ref.dtype)
 
 
 def local_grads(moved, stretch_gain, nb, br, sf, sg, scale, out_rows):
@@ -141,7 +137,8 @@
         return product.astype(jnp.bfloat16)
 
     if stretch_width % 128 == 0:
-        column_block = pl.BlockSpec((block_rows, stretch_width), lambda j: (0, j))
+        per_step = seq_count // 2 if seq_count % 2 == 0 else seq_count
+        column_block = pl.BlockSpec((block_rows, per_step * stretch_width), lambda j: (0, j))
         packed = pl.pallas_call(
             functools.partial(
                 pack_kernel,
@@ -149,21 +146,22 @@
                 sw=stretch_width,
                 sf=stretch_filters,
                 gw=group_width,
+                per_step=per_step,
             ),
-            grid=(seq_count,),
+            grid=(seq_count // per_step,),
             in_specs=[
                 column_block,
                 column_block,
                 column_block,
-                pl.BlockSpec((block_rows, filters), lambda j: (0, 0)),
+                pl.BlockSpec((filters, block_rows), lambda j: (0, 0)),
             ],
             out_specs=pl.BlockSpec(
-                (None, block_rows + 8, 2 * stretch_width), lambda j: (j, 0, 0)
+                (per_step, block_rows + 8, 2 * stretch_width), lambda j: (j, 0, 0)
             ),
             out_shape=jax.ShapeDtypeStruct(
                 (seq_count, block_rows + 8, 2 * stretch_width), jnp.bfloat16
             ),
-        )(out_grad, cached_gate, cached_input, filter_taps)
+        )(out_grad, cached_gate, cached_input, jnp.transpose(filter_taps))
     else:
         routed_taps = jnp.transpose(filter_taps[:, tap_columns]).reshape(
             seq_count, stretch_filters, block_rows
@@ -208,20 +206,9 @@
     split = jnp.pad(split, ((0, 0), (0, extra_rows - used_rows), (0, 0)))
     outgoing = lax.dynamic_update_slice_in_dim(local_grad, split, block_rows, 1)
     returned = lax.all_to_all(outgoing, "seq", split_axis=0, concat_axis=0, tiled=True)
-    if stretch_width % 128 == 0:
-        input_grad = pl.pallas_call(
-            functools.partial(unpack_kernel, br=block_rows),
-            grid=(seq_count,),
-            in_specs=[
-                pl.BlockSpec((None, block_rows + extra_rows, stretch_width), lambda j: (j, 0, 0))
-            ],
-            out_specs=pl.BlockSpec((block_rows, stretch_width), lambda j: (0, j)),
-            out_shape=jax.ShapeDtypeStruct((block_rows, chan_width), jnp.bfloat16),
-        )(returned)
-    else:
-        input_grad = jnp.transpose(returned[:, :block_rows, :], (1, 0, 2)).reshape(
-            block_rows, chan_width
-        )
+    input_grad = jnp.transpose(returned[:, :block_rows, :], (1, 0, 2)).reshape(
+        block_rows, chan_width
+    )
     parts = returned[:, block_rows : block_rows + used_rows, :].astype(jnp.float32)
     parts = parts.reshape(seq_count, 3, stretch_filters, block_rows).sum(axis=1)
     sharers = seq_count * stretch_filters // filters

time: 75.2 us -> 66 us (0.88)
  Pallas kernels: 14.6 us -> 6.35 us
    pallas_call x1 -> x0, Pallas kernels: 4.91 us -> none  [per_device(): pl.pallas_call(functools.partial(unpack_kernel, br=block_rows), grid=(seq...]
    pallas_call x1, Pallas kernels: 5.71 us -> 2.32 us  [per_device(): pl.pallas_call(functools.partial(pack_kernel, br=block_rows, sw=stretch_w...]
    unnamed x6 -> x4, local copies, waits for them, and re-layouts: 2.51 us -> 2.01 us
where the time goes in v8:
time: 66 us; the launch traced here: 65.7 us
  waiting for transfers between devices  25.9 us (39%)
  blocking collectives  19.8 us (30%)
  starting transfers between devices  7.28 us (11%)
  Pallas kernels  6.35 us (10%)
  local copies, waits for them, and re-layouts  5.6 us (8%)
  between operations  0.68 us (1%)
    all_to_all x1, waiting for transfers between devices, per_device(): lax.all_to_all(packed, 'seq', split_axis=0, concat_axis=0, tiled=True)  25.9 us
    all_to_all x1, blocking collectives, per_device(): lax.all_to_all(outgoing, 'seq', split_axis=0, concat_axis=0, tiled=True)  19.8 us
    all_to_all x1, starting transfers between devices, per_device(): lax.all_to_all(packed, 'seq', split_axis=0, concat_axis=0, tiled=True)  7.28 us
    pallas_call x1, Pallas kernels, local_grads(): pl.pallas_call(functools.partial(local_kernel, nb=nb, br=br, scale=scale)...  4.03 us
    pallas_call x1, Pallas kernels, per_device(): pl.pallas_call(functools.partial(pack_kernel, br=block_rows, sw=stretch_w...  2.32 us
    unnamed x4, local copies, waits for them, and re-layouts  2.01 us
    dynamic_slice x1, local copies, waits for them, and re-layouts, per_device(): lax.dynamic_slice_in_dim(skip_gain, seq_index * stretch_width, stretch_wi...  1.32 us
  transfers between devices with their start and end apart: 1, of which 1 were waited for; matrix products, arithmetic and copies ran while one was open for 2% of the time, Pallas kernels for 0%

profile of v8, /device:TPU:0, one launch (start us, length us, event | category | flops | bytes accessed | tf_op | source)
XLA Modules:
  0.0 65.7 jit_solution(1048283652345906236)
XLA Ops:
  0.6 2.3 %shard_map.68 = bf16[8,136,512]{2,1,0:T(8,128)(2,1)} custom-call(bf16[128,2048]{1,0:T(8,128)(2,1)} %og_ref.1, bf16[128,2048]{1,0:T(8,128)(2,1)} %gate_ref.1, bf16[128,2048]{1,0:T(8,128)(2,1)} %x_ref.1, bf16[16,128]{1,0:T(8,128)(2,1)} %bitcast.24), custom_call_target="tpu_custom_call" | custom-call | tf_op jit(solution)/shard_map/pallas_call | solution.py:142
  3.0 7.3 %all-to-all-start = ((bf16[8,136,512]{2,1,0:T(8,128)(2,1)}), bf16[8,136,512]{2,1,0:T(8,128)(2,1)S(1)}, u32[]{:S(2)}, u32[]{:S(2)}) async-start(bf16[8,136,512]{2,1,0:T(8,128)(2,1)} %shard_map.68), calls=%async_computation | async-start | bytes 2228224 | tf_op jit(solution)/shard_map/all_to_all | solution.py:181
  10.2 1.3 %dynamic_slice.3 = f32[256]{0:T(256)} dynamic-slice(f32[2048]{0:T(1024)} %param.9, s32[]{:T(128)S(6)} %select_n.3), dynamic_slice_sizes={256} | dynamic-slice | bytes 2052 | tf_op jit(solution)/shard_map/dynamic_slice | solution.py:182
  11.6 25.9 %all-to-all-done.g_ref.x_ref.t_ref = bf16[8,136,512]{2,1,0:T(8,128)(2,1)S(1)} async-done(((bf16[8,136,512]{2,1,0:T(8,128)(2,1)}), bf16[8,136,512]{2,1,0:T(8,128)(2,1)S(1)}, u32[]{:S(2)}, u32[]{:S(2)}) %all-to-all-start) | async-done | bytes 1114144 | tf_op jit(solution)/shard_map/all_to_all | solution.py:181
  37.4 0.0 copy-start
  37.4 1.0 %copy-done = bf16[8,136,512]{2,1,0:T(8,128)(2,1)} copy-done((bf16[8,136,512]{2,1,0:T(8,128)(2,1)}, bf16[8,136,512]{2,1,0:T(8,128)(2,1)S(1)}, u32[]{:S(2)}) %copy-start) | copy-done | bytes 1114136
  38.4 4.0 %shard_map.69 = (bf16[8,136,256]{2,1,0:T(8,128)(2,1)}, f32[2,8,256]{2,1,0:T(8,128)}) custom-call(bf16[8,136,512]{2,1,0:T(8,128)(2,1)} %copy-done, bf16[8,136,512]{2,1,0:T(8,128)(2,1)} %copy-done, bf16[8,136,512]{2,1,0:T(8,128)(2,1)} %copy-done, f32[2,1,128]{2,1,0:T(1,128)} %bitcast.25), custom_call_target="tpu_custom_call" | custom-call | tf_op jit(solution)/shard_map/pallas_call | solution.py:92
  42.4 0.7 %fusion.4 = (f32[2,8,128]{2,1,0:T(8,128)S(1)}, f32[2,8,128]{2,1,0:T(8,128)S(1)}) fusion(f32[2,8,256]{2,1,0:T(8,128)} %get-tuple-element.5), kind=kLoop, calls=%fused_computation.15 | loop fusion | bytes 32768 | tf_op jit(solution)/shard_map/slice | solution.py:195
  43.2 0.1 fusion.3
  43.3 0.6 pad_dynamic-update-slice_fusion
  43.9 19.8 %all_to_all.10 = bf16[8,136,256]{2,1,0:T(8,128)(2,1)S(1)} all-to-all(bf16[8,136,256]{2,1,0:T(8,128)(2,1)} %pad_dynamic-update-slice_fusion), channel_id=1, replica_groups=mesh['groups'=2,'seq'=8,'chan'=2] {'seq'}, dimensions={0} | all-to-all | bytes 1114112 | tf_op jit(solution)/shard_map/all_to_all | solution.py:208
  63.7 0.3 copy.14
  64.0 1.0 %copy.15 = bf16[128,2048]{1,0:T(8,128)(2,1)} copy(bf16[128,2048]{0,1:T(8,128)(2,1)S(1)} %bitcast.21) | data formatting | bytes 1048576
  65.1 0.6 reduce_sum.16
  (7 shorter events, 0.1 us)
Async XLA Ops:
  3.0 34.5 %all-to-all-start = ((bf16[8,136,512]{2,1,0:T(8,128)(2,1)}), bf16[8,136,512]{2,1,0:T(8,128)(2,1)S(1)}, u32[]{:S(2)}, u32[]{:S(2)}) async-start(bf16[8,136,512]{2,1,0:T(8,128)(2,1)} %shard_map.68), calls=%async_computation | async-start | bytes 2228224 | tf_op jit(solution)/shard_map/all_to_all | solution.py:181
  37.4 1.0 %copy-start = (bf16[8,136,512]{2,1,0:T(8,128)(2,1)}, bf16[8,136,512]{2,1,0:T(8,128)(2,1)S(1)}, u32[]{:S(2)}) copy-start(bf16[8,136,512]{2,1,0:T(8,128)(2,1)S(1)} %all-to-all-done.g_ref.x_ref.t_ref) | copy-start | bytes 3342340

commit v9 on v8

--- a/solution.py
+++ b/solution.py
@@ -10,7 +10,7 @@
 from jax.sharding import PartitionSpec as P
 
 
-def local_kernel(g_ref, x_ref, t_ref, gain_ref, out_ref, diag_ref, g_scr, xrev_ref, *, nb, br, scale):
+def local_kernel(g_ref, x_ref, t_ref, gain_ref, out_ref, diag_ref, g_scr, xrev_ref, *, nb, br, scale, fold_rows):
     f = pl.program_id(0)
     n = nb * br
     width = n + br
@@ -42,7 +42,7 @@
             toeplitz[:, : n - i * br], g_scr[i * br :, :], preferred_element_type=jnp.float32
         )
         own = g_ref[i].astype(jnp.float32)
-        out_ref[i] = (conv * scale + gain * own).astype(out_ref.dtype)
+        out_ref[i, :br, :] = (conv * scale + gain * own).astype(out_ref.dtype)
     sums = [None] * nb
     for j in range(nb):
         row = lax.dot_general(
@@ -59,6 +59,23 @@
         padded = jnp.concatenate([sums[k], zeros], axis=1)
         skewed = pltpu.roll(padded, 0, 1, stride=1, stride_axis=0)
         diag_ref[k : k + 1, :] = jnp.sum(skewed, axis=0, keepdims=True)
+    if fold_rows:
+        diag = diag_ref[...]
+        own = pltpu.roll(diag, br + 1, 1)[:, :br]
+        nxt = pltpu.roll(diag, 1, 1)[:, :br]
+        nxt = jnp.concatenate([nxt[1:], jnp.zeros((1, br), jnp.float32)], axis=0)
+        lag_term = (own + nxt) * scale
+        high = lag_term.astype(jnp.bfloat16).astype(jnp.float32)
+        rest = lag_term - high
+        middle = rest.astype(jnp.bfloat16).astype(jnp.float32)
+        low = rest - middle
+        pick = lax.broadcasted_iota(jnp.int32, (nb, 8, br), 1)
+        tile = jnp.where(
+            pick == 0,
+            high[:, None, :],
+            jnp.where(pick == 1, middle[:, None, :], jnp.where(pick == 2, low[:, None, :], 0.0)),
+        )
+        out_ref[:, br : br + 8, :br] = tile.astype(out_ref.dtype)
 
 
 def pack_kernel(og_ref, gate_ref, x_ref, taps_ref, out_ref, *, br, sw, sf, gw, per_step):
@@ -79,6 +96,7 @@
 
 def local_grads(moved, stretch_gain, nb, br, sf, sg, scale, out_rows):
     sw = sf * sg
+    fold_rows = sg % 128 == 0
     if sg % 128 == 0:
         grad_in, input_in, input_base = moved, moved, sf
     else:
@@ -90,7 +108,7 @@
     else:
         tap_in, tap_base = moved[:, br : br + 8, :128], 0
     return pl.pallas_call(
-        functools.partial(local_kernel, nb=nb, br=br, scale=scale),
+        functools.partial(local_kernel, nb=nb, br=br, scale=scale, fold_rows=fold_rows),
         grid=(sf,),
         in_specs=[
             pl.BlockSpec((nb, br, sg), lambda f: (0, 0, f)),
@@ -99,7 +117,7 @@
             pl.BlockSpec((None, 1, sg), lambda f: (f, 0, 0)),
         ],
         out_specs=[
-            pl.BlockSpec((nb, br, sg), lambda f: (0, 0, f)),
+            pl.BlockSpec((nb, out_rows if fold_rows else br, sg), lambda f: (0, 0, f)),
             pl.BlockSpec((None, nb, 2 * br), lambda f: (f, 0, 0)),
         ],
         out_shape=[
@@ -192,26 +210,34 @@
         taps_scale,
         block_rows + extra_rows,
     )
-    front = jnp.pad(diag[:, :, :block_rows], ((0, 0), (0, 1), (0, 0)))
-    back = jnp.pad(diag[:, :, block_rows:], ((0, 0), (1, 0), (0, 0)))
-    lag_sums = (front + back).reshape(stretch_filters, (seq_count + 1) * block_rows)
-    stretch_term = lag_sums[:, block_rows - 1 : block_rows - 1 + length] * taps_scale
-    high = lax.reduce_precision(stretch_term, exponent_bits=8, mantissa_bits=7)
-    rest = stretch_term - high
-    middle = lax.reduce_precision(rest, exponent_bits=8, mantissa_bits=7)
-    low = rest - middle
-    split = jnp.stack([high, middle, low], axis=0).astype(jnp.bfloat16)
-    split = jnp.transpose(split.reshape(3, stretch_filters, seq_count, block_rows), (2, 0, 1, 3))
-    split = split.reshape(seq_count, used_rows, stretch_width)
-    split = jnp.pad(split, ((0, 0), (0, extra_rows - used_rows), (0, 0)))
-    outgoing = lax.dynamic_update_slice_in_dim(local_grad, split, block_rows, 1)
+    if stretch_group % 128 == 0:
+        outgoing = local_grad
+    else:
+        front = jnp.pad(diag[:, :, :block_rows], ((0, 0), (0, 1), (0, 0)))
+        back = jnp.pad(diag[:, :, block_rows:], ((0, 0), (1, 0), (0, 0)))
+        lag_sums = (front + back).reshape(stretch_filters, (seq_count + 1) * block_rows)
+        stretch_term = lag_sums[:, block_rows - 1 : block_rows - 1 + length] * taps_scale
+        high = lax.reduce_precision(stretch_term, exponent_bits=8, mantissa_bits=7)
+        rest = stretch_term - high
+        middle = lax.reduce_precision(rest, exponent_bits=8, mantissa_bits=7)
+        low = rest - middle
+        split = jnp.stack([high, middle, low], axis=0).astype(jnp.bfloat16)
+        split = jnp.transpose(split.reshape(3, stretch_filters, seq_count, block_rows), (2, 0, 1, 3))
+        split = split.reshape(seq_count, used_rows, stretch_width)
+        split = jnp.pad(split, ((0, 0), (0, extra_rows - used_rows), (0, 0)))
+        outgoing = lax.dynamic_update_slice_in_dim(local_grad, split, block_rows, 1)
     returned = lax.all_to_all(outgoing, "seq", split_axis=0, concat_axis=0, tiled=True)
     input_grad = jnp.transpose(returned[:, :block_rows, :], (1, 0, 2)).reshape(
         block_rows, chan_width
     )
-    parts = returned[:, block_rows : block_rows + used_rows, :].astype(jnp.float32)
-    parts = parts.reshape(seq_count, 3, stretch_filters, block_rows).sum(axis=1)
     sharers = seq_count * stretch_filters // filters
+    if stretch_group % 128 == 0:
+        parts = returned[:, block_rows : block_rows + 3, :].astype(jnp.float32)
+        parts = parts.reshape(seq_count, 3, stretch_filters, stretch_group)[..., :block_rows]
+        parts = parts[:, 0] + parts[:, 1] + parts[:, 2]
+    else:
+        parts = returned[:, block_rows : block_rows + used_rows, :].astype(jnp.float32)
+        parts = parts.reshape(seq_count, 3, stretch_filters, block_rows).sum(axis=1)
     filter_grad = jnp.transpose(
         parts.reshape(filters, sharers, block_rows).sum(axis=1)
     )

time: 66 us -> 64.7 us (0.980)
  local copies, waits for them, and re-layouts: 5.6 us -> 3.65 us
    slice x1 -> x0, local copies, waits for them, and re-layouts: 0.72 us -> none  [per_device(): front = jnp.pad(diag[:, :, :block_rows], ((0, 0), (0, 1), (0, 0)))]
    unnamed x4 -> x3, local copies, waits for them, and re-layouts: 2.01 us -> 2 us
where the time goes in v9:
time: 64.7 us; the launch traced here: 64.4 us
  waiting for transfers between devices  25.9 us (40%)
  blocking collectives  19.8 us (31%)
  starting transfers between devices  7.28 us (11%)
  Pallas kernels  6.54 us (10%)
  local copies, waits for them, and re-layouts  3.65 us (6%)
  between operations  0.65 us (1%)
    all_to_all x1, waiting for transfers between devices, per_device(): lax.all_to_all(packed, 'seq', split_axis=0, concat_axis=0, tiled=True)  25.9 us
    all_to_all x1, blocking collectives, per_device(): lax.all_to_all(outgoing, 'seq', split_axis=0, concat_axis=0, tiled=True)  19.8 us
    all_to_all x1, starting transfers between devices, per_device(): lax.all_to_all(packed, 'seq', split_axis=0, concat_axis=0, tiled=True)  7.28 us
    pallas_call x1, Pallas kernels, local_grads(): pl.pallas_call(functools.partial(local_kernel, nb=nb, br=br, scale=scale,...  4.22 us
    pallas_call x1, Pallas kernels, per_device(): pl.pallas_call(functools.partial(pack_kernel, br=block_rows, sw=stretch_w...  2.32 us
    unnamed x3, local copies, waits for them, and re-layouts  2 us
    dynamic_slice x1, local copies, waits for them, and re-layouts, per_device(): lax.dynamic_slice_in_dim(skip_gain, seq_index * stretch_width, stretch_wi...  1.32 us
  transfers between devices with their start and end apart: 1, of which 1 were waited for; matrix products, arithmetic and copies ran while one was open for 2% of the time, Pallas kernels for 0%

profile of v9, /device:TPU:0, one launch (start us, length us, event | category | flops | bytes accessed | tf_op | source)
XLA Modules:
  0.0 64.4 jit_solution(11017268761101182881)
XLA Ops:
  0.6 2.3 %shard_map.68 = bf16[8,136,512]{2,1,0:T(8,128)(2,1)} custom-call(bf16[128,2048]{1,0:T(8,128)(2,1)} %og_ref.1, bf16[128,2048]{1,0:T(8,128)(2,1)} %gate_ref.1, bf16[128,2048]{1,0:T(8,128)(2,1)} %x_ref.1, bf16[16,128]{1,0:T(8,128)(2,1)} %bitcast.24), custom_call_target="tpu_custom_call" | custom-call | tf_op jit(solution)/shard_map/pallas_call | solution.py:160
  3.0 7.3 %all-to-all-start = ((bf16[8,136,512]{2,1,0:T(8,128)(2,1)}), bf16[8,136,512]{2,1,0:T(8,128)(2,1)S(1)}, u32[]{:S(2)}, u32[]{:S(2)}) async-start(bf16[8,136,512]{2,1,0:T(8,128)(2,1)} %shard_map.68), calls=%async_computation | async-start | bytes 2228224 | tf_op jit(solution)/shard_map/all_to_all | solution.py:199
  10.2 1.3 %dynamic_slice.3 = f32[256]{0:T(256)} dynamic-slice(f32[2048]{0:T(1024)} %param.9, s32[]{:T(128)S(6)} %select_n.3), dynamic_slice_sizes={256} | dynamic-slice | bytes 2052 | tf_op jit(solution)/shard_map/dynamic_slice | solution.py:200
  11.6 25.9 %all-to-all-done.g_ref.x_ref.t_ref = bf16[8,136,512]{2,1,0:T(8,128)(2,1)S(1)} async-done(((bf16[8,136,512]{2,1,0:T(8,128)(2,1)}), bf16[8,136,512]{2,1,0:T(8,128)(2,1)S(1)}, u32[]{:S(2)}, u32[]{:S(2)}) %all-to-all-start) | async-done | bytes 1114144 | tf_op jit(solution)/shard_map/all_to_all | solution.py:199
  37.4 0.0 copy-start
  37.4 1.0 %copy-done = bf16[8,136,512]{2,1,0:T(8,128)(2,1)} copy-done((bf16[8,136,512]{2,1,0:T(8,128)(2,1)}, bf16[8,136,512]{2,1,0:T(8,128)(2,1)S(1)}, u32[]{:S(2)}) %copy-start) | copy-done | bytes 1114136
  38.4 4.2 %shard_map.69 = (bf16[8,136,256]{2,1,0:T(8,128)(2,1)}, f32[2,8,256]{2,1,0:T(8,128)}) custom-call(bf16[8,136,512]{2,1,0:T(8,128)(2,1)} %copy-done, bf16[8,136,512]{2,1,0:T(8,128)(2,1)} %copy-done, bf16[8,136,512]{2,1,0:T(8,128)(2,1)} %copy-done, f32[2,1,128]{2,1,0:T(1,128)} %bitcast.25), custom_call_target="tpu_custom_call" | custom-call | tf_op jit(solution)/shard_map/pallas_call | solution.py:110
  42.6 19.8 %all_to_all.10 = bf16[8,136,256]{2,1,0:T(8,128)(2,1)S(1)} all-to-all(bf16[8,136,256]{2,1,0:T(8,128)(2,1)} %get-tuple-element.3), channel_id=1, replica_groups=mesh['groups'=2,'seq'=8,'chan'=2] {'seq'}, dimensions={0} | all-to-all | bytes 1114112 | tf_op jit(solution)/shard_map/all_to_all | solution.py:229
  62.4 0.3 copy.10
  62.7 1.0 %copy.12 = bf16[128,2048]{1,0:T(8,128)(2,1)} copy(bf16[128,2048]{0,1:T(8,128)(2,1)S(1)} %bitcast.22) | data formatting | bytes 1048576
  63.7 0.6 fusion
  (3 shorter events, 0.1 us)
Async XLA Ops:
  3.0 34.5 %all-to-all-start = ((bf16[8,136,512]{2,1,0:T(8,128)(2,1)}), bf16[8,136,512]{2,1,0:T(8,128)(2,1)S(1)}, u32[]{:S(2)}, u32[]{:S(2)}) async-start(bf16[8,136,512]{2,1,0:T(8,128)(2,1)} %shard_map.68), calls=%async_computation | async-start | bytes 2228224 | tf_op jit(solution)/shard_map/all_to_all | solution.py:199
  37.4 1.0 %copy-start = (bf16[8,136,512]{2,1,0:T(8,128)(2,1)}, bf16[8,136,512]{2,1,0:T(8,128)(2,1)S(1)}, u32[]{:S(2)}) copy-start(bf16[8,136,512]{2,1,0:T(8,128)(2,1)S(1)} %all-to-all-done.g_ref.x_ref.t_ref) | copy-start | bytes 3342340

commit v10 on v9

--- a/solution.py
+++ b/solution.py
@@ -155,7 +155,7 @@
         return product.astype(jnp.bfloat16)
 
     if stretch_width % 128 == 0:
-        per_step = seq_count // 2 if seq_count % 2 == 0 else seq_count
+        per_step = seq_count // 4 if seq_count % 4 == 0 else seq_count
         column_block = pl.BlockSpec((block_rows, per_step * stretch_width), lambda j: (0, j))
         packed = pl.pallas_call(
             functools.partial(

time: 64.7 us -> 66.2 us (1.023)
  Pallas kernels: 6.54 us -> 7.97 us
    pallas_call x1, Pallas kernels: 2.32 us -> 3.75 us  [per_device(): pl.pallas_call(functools.partial(pack_kernel, br=block_rows, sw=stretch_w...]
where the time goes in v10:
time: 66.2 us; the launch traced here: 65.8 us
  waiting for transfers between devices  25.9 us (39%)
  blocking collectives  19.8 us (30%)
  Pallas kernels  7.97 us (12%)
  starting transfers between devices  7.28 us (11%)
  local copies, waits for them, and re-layouts  3.65 us (6%)
    all_to_all x1, waiting for transfers between devices, per_device(): lax.all_to_all(packed, 'seq', split_axis=0, concat_axis=0, tiled=True)  25.9 us
    all_to_all x1, blocking collectives, per_device(): lax.all_to_all(outgoing, 'seq', split_axis=0, concat_axis=0, tiled=True)  19.8 us
    all_to_all x1, starting transfers between devices, per_device(): lax.all_to_all(packed, 'seq', split_axis=0, concat_axis=0, tiled=True)  7.28 us
    pallas_call x1, Pallas kernels, local_grads(): pl.pallas_call(functools.partial(local_kernel, nb=nb, br=br, scale=scale,...  4.22 us
    pallas_call x1, Pallas kernels, per_device(): pl.pallas_call(functools.partial(pack_kernel, br=block_rows, sw=stretch_w...  3.75 us
    unnamed x3, local copies, waits for them, and re-layouts  2 us
  transfers between devices with their start and end apart: 1, of which 1 were waited for; matrix products, arithmetic and copies ran while one was open for 2% of the time, Pallas kernels for 0%

profile of v10, /device:TPU:0, one launch (start us, length us, event | category | flops | bytes accessed | tf_op | source)
XLA Modules:
  0.0 65.8 jit_solution(8022255665709728090)
XLA Ops:
  0.6 3.8 %shard_map.68 = bf16[8,136,512]{2,1,0:T(8,128)(2,1)} custom-call(bf16[128,2048]{1,0:T(8,128)(2,1)} %og_ref.1, bf16[128,2048]{1,0:T(8,128)(2,1)} %gate_ref.1, bf16[128,2048]{1,0:T(8,128)(2,1)} %x_ref.1, bf16[16,128]{1,0:T(8,128)(2,1)} %bitcast.24), custom_call_target="tpu_custom_call" | custom-call | tf_op jit(solution)/shard_map/pallas_call | solution.py:160
  4.4 7.3 %all-to-all-start = ((bf16[8,136,512]{2,1,0:T(8,128)(2,1)}), bf16[8,136,512]{2,1,0:T(8,128)(2,1)S(1)}, u32[]{:S(2)}, u32[]{:S(2)}) async-start(bf16[8,136,512]{2,1,0:T(8,128)(2,1)} %shard_map.68), calls=%async_computation | async-start | bytes 2228224 | tf_op jit(solution)/shard_map/all_to_all | solution.py:199
  11.7 1.3 %dynamic_slice.3 = f32[256]{0:T(256)} dynamic-slice(f32[2048]{0:T(1024)} %param.9, s32[]{:T(128)S(6)} %select_n.3), dynamic_slice_sizes={256} | dynamic-slice | bytes 2052 | tf_op jit(solution)/shard_map/dynamic_slice | solution.py:200
  13.0 25.9 %all-to-all-done.g_ref.x_ref.t_ref = bf16[8,136,512]{2,1,0:T(8,128)(2,1)S(1)} async-done(((bf16[8,136,512]{2,1,0:T(8,128)(2,1)}), bf16[8,136,512]{2,1,0:T(8,128)(2,1)S(1)}, u32[]{:S(2)}, u32[]{:S(2)}) %all-to-all-start) | async-done | bytes 1114144 | tf_op jit(solution)/shard_map/all_to_all | solution.py:199
  38.8 0.0 copy-start
  38.8 1.0 %copy-done = bf16[8,136,512]{2,1,0:T(8,128)(2,1)} copy-done((bf16[8,136,512]{2,1,0:T(8,128)(2,1)}, bf16[8,136,512]{2,1,0:T(8,128)(2,1)S(1)}, u32[]{:S(2)}) %copy-start) | copy-done | bytes 1114136
  39.8 4.2 %shard_map.69 = (bf16[8,136,256]{2,1,0:T(8,128)(2,1)}, f32[2,8,256]{2,1,0:T(8,128)}) custom-call(bf16[8,136,512]{2,1,0:T(8,128)(2,1)} %copy-done, bf16[8,136,512]{2,1,0:T(8,128)(2,1)} %copy-done, bf16[8,136,512]{2,1,0:T(8,128)(2,1)} %copy-done, f32[2,1,128]{2,1,0:T(1,128)} %bitcast.25), custom_call_target="tpu_custom_call" | custom-call | tf_op jit(solution)/shard_map/pallas_call | solution.py:110
  44.0 19.8 %all_to_all.10 = bf16[8,136,256]{2,1,0:T(8,128)(2,1)S(1)} all-to-all(bf16[8,136,256]{2,1,0:T(8,128)(2,1)} %get-tuple-element.3), channel_id=1, replica_groups=mesh['groups'=2,'seq'=8,'chan'=2] {'seq'}, dimensions={0} | all-to-all | bytes 1114112 | tf_op jit(solution)/shard_map/all_to_all | solution.py:229
  63.9 0.3 copy.10
  64.1 1.0 %copy.12 = bf16[128,2048]{1,0:T(8,128)(2,1)} copy(bf16[128,2048]{0,1:T(8,128)(2,1)S(1)} %bitcast.22) | data formatting | bytes 1048576
  65.2 0.6 fusion
  (3 shorter events, 0.1 us)
Async XLA Ops:
  4.4 34.5 %all-to-all-start = ((bf16[8,136,512]{2,1,0:T(8,128)(2,1)}), bf16[8,136,512]{2,1,0:T(8,128)(2,1)S(1)}, u32[]{:S(2)}, u32[]{:S(2)}) async-start(bf16[8,136,512]{2,1,0:T(8,128)(2,1)} %shard_map.68), calls=%async_computation | async-start | bytes 2228224 | tf_op jit(solution)/shard_map/all_to_all | solution.py:199
  38.8 1.0 %copy-start = (bf16[8,136,512]{2,1,0:T(8,128)(2,1)}, bf16[8,136,512]{2,1,0:T(8,128)(2,1)S(1)}, u32[]{:S(2)}) copy-start(bf16[8,136,512]{2,1,0:T(8,128)(2,1)S(1)} %all-to-all-done.g_ref.x_ref.t_ref) | copy-start | bytes 3342340

commit v11 on v9

--- a/solution.py
+++ b/solution.py
@@ -12,6 +12,8 @@
 
 def local_kernel(g_ref, x_ref, t_ref, gain_ref, out_ref, diag_ref, g_scr, xrev_ref, *, nb, br, scale, fold_rows):
     f = pl.program_id(0)
+    me = lax.axis_index("seq")
+    slot = [(me - i + nb) % nb for i in range(nb)]
     n = nb * br
     width = n + br
     pick = lax.broadcasted_iota(jnp.int32, (8, 128), 0) == f
@@ -19,7 +21,7 @@
         [jnp.zeros((1, br), jnp.float32)]
         + [
             jnp.sum(
-                jnp.where(pick, t_ref[j].astype(jnp.float32), 0.0), axis=0, keepdims=True
+                jnp.where(pick, t_ref[slot[j]].astype(jnp.float32), 0.0), axis=0, keepdims=True
             )
             for j in range(nb)
         ],
@@ -32,21 +34,21 @@
     cols = lax.broadcasted_iota(jnp.int32, (br, br), 1)
     flip = (rows + cols == br - 1).astype(jnp.bfloat16)
     for i in range(nb):
-        g_scr[i * br : (i + 1) * br, :] = g_ref[i]
+        g_scr[i * br : (i + 1) * br, :] = g_ref[slot[i]]
         xrev_ref[i * br : (i + 1) * br, :] = jnp.dot(
-            flip, x_ref[i], preferred_element_type=jnp.float32
+            flip, x_ref[slot[i]], preferred_element_type=jnp.float32
         ).astype(xrev_ref.dtype)
     gain = gain_ref[...]
     for i in range(nb):
         conv = jnp.dot(
             toeplitz[:, : n - i * br], g_scr[i * br :, :], preferred_element_type=jnp.float32
         )
-        own = g_ref[i].astype(jnp.float32)
+        own = g_scr[i * br : (i + 1) * br, :].astype(jnp.float32)
         out_ref[i, :br, :] = (conv * scale + gain * own).astype(out_ref.dtype)
     sums = [None] * nb
     for j in range(nb):
         row = lax.dot_general(
-            g_ref[j],
+            g_scr[j * br : (j + 1) * br, :],
             xrev_ref[: (j + 1) * br, :],
             (((1,), (1,)), ((), ())),
             preferred_element_type=jnp.float32,
@@ -196,7 +198,12 @@
             axis=2,
         )
         packed = jnp.concatenate([body, tap_rows], axis=1)
-    moved = lax.all_to_all(packed, "seq", split_axis=0, concat_axis=0, tiled=True)
+    arrived = [lax.dynamic_index_in_dim(packed, seq_index, 0, keepdims=True)]
+    for shift in range(1, seq_count):
+        chunk = lax.dynamic_index_in_dim(packed, (seq_index + shift) % seq_count, 0, keepdims=True)
+        pairs = [(i, (i + shift) % seq_count) for i in range(seq_count)]
+        arrived.append(lax.ppermute(chunk, "seq", pairs))
+    moved = jnp.concatenate(arrived, axis=0)
     stretch_gain = lax.dynamic_slice_in_dim(skip_gain, seq_index * stretch_width, stretch_width, 0)
     used_rows = 3 * stretch_filters * block_rows // stretch_width
     extra_rows = -(-used_rows // 8) * 8

time: 64.7 us -> 61.9 us (0.957)
  waiting for transfers between devices: 25.9 us -> 6.96 us
  blocking collectives: 19.8 us -> 27.7 us
  starting transfers between devices: 7.28 us -> 13.8 us
  local copies, waits for them, and re-layouts: 3.65 us -> 5.12 us
    all_to_all x1 -> x0, waiting for transfers between devices: 25.9 us -> none  [per_device(): lax.all_to_all(packed, 'seq', split_axis=0, concat_axis=0, tiled=True)]
    ppermute x0 -> x7, starting transfers between devices: none -> 13.8 us  [per_device(): arrived.append(lax.ppermute(chunk, 'seq', pairs))]
    all_to_all x1, blocking collectives: 19.8 us -> 27.7 us  [per_device(): lax.all_to_all(outgoing, 'seq', split_axis=0, concat_axis=0, tiled=True)]
    all_to_all x1 -> x0, starting transfers between devices: 7.28 us -> none  [per_device(): lax.all_to_all(packed, 'seq', split_axis=0, concat_axis=0, tiled=True)]
    ppermute x0 -> x7, waiting for transfers between devices: none -> 6.96 us  [per_device(): arrived.append(lax.ppermute(chunk, 'seq', pairs))]
    dynamic_slice x0 -> x1, local copies, waits for them, and re-layouts: none -> 1.4 us  [per_device(): lax.dynamic_index_in_dim(packed, (seq_index + shift) % seq_count, 0, keep...]
    unnamed x3 -> x9, local copies, waits for them, and re-layouts: 2 us -> 2.06 us
  transfers between devices with their start and end apart: 1 -> 7, of which waited for: 1 -> 2; matrix products, arithmetic and copies ran while one was open for 2% -> 2% of each run, Pallas kernels for 0% -> 0%
where the time goes in v11:
time: 61.9 us; the launch traced here: 61.6 us
  blocking collectives  27.7 us (45%)
  starting transfers between devices  13.8 us (22%)
  waiting for transfers between devices  6.96 us (11%)
  Pallas kernels  6.55 us (11%)
  local copies, waits for them, and re-layouts  5.12 us (8%)
  between operations  0.84 us (1%)
    all_to_all x1, blocking collectives, per_device(): lax.all_to_all(outgoing, 'seq', split_axis=0, concat_axis=0, tiled=True)  27.7 us
    ppermute x7, starting transfers between devices, per_device(): arrived.append(lax.ppermute(chunk, 'seq', pairs))  13.8 us
    ppermute x7, waiting for transfers between devices, per_device(): arrived.append(lax.ppermute(chunk, 'seq', pairs))  6.96 us
    pallas_call x1, Pallas kernels, local_grads(): pl.pallas_call(functools.partial(local_kernel, nb=nb, br=br, scale=scale,...  4.23 us
    pallas_call x1, Pallas kernels, per_device(): pl.pallas_call(functools.partial(pack_kernel, br=block_rows, sw=stretch_w...  2.32 us
    unnamed x9, local copies, waits for them, and re-layouts  2.06 us
    dynamic_slice x1, local copies, waits for them, and re-layouts, per_device(): lax.dynamic_index_in_dim(packed, (seq_index + shift) % seq_count, 0, keep...  1.4 us
    dynamic_slice x1, local copies, waits for them, and re-layouts, per_device(): lax.dynamic_slice_in_dim(skip_gain, seq_index * stretch_width, stretch_wi...  1.32 us
  transfers between devices with their start and end apart: 7, of which 2 were waited for; matrix products, arithmetic and copies ran while one was open for 2% of the time, Pallas kernels for 0%

profile of v11, /device:TPU:0, one launch (start us, length us, event | category | flops | bytes accessed | tf_op | source)
XLA Modules:
  0.0 61.6 jit_solution(982073528142583978)
XLA Ops:
  0.7 2.3 %shard_map.68 = bf16[8,136,512]{2,1,0:T(8,128)(2,1)} custom-call(bf16[128,2048]{1,0:T(8,128)(2,1)} %og_ref.1, bf16[128,2048]{1,0:T(8,128)(2,1)} %gate_ref.1, bf16[128,2048]{1,0:T(8,128)(2,1)} %x_ref.1, bf16[16,128]{1,0:T(8,128)(2,1)} %bitcast.24), custom_call_target="tpu_custom_call" | custom-call | tf_op jit(solution)/shard_map/pallas_call | solution.py:162
  3.1 1.4 %constant_dynamic-slice_fusion = (bf16[1,136,512]{2,1,0:T(8,128)(2,1)S(1)}, bf16[1,136,512]{2,1,0:T(8,128)(2,1)S(1)}, bf16[1,136,512]{2,1,0:T(8,128)(2,1)S(1)}, ...) fusion(bf16[8,136,512]{2,1,0:T(8,128)(2,1)} %shard_map.68, ...), kind=kLoop, calls=%fused_computation.15 | loop fusion | bytes 2228256 | tf_op jit(solution)/shard_map/jit(dynamic_index_in_dim)/dynamic_slice | solution.py:203
  4.5 3.0 %collective-permute-start = (bf16[1,136,512]{2,1,0:T(8,128)(2,1)S(1)}, bf16[1,136,512]{2,1,0:T(8,128)(2,1)S(1)}, u32[]{:S(2)}, u32[]{:S(2)}) collective-permute-start(bf16[1,136,512]{2,1,0:T(8,128)(2,1)S(1)} %get-tuple-element.14), channel_id=1, source_target_pairs={{0,2},{2,4},{4,6},{6,8},{8,10},{10,12},{12,14},{14,0},{1,3},{3,5},... | collective-permute-start | bytes 417800 | tf_op jit(solution)/shard_map/ppermute | solution.py:205
  7.5 1.6 %collective-permute-start.1 = (bf16[1,136,512]{2,1,0:T(8,128)(2,1)S(1)}, bf16[1,136,512]{2,1,0:T(8,128)(2,1)S(1)}, u32[]{:S(2)}, u32[]{:S(2)}) collective-permute-start(bf16[1,136,512]{2,1,0:T(8,128)(2,1)S(1)} %get-tuple-element.13), channel_id=1, source_target_pairs={{0,4},{2,6},{4,8},{6,10},{8,12},{10,14},{12,0},{14,2},{1,5},{3,7},... | collective-permute-start | bytes 417800 | tf_op jit(solution)/shard_map/ppermute | solution.py:205
  9.1 2.5 %collective-permute-start.2 = (bf16[1,136,512]{2,1,0:T(8,128)(2,1)S(1)}, bf16[1,136,512]{2,1,0:T(8,128)(2,1)S(1)}, u32[]{:S(2)}, u32[]{:S(2)}) collective-permute-start(bf16[1,136,512]{2,1,0:T(8,128)(2,1)S(1)} %get-tuple-element.12), channel_id=1, source_target_pairs={{0,6},{2,8},{4,10},{6,12},{8,14},{10,0},{12,2},{14,4},{1,7},{3,9},... | collective-permute-start | bytes 417800 | tf_op jit(solution)/shard_map/ppermute | solution.py:205
  11.6 1.2 %collective-permute-start.3 = (bf16[1,136,512]{2,1,0:T(8,128)(2,1)S(1)}, bf16[1,136,512]{2,1,0:T(8,128)(2,1)S(1)}, u32[]{:S(2)}, u32[]{:S(2)}) collective-permute-start(bf16[1,136,512]{2,1,0:T(8,128)(2,1)S(1)} %get-tuple-element.11), channel_id=1, source_target_pairs={{0,8},{2,10},{4,12},{6,14},{8,0},{10,2},{12,4},{14,6},{1,9},{3,11}... | collective-permute-start | bytes 417800 | tf_op jit(solution)/shard_map/ppermute | solution.py:205
  12.8 2.6 %collective-permute-start.4 = (bf16[1,136,512]{2,1,0:T(8,128)(2,1)S(1)}, bf16[1,136,512]{2,1,0:T(8,128)(2,1)S(1)}, u32[]{:S(2)}, u32[]{:S(2)}) collective-permute-start(bf16[1,136,512]{2,1,0:T(8,128)(2,1)S(1)} %get-tuple-element.10), channel_id=1, source_target_pairs={{0,10},{2,12},{4,14},{6,0},{8,2},{10,4},{12,6},{14,8},{1,11},{3,13... | collective-permute-start | bytes 417800 | tf_op jit(solution)/shard_map/ppermute | solution.py:205
  15.5 1.3 %dynamic_slice.36 = f32[256]{0:T(256)} dynamic-slice(f32[2048]{0:T(1024)} %param.9, s32[]{:T(128)S(6)} %select_n.74), dynamic_slice_sizes={256} | dynamic-slice | bytes 2052 | tf_op jit(solution)/shard_map/dynamic_slice | solution.py:207
  16.8 0.0 collective-permute-done
  16.8 1.3 %collective-permute-start.5 = (bf16[1,136,512]{2,1,0:T(8,128)(2,1)S(1)}, bf16[1,136,512]{2,1,0:T(8,128)(2,1)S(1)}, u32[]{:S(2)}, u32[]{:S(2)}) collective-permute-start(bf16[1,136,512]{2,1,0:T(8,128)(2,1)S(1)} %get-tuple-element.9), channel_id=1, source_target_pairs={{0,12},{2,14},{4,0},{6,2},{8,4},{10,6},{12,8},{14,10},{1,13},{3,15... | collective-permute-start | bytes 417800 | tf_op jit(solution)/shard_map/ppermute | solution.py:205
  18.2 0.0 collective-permute-done.1
  18.2 1.5 %collective-permute-start.6 = (bf16[1,136,512]{2,1,0:T(8,128)(2,1)S(1)}, bf16[1,136,512]{2,1,0:T(8,128)(2,1)S(1)}, u32[]{:S(2)}, u32[]{:S(2)}) collective-permute-start(bf16[1,136,512]{2,1,0:T(8,128)(2,1)S(1)} %get-tuple-element.8), channel_id=1, source_target_pairs={{0,14},{2,0},{4,2},{6,4},{8,6},{10,8},{12,10},{14,12},{1,15},{3,1}... | collective-permute-start | bytes 417800 | tf_op jit(solution)/shard_map/ppermute | solution.py:205
  19.6 6.6 %collective-permute-done.2 = bf16[1,136,512]{2,1,0:T(8,128)(2,1)S(1)} collective-permute-done((bf16[1,136,512]{2,1,0:T(8,128)(2,1)S(1)}, bf16[1,136,512]{2,1,0:T(8,128)(2,1)S(1)}, u32[]{:S(2)}, u32[]{:S(2)}) %collective-permute-start.2) | collective-permute-done | bytes 139296 | tf_op jit(solution)/shard_map/ppermute | solution.py:205
  26.2 0.4 collective-permute-done.3
  26.6 0.0 collective-permute-done.4
  26.7 0.0 collective-permute-done.5
  26.7 0.0 collective-permute-done.6
  26.7 0.0 copy-start
  26.7 1.0 %copy-done = bf16[8,136,512]{2,1,0:T(8,128)(2,1)} copy-done((bf16[8,136,512]{2,1,0:T(8,128)(2,1)}, bf16[8,136,512]{2,1,0:T(8,128)(2,1)S(1)}, u32[]{:S(2)}) %copy-start) | copy-done | bytes 1114136
  27.7 4.2 %shard_map.69 = (bf16[8,136,256]{2,1,0:T(8,128)(2,1)}, f32[2,8,256]{2,1,0:T(8,128)}) custom-call(bf16[8,136,512]{2,1,0:T(8,128)(2,1)} %copy-done, bf16[8,136,512]{2,1,0:T(8,128)(2,1)} %copy-done, bf16[8,136,512]{2,1,0:T(8,128)(2,1)} %copy-done, f32[2,1,128]{2,1,0:T(1,128)} %bitcast.25), custom_call_target="tpu_custom_call" | custom-call | tf_op jit(solution)/shard_map/pallas_call | solution.py:112
  31.9 27.7 %all_to_all.5 = bf16[8,136,256]{2,1,0:T(8,128)(2,1)S(1)} all-to-all(bf16[8,136,256]{2,1,0:T(8,128)(2,1)} %get-tuple-element.3), channel_id=1, replica_groups=mesh['groups'=2,'seq'=8,'chan'=2] {'seq'}, dimensions={0} | all-to-all | bytes 1114112 | tf_op jit(solution)/shard_map/all_to_all | solution.py:236
  59.6 0.3 copy.10
  59.9 1.0 %copy.12 = bf16[128,2048]{1,0:T(8,128)(2,1)} copy(bf16[128,2048]{0,1:T(8,128)(2,1)S(1)} %bitcast.22) | data formatting | bytes 1048576
  60.9 0.6 fusion
  (10 shorter events, 0.1 us)
Async XLA Ops:
  4.5 12.3 %collective-permute-start = (bf16[1,136,512]{2,1,0:T(8,128)(2,1)S(1)}, bf16[1,136,512]{2,1,0:T(8,128)(2,1)S(1)}, u32[]{:S(2)}, u32[]{:S(2)}) collective-permute-start(bf16[1,136,512]{2,1,0:T(8,128)(2,1)S(1)} %get-tuple-element.14), channel_id=1, source_target_pairs={{0,2},{2,4},{4,6},{6,8},{8,10},{10,12},{12,14},{14,0},{1,3},{3,5},... | collective-permute-start | bytes 417800 | tf_op jit(solution)/shard_map/ppermute | solution.py:205
  7.5 10.7 %collective-permute-start.1 = (bf16[1,136,512]{2,1,0:T(8,128)(2,1)S(1)}, bf16[1,136,512]{2,1,0:T(8,128)(2,1)S(1)}, u32[]{:S(2)}, u32[]{:S(2)}) collective-permute-start(bf16[1,136,512]{2,1,0:T(8,128)(2,1)S(1)} %get-tuple-element.13), channel_id=1, source_target_pairs={{0,4},{2,6},{4,8},{6,10},{8,12},{10,14},{12,0},{14,2},{1,5},{3,7},... | collective-permute-start | bytes 417800 | tf_op jit(solution)/shard_map/ppermute | solution.py:205
  9.1 17.2 %collective-permute-start.2 = (bf16[1,136,512]{2,1,0:T(8,128)(2,1)S(1)}, bf16[1,136,512]{2,1,0:T(8,128)(2,1)S(1)}, u32[]{:S(2)}, u32[]{:S(2)}) collective-permute-start(bf16[1,136,512]{2,1,0:T(8,128)(2,1)S(1)} %get-tuple-element.12), channel_id=1, source_target_pairs={{0,6},{2,8},{4,10},{6,12},{8,14},{10,0},{12,2},{14,4},{1,7},{3,9},... | collective-permute-start | bytes 417800 | tf_op jit(solution)/shard_map/ppermute | solution.py:205
  11.6 15.0 %collective-permute-start.3 = (bf16[1,136,512]{2,1,0:T(8,128)(2,1)S(1)}, bf16[1,136,512]{2,1,0:T(8,128)(2,1)S(1)}, u32[]{:S(2)}, u32[]{:S(2)}) collective-permute-start(bf16[1,136,512]{2,1,0:T(8,128)(2,1)S(1)} %get-tuple-element.11), channel_id=1, source_target_pairs={{0,8},{2,10},{4,12},{6,14},{8,0},{10,2},{12,4},{14,6},{1,9},{3,11}... | collective-permute-start | bytes 417800 | tf_op jit(solution)/shard_map/ppermute | solution.py:205
  12.8 13.8 %collective-permute-start.4 = (bf16[1,136,512]{2,1,0:T(8,128)(2,1)S(1)}, bf16[1,136,512]{2,1,0:T(8,128)(2,1)S(1)}, u32[]{:S(2)}, u32[]{:S(2)}) collective-permute-start(bf16[1,136,512]{2,1,0:T(8,128)(2,1)S(1)} %get-tuple-element.10), channel_id=1, source_target_pairs={{0,10},{2,12},{4,14},{6,0},{8,2},{10,4},{12,6},{14,8},{1,11},{3,13... | collective-permute-start | bytes 417800 | tf_op jit(solution)/shard_map/ppermute | solution.py:205
  16.8 9.9 %collective-permute-start.5 = (bf16[1,136,512]{2,1,0:T(8,128)(2,1)S(1)}, bf16[1,136,512]{2,1,0:T(8,128)(2,1)S(1)}, u32[]{:S(2)}, u32[]{:S(2)}) collective-permute-start(bf16[1,136,512]{2,1,0:T(8,128)(2,1)S(1)} %get-tuple-element.9), channel_id=1, source_target_pairs={{0,12},{2,14},{4,0},{6,2},{8,4},{10,6},{12,8},{14,10},{1,13},{3,15... | collective-permute-start | bytes 417800 | tf_op jit(solution)/shard_map/ppermute | solution.py:205
  18.2 8.5 %collective-permute-start.6 = (bf16[1,136,512]{2,1,0:T(8,128)(2,1)S(1)}, bf16[1,136,512]{2,1,0:T(8,128)(2,1)S(1)}, u32[]{:S(2)}, u32[]{:S(2)}) collective-permute-start(bf16[1,136,512]{2,1,0:T(8,128)(2,1)S(1)} %get-tuple-element.8), channel_id=1, source_target_pairs={{0,14},{2,0},{4,2},{6,4},{8,6},{10,8},{12,10},{14,12},{1,15},{3,1}... | collective-permute-start | bytes 417800 | tf_op jit(solution)/shard_map/ppermute | solution.py:205
  26.7 1.0 %copy-start = (bf16[8,136,512]{2,1,0:T(8,128)(2,1)}, bf16[8,136,512]{2,1,0:T(8,128)(2,1)S(1)}, u32[]{:S(2)}) copy-start(bf16[8,136,512]{2,1,0:T(8,128)(2,1)S(1)} %constant_dynamic-update-slice_fusion.g_ref.x_ref.t_ref) | copy-start | bytes 3342340

commit v12 on v11

--- a/solution.py
+++ b/solution.py
@@ -233,16 +233,30 @@
         split = split.reshape(seq_count, used_rows, stretch_width)
         split = jnp.pad(split, ((0, 0), (0, extra_rows - used_rows), (0, 0)))
         outgoing = lax.dynamic_update_slice_in_dim(local_grad, split, block_rows, 1)
-    returned = lax.all_to_all(outgoing, "seq", split_axis=0, concat_axis=0, tiled=True)
-    input_grad = jnp.transpose(returned[:, :block_rows, :], (1, 0, 2)).reshape(
-        block_rows, chan_width
-    )
     sharers = seq_count * stretch_filters // filters
     if stretch_group % 128 == 0:
-        parts = returned[:, block_rows : block_rows + 3, :].astype(jnp.float32)
-        parts = parts.reshape(seq_count, 3, stretch_filters, stretch_group)[..., :block_rows]
-        parts = parts[:, 0] + parts[:, 1] + parts[:, 2]
-    else:
+        input_grad = jnp.zeros((block_rows, chan_width), outgoing.dtype)
+        lag_slots = []
+        for shift in range(seq_count):
+            chunk = lax.dynamic_index_in_dim(
+                outgoing, (seq_index - shift) % seq_count, 0, keepdims=False
+            )
+            if shift:
+                pairs = [(i, (i - shift) % seq_count) for i in range(seq_count)]
+                chunk = lax.ppermute(chunk, "seq", pairs)
+            source = (seq_index + shift) % seq_count
+            input_grad = lax.dynamic_update_slice_in_dim(
+                input_grad, chunk[:block_rows], source * stretch_width, 1
+            )
+            rows = chunk[block_rows : block_rows + 3].astype(jnp.float32)
+            rows = rows.reshape(3, stretch_filters, stretch_group)[..., :block_rows]
+            lag_slots.append(rows[0] + rows[1] + rows[2])
+        parts = jnp.roll(jnp.stack(lag_slots, axis=0), seq_index, axis=0)
+    else:
+        returned = lax.all_to_all(outgoing, "seq", split_axis=0, concat_axis=0, tiled=True)
+        input_grad = jnp.transpose(returned[:, :block_rows, :], (1, 0, 2)).reshape(
+            block_rows, chan_width
+        )
         parts = returned[:, block_rows : block_rows + used_rows, :].astype(jnp.float32)
         parts = parts.reshape(seq_count, 3, stretch_filters, block_rows).sum(axis=1)
     filter_grad = jnp.transpose(

time: 61.9 us -> 61.6 us (level)
  blocking collectives: 27.7 us -> 0 us
  starting transfers between devices: 13.8 us -> 31.7 us
  waiting for transfers between devices: 6.96 us -> 13.8 us
  local copies, waits for them, and re-layouts: 5.12 us -> 7.43 us
    all_to_all x1 -> x0, blocking collectives: 27.7 us -> none  [per_device(): lax.all_to_all(outgoing, 'seq', split_axis=0, concat_axis=0, tiled=True)]
    ppermute x0 -> x7, starting transfers between devices: none -> 17.9 us  [per_device(): chunk = lax.ppermute(chunk, 'seq', pairs)]
    ppermute x0 -> x7, waiting for transfers between devices: none -> 6.83 us  [per_device(): chunk = lax.ppermute(chunk, 'seq', pairs)]
    squeeze x0 -> x1, local copies, waits for them, and re-layouts: none -> 1.12 us  [per_device(): lax.dynamic_index_in_dim(outgoing, (seq_index - shift) % seq_count, 0, ke...]
    dynamic_update_slice x0 -> x8, local copies, waits for them, and re-layouts: none -> 0.93 us  [per_device(): lax.dynamic_update_slice_in_dim(input_grad, chunk[:block_rows], source *...]
    convert_element_type x0 -> x8, other arithmetic: none -> 0.7 us  [per_device(): rows = chunk[block_rows:block_rows + 3].astype(jnp.float32)]
    unnamed x9 -> x25, local copies, waits for them, and re-layouts: 2.06 us -> 1.99 us
  transfers between devices with their start and end apart: 7 -> 14, of which waited for: 2 -> 5; matrix products, arithmetic and copies ran while one was open for 2% -> 5% of each run, Pallas kernels for 0% -> 0%
where the time goes in v12:
time: 61.6 us; the launch traced here: 61.2 us
  starting transfers between devices  31.7 us (51%)
  waiting for transfers between devices  13.8 us (22%)
  local copies, waits for them, and re-layouts  7.43 us (12%)
  Pallas kernels  6.54 us (11%)
  between operations  1 us (2%)
  other arithmetic  0.77 us (1%)
    ppermute x7, starting transfers between devices, per_device(): chunk = lax.ppermute(chunk, 'seq', pairs)  17.9 us
    ppermute x7, starting transfers between devices, per_device(): arrived.append(lax.ppermute(chunk, 'seq', pairs))  13.8 us
    ppermute x7, waiting for transfers between devices, per_device(): arrived.append(lax.ppermute(chunk, 'seq', pairs))  6.96 us
    ppermute x7, waiting for transfers between devices, per_device(): chunk = lax.ppermute(chunk, 'seq', pairs)  6.83 us
    pallas_call x1, Pallas kernels, local_grads(): pl.pallas_call(functools.partial(local_kernel, nb=nb, br=br, scale=scale,...  4.21 us
    pallas_call x1, Pallas kernels, per_device(): pl.pallas_call(functools.partial(pack_kernel, br=block_rows, sw=stretch_w...  2.33 us
    unnamed x25, local copies, waits for them, and re-layouts  1.99 us
    dynamic_slice x1, local copies, waits for them, and re-layouts, per_device(): lax.dynamic_index_in_dim(packed, (seq_index + shift) % seq_count, 0, keep...  1.4 us
  transfers between devices with their start and end apart: 14, of which 5 were waited for; matrix products, arithmetic and copies ran while one was open for 5% of the time, Pallas kernels for 0%

profile of v12, /device:TPU:0, one launch (start us, length us, event | category | flops | bytes accessed | tf_op | source)
XLA Modules:
  0.0 61.2 jit_solution(12053511273889340278)
XLA Ops:
  0.7 2.3 %shard_map.68 = bf16[8,136,512]{2,1,0:T(8,128)(2,1)} custom-call(bf16[128,2048]{1,0:T(8,128)(2,1)} %og_ref.1, bf16[128,2048]{1,0:T(8,128)(2,1)} %gate_ref.1, bf16[128,2048]{1,0:T(8,128)(2,1)} %x_ref.1, bf16[16,128]{1,0:T(8,128)(2,1)} %bitcast.48), custom_call_target="tpu_custom_call" | custom-call | tf_op jit(solution)/shard_map/pallas_call | solution.py:162
  3.1 1.4 %constant_dynamic-slice_fusion.2 = (bf16[1,136,512]{2,1,0:T(8,128)(2,1)S(1)}, bf16[1,136,512]{2,1,0:T(8,128)(2,1)S(1)}, bf16[1,136,512]{2,1,0:T(8,128)(2,1)S(1)}...) fusion(bf16[8,136,512]{2,1,0:T(8,128)(2,1)} %shard_map.68, ...), kind=kLoop, calls=%fused_computation.42 | loop fusion | bytes 2228256 | tf_op jit(solution)/shard_map/jit(dynamic_index_in_dim)/dynamic_slice | solution.py:203
  4.5 3.0 %collective-permute-start = (bf16[1,136,512]{2,1,0:T(8,128)(2,1)S(1)}, bf16[1,136,512]{2,1,0:T(8,128)(2,1)S(1)}, u32[]{:S(2)}, u32[]{:S(2)}) collective-permute-start(bf16[1,136,512]{2,1,0:T(8,128)(2,1)S(1)} %get-tuple-element.10), channel_id=1, source_target_pairs={{0,2},{2,4},{4,6},{6,8},{8,10},{10,12},{12,14},{14,0},{1,3},{3,5},... | collective-permute-start | bytes 417800 | tf_op jit(solution)/shard_map/ppermute | solution.py:205
  7.5 1.6 %collective-permute-start.1 = (bf16[1,136,512]{2,1,0:T(8,128)(2,1)S(1)}, bf16[1,136,512]{2,1,0:T(8,128)(2,1)S(1)}, u32[]{:S(2)}, u32[]{:S(2)}) collective-permute-start(bf16[1,136,512]{2,1,0:T(8,128)(2,1)S(1)} %get-tuple-element.9), channel_id=1, source_target_pairs={{0,4},{2,6},{4,8},{6,10},{8,12},{10,14},{12,0},{14,2},{1,5},{3,7},... | collective-permute-start | bytes 417800 | tf_op jit(solution)/shard_map/ppermute | solution.py:205
  9.1 2.5 %collective-permute-start.2 = (bf16[1,136,512]{2,1,0:T(8,128)(2,1)S(1)}, bf16[1,136,512]{2,1,0:T(8,128)(2,1)S(1)}, u32[]{:S(2)}, u32[]{:S(2)}) collective-permute-start(bf16[1,136,512]{2,1,0:T(8,128)(2,1)S(1)} %get-tuple-element.8), channel_id=1, source_target_pairs={{0,6},{2,8},{4,10},{6,12},{8,14},{10,0},{12,2},{14,4},{1,7},{3,9},... | collective-permute-start | bytes 417800 | tf_op jit(solution)/shard_map/ppermute | solution.py:205
  11.6 1.2 %collective-permute-start.3 = (bf16[1,136,512]{2,1,0:T(8,128)(2,1)S(1)}, bf16[1,136,512]{2,1,0:T(8,128)(2,1)S(1)}, u32[]{:S(2)}, u32[]{:S(2)}) collective-permute-start(bf16[1,136,512]{2,1,0:T(8,128)(2,1)S(1)} %get-tuple-element.7), channel_id=1, source_target_pairs={{0,8},{2,10},{4,12},{6,14},{8,0},{10,2},{12,4},{14,6},{1,9},{3,11}... | collective-permute-start | bytes 417800 | tf_op jit(solution)/shard_map/ppermute | solution.py:205
  12.8 2.6 %collective-permute-start.4 = (bf16[1,136,512]{2,1,0:T(8,128)(2,1)S(1)}, bf16[1,136,512]{2,1,0:T(8,128)(2,1)S(1)}, u32[]{:S(2)}, u32[]{:S(2)}) collective-permute-start(bf16[1,136,512]{2,1,0:T(8,128)(2,1)S(1)} %get-tuple-element.6), channel_id=1, source_target_pairs={{0,10},{2,12},{4,14},{6,0},{8,2},{10,4},{12,6},{14,8},{1,11},{3,13... | collective-permute-start | bytes 417800 | tf_op jit(solution)/shard_map/ppermute | solution.py:205
  15.5 1.3 %dynamic_slice.65 = f32[256]{0:T(256)} dynamic-slice(f32[2048]{0:T(1024)} %param.9, s32[]{:T(128)S(6)} %select_n.181), dynamic_slice_sizes={256} | dynamic-slice | bytes 2052 | tf_op jit(solution)/shard_map/dynamic_slice | solution.py:207
  16.8 0.0 collective-permute-done
  16.8 1.3 %collective-permute-start.5 = (bf16[1,136,512]{2,1,0:T(8,128)(2,1)S(1)}, bf16[1,136,512]{2,1,0:T(8,128)(2,1)S(1)}, u32[]{:S(2)}, u32[]{:S(2)}) collective-permute-start(bf16[1,136,512]{2,1,0:T(8,128)(2,1)S(1)} %get-tuple-element.5), channel_id=1, source_target_pairs={{0,12},{2,14},{4,0},{6,2},{8,4},{10,6},{12,8},{14,10},{1,13},{3,15... | collective-permute-start | bytes 417800 | tf_op jit(solution)/shard_map/ppermute | solution.py:205
  18.2 0.0 collective-permute-done.1
  18.2 1.5 %collective-permute-start.6 = (bf16[1,136,512]{2,1,0:T(8,128)(2,1)S(1)}, bf16[1,136,512]{2,1,0:T(8,128)(2,1)S(1)}, u32[]{:S(2)}, u32[]{:S(2)}) collective-permute-start(bf16[1,136,512]{2,1,0:T(8,128)(2,1)S(1)} %get-tuple-element.4), channel_id=1, source_target_pairs={{0,14},{2,0},{4,2},{6,4},{8,6},{10,8},{12,10},{14,12},{1,15},{3,1}... | collective-permute-start | bytes 417800 | tf_op jit(solution)/shard_map/ppermute | solution.py:205
  19.7 6.6 %collective-permute-done.2 = bf16[1,136,512]{2,1,0:T(8,128)(2,1)S(1)} collective-permute-done((bf16[1,136,512]{2,1,0:T(8,128)(2,1)S(1)}, bf16[1,136,512]{2,1,0:T(8,128)(2,1)S(1)}, u32[]{:S(2)}, u32[]{:S(2)}) %collective-permute-start.2) | collective-permute-done | bytes 139296 | tf_op jit(solution)/shard_map/ppermute | solution.py:205
  26.3 0.4 collective-permute-done.3
  26.6 0.0 collective-permute-done.4
  26.7 0.0 collective-permute-done.5
  26.7 0.0 collective-permute-done.6
  26.7 0.0 copy-start
  26.7 1.0 %copy-done = bf16[8,136,512]{2,1,0:T(8,128)(2,1)} copy-done((bf16[8,136,512]{2,1,0:T(8,128)(2,1)}, bf16[8,136,512]{2,1,0:T(8,128)(2,1)S(1)}, u32[]{:S(2)}) %copy-start) | copy-done | bytes 1114136
  27.7 4.2 %shard_map.69 = (bf16[8,136,256]{2,1,0:T(8,128)(2,1)}, f32[2,8,256]{2,1,0:T(8,128)}) custom-call(bf16[8,136,512]{2,1,0:T(8,128)(2,1)} %copy-done, bf16[8,136,512]{2,1,0:T(8,128)(2,1)} %copy-done, bf16[8,136,512]{2,1,0:T(8,128)(2,1)} %copy-done, f32[2,1,128]{2,1,0:T(1,128)} %bitcast.49), custom_call_target="tpu_custom_call" | custom-call | tf_op jit(solution)/shard_map/pallas_call | solution.py:112
  32.0 1.1 %dynamic-slice_bitcast_fusion = (bf16[136,256]{1,0:T(8,128)(2,1)S(1)}, bf16[136,256]{1,0:T(8,128)(2,1)S(1)}, bf16[136,256]{1,0:T(8,128)(2,1)S(1)}, bf16[136,256]...) fusion(bf16[8,136,256]{2,1,0:T(8,128)(2,1)} %get-tuple-element.3,, ...), kind=kLoop, calls=%fused_computation.1 | loop fusion | bytes 974876 | tf_op jit(solution)/shard_map/jit(dynamic_index_in_dim)/squeeze | solution.py:241
  33.1 11.3 %collective-permute-start.7 = (bf16[136,256]{1,0:T(8,128)(2,1)S(1)}, bf16[136,256]{1,0:T(8,128)(2,1)S(1)}, u32[]{:S(2)}, u32[]{:S(2)}) collective-permute-start(bf16[136,256]{1,0:T(8,128)(2,1)S(1)} %get-tuple-element.18), channel_id=1, source_target_pairs={{0,14},{2,0},{4,2},{6,4},{8,6},{10,8},{12,10},{14,12},{1,15},{3,1}... | collective-permute-start | bytes 208904 | tf_op jit(solution)/shard_map/ppermute | solution.py:246
  44.4 0.7 %fusion.1 = f32[1,3,256]{2,1,0:T(4,128)S(1)} fusion(bf16[8,136,256]{2,1,0:T(8,128)(2,1)} %get-tuple-element.3, s32[]{:T(128)S(6)} %select_n.183, s32[]{:T(128)S(6)} %add.439), kind=kLoop, calls=%fused_computation.49 | loop fusion | flops 768 | bytes 4616 | tf_op jit(solution)/shard_map/convert_element_type | solution.py:251
  45.1 0.4 collective-permute-start.8
  45.5 0.0 collective-permute-start.9
  45.5 2.5 %collective-permute-start.10 = (bf16[136,256]{1,0:T(8,128)(2,1)S(1)}, bf16[136,256]{1,0:T(8,128)(2,1)S(1)}, u32[]{:S(2)}, u32[]{:S(2)}) collective-permute-start(bf16[136,256]{1,0:T(8,128)(2,1)S(1)} %get-tuple-element.15), channel_id=1, source_target_pairs={{0,8},{2,10},{4,12},{6,14},{8,0},{10,2},{12,4},{14,6},{1,9},{3,11}... | collective-permute-start | bytes 208904 | tf_op jit(solution)/shard_map/ppermute | solution.py:246
  48.0 0.4 collective-permute-start.11
  48.5 0.9 %fusion = bf16[128,2048]{1,0:T(8,128)(2,1)S(1)} fusion(bf16[128,2048]{1,0:T(8,128)(2,1)S(1)} %broadcast_in_dim.3, s32[]{:T(128)S(6)} %select_n.184, bf16[8,136,256]{2,1,0:T(8,128)(2,1)} %get-tuple-element.3, s32[]{:T(128)S(6)} %select_n.183), kind=kLoop, calls=%fused_computation.16 | loop fusion | bytes 131080 | tf_op jit(solution)/shard_map/dynamic_update_slice | solution.py:248
  49.4 0.0 collective-permute-done.7
  49.4 2.9 %collective-permute-start.12 = (bf16[136,256]{1,0:T(8,128)(2,1)S(1)}, bf16[136,256]{1,0:T(8,128)(2,1)S(1)}, u32[]{:S(2)}, u32[]{:S(2)}) collective-permute-start(bf16[136,256]{1,0:T(8,128)(2,1)S(1)} %get-tuple-element.13), channel_id=1, source_target_pairs={{0,4},{2,6},{4,8},{6,10},{8,12},{10,14},{12,0},{14,2},{1,5},{3,7},... | collective-permute-start | bytes 208904 | tf_op jit(solution)/shard_map/ppermute | solution.py:246
  52.3 0.0 collective-permute-done.8
  52.3 0.2 collective-permute-start.13
  52.6 0.0 collective-permute-done.9
  52.6 4.7 %collective-permute-done.10 = bf16[136,256]{1,0:T(8,128)(2,1)S(1)} collective-permute-done((bf16[136,256]{1,0:T(8,128)(2,1)S(1)}, bf16[136,256]{1,0:T(8,128)(2,1)S(1)}, u32[]{:S(2)}, u32[]{:S(2)}) %collective-permute-start.10) | collective-permute-done | bytes 69664 | tf_op jit(solution)/shard_map/ppermute | solution.py:246
  57.3 1.4 %collective-permute-done.11 = bf16[136,256]{1,0:T(8,128)(2,1)S(1)} collective-permute-done((bf16[136,256]{1,0:T(8,128)(2,1)S(1)}, bf16[136,256]{1,0:T(8,128)(2,1)S(1)}, u32[]{:S(2)}, u32[]{:S(2)}) %collective-permute-start.11) | collective-permute-done | bytes 69664 | tf_op jit(solution)/shard_map/ppermute | solution.py:246
  58.7 0.0 collective-permute-done.12
  58.8 0.7 %collective-permute-done.13 = bf16[136,256]{1,0:T(8,128)(2,1)S(1)} collective-permute-done((bf16[136,256]{1,0:T(8,128)(2,1)S(1)}, bf16[136,256]{1,0:T(8,128)(2,1)S(1)}, u32[]{:S(2)}, u32[]{:S(2)}) %collective-permute-start.13) | collective-permute-done | bytes 69664 | tf_op jit(solution)/shard_map/ppermute | solution.py:246
  59.7 0.6 constant_dynamic-slice_fusion
  60.4 0.0 copy-start.1
  60.4 0.8 %copy-done.1 = bf16[128,2048]{1,0:T(8,128)(2,1)} copy-done((bf16[128,2048]{1,0:T(8,128)(2,1)}, bf16[128,2048]{1,0:T(8,128)(2,1)S(1)}, u32[]{:S(2)}) %copy-start.1) | copy-done | bytes 524312
  (46 shorter events, 0.4 us)
Async XLA Ops:
  4.5 12.3 %collective-permute-start = (bf16[1,136,512]{2,1,0:T(8,128)(2,1)S(1)}, bf16[1,136,512]{2,1,0:T(8,128)(2,1)S(1)}, u32[]{:S(2)}, u32[]{:S(2)}) collective-permute-start(bf16[1,136,512]{2,1,0:T(8,128)(2,1)S(1)} %get-tuple-element.10), channel_id=1, source_target_pairs={{0,2},{2,4},{4,6},{6,8},{8,10},{10,12},{12,14},{14,0},{1,3},{3,5},... | collective-permute-start | bytes 417800 | tf_op jit(solution)/shard_map/ppermute | solution.py:205
  7.5 10.7 %collective-permute-start.1 = (bf16[1,136,512]{2,1,0:T(8,128)(2,1)S(1)}, bf16[1,136,512]{2,1,0:T(8,128)(2,1)S(1)}, u32[]{:S(2)}, u32[]{:S(2)}) collective-permute-start(bf16[1,136,512]{2,1,0:T(8,128)(2,1)S(1)} %get-tuple-element.9), channel_id=1, source_target_pairs={{0,4},{2,6},{4,8},{6,10},{8,12},{10,14},{12,0},{14,2},{1,5},{3,7},... | collective-permute-start | bytes 417800 | tf_op jit(solution)/shard_map/ppermute | solution.py:205
  9.1 17.2 %collective-permute-start.2 = (bf16[1,136,512]{2,1,0:T(8,128)(2,1)S(1)}, bf16[1,136,512]{2,1,0:T(8,128)(2,1)S(1)}, u32[]{:S(2)}, u32[]{:S(2)}) collective-permute-start(bf16[1,136,512]{2,1,0:T(8,128)(2,1)S(1)} %get-tuple-element.8), channel_id=1, source_target_pairs={{0,6},{2,8},{4,10},{6,12},{8,14},{10,0},{12,2},{14,4},{1,7},{3,9},... | collective-permute-start | bytes 417800 | tf_op jit(solution)/shard_map/ppermute | solution.py:205
  11.6 15.0 %collective-permute-start.3 = (bf16[1,136,512]{2,1,0:T(8,128)(2,1)S(1)}, bf16[1,136,512]{2,1,0:T(8,128)(2,1)S(1)}, u32[]{:S(2)}, u32[]{:S(2)}) collective-permute-start(bf16[1,136,512]{2,1,0:T(8,128)(2,1)S(1)} %get-tuple-element.7), channel_id=1, source_target_pairs={{0,8},{2,10},{4,12},{6,14},{8,0},{10,2},{12,4},{14,6},{1,9},{3,11}... | collective-permute-start | bytes 417800 | tf_op jit(solution)/shard_map/ppermute | solution.py:205
  12.8 13.8 %collective-permute-start.4 = (bf16[1,136,512]{2,1,0:T(8,128)(2,1)S(1)}, bf16[1,136,512]{2,1,0:T(8,128)(2,1)S(1)}, u32[]{:S(2)}, u32[]{:S(2)}) collective-permute-start(bf16[1,136,512]{2,1,0:T(8,128)(2,1)S(1)} %get-tuple-element.6), channel_id=1, source_target_pairs={{0,10},{2,12},{4,14},{6,0},{8,2},{10,4},{12,6},{14,8},{1,11},{3,13... | collective-permute-start | bytes 417800 | tf_op jit(solution)/shard_map/ppermute | solution.py:205
  16.8 9.9 %collective-permute-start.5 = (bf16[1,136,512]{2,1,0:T(8,128)(2,1)S(1)}, bf16[1,136,512]{2,1,0:T(8,128)(2,1)S(1)}, u32[]{:S(2)}, u32[]{:S(2)}) collective-permute-start(bf16[1,136,512]{2,1,0:T(8,128)(2,1)S(1)} %get-tuple-element.5), channel_id=1, source_target_pairs={{0,12},{2,14},{4,0},{6,2},{8,4},{10,6},{12,8},{14,10},{1,13},{3,15... | collective-permute-start | bytes 417800 | tf_op jit(solution)/shard_map/ppermute | solution.py:205
  18.2 8.5 %collective-permute-start.6 = (bf16[1,136,512]{2,1,0:T(8,128)(2,1)S(1)}, bf16[1,136,512]{2,1,0:T(8,128)(2,1)S(1)}, u32[]{:S(2)}, u32[]{:S(2)}) collective-permute-start(bf16[1,136,512]{2,1,0:T(8,128)(2,1)S(1)} %get-tuple-element.4), channel_id=1, source_target_pairs={{0,14},{2,0},{4,2},{6,4},{8,6},{10,8},{12,10},{14,12},{1,15},{3,1}... | collective-permute-start | bytes 417800 | tf_op jit(solution)/shard_map/ppermute | solution.py:205
  26.7 1.0 %copy-start = (bf16[8,136,512]{2,1,0:T(8,128)(2,1)}, bf16[8,136,512]{2,1,0:T(8,128)(2,1)S(1)}, u32[]{:S(2)}) copy-start(bf16[8,136,512]{2,1,0:T(8,128)(2,1)S(1)} %constant_dynamic-update-slice_fusion.g_ref.x_ref.t_ref) | copy-start | bytes 3342340
  33.1 16.3 %collective-permute-start.7 = (bf16[136,256]{1,0:T(8,128)(2,1)S(1)}, bf16[136,256]{1,0:T(8,128)(2,1)S(1)}, u32[]{:S(2)}, u32[]{:S(2)}) collective-permute-start(bf16[136,256]{1,0:T(8,128)(2,1)S(1)} %get-tuple-element.18), channel_id=1, source_target_pairs={{0,14},{2,0},{4,2},{6,4},{8,6},{10,8},{12,10},{14,12},{1,15},{3,1}... | collective-permute-start | bytes 208904 | tf_op jit(solution)/shard_map/ppermute | solution.py:246
  45.1 7.2 %collective-permute-start.8 = (bf16[136,256]{1,0:T(8,128)(2,1)S(1)}, bf16[136,256]{1,0:T(8,128)(2,1)S(1)}, u32[]{:S(2)}, u32[]{:S(2)}) collective-permute-start(bf16[136,256]{1,0:T(8,128)(2,1)S(1)} %get-tuple-element.17), channel_id=1, source_target_pairs={{0,12},{2,14},{4,0},{6,2},{8,4},{10,6},{12,8},{14,10},{1,13},{3,15... | collective-permute-start | bytes 208904 | tf_op jit(solution)/shard_map/ppermute | solution.py:246
  45.5 7.1 %collective-permute-start.9 = (bf16[136,256]{1,0:T(8,128)(2,1)S(1)}, bf16[136,256]{1,0:T(8,128)(2,1)S(1)}, u32[]{:S(2)}, u32[]{:S(2)}) collective-permute-start(bf16[136,256]{1,0:T(8,128)(2,1)S(1)} %get-tuple-element.16), channel_id=1, source_target_pairs={{0,10},{2,12},{4,14},{6,0},{8,2},{10,4},{12,6},{14,8},{1,11},{3,13... | collective-permute-start | bytes 208904 | tf_op jit(solution)/shard_map/ppermute | solution.py:246
  45.5 11.8 %collective-permute-start.10 = (bf16[136,256]{1,0:T(8,128)(2,1)S(1)}, bf16[136,256]{1,0:T(8,128)(2,1)S(1)}, u32[]{:S(2)}, u32[]{:S(2)}) collective-permute-start(bf16[136,256]{1,0:T(8,128)(2,1)S(1)} %get-tuple-element.15), channel_id=1, source_target_pairs={{0,8},{2,10},{4,12},{6,14},{8,0},{10,2},{12,4},{14,6},{1,9},{3,11}... | collective-permute-start | bytes 208904 | tf_op jit(solution)/shard_map/ppermute | solution.py:246
  48.0 10.7 %collective-permute-start.11 = (bf16[136,256]{1,0:T(8,128)(2,1)S(1)}, bf16[136,256]{1,0:T(8,128)(2,1)S(1)}, u32[]{:S(2)}, u32[]{:S(2)}) collective-permute-start(bf16[136,256]{1,0:T(8,128)(2,1)S(1)} %get-tuple-element.14), channel_id=1, source_target_pairs={{0,6},{2,8},{4,10},{6,12},{8,14},{10,0},{12,2},{14,4},{1,7},{3,9},... | collective-permute-start | bytes 208904 | tf_op jit(solution)/shard_map/ppermute | solution.py:246
  49.4 9.4 %collective-permute-start.12 = (bf16[136,256]{1,0:T(8,128)(2,1)S(1)}, bf16[136,256]{1,0:T(8,128)(2,1)S(1)}, u32[]{:S(2)}, u32[]{:S(2)}) collective-permute-start(bf16[136,256]{1,0:T(8,128)(2,1)S(1)} %get-tuple-element.13), channel_id=1, source_target_pairs={{0,4},{2,6},{4,8},{6,10},{8,12},{10,14},{12,0},{14,2},{1,5},{3,7},... | collective-permute-start | bytes 208904 | tf_op jit(solution)/shard_map/ppermute | solution.py:246
  52.3 7.2 %collective-permute-start.13 = (bf16[136,256]{1,0:T(8,128)(2,1)S(1)}, bf16[136,256]{1,0:T(8,128)(2,1)S(1)}, u32[]{:S(2)}, u32[]{:S(2)}) collective-permute-start(bf16[136,256]{1,0:T(8,128)(2,1)S(1)} %get-tuple-element.12), channel_id=1, source_target_pairs={{0,2},{2,4},{4,6},{6,8},{8,10},{10,12},{12,14},{14,0},{1,3},{3,5},... | collective-permute-start | bytes 208904 | tf_op jit(solution)/shard_map/ppermute | solution.py:246
  60.4 0.8 %copy-start.1 = (bf16[128,2048]{1,0:T(8,128)(2,1)}, bf16[128,2048]{1,0:T(8,128)(2,1)S(1)}, u32[]{:S(2)}) copy-start(bf16[128,2048]{1,0:T(8,128)(2,1)S(1)} %slice_dynamic-update-slice_fusion) | copy-start | bytes 1572868

commit v13 on v12

--- a/solution.py
+++ b/solution.py
@@ -198,11 +198,15 @@
             axis=2,
         )
         packed = jnp.concatenate([body, tap_rows], axis=1)
-    arrived = [lax.dynamic_index_in_dim(packed, seq_index, 0, keepdims=True)]
-    for shift in range(1, seq_count):
+    order = []
+    for step in range(1, seq_count // 2 + 1):
+        order += [step] if step == seq_count - step else [step, seq_count - step]
+    arrived = [None] * seq_count
+    arrived[0] = lax.dynamic_index_in_dim(packed, seq_index, 0, keepdims=True)
+    for shift in order:
         chunk = lax.dynamic_index_in_dim(packed, (seq_index + shift) % seq_count, 0, keepdims=True)
         pairs = [(i, (i + shift) % seq_count) for i in range(seq_count)]
-        arrived.append(lax.ppermute(chunk, "seq", pairs))
+        arrived[shift] = lax.ppermute(chunk, "seq", pairs)
     moved = jnp.concatenate(arrived, axis=0)
     stretch_gain = lax.dynamic_slice_in_dim(skip_gain, seq_index * stretch_width, stretch_width, 0)
     used_rows = 3 * stretch_filters * block_rows // stretch_width

time: 61.6 us -> 61.6 us (level)
  no operation moved by 1% of the time
where the time goes in v13:
time: 61.6 us; the launch traced here: 61.2 us
  starting transfers between devices  31.7 us (51%)
  waiting for transfers between devices  13.8 us (22%)
  local copies, waits for them, and re-layouts  7.43 us (12%)
  Pallas kernels  6.54 us (11%)
  between operations  1 us (2%)
  other arithmetic  0.77 us (1%)
    ppermute x7, starting transfers between devices, per_device(): chunk = lax.ppermute(chunk, 'seq', pairs)  17.9 us
    ppermute x7, starting transfers between devices, per_device(): arrived[shift] = lax.ppermute(chunk, 'seq', pairs)  13.8 us
    ppermute x7, waiting for transfers between devices, per_device(): arrived[shift] = lax.ppermute(chunk, 'seq', pairs)  6.96 us
    ppermute x7, waiting for transfers between devices, per_device(): chunk = lax.ppermute(chunk, 'seq', pairs)  6.83 us
    pallas_call x1, Pallas kernels, local_grads(): pl.pallas_call(functools.partial(local_kernel, nb=nb, br=br, scale=scale,...  4.21 us
    pallas_call x1, Pallas kernels, per_device(): pl.pallas_call(functools.partial(pack_kernel, br=block_rows, sw=stretch_w...  2.33 us
    unnamed x25, local copies, waits for them, and re-layouts  1.99 us
    dynamic_slice x1, local copies, waits for them, and re-layouts, per_device(): lax.dynamic_index_in_dim(packed, (seq_index + shift) % seq_count, 0, keep...  1.4 us
  transfers between devices with their start and end apart: 14, of which 5 were waited for; matrix products, arithmetic and copies ran while one was open for 5% of the time, Pallas kernels for 0%

profile of v13, /device:TPU:0, one launch (start us, length us, event | category | flops | bytes accessed | tf_op | source)
XLA Modules:
  0.0 61.2 jit_solution(12053511273889340278)
XLA Ops:
  0.7 2.3 %shard_map.68 = bf16[8,136,512]{2,1,0:T(8,128)(2,1)} custom-call(bf16[128,2048]{1,0:T(8,128)(2,1)} %og_ref.1, bf16[128,2048]{1,0:T(8,128)(2,1)} %gate_ref.1, bf16[128,2048]{1,0:T(8,128)(2,1)} %x_ref.1, bf16[16,128]{1,0:T(8,128)(2,1)} %bitcast.48), custom_call_target="tpu_custom_call" | custom-call | tf_op jit(solution)/shard_map/pallas_call | solution.py:162
  3.1 1.4 %constant_dynamic-slice_fusion.2 = (bf16[1,136,512]{2,1,0:T(8,128)(2,1)S(1)}, bf16[1,136,512]{2,1,0:T(8,128)(2,1)S(1)}, bf16[1,136,512]{2,1,0:T(8,128)(2,1)S(1)}...) fusion(bf16[8,136,512]{2,1,0:T(8,128)(2,1)} %shard_map.68, ...), kind=kLoop, calls=%fused_computation.42 | loop fusion | bytes 2228256 | tf_op jit(solution)/shard_map/jit(dynamic_index_in_dim)/dynamic_slice | solution.py:207
  4.5 3.0 %collective-permute-start = (bf16[1,136,512]{2,1,0:T(8,128)(2,1)S(1)}, bf16[1,136,512]{2,1,0:T(8,128)(2,1)S(1)}, u32[]{:S(2)}, u32[]{:S(2)}) collective-permute-start(bf16[1,136,512]{2,1,0:T(8,128)(2,1)S(1)} %get-tuple-element.10), channel_id=1, source_target_pairs={{0,2},{2,4},{4,6},{6,8},{8,10},{10,12},{12,14},{14,0},{1,3},{3,5},... | collective-permute-start | bytes 417800 | tf_op jit(solution)/shard_map/ppermute | solution.py:209
  7.5 1.6 %collective-permute-start.1 = (bf16[1,136,512]{2,1,0:T(8,128)(2,1)S(1)}, bf16[1,136,512]{2,1,0:T(8,128)(2,1)S(1)}, u32[]{:S(2)}, u32[]{:S(2)}) collective-permute-start(bf16[1,136,512]{2,1,0:T(8,128)(2,1)S(1)} %get-tuple-element.9), channel_id=1, source_target_pairs={{0,4},{2,6},{4,8},{6,10},{8,12},{10,14},{12,0},{14,2},{1,5},{3,7},... | collective-permute-start | bytes 417800 | tf_op jit(solution)/shard_map/ppermute | solution.py:209
  9.1 2.5 %collective-permute-start.2 = (bf16[1,136,512]{2,1,0:T(8,128)(2,1)S(1)}, bf16[1,136,512]{2,1,0:T(8,128)(2,1)S(1)}, u32[]{:S(2)}, u32[]{:S(2)}) collective-permute-start(bf16[1,136,512]{2,1,0:T(8,128)(2,1)S(1)} %get-tuple-element.8), channel_id=1, source_target_pairs={{0,6},{2,8},{4,10},{6,12},{8,14},{10,0},{12,2},{14,4},{1,7},{3,9},... | collective-permute-start | bytes 417800 | tf_op jit(solution)/shard_map/ppermute | solution.py:209
  11.6 1.2 %collective-permute-start.3 = (bf16[1,136,512]{2,1,0:T(8,128)(2,1)S(1)}, bf16[1,136,512]{2,1,0:T(8,128)(2,1)S(1)}, u32[]{:S(2)}, u32[]{:S(2)}) collective-permute-start(bf16[1,136,512]{2,1,0:T(8,128)(2,1)S(1)} %get-tuple-element.7), channel_id=1, source_target_pairs={{0,8},{2,10},{4,12},{6,14},{8,0},{10,2},{12,4},{14,6},{1,9},{3,11}... | collective-permute-start | bytes 417800 | tf_op jit(solution)/shard_map/ppermute | solution.py:209
  12.8 2.6 %collective-permute-start.4 = (bf16[1,136,512]{2,1,0:T(8,128)(2,1)S(1)}, bf16[1,136,512]{2,1,0:T(8,128)(2,1)S(1)}, u32[]{:S(2)}, u32[]{:S(2)}) collective-permute-start(bf16[1,136,512]{2,1,0:T(8,128)(2,1)S(1)} %get-tuple-element.6), channel_id=1, source_target_pairs={{0,10},{2,12},{4,14},{6,0},{8,2},{10,4},{12,6},{14,8},{1,11},{3,13... | collective-permute-start | bytes 417800 | tf_op jit(solution)/shard_map/ppermute | solution.py:209
  15.5 1.3 %dynamic_slice.65 = f32[256]{0:T(256)} dynamic-slice(f32[2048]{0:T(1024)} %param.9, s32[]{:T(128)S(6)} %select_n.181), dynamic_slice_sizes={256} | dynamic-slice | bytes 2052 | tf_op jit(solution)/shard_map/dynamic_slice | solution.py:211
  16.8 0.0 collective-permute-done
  16.8 1.3 %collective-permute-start.5 = (bf16[1,136,512]{2,1,0:T(8,128)(2,1)S(1)}, bf16[1,136,512]{2,1,0:T(8,128)(2,1)S(1)}, u32[]{:S(2)}, u32[]{:S(2)}) collective-permute-start(bf16[1,136,512]{2,1,0:T(8,128)(2,1)S(1)} %get-tuple-element.5), channel_id=1, source_target_pairs={{0,12},{2,14},{4,0},{6,2},{8,4},{10,6},{12,8},{14,10},{1,13},{3,15... | collective-permute-start | bytes 417800 | tf_op jit(solution)/shard_map/ppermute | solution.py:209
  18.2 0.0 collective-permute-done.1
  18.2 1.5 %collective-permute-start.6 = (bf16[1,136,512]{2,1,0:T(8,128)(2,1)S(1)}, bf16[1,136,512]{2,1,0:T(8,128)(2,1)S(1)}, u32[]{:S(2)}, u32[]{:S(2)}) collective-permute-start(bf16[1,136,512]{2,1,0:T(8,128)(2,1)S(1)} %get-tuple-element.4), channel_id=1, source_target_pairs={{0,14},{2,0},{4,2},{6,4},{8,6},{10,8},{12,10},{14,12},{1,15},{3,1}... | collective-permute-start | bytes 417800 | tf_op jit(solution)/shard_map/ppermute | solution.py:209
  19.7 6.6 %collective-permute-done.2 = bf16[1,136,512]{2,1,0:T(8,128)(2,1)S(1)} collective-permute-done((bf16[1,136,512]{2,1,0:T(8,128)(2,1)S(1)}, bf16[1,136,512]{2,1,0:T(8,128)(2,1)S(1)}, u32[]{:S(2)}, u32[]{:S(2)}) %collective-permute-start.2) | collective-permute-done | bytes 139296 | tf_op jit(solution)/shard_map/ppermute | solution.py:209
  26.3 0.4 collective-permute-done.3
  26.6 0.0 collective-permute-done.4
  26.7 0.0 collective-permute-done.5
  26.7 0.0 collective-permute-done.6
  26.7 0.0 copy-start
  26.7 1.0 %copy-done = bf16[8,136,512]{2,1,0:T(8,128)(2,1)} copy-done((bf16[8,136,512]{2,1,0:T(8,128)(2,1)}, bf16[8,136,512]{2,1,0:T(8,128)(2,1)S(1)}, u32[]{:S(2)}) %copy-start) | copy-done | bytes 1114136
  27.7 4.2 %shard_map.69 = (bf16[8,136,256]{2,1,0:T(8,128)(2,1)}, f32[2,8,256]{2,1,0:T(8,128)}) custom-call(bf16[8,136,512]{2,1,0:T(8,128)(2,1)} %copy-done, bf16[8,136,512]{2,1,0:T(8,128)(2,1)} %copy-done, bf16[8,136,512]{2,1,0:T(8,128)(2,1)} %copy-done, f32[2,1,128]{2,1,0:T(1,128)} %bitcast.49), custom_call_target="tpu_custom_call" | custom-call | tf_op jit(solution)/shard_map/pallas_call | solution.py:112
  32.0 1.1 %dynamic-slice_bitcast_fusion = (bf16[136,256]{1,0:T(8,128)(2,1)S(1)}, bf16[136,256]{1,0:T(8,128)(2,1)S(1)}, bf16[136,256]{1,0:T(8,128)(2,1)S(1)}, bf16[136,256]...) fusion(bf16[8,136,256]{2,1,0:T(8,128)(2,1)} %get-tuple-element.3,, ...), kind=kLoop, calls=%fused_computation.1 | loop fusion | bytes 974876 | tf_op jit(solution)/shard_map/jit(dynamic_index_in_dim)/squeeze | solution.py:245
  33.1 11.3 %collective-permute-start.7 = (bf16[136,256]{1,0:T(8,128)(2,1)S(1)}, bf16[136,256]{1,0:T(8,128)(2,1)S(1)}, u32[]{:S(2)}, u32[]{:S(2)}) collective-permute-start(bf16[136,256]{1,0:T(8,128)(2,1)S(1)} %get-tuple-element.18), channel_id=1, source_target_pairs={{0,14},{2,0},{4,2},{6,4},{8,6},{10,8},{12,10},{14,12},{1,15},{3,1}... | collective-permute-start | bytes 208904 | tf_op jit(solution)/shard_map/ppermute | solution.py:250
  44.4 0.7 %fusion.1 = f32[1,3,256]{2,1,0:T(4,128)S(1)} fusion(bf16[8,136,256]{2,1,0:T(8,128)(2,1)} %get-tuple-element.3, s32[]{:T(128)S(6)} %select_n.183, s32[]{:T(128)S(6)} %add.439), kind=kLoop, calls=%fused_computation.49 | loop fusion | flops 768 | bytes 4616 | tf_op jit(solution)/shard_map/convert_element_type | solution.py:255
  45.1 0.4 collective-permute-start.8
  45.5 0.0 collective-permute-start.9
  45.5 2.5 %collective-permute-start.10 = (bf16[136,256]{1,0:T(8,128)(2,1)S(1)}, bf16[136,256]{1,0:T(8,128)(2,1)S(1)}, u32[]{:S(2)}, u32[]{:S(2)}) collective-permute-start(bf16[136,256]{1,0:T(8,128)(2,1)S(1)} %get-tuple-element.15), channel_id=1, source_target_pairs={{0,8},{2,10},{4,12},{6,14},{8,0},{10,2},{12,4},{14,6},{1,9},{3,11}... | collective-permute-start | bytes 208904 | tf_op jit(solution)/shard_map/ppermute | solution.py:250
  48.0 0.4 collective-permute-start.11
  48.5 0.9 %fusion = bf16[128,2048]{1,0:T(8,128)(2,1)S(1)} fusion(bf16[128,2048]{1,0:T(8,128)(2,1)S(1)} %broadcast_in_dim.3, s32[]{:T(128)S(6)} %select_n.184, bf16[8,136,256]{2,1,0:T(8,128)(2,1)} %get-tuple-element.3, s32[]{:T(128)S(6)} %select_n.183), kind=kLoop, calls=%fused_computation.16 | loop fusion | bytes 131080 | tf_op jit(solution)/shard_map/dynamic_update_slice | solution.py:252
  49.4 0.0 collective-permute-done.7
  49.4 2.9 %collective-permute-start.12 = (bf16[136,256]{1,0:T(8,128)(2,1)S(1)}, bf16[136,256]{1,0:T(8,128)(2,1)S(1)}, u32[]{:S(2)}, u32[]{:S(2)}) collective-permute-start(bf16[136,256]{1,0:T(8,128)(2,1)S(1)} %get-tuple-element.13), channel_id=1, source_target_pairs={{0,4},{2,6},{4,8},{6,10},{8,12},{10,14},{12,0},{14,2},{1,5},{3,7},... | collective-permute-start | bytes 208904 | tf_op jit(solution)/shard_map/ppermute | solution.py:250
  52.3 0.0 collective-permute-done.8
  52.3 0.2 collective-permute-start.13
  52.6 0.0 collective-permute-done.9
  52.6 4.7 %collective-permute-done.10 = bf16[136,256]{1,0:T(8,128)(2,1)S(1)} collective-permute-done((bf16[136,256]{1,0:T(8,128)(2,1)S(1)}, bf16[136,256]{1,0:T(8,128)(2,1)S(1)}, u32[]{:S(2)}, u32[]{:S(2)}) %collective-permute-start.10) | collective-permute-done | bytes 69664 | tf_op jit(solution)/shard_map/ppermute | solution.py:250
  57.3 1.4 %collective-permute-done.11 = bf16[136,256]{1,0:T(8,128)(2,1)S(1)} collective-permute-done((bf16[136,256]{1,0:T(8,128)(2,1)S(1)}, bf16[136,256]{1,0:T(8,128)(2,1)S(1)}, u32[]{:S(2)}, u32[]{:S(2)}) %collective-permute-start.11) | collective-permute-done | bytes 69664 | tf_op jit(solution)/shard_map/ppermute | solution.py:250
  58.7 0.0 collective-permute-done.12
  58.8 0.7 %collective-permute-done.13 = bf16[136,256]{1,0:T(8,128)(2,1)S(1)} collective-permute-done((bf16[136,256]{1,0:T(8,128)(2,1)S(1)}, bf16[136,256]{1,0:T(8,128)(2,1)S(1)}, u32[]{:S(2)}, u32[]{:S(2)}) %collective-permute-start.13) | collective-permute-done | bytes 69664 | tf_op jit(solution)/shard_map/ppermute | solution.py:250
  59.7 0.6 constant_dynamic-slice_fusion
  60.4 0.0 copy-start.1
  60.4 0.8 %copy-done.1 = bf16[128,2048]{1,0:T(8,128)(2,1)} copy-done((bf16[128,2048]{1,0:T(8,128)(2,1)}, bf16[128,2048]{1,0:T(8,128)(2,1)S(1)}, u32[]{:S(2)}) %copy-start.1) | copy-done | bytes 524312
  (46 shorter events, 0.4 us)
Async XLA Ops:
  4.5 12.3 %collective-permute-start = (bf16[1,136,512]{2,1,0:T(8,128)(2,1)S(1)}, bf16[1,136,512]{2,1,0:T(8,128)(2,1)S(1)}, u32[]{:S(2)}, u32[]{:S(2)}) collective-permute-start(bf16[1,136,512]{2,1,0:T(8,128)(2,1)S(1)} %get-tuple-element.10), channel_id=1, source_target_pairs={{0,2},{2,4},{4,6},{6,8},{8,10},{10,12},{12,14},{14,0},{1,3},{3,5},... | collective-permute-start | bytes 417800 | tf_op jit(solution)/shard_map/ppermute | solution.py:209
  7.5 10.7 %collective-permute-start.1 = (bf16[1,136,512]{2,1,0:T(8,128)(2,1)S(1)}, bf16[1,136,512]{2,1,0:T(8,128)(2,1)S(1)}, u32[]{:S(2)}, u32[]{:S(2)}) collective-permute-start(bf16[1,136,512]{2,1,0:T(8,128)(2,1)S(1)} %get-tuple-element.9), channel_id=1, source_target_pairs={{0,4},{2,6},{4,8},{6,10},{8,12},{10,14},{12,0},{14,2},{1,5},{3,7},... | collective-permute-start | bytes 417800 | tf_op jit(solution)/shard_map/ppermute | solution.py:209
  9.1 17.2 %collective-permute-start.2 = (bf16[1,136,512]{2,1,0:T(8,128)(2,1)S(1)}, bf16[1,136,512]{2,1,0:T(8,128)(2,1)S(1)}, u32[]{:S(2)}, u32[]{:S(2)}) collective-permute-start(bf16[1,136,512]{2,1,0:T(8,128)(2,1)S(1)} %get-tuple-element.8), channel_id=1, source_target_pairs={{0,6},{2,8},{4,10},{6,12},{8,14},{10,0},{12,2},{14,4},{1,7},{3,9},... | collective-permute-start | bytes 417800 | tf_op jit(solution)/shard_map/ppermute | solution.py:209
  11.6 15.0 %collective-permute-start.3 = (bf16[1,136,512]{2,1,0:T(8,128)(2,1)S(1)}, bf16[1,136,512]{2,1,0:T(8,128)(2,1)S(1)}, u32[]{:S(2)}, u32[]{:S(2)}) collective-permute-start(bf16[1,136,512]{2,1,0:T(8,128)(2,1)S(1)} %get-tuple-element.7), channel_id=1, source_target_pairs={{0,8},{2,10},{4,12},{6,14},{8,0},{10,2},{12,4},{14,6},{1,9},{3,11}... | collective-permute-start | bytes 417800 | tf_op jit(solution)/shard_map/ppermute | solution.py:209
  12.8 13.8 %collective-permute-start.4 = (bf16[1,136,512]{2,1,0:T(8,128)(2,1)S(1)}, bf16[1,136,512]{2,1,0:T(8,128)(2,1)S(1)}, u32[]{:S(2)}, u32[]{:S(2)}) collective-permute-start(bf16[1,136,512]{2,1,0:T(8,128)(2,1)S(1)} %get-tuple-element.6), channel_id=1, source_target_pairs={{0,10},{2,12},{4,14},{6,0},{8,2},{10,4},{12,6},{14,8},{1,11},{3,13... | collective-permute-start | bytes 417800 | tf_op jit(solution)/shard_map/ppermute | solution.py:209
  16.8 9.9 %collective-permute-start.5 = (bf16[1,136,512]{2,1,0:T(8,128)(2,1)S(1)}, bf16[1,136,512]{2,1,0:T(8,128)(2,1)S(1)}, u32[]{:S(2)}, u32[]{:S(2)}) collective-permute-start(bf16[1,136,512]{2,1,0:T(8,128)(2,1)S(1)} %get-tuple-element.5), channel_id=1, source_target_pairs={{0,12},{2,14},{4,0},{6,2},{8,4},{10,6},{12,8},{14,10},{1,13},{3,15... | collective-permute-start | bytes 417800 | tf_op jit(solution)/shard_map/ppermute | solution.py:209
  18.2 8.5 %collective-permute-start.6 = (bf16[1,136,512]{2,1,0:T(8,128)(2,1)S(1)}, bf16[1,136,512]{2,1,0:T(8,128)(2,1)S(1)}, u32[]{:S(2)}, u32[]{:S(2)}) collective-permute-start(bf16[1,136,512]{2,1,0:T(8,128)(2,1)S(1)} %get-tuple-element.4), channel_id=1, source_target_pairs={{0,14},{2,0},{4,2},{6,4},{8,6},{10,8},{12,10},{14,12},{1,15},{3,1}... | collective-permute-start | bytes 417800 | tf_op jit(solution)/shard_map/ppermute | solution.py:209
  26.7 1.0 %copy-start = (bf16[8,136,512]{2,1,0:T(8,128)(2,1)}, bf16[8,136,512]{2,1,0:T(8,128)(2,1)S(1)}, u32[]{:S(2)}) copy-start(bf16[8,136,512]{2,1,0:T(8,128)(2,1)S(1)} %constant_dynamic-update-slice_fusion.g_ref.x_ref.t_ref) | copy-start | bytes 3342340
  33.1 16.3 %collective-permute-start.7 = (bf16[136,256]{1,0:T(8,128)(2,1)S(1)}, bf16[136,256]{1,0:T(8,128)(2,1)S(1)}, u32[]{:S(2)}, u32[]{:S(2)}) collective-permute-start(bf16[136,256]{1,0:T(8,128)(2,1)S(1)} %get-tuple-element.18), channel_id=1, source_target_pairs={{0,14},{2,0},{4,2},{6,4},{8,6},{10,8},{12,10},{14,12},{1,15},{3,1}... | collective-permute-start | bytes 208904 | tf_op jit(solution)/shard_map/ppermute | solution.py:250
  45.1 7.2 %collective-permute-start.8 = (bf16[136,256]{1,0:T(8,128)(2,1)S(1)}, bf16[136,256]{1,0:T(8,128)(2,1)S(1)}, u32[]{:S(2)}, u32[]{:S(2)}) collective-permute-start(bf16[136,256]{1,0:T(8,128)(2,1)S(1)} %get-tuple-element.17), channel_id=1, source_target_pairs={{0,12},{2,14},{4,0},{6,2},{8,4},{10,6},{12,8},{14,10},{1,13},{3,15... | collective-permute-start | bytes 208904 | tf_op jit(solution)/shard_map/ppermute | solution.py:250
  45.5 7.1 %collective-permute-start.9 = (bf16[136,256]{1,0:T(8,128)(2,1)S(1)}, bf16[136,256]{1,0:T(8,128)(2,1)S(1)}, u32[]{:S(2)}, u32[]{:S(2)}) collective-permute-start(bf16[136,256]{1,0:T(8,128)(2,1)S(1)} %get-tuple-element.16), channel_id=1, source_target_pairs={{0,10},{2,12},{4,14},{6,0},{8,2},{10,4},{12,6},{14,8},{1,11},{3,13... | collective-permute-start | bytes 208904 | tf_op jit(solution)/shard_map/ppermute | solution.py:250
  45.5 11.8 %collective-permute-start.10 = (bf16[136,256]{1,0:T(8,128)(2,1)S(1)}, bf16[136,256]{1,0:T(8,128)(2,1)S(1)}, u32[]{:S(2)}, u32[]{:S(2)}) collective-permute-start(bf16[136,256]{1,0:T(8,128)(2,1)S(1)} %get-tuple-element.15), channel_id=1, source_target_pairs={{0,8},{2,10},{4,12},{6,14},{8,0},{10,2},{12,4},{14,6},{1,9},{3,11}... | collective-permute-start | bytes 208904 | tf_op jit(solution)/shard_map/ppermute | solution.py:250
  48.0 10.7 %collective-permute-start.11 = (bf16[136,256]{1,0:T(8,128)(2,1)S(1)}, bf16[136,256]{1,0:T(8,128)(2,1)S(1)}, u32[]{:S(2)}, u32[]{:S(2)}) collective-permute-start(bf16[136,256]{1,0:T(8,128)(2,1)S(1)} %get-tuple-element.14), channel_id=1, source_target_pairs={{0,6},{2,8},{4,10},{6,12},{8,14},{10,0},{12,2},{14,4},{1,7},{3,9},... | collective-permute-start | bytes 208904 | tf_op jit(solution)/shard_map/ppermute | solution.py:250
  49.4 9.4 %collective-permute-start.12 = (bf16[136,256]{1,0:T(8,128)(2,1)S(1)}, bf16[136,256]{1,0:T(8,128)(2,1)S(1)}, u32[]{:S(2)}, u32[]{:S(2)}) collective-permute-start(bf16[136,256]{1,0:T(8,128)(2,1)S(1)} %get-tuple-element.13), channel_id=1, source_target_pairs={{0,4},{2,6},{4,8},{6,10},{8,12},{10,14},{12,0},{14,2},{1,5},{3,7},... | collective-permute-start | bytes 208904 | tf_op jit(solution)/shard_map/ppermute | solution.py:250
  52.3 7.2 %collective-permute-start.13 = (bf16[136,256]{1,0:T(8,128)(2,1)S(1)}, bf16[136,256]{1,0:T(8,128)(2,1)S(1)}, u32[]{:S(2)}, u32[]{:S(2)}) collective-permute-start(bf16[136,256]{1,0:T(8,128)(2,1)S(1)} %get-tuple-element.12), channel_id=1, source_target_pairs={{0,2},{2,4},{4,6},{6,8},{8,10},{10,12},{12,14},{14,0},{1,3},{3,5},... | collective-permute-start | bytes 208904 | tf_op jit(solution)/shard_map/ppermute | solution.py:250
  60.4 0.8 %copy-start.1 = (bf16[128,2048]{1,0:T(8,128)(2,1)}, bf16[128,2048]{1,0:T(8,128)(2,1)S(1)}, u32[]{:S(2)}) copy-start(bf16[128,2048]{1,0:T(8,128)(2,1)S(1)} %slice_dynamic-update-slice_fusion) | copy-start | bytes 1572868

commit v14 on v13

--- a/solution.py
+++ b/solution.py
@@ -10,7 +10,7 @@
 from jax.sharding import PartitionSpec as P
 
 
-def local_kernel(g_ref, x_ref, t_ref, gain_ref, out_ref, diag_ref, g_scr, xrev_ref, *, nb, br, scale, fold_rows):
+def local_kernel(g_ref, x_ref, t_ref, gain_ref, out_ref, diag_ref, g_scr, xrev_ref, gt_ref, *, nb, br, sg, scale, fold_rows):
     f = pl.program_id(0)
     me = lax.axis_index("seq")
     slot = [(me - i + nb) % nb for i in range(nb)]
@@ -35,9 +35,12 @@
     flip = (rows + cols == br - 1).astype(jnp.bfloat16)
     for i in range(nb):
         g_scr[i * br : (i + 1) * br, :] = g_ref[slot[i]]
-        xrev_ref[i * br : (i + 1) * br, :] = jnp.dot(
-            flip, x_ref[slot[i]], preferred_element_type=jnp.float32
-        ).astype(xrev_ref.dtype)
+        flipped = jnp.dot(flip, x_ref[slot[i]], preferred_element_type=jnp.float32)
+        if fold_rows:
+            gt_ref[:, i * sg : (i + 1) * sg] = g_ref[slot[i]]
+            xrev_ref[:, i * sg : (i + 1) * sg] = flipped.astype(xrev_ref.dtype)
+        else:
+            xrev_ref[i * br : (i + 1) * br, :] = flipped.astype(xrev_ref.dtype)
     gain = gain_ref[...]
     for i in range(nb):
         conv = jnp.dot(
@@ -46,16 +49,25 @@
         own = g_scr[i * br : (i + 1) * br, :].astype(jnp.float32)
         out_ref[i, :br, :] = (conv * scale + gain * own).astype(out_ref.dtype)
     sums = [None] * nb
-    for j in range(nb):
-        row = lax.dot_general(
-            g_scr[j * br : (j + 1) * br, :],
-            xrev_ref[: (j + 1) * br, :],
-            (((1,), (1,)), ((), ())),
-            preferred_element_type=jnp.float32,
-        )
-        for i in range(j + 1):
-            piece = row[:, i * br : (i + 1) * br]
-            sums[j - i] = piece if sums[j - i] is None else sums[j - i] + piece
+    if fold_rows:
+        for k in range(nb):
+            sums[k] = lax.dot_general(
+                gt_ref[:, k * sg :],
+                xrev_ref[:, : (nb - k) * sg],
+                (((1,), (1,)), ((), ())),
+                preferred_element_type=jnp.float32,
+            )
+    else:
+        for j in range(nb):
+            row = lax.dot_general(
+                g_scr[j * br : (j + 1) * br, :],
+                xrev_ref[: (j + 1) * br, :],
+                (((1,), (1,)), ((), ())),
+                preferred_element_type=jnp.float32,
+            )
+            for i in range(j + 1):
+                piece = row[:, i * br : (i + 1) * br]
+                sums[j - i] = piece if sums[j - i] is None else sums[j - i] + piece
     zeros = jnp.zeros((br, br), jnp.float32)
     for k in range(nb):
         padded = jnp.concatenate([sums[k], zeros], axis=1)
@@ -110,7 +122,7 @@
     else:
         tap_in, tap_base = moved[:, br : br + 8, :128], 0
     return pl.pallas_call(
-        functools.partial(local_kernel, nb=nb, br=br, scale=scale, fold_rows=fold_rows),
+        functools.partial(local_kernel, nb=nb, br=br, sg=sg, scale=scale, fold_rows=fold_rows),
         grid=(sf,),
         in_specs=[
             pl.BlockSpec((nb, br, sg), lambda f: (0, 0, f)),
@@ -128,7 +140,8 @@
         ],
         scratch_shapes=[
             pltpu.VMEM((nb * br, sg), jnp.bfloat16),
-            pltpu.VMEM((nb * br, sg), jnp.bfloat16),
+            pltpu.VMEM((br, nb * sg) if fold_rows else (nb * br, sg), jnp.bfloat16),
+            pltpu.VMEM((br, nb * sg) if fold_rows else (8, 128), jnp.bfloat16),
         ],
     )(grad_in, input_in, tap_in, stretch_gain.reshape(sf, 1, sg))
 

time: 61.6 us -> 61.4 us (level)
  no operation moved by 1% of the time
where the time goes in v14:
time: 61.4 us; the launch traced here: 61 us
  starting transfers between devices  31.6 us (51%)
  waiting for transfers between devices  13.8 us (22%)
  local copies, waits for them, and re-layouts  7.43 us (12%)
  Pallas kernels  6.37 us (10%)
  between operations  1 us (2%)
  other arithmetic  0.77 us (1%)
    ppermute x7, starting transfers between devices, per_device(): chunk = lax.ppermute(chunk, 'seq', pairs)  17.8 us
    ppermute x7, starting transfers between devices, per_device(): arrived[shift] = lax.ppermute(chunk, 'seq', pairs)  13.8 us
    ppermute x7, waiting for transfers between devices, per_device(): arrived[shift] = lax.ppermute(chunk, 'seq', pairs)  6.96 us
    ppermute x7, waiting for transfers between devices, per_device(): chunk = lax.ppermute(chunk, 'seq', pairs)  6.83 us
    pallas_call x1, Pallas kernels, local_grads(): pl.pallas_call(functools.partial(local_kernel, nb=nb, br=br, sg=sg, scale...  4.04 us
    pallas_call x1, Pallas kernels, per_device(): pl.pallas_call(functools.partial(pack_kernel, br=block_rows, sw=stretch_w...  2.33 us
    unnamed x25, local copies, waits for them, and re-layouts  1.99 us
    dynamic_slice x1, local copies, waits for them, and re-layouts, per_device(): lax.dynamic_index_in_dim(packed, (seq_index + shift) % seq_count, 0, keep...  1.4 us
  transfers between devices with their start and end apart: 14, of which 5 were waited for; matrix products, arithmetic and copies ran while one was open for 5% of the time, Pallas kernels for 0%

profile of v14, /device:TPU:0, one launch (start us, length us, event | category | flops | bytes accessed | tf_op | source)
XLA Modules:
  0.0 61.0 jit_solution(7309573377066744786)
XLA Ops:
  0.7 2.3 %shard_map.68 = bf16[8,136,512]{2,1,0:T(8,128)(2,1)} custom-call(bf16[128,2048]{1,0:T(8,128)(2,1)} %og_ref.1, bf16[128,2048]{1,0:T(8,128)(2,1)} %gate_ref.1, bf16[128,2048]{1,0:T(8,128)(2,1)} %x_ref.1, bf16[16,128]{1,0:T(8,128)(2,1)} %bitcast.48), custom_call_target="tpu_custom_call" | custom-call | tf_op jit(solution)/shard_map/pallas_call | solution.py:175
  3.1 1.4 %constant_dynamic-slice_fusion.2 = (bf16[1,136,512]{2,1,0:T(8,128)(2,1)S(1)}, bf16[1,136,512]{2,1,0:T(8,128)(2,1)S(1)}, bf16[1,136,512]{2,1,0:T(8,128)(2,1)S(1)}...) fusion(bf16[8,136,512]{2,1,0:T(8,128)(2,1)} %shard_map.68, ...), kind=kLoop, calls=%fused_computation.42 | loop fusion | bytes 2228256 | tf_op jit(solution)/shard_map/jit(dynamic_index_in_dim)/dynamic_slice | solution.py:220
  4.5 3.0 %collective-permute-start = (bf16[1,136,512]{2,1,0:T(8,128)(2,1)S(1)}, bf16[1,136,512]{2,1,0:T(8,128)(2,1)S(1)}, u32[]{:S(2)}, u32[]{:S(2)}) collective-permute-start(bf16[1,136,512]{2,1,0:T(8,128)(2,1)S(1)} %get-tuple-element.10), channel_id=1, source_target_pairs={{0,2},{2,4},{4,6},{6,8},{8,10},{10,12},{12,14},{14,0},{1,3},{3,5},... | collective-permute-start | bytes 417800 | tf_op jit(solution)/shard_map/ppermute | solution.py:222
  7.5 1.6 %collective-permute-start.1 = (bf16[1,136,512]{2,1,0:T(8,128)(2,1)S(1)}, bf16[1,136,512]{2,1,0:T(8,128)(2,1)S(1)}, u32[]{:S(2)}, u32[]{:S(2)}) collective-permute-start(bf16[1,136,512]{2,1,0:T(8,128)(2,1)S(1)} %get-tuple-element.9), channel_id=1, source_target_pairs={{0,4},{2,6},{4,8},{6,10},{8,12},{10,14},{12,0},{14,2},{1,5},{3,7},... | collective-permute-start | bytes 417800 | tf_op jit(solution)/shard_map/ppermute | solution.py:222
  9.1 2.5 %collective-permute-start.2 = (bf16[1,136,512]{2,1,0:T(8,128)(2,1)S(1)}, bf16[1,136,512]{2,1,0:T(8,128)(2,1)S(1)}, u32[]{:S(2)}, u32[]{:S(2)}) collective-permute-start(bf16[1,136,512]{2,1,0:T(8,128)(2,1)S(1)} %get-tuple-element.8), channel_id=1, source_target_pairs={{0,6},{2,8},{4,10},{6,12},{8,14},{10,0},{12,2},{14,4},{1,7},{3,9},... | collective-permute-start | bytes 417800 | tf_op jit(solution)/shard_map/ppermute | solution.py:222
  11.6 1.2 %collective-permute-start.3 = (bf16[1,136,512]{2,1,0:T(8,128)(2,1)S(1)}, bf16[1,136,512]{2,1,0:T(8,128)(2,1)S(1)}, u32[]{:S(2)}, u32[]{:S(2)}) collective-permute-start(bf16[1,136,512]{2,1,0:T(8,128)(2,1)S(1)} %get-tuple-element.7), channel_id=1, source_target_pairs={{0,8},{2,10},{4,12},{6,14},{8,0},{10,2},{12,4},{14,6},{1,9},{3,11}... | collective-permute-start | bytes 417800 | tf_op jit(solution)/shard_map/ppermute | solution.py:222
  12.8 2.6 %collective-permute-start.4 = (bf16[1,136,512]{2,1,0:T(8,128)(2,1)S(1)}, bf16[1,136,512]{2,1,0:T(8,128)(2,1)S(1)}, u32[]{:S(2)}, u32[]{:S(2)}) collective-permute-start(bf16[1,136,512]{2,1,0:T(8,128)(2,1)S(1)} %get-tuple-element.6), channel_id=1, source_target_pairs={{0,10},{2,12},{4,14},{6,0},{8,2},{10,4},{12,6},{14,8},{1,11},{3,13... | collective-permute-start | bytes 417800 | tf_op jit(solution)/shard_map/ppermute | solution.py:222
  15.5 1.3 %dynamic_slice.65 = f32[256]{0:T(256)} dynamic-slice(f32[2048]{0:T(1024)} %param.9, s32[]{:T(128)S(6)} %select_n.181), dynamic_slice_sizes={256} | dynamic-slice | bytes 2052 | tf_op jit(solution)/shard_map/dynamic_slice | solution.py:224
  16.8 0.0 collective-permute-done
  16.8 1.3 %collective-permute-start.5 = (bf16[1,136,512]{2,1,0:T(8,128)(2,1)S(1)}, bf16[1,136,512]{2,1,0:T(8,128)(2,1)S(1)}, u32[]{:S(2)}, u32[]{:S(2)}) collective-permute-start(bf16[1,136,512]{2,1,0:T(8,128)(2,1)S(1)} %get-tuple-element.5), channel_id=1, source_target_pairs={{0,12},{2,14},{4,0},{6,2},{8,4},{10,6},{12,8},{14,10},{1,13},{3,15... | collective-permute-start | bytes 417800 | tf_op jit(solution)/shard_map/ppermute | solution.py:222
  18.2 0.0 collective-permute-done.1
  18.2 1.5 %collective-permute-start.6 = (bf16[1,136,512]{2,1,0:T(8,128)(2,1)S(1)}, bf16[1,136,512]{2,1,0:T(8,128)(2,1)S(1)}, u32[]{:S(2)}, u32[]{:S(2)}) collective-permute-start(bf16[1,136,512]{2,1,0:T(8,128)(2,1)S(1)} %get-tuple-element.4), channel_id=1, source_target_pairs={{0,14},{2,0},{4,2},{6,4},{8,6},{10,8},{12,10},{14,12},{1,15},{3,1}... | collective-permute-start | bytes 417800 | tf_op jit(solution)/shard_map/ppermute | solution.py:222
  19.7 6.6 %collective-permute-done.2 = bf16[1,136,512]{2,1,0:T(8,128)(2,1)S(1)} collective-permute-done((bf16[1,136,512]{2,1,0:T(8,128)(2,1)S(1)}, bf16[1,136,512]{2,1,0:T(8,128)(2,1)S(1)}, u32[]{:S(2)}, u32[]{:S(2)}) %collective-permute-start.2) | collective-permute-done | bytes 139296 | tf_op jit(solution)/shard_map/ppermute | solution.py:222
  26.3 0.4 collective-permute-done.3
  26.6 0.0 collective-permute-done.4
  26.7 0.0 collective-permute-done.5
  26.7 0.0 collective-permute-done.6
  26.7 0.0 copy-start
  26.7 1.0 %copy-done = bf16[8,136,512]{2,1,0:T(8,128)(2,1)} copy-done((bf16[8,136,512]{2,1,0:T(8,128)(2,1)}, bf16[8,136,512]{2,1,0:T(8,128)(2,1)S(1)}, u32[]{:S(2)}) %copy-start) | copy-done | bytes 1114136
  27.7 4.0 %shard_map.69 = (bf16[8,136,256]{2,1,0:T(8,128)(2,1)}, f32[2,8,256]{2,1,0:T(8,128)}) custom-call(bf16[8,136,512]{2,1,0:T(8,128)(2,1)} %copy-done, bf16[8,136,512]{2,1,0:T(8,128)(2,1)} %copy-done, bf16[8,136,512]{2,1,0:T(8,128)(2,1)} %copy-done, f32[2,1,128]{2,1,0:T(1,128)} %bitcast.49), custom_call_target="tpu_custom_call" | custom-call | tf_op jit(solution)/shard_map/pallas_call | solution.py:124
  31.8 1.1 %dynamic-slice_bitcast_fusion = (bf16[136,256]{1,0:T(8,128)(2,1)S(1)}, bf16[136,256]{1,0:T(8,128)(2,1)S(1)}, bf16[136,256]{1,0:T(8,128)(2,1)S(1)}, bf16[136,256]...) fusion(bf16[8,136,256]{2,1,0:T(8,128)(2,1)} %get-tuple-element.3,, ...), kind=kLoop, calls=%fused_computation.1 | loop fusion | bytes 974876 | tf_op jit(solution)/shard_map/jit(dynamic_index_in_dim)/squeeze | solution.py:258
  32.9 11.3 %collective-permute-start.7 = (bf16[136,256]{1,0:T(8,128)(2,1)S(1)}, bf16[136,256]{1,0:T(8,128)(2,1)S(1)}, u32[]{:S(2)}, u32[]{:S(2)}) collective-permute-start(bf16[136,256]{1,0:T(8,128)(2,1)S(1)} %get-tuple-element.18), channel_id=1, source_target_pairs={{0,14},{2,0},{4,2},{6,4},{8,6},{10,8},{12,10},{14,12},{1,15},{3,1}... | collective-permute-start | bytes 208904 | tf_op jit(solution)/shard_map/ppermute | solution.py:263
  44.2 0.7 %fusion.1 = f32[1,3,256]{2,1,0:T(4,128)S(1)} fusion(bf16[8,136,256]{2,1,0:T(8,128)(2,1)} %get-tuple-element.3, s32[]{:T(128)S(6)} %select_n.183, s32[]{:T(128)S(6)} %add.439), kind=kLoop, calls=%fused_computation.49 | loop fusion | flops 768 | bytes 4616 | tf_op jit(solution)/shard_map/convert_element_type | solution.py:268
  44.9 0.4 collective-permute-start.8
  45.3 0.0 collective-permute-start.9
  45.3 2.5 %collective-permute-start.10 = (bf16[136,256]{1,0:T(8,128)(2,1)S(1)}, bf16[136,256]{1,0:T(8,128)(2,1)S(1)}, u32[]{:S(2)}, u32[]{:S(2)}) collective-permute-start(bf16[136,256]{1,0:T(8,128)(2,1)S(1)} %get-tuple-element.15), channel_id=1, source_target_pairs={{0,8},{2,10},{4,12},{6,14},{8,0},{10,2},{12,4},{14,6},{1,9},{3,11}... | collective-permute-start | bytes 208904 | tf_op jit(solution)/shard_map/ppermute | solution.py:263
  47.9 0.4 collective-permute-start.11
  48.3 0.9 %fusion = bf16[128,2048]{1,0:T(8,128)(2,1)S(1)} fusion(bf16[128,2048]{1,0:T(8,128)(2,1)S(1)} %broadcast_in_dim.3, s32[]{:T(128)S(6)} %select_n.184, bf16[8,136,256]{2,1,0:T(8,128)(2,1)} %get-tuple-element.3, s32[]{:T(128)S(6)} %select_n.183), kind=kLoop, calls=%fused_computation.16 | loop fusion | bytes 131080 | tf_op jit(solution)/shard_map/dynamic_update_slice | solution.py:265
  49.2 0.0 collective-permute-done.7
  49.2 2.9 %collective-permute-start.12 = (bf16[136,256]{1,0:T(8,128)(2,1)S(1)}, bf16[136,256]{1,0:T(8,128)(2,1)S(1)}, u32[]{:S(2)}, u32[]{:S(2)}) collective-permute-start(bf16[136,256]{1,0:T(8,128)(2,1)S(1)} %get-tuple-element.13), channel_id=1, source_target_pairs={{0,4},{2,6},{4,8},{6,10},{8,12},{10,14},{12,0},{14,2},{1,5},{3,7},... | collective-permute-start | bytes 208904 | tf_op jit(solution)/shard_map/ppermute | solution.py:263
  52.1 0.0 collective-permute-done.8
  52.1 0.2 collective-permute-start.13
  52.4 0.0 collective-permute-done.9
  52.4 4.7 %collective-permute-done.10 = bf16[136,256]{1,0:T(8,128)(2,1)S(1)} collective-permute-done((bf16[136,256]{1,0:T(8,128)(2,1)S(1)}, bf16[136,256]{1,0:T(8,128)(2,1)S(1)}, u32[]{:S(2)}, u32[]{:S(2)}) %collective-permute-start.10) | collective-permute-done | bytes 69664 | tf_op jit(solution)/shard_map/ppermute | solution.py:263
  57.1 1.4 %collective-permute-done.11 = bf16[136,256]{1,0:T(8,128)(2,1)S(1)} collective-permute-done((bf16[136,256]{1,0:T(8,128)(2,1)S(1)}, bf16[136,256]{1,0:T(8,128)(2,1)S(1)}, u32[]{:S(2)}, u32[]{:S(2)}) %collective-permute-start.11) | collective-permute-done | bytes 69664 | tf_op jit(solution)/shard_map/ppermute | solution.py:263
  58.6 0.0 collective-permute-done.12
  58.6 0.7 %collective-permute-done.13 = bf16[136,256]{1,0:T(8,128)(2,1)S(1)} collective-permute-done((bf16[136,256]{1,0:T(8,128)(2,1)S(1)}, bf16[136,256]{1,0:T(8,128)(2,1)S(1)}, u32[]{:S(2)}, u32[]{:S(2)}) %collective-permute-start.13) | collective-permute-done | bytes 69664 | tf_op jit(solution)/shard_map/ppermute | solution.py:263
  59.5 0.6 constant_dynamic-slice_fusion
  60.2 0.0 copy-start.1
  60.2 0.8 %copy-done.1 = bf16[128,2048]{1,0:T(8,128)(2,1)} copy-done((bf16[128,2048]{1,0:T(8,128)(2,1)}, bf16[128,2048]{1,0:T(8,128)(2,1)S(1)}, u32[]{:S(2)}) %copy-start.1) | copy-done | bytes 524312
  (46 shorter events, 0.4 us)
Async XLA Ops:
  4.5 12.3 %collective-permute-start = (bf16[1,136,512]{2,1,0:T(8,128)(2,1)S(1)}, bf16[1,136,512]{2,1,0:T(8,128)(2,1)S(1)}, u32[]{:S(2)}, u32[]{:S(2)}) collective-permute-start(bf16[1,136,512]{2,1,0:T(8,128)(2,1)S(1)} %get-tuple-element.10), channel_id=1, source_target_pairs={{0,2},{2,4},{4,6},{6,8},{8,10},{10,12},{12,14},{14,0},{1,3},{3,5},... | collective-permute-start | bytes 417800 | tf_op jit(solution)/shard_map/ppermute | solution.py:222
  7.5 10.7 %collective-permute-start.1 = (bf16[1,136,512]{2,1,0:T(8,128)(2,1)S(1)}, bf16[1,136,512]{2,1,0:T(8,128)(2,1)S(1)}, u32[]{:S(2)}, u32[]{:S(2)}) collective-permute-start(bf16[1,136,512]{2,1,0:T(8,128)(2,1)S(1)} %get-tuple-element.9), channel_id=1, source_target_pairs={{0,4},{2,6},{4,8},{6,10},{8,12},{10,14},{12,0},{14,2},{1,5},{3,7},... | collective-permute-start | bytes 417800 | tf_op jit(solution)/shard_map/ppermute | solution.py:222
  9.1 17.2 %collective-permute-start.2 = (bf16[1,136,512]{2,1,0:T(8,128)(2,1)S(1)}, bf16[1,136,512]{2,1,0:T(8,128)(2,1)S(1)}, u32[]{:S(2)}, u32[]{:S(2)}) collective-permute-start(bf16[1,136,512]{2,1,0:T(8,128)(2,1)S(1)} %get-tuple-element.8), channel_id=1, source_target_pairs={{0,6},{2,8},{4,10},{6,12},{8,14},{10,0},{12,2},{14,4},{1,7},{3,9},... | collective-permute-start | bytes 417800 | tf_op jit(solution)/shard_map/ppermute | solution.py:222
  11.6 15.0 %collective-permute-start.3 = (bf16[1,136,512]{2,1,0:T(8,128)(2,1)S(1)}, bf16[1,136,512]{2,1,0:T(8,128)(2,1)S(1)}, u32[]{:S(2)}, u32[]{:S(2)}) collective-permute-start(bf16[1,136,512]{2,1,0:T(8,128)(2,1)S(1)} %get-tuple-element.7), channel_id=1, source_target_pairs={{0,8},{2,10},{4,12},{6,14},{8,0},{10,2},{12,4},{14,6},{1,9},{3,11}... | collective-permute-start | bytes 417800 | tf_op jit(solution)/shard_map/ppermute | solution.py:222
  12.8 13.8 %collective-permute-start.4 = (bf16[1,136,512]{2,1,0:T(8,128)(2,1)S(1)}, bf16[1,136,512]{2,1,0:T(8,128)(2,1)S(1)}, u32[]{:S(2)}, u32[]{:S(2)}) collective-permute-start(bf16[1,136,512]{2,1,0:T(8,128)(2,1)S(1)} %get-tuple-element.6), channel_id=1, source_target_pairs={{0,10},{2,12},{4,14},{6,0},{8,2},{10,4},{12,6},{14,8},{1,11},{3,13... | collective-permute-start | bytes 417800 | tf_op jit(solution)/shard_map/ppermute | solution.py:222
  16.8 9.9 %collective-permute-start.5 = (bf16[1,136,512]{2,1,0:T(8,128)(2,1)S(1)}, bf16[1,136,512]{2,1,0:T(8,128)(2,1)S(1)}, u32[]{:S(2)}, u32[]{:S(2)}) collective-permute-start(bf16[1,136,512]{2,1,0:T(8,128)(2,1)S(1)} %get-tuple-element.5), channel_id=1, source_target_pairs={{0,12},{2,14},{4,0},{6,2},{8,4},{10,6},{12,8},{14,10},{1,13},{3,15... | collective-permute-start | bytes 417800 | tf_op jit(solution)/shard_map/ppermute | solution.py:222
  18.2 8.5 %collective-permute-start.6 = (bf16[1,136,512]{2,1,0:T(8,128)(2,1)S(1)}, bf16[1,136,512]{2,1,0:T(8,128)(2,1)S(1)}, u32[]{:S(2)}, u32[]{:S(2)}) collective-permute-start(bf16[1,136,512]{2,1,0:T(8,128)(2,1)S(1)} %get-tuple-element.4), channel_id=1, source_target_pairs={{0,14},{2,0},{4,2},{6,4},{8,6},{10,8},{12,10},{14,12},{1,15},{3,1}... | collective-permute-start | bytes 417800 | tf_op jit(solution)/shard_map/ppermute | solution.py:222
  26.7 1.0 %copy-start = (bf16[8,136,512]{2,1,0:T(8,128)(2,1)}, bf16[8,136,512]{2,1,0:T(8,128)(2,1)S(1)}, u32[]{:S(2)}) copy-start(bf16[8,136,512]{2,1,0:T(8,128)(2,1)S(1)} %constant_dynamic-update-slice_fusion.g_ref.x_ref.t_ref) | copy-start | bytes 3342340
  32.9 16.3 %collective-permute-start.7 = (bf16[136,256]{1,0:T(8,128)(2,1)S(1)}, bf16[136,256]{1,0:T(8,128)(2,1)S(1)}, u32[]{:S(2)}, u32[]{:S(2)}) collective-permute-start(bf16[136,256]{1,0:T(8,128)(2,1)S(1)} %get-tuple-element.18), channel_id=1, source_target_pairs={{0,14},{2,0},{4,2},{6,4},{8,6},{10,8},{12,10},{14,12},{1,15},{3,1}... | collective-permute-start | bytes 208904 | tf_op jit(solution)/shard_map/ppermute | solution.py:263
  44.9 7.2 %collective-permute-start.8 = (bf16[136,256]{1,0:T(8,128)(2,1)S(1)}, bf16[136,256]{1,0:T(8,128)(2,1)S(1)}, u32[]{:S(2)}, u32[]{:S(2)}) collective-permute-start(bf16[136,256]{1,0:T(8,128)(2,1)S(1)} %get-tuple-element.17), channel_id=1, source_target_pairs={{0,12},{2,14},{4,0},{6,2},{8,4},{10,6},{12,8},{14,10},{1,13},{3,15... | collective-permute-start | bytes 208904 | tf_op jit(solution)/shard_map/ppermute | solution.py:263
  45.3 7.1 %collective-permute-start.9 = (bf16[136,256]{1,0:T(8,128)(2,1)S(1)}, bf16[136,256]{1,0:T(8,128)(2,1)S(1)}, u32[]{:S(2)}, u32[]{:S(2)}) collective-permute-start(bf16[136,256]{1,0:T(8,128)(2,1)S(1)} %get-tuple-element.16), channel_id=1, source_target_pairs={{0,10},{2,12},{4,14},{6,0},{8,2},{10,4},{12,6},{14,8},{1,11},{3,13... | collective-permute-start | bytes 208904 | tf_op jit(solution)/shard_map/ppermute | solution.py:263
  45.3 11.8 %collective-permute-start.10 = (bf16[136,256]{1,0:T(8,128)(2,1)S(1)}, bf16[136,256]{1,0:T(8,128)(2,1)S(1)}, u32[]{:S(2)}, u32[]{:S(2)}) collective-permute-start(bf16[136,256]{1,0:T(8,128)(2,1)S(1)} %get-tuple-element.15), channel_id=1, source_target_pairs={{0,8},{2,10},{4,12},{6,14},{8,0},{10,2},{12,4},{14,6},{1,9},{3,11}... | collective-permute-start | bytes 208904 | tf_op jit(solution)/shard_map/ppermute | solution.py:263
  47.9 10.7 %collective-permute-start.11 = (bf16[136,256]{1,0:T(8,128)(2,1)S(1)}, bf16[136,256]{1,0:T(8,128)(2,1)S(1)}, u32[]{:S(2)}, u32[]{:S(2)}) collective-permute-start(bf16[136,256]{1,0:T(8,128)(2,1)S(1)} %get-tuple-element.14), channel_id=1, source_target_pairs={{0,6},{2,8},{4,10},{6,12},{8,14},{10,0},{12,2},{14,4},{1,7},{3,9},... | collective-permute-start | bytes 208904 | tf_op jit(solution)/shard_map/ppermute | solution.py:263
  49.2 9.4 %collective-permute-start.12 = (bf16[136,256]{1,0:T(8,128)(2,1)S(1)}, bf16[136,256]{1,0:T(8,128)(2,1)S(1)}, u32[]{:S(2)}, u32[]{:S(2)}) collective-permute-start(bf16[136,256]{1,0:T(8,128)(2,1)S(1)} %get-tuple-element.13), channel_id=1, source_target_pairs={{0,4},{2,6},{4,8},{6,10},{8,12},{10,14},{12,0},{14,2},{1,5},{3,7},... | collective-permute-start | bytes 208904 | tf_op jit(solution)/shard_map/ppermute | solution.py:263
  52.1 7.1 %collective-permute-start.13 = (bf16[136,256]{1,0:T(8,128)(2,1)S(1)}, bf16[136,256]{1,0:T(8,128)(2,1)S(1)}, u32[]{:S(2)}, u32[]{:S(2)}) collective-permute-start(bf16[136,256]{1,0:T(8,128)(2,1)S(1)} %get-tuple-element.12), channel_id=1, source_target_pairs={{0,2},{2,4},{4,6},{6,8},{8,10},{10,12},{12,14},{14,0},{1,3},{3,5},... | collective-permute-start | bytes 208904 | tf_op jit(solution)/shard_map/ppermute | solution.py:263
  60.2 0.8 %copy-start.1 = (bf16[128,2048]{1,0:T(8,128)(2,1)}, bf16[128,2048]{1,0:T(8,128)(2,1)S(1)}, u32[]{:S(2)}) copy-start(bf16[128,2048]{1,0:T(8,128)(2,1)S(1)} %slice_dynamic-update-slice_fusion) | copy-start | bytes 1572868

commit v15 on v14

--- a/solution.py
+++ b/solution.py
@@ -10,8 +10,7 @@
 from jax.sharding import PartitionSpec as P
 
 
-def local_kernel(g_ref, x_ref, t_ref, gain_ref, out_ref, diag_ref, g_scr, xrev_ref, gt_ref, *, nb, br, sg, scale, fold_rows):
-    f = pl.program_id(0)
+def filter_pass(g_ref, x_ref, t_ref, gain_ref, out_ref, diag_ref, g_scr, xrev_ref, gt_ref, f, nb, br, sg, scale, fold_rows):
     me = lax.axis_index("seq")
     slot = [(me - i + nb) % nb for i in range(nb)]
     n = nb * br
@@ -108,32 +107,53 @@
         out_ref[d, br:, br:] = jnp.zeros((8, 2 * sw - br), out_ref.dtype)
 
 
+def local_kernel(g_ref, x_ref, t_ref, gain_ref, out_ref, diag_ref, g_scr, xrev_ref, gt_ref, *, nb, br, sf, sg, x_base, t_base, scale, fold_rows):
+    for f in range(sf):
+        filter_pass(
+            g_ref.at[:, :br, f * sg : (f + 1) * sg],
+            x_ref.at[:, :br, x_base + f * sg : x_base + (f + 1) * sg],
+            t_ref.at[:, t_base : t_base + 8, :128],
+            gain_ref.at[f],
+            out_ref.at[:, :, f * sg : (f + 1) * sg],
+            diag_ref.at[f],
+            g_scr,
+            xrev_ref,
+            gt_ref,
+            f,
+            nb,
+            br,
+            sg,
+            scale,
+            fold_rows,
+        )
+
+
 def local_grads(moved, stretch_gain, nb, br, sf, sg, scale, out_rows):
     sw = sf * sg
     fold_rows = sg % 128 == 0
-    if sg % 128 == 0:
-        grad_in, input_in, input_base = moved, moved, sf
-    else:
-        grad_in = moved[:, :br, :sw]
-        input_in = moved[:, :br, sw : 2 * sw]
-        input_base = 0
-    if sg % 128 == 0:
-        tap_in, tap_base = moved, br // 8
-    else:
-        tap_in, tap_base = moved[:, br : br + 8, :128], 0
+    if fold_rows:
+        operands = (moved,)
+        x_base, t_base = sw, br
+    else:
+        operands = (moved[:, :br, :sw], moved[:, :br, sw : 2 * sw], moved[:, br : br + 8, :128])
+        x_base, t_base = 0, 0
+    def body(*refs):
+        if fold_rows:
+            refs = refs[:1] * 3 + refs[1:]
+        local_kernel(*refs, **params)
+
+    params = dict(
+        nb=nb,
+        br=br,
+        sf=sf,
+        sg=sg,
+        x_base=x_base,
+        t_base=t_base,
+        scale=scale,
+        fold_rows=fold_rows,
+    )
     return pl.pallas_call(
-        functools.partial(local_kernel, nb=nb, br=br, sg=sg, scale=scale, fold_rows=fold_rows),
-        grid=(sf,),
-        in_specs=[
-            pl.BlockSpec((nb, br, sg), lambda f: (0, 0, f)),
-            pl.BlockSpec((nb, br, sg), lambda f: (0, 0, input_base + f)),
-            pl.BlockSpec((nb, 8, 128), lambda f: (0, tap_base, 0)),
-            pl.BlockSpec((None, 1, sg), lambda f: (f, 0, 0)),
-        ],
-        out_specs=[
-            pl.BlockSpec((nb, out_rows if fold_rows else br, sg), lambda f: (0, 0, f)),
-            pl.BlockSpec((None, nb, 2 * br), lambda f: (f, 0, 0)),
-        ],
+        body,
         out_shape=[
             jax.ShapeDtypeStruct((nb, out_rows, sw), jnp.bfloat16),
             jax.ShapeDtypeStruct((sf, nb, 2 * br), jnp.float32),
@@ -143,7 +163,7 @@
             pltpu.VMEM((br, nb * sg) if fold_rows else (nb * br, sg), jnp.bfloat16),
             pltpu.VMEM((br, nb * sg) if fold_rows else (8, 128), jnp.bfloat16),
         ],
-    )(grad_in, input_in, tap_in, stretch_gain.reshape(sf, 1, sg))
+    )(*operands, stretch_gain.reshape(sf, 1, sg))
 
 
 def per_device(cached_input, cached_gate, out_grad, filter_taps, skip_gain):

time: 61.4 us -> 61.3 us (level)
  no operation moved by 1% of the time
where the time goes in v15:
time: 61.3 us; the launch traced here: 61 us
  starting transfers between devices  31.6 us (52%)
  waiting for transfers between devices  13.8 us (23%)
  local copies, waits for them, and re-layouts  7.43 us (12%)
  Pallas kernels  6.34 us (10%)
  between operations  1 us (2%)
  other arithmetic  0.77 us (1%)
    ppermute x7, starting transfers between devices, per_device(): chunk = lax.ppermute(chunk, 'seq', pairs)  17.8 us
    ppermute x7, starting transfers between devices, per_device(): arrived[shift] = lax.ppermute(chunk, 'seq', pairs)  13.8 us
    ppermute x7, waiting for transfers between devices, per_device(): arrived[shift] = lax.ppermute(chunk, 'seq', pairs)  6.96 us
    ppermute x7, waiting for transfers between devices, per_device(): chunk = lax.ppermute(chunk, 'seq', pairs)  6.83 us
    pallas_call x1, Pallas kernels, local_grads(): pl.pallas_call(body, out_shape=[jax.ShapeDtypeStruct((nb, out_rows, sw),...  4.01 us
    pallas_call x1, Pallas kernels, per_device(): pl.pallas_call(functools.partial(pack_kernel, br=block_rows, sw=stretch_w...  2.33 us
    unnamed x25, local copies, waits for them, and re-layouts  1.99 us
    dynamic_slice x1, local copies, waits for them, and re-layouts, per_device(): lax.dynamic_index_in_dim(packed, (seq_index + shift) % seq_count, 0, keep...  1.4 us
  transfers between devices with their start and end apart: 14, of which 5 were waited for; matrix products, arithmetic and copies ran while one was open for 5% of the time, Pallas kernels for 0%

profile of v15, /device:TPU:0, one launch (start us, length us, event | category | flops | bytes accessed | tf_op | source)
XLA Modules:
  0.0 61.0 jit_solution(6987694146066224748)
XLA Ops:
  0.7 2.3 %shard_map.68 = bf16[8,136,512]{2,1,0:T(8,128)(2,1)} custom-call(bf16[128,2048]{1,0:T(8,128)(2,1)} %og_ref.1, bf16[128,2048]{1,0:T(8,128)(2,1)} %gate_ref.1, bf16[128,2048]{1,0:T(8,128)(2,1)} %x_ref.1, bf16[16,128]{1,0:T(8,128)(2,1)} %bitcast.48), custom_call_target="tpu_custom_call" | custom-call | tf_op jit(solution)/shard_map/pallas_call | solution.py:195
  3.1 1.4 %constant_dynamic-slice_fusion.2 = (bf16[1,136,512]{2,1,0:T(8,128)(2,1)S(1)}, bf16[1,136,512]{2,1,0:T(8,128)(2,1)S(1)}, bf16[1,136,512]{2,1,0:T(8,128)(2,1)S(1)}...) fusion(bf16[8,136,512]{2,1,0:T(8,128)(2,1)} %shard_map.68, ...), kind=kLoop, calls=%fused_computation.42 | loop fusion | bytes 2228256 | tf_op jit(solution)/shard_map/jit(dynamic_index_in_dim)/dynamic_slice | solution.py:240
  4.5 3.0 %collective-permute-start = (bf16[1,136,512]{2,1,0:T(8,128)(2,1)S(1)}, bf16[1,136,512]{2,1,0:T(8,128)(2,1)S(1)}, u32[]{:S(2)}, u32[]{:S(2)}) collective-permute-start(bf16[1,136,512]{2,1,0:T(8,128)(2,1)S(1)} %get-tuple-element.10), channel_id=1, source_target_pairs={{0,2},{2,4},{4,6},{6,8},{8,10},{10,12},{12,14},{14,0},{1,3},{3,5},... | collective-permute-start | bytes 417800 | tf_op jit(solution)/shard_map/ppermute | solution.py:242
  7.5 1.6 %collective-permute-start.1 = (bf16[1,136,512]{2,1,0:T(8,128)(2,1)S(1)}, bf16[1,136,512]{2,1,0:T(8,128)(2,1)S(1)}, u32[]{:S(2)}, u32[]{:S(2)}) collective-permute-start(bf16[1,136,512]{2,1,0:T(8,128)(2,1)S(1)} %get-tuple-element.9), channel_id=1, source_target_pairs={{0,4},{2,6},{4,8},{6,10},{8,12},{10,14},{12,0},{14,2},{1,5},{3,7},... | collective-permute-start | bytes 417800 | tf_op jit(solution)/shard_map/ppermute | solution.py:242
  9.1 2.5 %collective-permute-start.2 = (bf16[1,136,512]{2,1,0:T(8,128)(2,1)S(1)}, bf16[1,136,512]{2,1,0:T(8,128)(2,1)S(1)}, u32[]{:S(2)}, u32[]{:S(2)}) collective-permute-start(bf16[1,136,512]{2,1,0:T(8,128)(2,1)S(1)} %get-tuple-element.8), channel_id=1, source_target_pairs={{0,6},{2,8},{4,10},{6,12},{8,14},{10,0},{12,2},{14,4},{1,7},{3,9},... | collective-permute-start | bytes 417800 | tf_op jit(solution)/shard_map/ppermute | solution.py:242
  11.6 1.2 %collective-permute-start.3 = (bf16[1,136,512]{2,1,0:T(8,128)(2,1)S(1)}, bf16[1,136,512]{2,1,0:T(8,128)(2,1)S(1)}, u32[]{:S(2)}, u32[]{:S(2)}) collective-permute-start(bf16[1,136,512]{2,1,0:T(8,128)(2,1)S(1)} %get-tuple-element.7), channel_id=1, source_target_pairs={{0,8},{2,10},{4,12},{6,14},{8,0},{10,2},{12,4},{14,6},{1,9},{3,11}... | collective-permute-start | bytes 417800 | tf_op jit(solution)/shard_map/ppermute | solution.py:242
  12.8 2.6 %collective-permute-start.4 = (bf16[1,136,512]{2,1,0:T(8,128)(2,1)S(1)}, bf16[1,136,512]{2,1,0:T(8,128)(2,1)S(1)}, u32[]{:S(2)}, u32[]{:S(2)}) collective-permute-start(bf16[1,136,512]{2,1,0:T(8,128)(2,1)S(1)} %get-tuple-element.6), channel_id=1, source_target_pairs={{0,10},{2,12},{4,14},{6,0},{8,2},{10,4},{12,6},{14,8},{1,11},{3,13... | collective-permute-start | bytes 417800 | tf_op jit(solution)/shard_map/ppermute | solution.py:242
  15.5 1.3 %dynamic_slice.65 = f32[256]{0:T(256)} dynamic-slice(f32[2048]{0:T(1024)} %param.9, s32[]{:T(128)S(6)} %select_n.181), dynamic_slice_sizes={256} | dynamic-slice | bytes 2052 | tf_op jit(solution)/shard_map/dynamic_slice | solution.py:244
  16.8 0.0 collective-permute-done
  16.8 1.3 %collective-permute-start.5 = (bf16[1,136,512]{2,1,0:T(8,128)(2,1)S(1)}, bf16[1,136,512]{2,1,0:T(8,128)(2,1)S(1)}, u32[]{:S(2)}, u32[]{:S(2)}) collective-permute-start(bf16[1,136,512]{2,1,0:T(8,128)(2,1)S(1)} %get-tuple-element.5), channel_id=1, source_target_pairs={{0,12},{2,14},{4,0},{6,2},{8,4},{10,6},{12,8},{14,10},{1,13},{3,15... | collective-permute-start | bytes 417800 | tf_op jit(solution)/shard_map/ppermute | solution.py:242
  18.2 0.0 collective-permute-done.1
  18.2 1.5 %collective-permute-start.6 = (bf16[1,136,512]{2,1,0:T(8,128)(2,1)S(1)}, bf16[1,136,512]{2,1,0:T(8,128)(2,1)S(1)}, u32[]{:S(2)}, u32[]{:S(2)}) collective-permute-start(bf16[1,136,512]{2,1,0:T(8,128)(2,1)S(1)} %get-tuple-element.4), channel_id=1, source_target_pairs={{0,14},{2,0},{4,2},{6,4},{8,6},{10,8},{12,10},{14,12},{1,15},{3,1}... | collective-permute-start | bytes 417800 | tf_op jit(solution)/shard_map/ppermute | solution.py:242
  19.7 6.6 %collective-permute-done.2 = bf16[1,136,512]{2,1,0:T(8,128)(2,1)S(1)} collective-permute-done((bf16[1,136,512]{2,1,0:T(8,128)(2,1)S(1)}, bf16[1,136,512]{2,1,0:T(8,128)(2,1)S(1)}, u32[]{:S(2)}, u32[]{:S(2)}) %collective-permute-start.2) | collective-permute-done | bytes 139296 | tf_op jit(solution)/shard_map/ppermute | solution.py:242
  26.3 0.4 collective-permute-done.3
  26.6 0.0 collective-permute-done.4
  26.7 0.0 collective-permute-done.5
  26.7 0.0 collective-permute-done.6
  26.7 0.0 copy-start
  26.7 1.0 %copy-done = bf16[8,136,512]{2,1,0:T(8,128)(2,1)} copy-done((bf16[8,136,512]{2,1,0:T(8,128)(2,1)}, bf16[8,136,512]{2,1,0:T(8,128)(2,1)S(1)}, u32[]{:S(2)}) %copy-start) | copy-done | bytes 1114136
  27.7 4.0 %shard_map.69 = (bf16[8,136,256]{2,1,0:T(8,128)(2,1)}, f32[2,8,256]{2,1,0:T(8,128)}) custom-call(bf16[8,136,512]{2,1,0:T(8,128)(2,1)} %copy-done, f32[2,1,128]{2,1,0:T(1,128)} %bitcast.49), custom_call_target="tpu_custom_call" | custom-call | tf_op jit(solution)/shard_map/pallas_call | solution.py:155
  31.8 1.1 %dynamic-slice_bitcast_fusion = (bf16[136,256]{1,0:T(8,128)(2,1)S(1)}, bf16[136,256]{1,0:T(8,128)(2,1)S(1)}, bf16[136,256]{1,0:T(8,128)(2,1)S(1)}, bf16[136,256]...) fusion(bf16[8,136,256]{2,1,0:T(8,128)(2,1)} %get-tuple-element.3,, ...), kind=kLoop, calls=%fused_computation.1 | loop fusion | bytes 974876 | tf_op jit(solution)/shard_map/jit(dynamic_index_in_dim)/squeeze | solution.py:278
  32.9 11.3 %collective-permute-start.7 = (bf16[136,256]{1,0:T(8,128)(2,1)S(1)}, bf16[136,256]{1,0:T(8,128)(2,1)S(1)}, u32[]{:S(2)}, u32[]{:S(2)}) collective-permute-start(bf16[136,256]{1,0:T(8,128)(2,1)S(1)} %get-tuple-element.18), channel_id=1, source_target_pairs={{0,14},{2,0},{4,2},{6,4},{8,6},{10,8},{12,10},{14,12},{1,15},{3,1}... | collective-permute-start | bytes 208904 | tf_op jit(solution)/shard_map/ppermute | solution.py:283
  44.2 0.7 %fusion.1 = f32[1,3,256]{2,1,0:T(4,128)S(1)} fusion(bf16[8,136,256]{2,1,0:T(8,128)(2,1)} %get-tuple-element.3, s32[]{:T(128)S(6)} %select_n.183, s32[]{:T(128)S(6)} %add.439), kind=kLoop, calls=%fused_computation.49 | loop fusion | flops 768 | bytes 4616 | tf_op jit(solution)/shard_map/convert_element_type | solution.py:288
  44.9 0.4 collective-permute-start.8
  45.3 0.0 collective-permute-start.9
  45.3 2.5 %collective-permute-start.10 = (bf16[136,256]{1,0:T(8,128)(2,1)S(1)}, bf16[136,256]{1,0:T(8,128)(2,1)S(1)}, u32[]{:S(2)}, u32[]{:S(2)}) collective-permute-start(bf16[136,256]{1,0:T(8,128)(2,1)S(1)} %get-tuple-element.15), channel_id=1, source_target_pairs={{0,8},{2,10},{4,12},{6,14},{8,0},{10,2},{12,4},{14,6},{1,9},{3,11}... | collective-permute-start | bytes 208904 | tf_op jit(solution)/shard_map/ppermute | solution.py:283
  47.8 0.4 collective-permute-start.11
  48.3 0.9 %fusion = bf16[128,2048]{1,0:T(8,128)(2,1)S(1)} fusion(bf16[128,2048]{1,0:T(8,128)(2,1)S(1)} %broadcast_in_dim.3, s32[]{:T(128)S(6)} %select_n.184, bf16[8,136,256]{2,1,0:T(8,128)(2,1)} %get-tuple-element.3, s32[]{:T(128)S(6)} %select_n.183), kind=kLoop, calls=%fused_computation.16 | loop fusion | bytes 131080 | tf_op jit(solution)/shard_map/dynamic_update_slice | solution.py:285
  49.2 0.0 collective-permute-done.7
  49.2 2.9 %collective-permute-start.12 = (bf16[136,256]{1,0:T(8,128)(2,1)S(1)}, bf16[136,256]{1,0:T(8,128)(2,1)S(1)}, u32[]{:S(2)}, u32[]{:S(2)}) collective-permute-start(bf16[136,256]{1,0:T(8,128)(2,1)S(1)} %get-tuple-element.13), channel_id=1, source_target_pairs={{0,4},{2,6},{4,8},{6,10},{8,12},{10,14},{12,0},{14,2},{1,5},{3,7},... | collective-permute-start | bytes 208904 | tf_op jit(solution)/shard_map/ppermute | solution.py:283
  52.1 0.0 collective-permute-done.8
  52.1 0.2 collective-permute-start.13
  52.3 0.0 collective-permute-done.9
  52.4 4.7 %collective-permute-done.10 = bf16[136,256]{1,0:T(8,128)(2,1)S(1)} collective-permute-done((bf16[136,256]{1,0:T(8,128)(2,1)S(1)}, bf16[136,256]{1,0:T(8,128)(2,1)S(1)}, u32[]{:S(2)}, u32[]{:S(2)}) %collective-permute-start.10) | collective-permute-done | bytes 69664 | tf_op jit(solution)/shard_map/ppermute | solution.py:283
  57.1 1.4 %collective-permute-done.11 = bf16[136,256]{1,0:T(8,128)(2,1)S(1)} collective-permute-done((bf16[136,256]{1,0:T(8,128)(2,1)S(1)}, bf16[136,256]{1,0:T(8,128)(2,1)S(1)}, u32[]{:S(2)}, u32[]{:S(2)}) %collective-permute-start.11) | collective-permute-done | bytes 69664 | tf_op jit(solution)/shard_map/ppermute | solution.py:283
  58.5 0.0 collective-permute-done.12
  58.6 0.7 %collective-permute-done.13 = bf16[136,256]{1,0:T(8,128)(2,1)S(1)} collective-permute-done((bf16[136,256]{1,0:T(8,128)(2,1)S(1)}, bf16[136,256]{1,0:T(8,128)(2,1)S(1)}, u32[]{:S(2)}, u32[]{:S(2)}) %collective-permute-start.13) | collective-permute-done | bytes 69664 | tf_op jit(solution)/shard_map/ppermute | solution.py:283
  59.4 0.6 constant_dynamic-slice_fusion
  60.2 0.0 copy-start.1
  60.2 0.8 %copy-done.1 = bf16[128,2048]{1,0:T(8,128)(2,1)} copy-done((bf16[128,2048]{1,0:T(8,128)(2,1)}, bf16[128,2048]{1,0:T(8,128)(2,1)S(1)}, u32[]{:S(2)}) %copy-start.1) | copy-done | bytes 524312
  (46 shorter events, 0.4 us)
Async XLA Ops:
  4.5 12.3 %collective-permute-start = (bf16[1,136,512]{2,1,0:T(8,128)(2,1)S(1)}, bf16[1,136,512]{2,1,0:T(8,128)(2,1)S(1)}, u32[]{:S(2)}, u32[]{:S(2)}) collective-permute-start(bf16[1,136,512]{2,1,0:T(8,128)(2,1)S(1)} %get-tuple-element.10), channel_id=1, source_target_pairs={{0,2},{2,4},{4,6},{6,8},{8,10},{10,12},{12,14},{14,0},{1,3},{3,5},... | collective-permute-start | bytes 417800 | tf_op jit(solution)/shard_map/ppermute | solution.py:242
  7.5 10.7 %collective-permute-start.1 = (bf16[1,136,512]{2,1,0:T(8,128)(2,1)S(1)}, bf16[1,136,512]{2,1,0:T(8,128)(2,1)S(1)}, u32[]{:S(2)}, u32[]{:S(2)}) collective-permute-start(bf16[1,136,512]{2,1,0:T(8,128)(2,1)S(1)} %get-tuple-element.9), channel_id=1, source_target_pairs={{0,4},{2,6},{4,8},{6,10},{8,12},{10,14},{12,0},{14,2},{1,5},{3,7},... | collective-permute-start | bytes 417800 | tf_op jit(solution)/shard_map/ppermute | solution.py:242
  9.1 17.2 %collective-permute-start.2 = (bf16[1,136,512]{2,1,0:T(8,128)(2,1)S(1)}, bf16[1,136,512]{2,1,0:T(8,128)(2,1)S(1)}, u32[]{:S(2)}, u32[]{:S(2)}) collective-permute-start(bf16[1,136,512]{2,1,0:T(8,128)(2,1)S(1)} %get-tuple-element.8), channel_id=1, source_target_pairs={{0,6},{2,8},{4,10},{6,12},{8,14},{10,0},{12,2},{14,4},{1,7},{3,9},... | collective-permute-start | bytes 417800 | tf_op jit(solution)/shard_map/ppermute | solution.py:242
  11.6 15.0 %collective-permute-start.3 = (bf16[1,136,512]{2,1,0:T(8,128)(2,1)S(1)}, bf16[1,136,512]{2,1,0:T(8,128)(2,1)S(1)}, u32[]{:S(2)}, u32[]{:S(2)}) collective-permute-start(bf16[1,136,512]{2,1,0:T(8,128)(2,1)S(1)} %get-tuple-element.7), channel_id=1, source_target_pairs={{0,8},{2,10},{4,12},{6,14},{8,0},{10,2},{12,4},{14,6},{1,9},{3,11}... | collective-permute-start | bytes 417800 | tf_op jit(solution)/shard_map/ppermute | solution.py:242
  12.8 13.8 %collective-permute-start.4 = (bf16[1,136,512]{2,1,0:T(8,128)(2,1)S(1)}, bf16[1,136,512]{2,1,0:T(8,128)(2,1)S(1)}, u32[]{:S(2)}, u32[]{:S(2)}) collective-permute-start(bf16[1,136,512]{2,1,0:T(8,128)(2,1)S(1)} %get-tuple-element.6), channel_id=1, source_target_pairs={{0,10},{2,12},{4,14},{6,0},{8,2},{10,4},{12,6},{14,8},{1,11},{3,13... | collective-permute-start | bytes 417800 | tf_op jit(solution)/shard_map/ppermute | solution.py:242
  16.8 9.9 %collective-permute-start.5 = (bf16[1,136,512]{2,1,0:T(8,128)(2,1)S(1)}, bf16[1,136,512]{2,1,0:T(8,128)(2,1)S(1)}, u32[]{:S(2)}, u32[]{:S(2)}) collective-permute-start(bf16[1,136,512]{2,1,0:T(8,128)(2,1)S(1)} %get-tuple-element.5), channel_id=1, source_target_pairs={{0,12},{2,14},{4,0},{6,2},{8,4},{10,6},{12,8},{14,10},{1,13},{3,15... | collective-permute-start | bytes 417800 | tf_op jit(solution)/shard_map/ppermute | solution.py:242
  18.2 8.5 %collective-permute-start.6 = (bf16[1,136,512]{2,1,0:T(8,128)(2,1)S(1)}, bf16[1,136,512]{2,1,0:T(8,128)(2,1)S(1)}, u32[]{:S(2)}, u32[]{:S(2)}) collective-permute-start(bf16[1,136,512]{2,1,0:T(8,128)(2,1)S(1)} %get-tuple-element.4), channel_id=1, source_target_pairs={{0,14},{2,0},{4,2},{6,4},{8,6},{10,8},{12,10},{14,12},{1,15},{3,1}... | collective-permute-start | bytes 417800 | tf_op jit(solution)/shard_map/ppermute | solution.py:242
  26.7 1.0 %copy-start = (bf16[8,136,512]{2,1,0:T(8,128)(2,1)}, bf16[8,136,512]{2,1,0:T(8,128)(2,1)S(1)}, u32[]{:S(2)}) copy-start(bf16[8,136,512]{2,1,0:T(8,128)(2,1)S(1)} %constant_dynamic-update-slice_fusion.refs_0_) | copy-start | bytes 3342340
  32.9 16.3 %collective-permute-start.7 = (bf16[136,256]{1,0:T(8,128)(2,1)S(1)}, bf16[136,256]{1,0:T(8,128)(2,1)S(1)}, u32[]{:S(2)}, u32[]{:S(2)}) collective-permute-start(bf16[136,256]{1,0:T(8,128)(2,1)S(1)} %get-tuple-element.18), channel_id=1, source_target_pairs={{0,14},{2,0},{4,2},{6,4},{8,6},{10,8},{12,10},{14,12},{1,15},{3,1}... | collective-permute-start | bytes 208904 | tf_op jit(solution)/shard_map/ppermute | solution.py:283
  44.9 7.2 %collective-permute-start.8 = (bf16[136,256]{1,0:T(8,128)(2,1)S(1)}, bf16[136,256]{1,0:T(8,128)(2,1)S(1)}, u32[]{:S(2)}, u32[]{:S(2)}) collective-permute-start(bf16[136,256]{1,0:T(8,128)(2,1)S(1)} %get-tuple-element.17), channel_id=1, source_target_pairs={{0,12},{2,14},{4,0},{6,2},{8,4},{10,6},{12,8},{14,10},{1,13},{3,15... | collective-permute-start | bytes 208904 | tf_op jit(solution)/shard_map/ppermute | solution.py:283
  45.3 7.1 %collective-permute-start.9 = (bf16[136,256]{1,0:T(8,128)(2,1)S(1)}, bf16[136,256]{1,0:T(8,128)(2,1)S(1)}, u32[]{:S(2)}, u32[]{:S(2)}) collective-permute-start(bf16[136,256]{1,0:T(8,128)(2,1)S(1)} %get-tuple-element.16), channel_id=1, source_target_pairs={{0,10},{2,12},{4,14},{6,0},{8,2},{10,4},{12,6},{14,8},{1,11},{3,13... | collective-permute-start | bytes 208904 | tf_op jit(solution)/shard_map/ppermute | solution.py:283
  45.3 11.8 %collective-permute-start.10 = (bf16[136,256]{1,0:T(8,128)(2,1)S(1)}, bf16[136,256]{1,0:T(8,128)(2,1)S(1)}, u32[]{:S(2)}, u32[]{:S(2)}) collective-permute-start(bf16[136,256]{1,0:T(8,128)(2,1)S(1)} %get-tuple-element.15), channel_id=1, source_target_pairs={{0,8},{2,10},{4,12},{6,14},{8,0},{10,2},{12,4},{14,6},{1,9},{3,11}... | collective-permute-start | bytes 208904 | tf_op jit(solution)/shard_map/ppermute | solution.py:283
  47.8 10.7 %collective-permute-start.11 = (bf16[136,256]{1,0:T(8,128)(2,1)S(1)}, bf16[136,256]{1,0:T(8,128)(2,1)S(1)}, u32[]{:S(2)}, u32[]{:S(2)}) collective-permute-start(bf16[136,256]{1,0:T(8,128)(2,1)S(1)} %get-tuple-element.14), channel_id=1, source_target_pairs={{0,6},{2,8},{4,10},{6,12},{8,14},{10,0},{12,2},{14,4},{1,7},{3,9},... | collective-permute-start | bytes 208904 | tf_op jit(solution)/shard_map/ppermute | solution.py:283
  49.2 9.4 %collective-permute-start.12 = (bf16[136,256]{1,0:T(8,128)(2,1)S(1)}, bf16[136,256]{1,0:T(8,128)(2,1)S(1)}, u32[]{:S(2)}, u32[]{:S(2)}) collective-permute-start(bf16[136,256]{1,0:T(8,128)(2,1)S(1)} %get-tuple-element.13), channel_id=1, source_target_pairs={{0,4},{2,6},{4,8},{6,10},{8,12},{10,14},{12,0},{14,2},{1,5},{3,7},... | collective-permute-start | bytes 208904 | tf_op jit(solution)/shard_map/ppermute | solution.py:283
  52.1 7.2 %collective-permute-start.13 = (bf16[136,256]{1,0:T(8,128)(2,1)S(1)}, bf16[136,256]{1,0:T(8,128)(2,1)S(1)}, u32[]{:S(2)}, u32[]{:S(2)}) collective-permute-start(bf16[136,256]{1,0:T(8,128)(2,1)S(1)} %get-tuple-element.12), channel_id=1, source_target_pairs={{0,2},{2,4},{4,6},{6,8},{8,10},{10,12},{12,14},{14,0},{1,3},{3,5},... | collective-permute-start | bytes 208904 | tf_op jit(solution)/shard_map/ppermute | solution.py:283
  60.2 0.8 %copy-start.1 = (bf16[128,2048]{1,0:T(8,128)(2,1)}, bf16[128,2048]{1,0:T(8,128)(2,1)S(1)}, u32[]{:S(2)}) copy-start(bf16[128,2048]{1,0:T(8,128)(2,1)S(1)} %slice_dynamic-update-slice_fusion) | copy-start | bytes 1572868

commit v16 on v15

--- a/solution.py
+++ b/solution.py
@@ -40,7 +40,7 @@
             xrev_ref[:, i * sg : (i + 1) * sg] = flipped.astype(xrev_ref.dtype)
         else:
             xrev_ref[i * br : (i + 1) * br, :] = flipped.astype(xrev_ref.dtype)
-    gain = gain_ref[...]
+    gain = gain_ref[me, :, f * sg : (f + 1) * sg]
     for i in range(nb):
         conv = jnp.dot(
             toeplitz[:, : n - i * br], g_scr[i * br :, :], preferred_element_type=jnp.float32
@@ -113,7 +113,7 @@
             g_ref.at[:, :br, f * sg : (f + 1) * sg],
             x_ref.at[:, :br, x_base + f * sg : x_base + (f + 1) * sg],
             t_ref.at[:, t_base : t_base + 8, :128],
-            gain_ref.at[f],
+            gain_ref,
             out_ref.at[:, :, f * sg : (f + 1) * sg],
             diag_ref.at[f],
             g_scr,
@@ -128,7 +128,7 @@
         )
 
 
-def local_grads(moved, stretch_gain, nb, br, sf, sg, scale, out_rows):
+def local_grads(moved, gains, nb, br, sf, sg, scale, out_rows):
     sw = sf * sg
     fold_rows = sg % 128 == 0
     if fold_rows:
@@ -163,7 +163,7 @@
             pltpu.VMEM((br, nb * sg) if fold_rows else (nb * br, sg), jnp.bfloat16),
             pltpu.VMEM((br, nb * sg) if fold_rows else (8, 128), jnp.bfloat16),
         ],
-    )(*operands, stretch_gain.reshape(sf, 1, sg))
+    )(*operands, gains.reshape(nb, 1, sw))
 
 
 def per_device(cached_input, cached_gate, out_grad, filter_taps, skip_gain):
@@ -241,12 +241,11 @@
         pairs = [(i, (i + shift) % seq_count) for i in range(seq_count)]
         arrived[shift] = lax.ppermute(chunk, "seq", pairs)
     moved = jnp.concatenate(arrived, axis=0)
-    stretch_gain = lax.dynamic_slice_in_dim(skip_gain, seq_index * stretch_width, stretch_width, 0)
     used_rows = 3 * stretch_filters * block_rows // stretch_width
     extra_rows = -(-used_rows // 8) * 8
     local_grad, diag = local_grads(
         moved,
-        stretch_gain,
+        skip_gain,
         seq_count,
         block_rows,
         stretch_filters,

time: 61.3 us -> 61.2 us (level)
  local copies, waits for them, and re-layouts: 7.43 us -> 6.11 us
  starting transfers between devices: 31.6 us -> 32.6 us
    dynamic_slice x1 -> x0, local copies, waits for them, and re-layouts: 1.32 us -> none  [per_device(): lax.dynamic_slice_in_dim(skip_gain, seq_index * stretch_width, stretch_wi...]
    ppermute x7, starting transfers between devices: 13.8 us -> 14.8 us  [per_device(): arrived[shift] = lax.ppermute(chunk, 'seq', pairs)]
  transfers between devices with their start and end apart: 14 -> 14, of which waited for: 5 -> 6; matrix products, arithmetic and copies ran while one was open for 5% -> 3% of each run, Pallas kernels for 0% -> 0%
where the time goes in v16:
time: 61.2 us; the launch traced here: 60.9 us
  starting transfers between devices  32.6 us (53%)
  waiting for transfers between devices  14.1 us (23%)
  Pallas kernels  6.33 us (10%)
  local copies, waits for them, and re-layouts  6.11 us (10%)
  between operations  0.99 us (2%)
  other arithmetic  0.77 us (1%)
    ppermute x7, starting transfers between devices, per_device(): chunk = lax.ppermute(chunk, 'seq', pairs)  17.8 us
    ppermute x7, starting transfers between devices, per_device(): arrived[shift] = lax.ppermute(chunk, 'seq', pairs)  14.8 us
    ppermute x7, waiting for transfers between devices, per_device(): arrived[shift] = lax.ppermute(chunk, 'seq', pairs)  7.34 us
    ppermute x7, waiting for transfers between devices, per_device(): chunk = lax.ppermute(chunk, 'seq', pairs)  6.79 us
    pallas_call x1, Pallas kernels, local_grads(): pl.pallas_call(body, out_shape=[jax.ShapeDtypeStruct((nb, out_rows, sw),...  4 us
    pallas_call x1, Pallas kernels, per_device(): pl.pallas_call(functools.partial(pack_kernel, br=block_rows, sw=stretch_w...  2.33 us
    unnamed x25, local copies, waits for them, and re-layouts  1.99 us
    dynamic_slice x1, local copies, waits for them, and re-layouts, per_device(): lax.dynamic_index_in_dim(packed, (seq_index + shift) % seq_count, 0, keep...  1.4 us
  transfers between devices with their start and end apart: 14, of which 6 were waited for; matrix products, arithmetic and copies ran while one was open for 3% of the time, Pallas kernels for 0%

profile of v16, /device:TPU:0, one launch (start us, length us, event | category | flops | bytes accessed | tf_op | source)
XLA Modules:
  0.0 60.9 jit_solution(17275005175630588382)
XLA Ops:
  0.7 2.3 %shard_map.68 = bf16[8,136,512]{2,1,0:T(8,128)(2,1)} custom-call(bf16[128,2048]{1,0:T(8,128)(2,1)} %og_ref.1, bf16[128,2048]{1,0:T(8,128)(2,1)} %gate_ref.1, bf16[128,2048]{1,0:T(8,128)(2,1)} %x_ref.1, bf16[16,128]{1,0:T(8,128)(2,1)} %bitcast.49), custom_call_target="tpu_custom_call" | custom-call | tf_op jit(solution)/shard_map/pallas_call | solution.py:195
  3.1 1.4 %constant_dynamic-slice_fusion.2 = (bf16[1,136,512]{2,1,0:T(8,128)(2,1)S(1)}, bf16[1,136,512]{2,1,0:T(8,128)(2,1)S(1)}, bf16[1,136,512]{2,1,0:T(8,128)(2,1)S(1)}...) fusion(bf16[8,136,512]{2,1,0:T(8,128)(2,1)} %shard_map.68, ...), kind=kLoop, calls=%fused_computation.42 | loop fusion | bytes 2228256 | tf_op jit(solution)/shard_map/jit(dynamic_index_in_dim)/dynamic_slice | solution.py:240
  4.5 3.0 %collective-permute-start = (bf16[1,136,512]{2,1,0:T(8,128)(2,1)S(1)}, bf16[1,136,512]{2,1,0:T(8,128)(2,1)S(1)}, u32[]{:S(2)}, u32[]{:S(2)}) collective-permute-start(bf16[1,136,512]{2,1,0:T(8,128)(2,1)S(1)} %get-tuple-element.10), channel_id=1, source_target_pairs={{0,2},{2,4},{4,6},{6,8},{8,10},{10,12},{12,14},{14,0},{1,3},{3,5},... | collective-permute-start | bytes 417800 | tf_op jit(solution)/shard_map/ppermute | solution.py:242
  7.5 1.6 %collective-permute-start.1 = (bf16[1,136,512]{2,1,0:T(8,128)(2,1)S(1)}, bf16[1,136,512]{2,1,0:T(8,128)(2,1)S(1)}, u32[]{:S(2)}, u32[]{:S(2)}) collective-permute-start(bf16[1,136,512]{2,1,0:T(8,128)(2,1)S(1)} %get-tuple-element.9), channel_id=1, source_target_pairs={{0,4},{2,6},{4,8},{6,10},{8,12},{10,14},{12,0},{14,2},{1,5},{3,7},... | collective-permute-start | bytes 417800 | tf_op jit(solution)/shard_map/ppermute | solution.py:242
  9.1 2.5 %collective-permute-start.2 = (bf16[1,136,512]{2,1,0:T(8,128)(2,1)S(1)}, bf16[1,136,512]{2,1,0:T(8,128)(2,1)S(1)}, u32[]{:S(2)}, u32[]{:S(2)}) collective-permute-start(bf16[1,136,512]{2,1,0:T(8,128)(2,1)S(1)} %get-tuple-element.8), channel_id=1, source_target_pairs={{0,6},{2,8},{4,10},{6,12},{8,14},{10,0},{12,2},{14,4},{1,7},{3,9},... | collective-permute-start | bytes 417800 | tf_op jit(solution)/shard_map/ppermute | solution.py:242
  11.6 1.2 %collective-permute-start.3 = (bf16[1,136,512]{2,1,0:T(8,128)(2,1)S(1)}, bf16[1,136,512]{2,1,0:T(8,128)(2,1)S(1)}, u32[]{:S(2)}, u32[]{:S(2)}) collective-permute-start(bf16[1,136,512]{2,1,0:T(8,128)(2,1)S(1)} %get-tuple-element.7), channel_id=1, source_target_pairs={{0,8},{2,10},{4,12},{6,14},{8,0},{10,2},{12,4},{14,6},{1,9},{3,11}... | collective-permute-start | bytes 417800 | tf_op jit(solution)/shard_map/ppermute | solution.py:242
  12.8 2.6 %collective-permute-start.4 = (bf16[1,136,512]{2,1,0:T(8,128)(2,1)S(1)}, bf16[1,136,512]{2,1,0:T(8,128)(2,1)S(1)}, u32[]{:S(2)}, u32[]{:S(2)}) collective-permute-start(bf16[1,136,512]{2,1,0:T(8,128)(2,1)S(1)} %get-tuple-element.6), channel_id=1, source_target_pairs={{0,10},{2,12},{4,14},{6,0},{8,2},{10,4},{12,6},{14,8},{1,11},{3,13... | collective-permute-start | bytes 417800 | tf_op jit(solution)/shard_map/ppermute | solution.py:242
  15.5 0.0 collective-permute-done
  15.5 1.5 %collective-permute-start.5 = (bf16[1,136,512]{2,1,0:T(8,128)(2,1)S(1)}, bf16[1,136,512]{2,1,0:T(8,128)(2,1)S(1)}, u32[]{:S(2)}, u32[]{:S(2)}) collective-permute-start(bf16[1,136,512]{2,1,0:T(8,128)(2,1)S(1)} %get-tuple-element.5), channel_id=1, source_target_pairs={{0,12},{2,14},{4,0},{6,2},{8,4},{10,6},{12,8},{14,10},{1,13},{3,15... | collective-permute-start | bytes 417800 | tf_op jit(solution)/shard_map/ppermute | solution.py:242
  17.1 0.0 collective-permute-done.1
  17.1 2.2 %collective-permute-start.6 = (bf16[1,136,512]{2,1,0:T(8,128)(2,1)S(1)}, bf16[1,136,512]{2,1,0:T(8,128)(2,1)S(1)}, u32[]{:S(2)}, u32[]{:S(2)}) collective-permute-start(bf16[1,136,512]{2,1,0:T(8,128)(2,1)S(1)} %get-tuple-element.4), channel_id=1, source_target_pairs={{0,14},{2,0},{4,2},{6,4},{8,6},{10,8},{12,10},{14,12},{1,15},{3,1}... | collective-permute-start | bytes 417800 | tf_op jit(solution)/shard_map/ppermute | solution.py:242
  19.3 7.0 %collective-permute-done.2 = bf16[1,136,512]{2,1,0:T(8,128)(2,1)S(1)} collective-permute-done((bf16[1,136,512]{2,1,0:T(8,128)(2,1)S(1)}, bf16[1,136,512]{2,1,0:T(8,128)(2,1)S(1)}, u32[]{:S(2)}, u32[]{:S(2)}) %collective-permute-start.2) | collective-permute-done | bytes 139296 | tf_op jit(solution)/shard_map/ppermute | solution.py:242
  26.3 0.2 collective-permute-done.3
  26.5 0.0 collective-permute-done.4
  26.6 0.0 collective-permute-done.5
  26.6 0.1 collective-permute-done.6
  26.7 0.0 copy-start
  26.7 1.0 %copy-done = bf16[8,136,512]{2,1,0:T(8,128)(2,1)} copy-done((bf16[8,136,512]{2,1,0:T(8,128)(2,1)}, bf16[8,136,512]{2,1,0:T(8,128)(2,1)S(1)}, u32[]{:S(2)}) %copy-start) | copy-done | bytes 1114136
  27.7 4.0 %shard_map.69 = (bf16[8,136,256]{2,1,0:T(8,128)(2,1)}, f32[2,8,256]{2,1,0:T(8,128)}) custom-call(bf16[8,136,512]{2,1,0:T(8,128)(2,1)} %copy-done, f32[8,1,256]{2,1,0:T(1,128)} %bitcast.47), custom_call_target="tpu_custom_call" | custom-call | tf_op jit(solution)/shard_map/pallas_call | solution.py:155
  31.7 1.1 %dynamic-slice_bitcast_fusion = (bf16[136,256]{1,0:T(8,128)(2,1)S(1)}, bf16[136,256]{1,0:T(8,128)(2,1)S(1)}, bf16[136,256]{1,0:T(8,128)(2,1)S(1)}, bf16[136,256]...) fusion(bf16[8,136,256]{2,1,0:T(8,128)(2,1)} %get-tuple-element.3,, ...), kind=kLoop, calls=%fused_computation.1 | loop fusion | bytes 974876 | tf_op jit(solution)/shard_map/jit(dynamic_index_in_dim)/squeeze | solution.py:277
  32.9 11.3 %collective-permute-start.7 = (bf16[136,256]{1,0:T(8,128)(2,1)S(1)}, bf16[136,256]{1,0:T(8,128)(2,1)S(1)}, u32[]{:S(2)}, u32[]{:S(2)}) collective-permute-start(bf16[136,256]{1,0:T(8,128)(2,1)S(1)} %get-tuple-element.18), channel_id=1, source_target_pairs={{0,14},{2,0},{4,2},{6,4},{8,6},{10,8},{12,10},{14,12},{1,15},{3,1}... | collective-permute-start | bytes 208904 | tf_op jit(solution)/shard_map/ppermute | solution.py:282
  44.2 0.7 %fusion.1 = f32[1,3,256]{2,1,0:T(4,128)S(1)} fusion(bf16[8,136,256]{2,1,0:T(8,128)(2,1)} %get-tuple-element.3, s32[]{:T(128)S(6)} %select_n.179, s32[]{:T(128)S(6)} %add.435), kind=kLoop, calls=%fused_computation.49 | loop fusion | flops 768 | bytes 4616 | tf_op jit(solution)/shard_map/convert_element_type | solution.py:287
  44.9 0.4 collective-permute-start.8
  45.3 0.0 collective-permute-start.9
  45.3 2.5 %collective-permute-start.10 = (bf16[136,256]{1,0:T(8,128)(2,1)S(1)}, bf16[136,256]{1,0:T(8,128)(2,1)S(1)}, u32[]{:S(2)}, u32[]{:S(2)}) collective-permute-start(bf16[136,256]{1,0:T(8,128)(2,1)S(1)} %get-tuple-element.15), channel_id=1, source_target_pairs={{0,8},{2,10},{4,12},{6,14},{8,0},{10,2},{12,4},{14,6},{1,9},{3,11}... | collective-permute-start | bytes 208904 | tf_op jit(solution)/shard_map/ppermute | solution.py:282
  47.8 0.4 collective-permute-start.11
  48.2 0.9 %fusion = bf16[128,2048]{1,0:T(8,128)(2,1)S(1)} fusion(bf16[128,2048]{1,0:T(8,128)(2,1)S(1)} %broadcast_in_dim.3, s32[]{:T(128)S(6)} %select_n.180, bf16[8,136,256]{2,1,0:T(8,128)(2,1)} %get-tuple-element.3, s32[]{:T(128)S(6)} %select_n.179), kind=kLoop, calls=%fused_computation.16 | loop fusion | bytes 131080 | tf_op jit(solution)/shard_map/dynamic_update_slice | solution.py:284
  49.1 0.0 collective-permute-done.7
  49.1 2.9 %collective-permute-start.12 = (bf16[136,256]{1,0:T(8,128)(2,1)S(1)}, bf16[136,256]{1,0:T(8,128)(2,1)S(1)}, u32[]{:S(2)}, u32[]{:S(2)}) collective-permute-start(bf16[136,256]{1,0:T(8,128)(2,1)S(1)} %get-tuple-element.13), channel_id=1, source_target_pairs={{0,4},{2,6},{4,8},{6,10},{8,12},{10,14},{12,0},{14,2},{1,5},{3,7},... | collective-permute-start | bytes 208904 | tf_op jit(solution)/shard_map/ppermute | solution.py:282
  52.0 0.0 collective-permute-done.8
  52.0 0.3 collective-permute-start.13
  52.3 0.0 collective-permute-done.9
  52.3 4.7 %collective-permute-done.10 = bf16[136,256]{1,0:T(8,128)(2,1)S(1)} collective-permute-done((bf16[136,256]{1,0:T(8,128)(2,1)S(1)}, bf16[136,256]{1,0:T(8,128)(2,1)S(1)}, u32[]{:S(2)}, u32[]{:S(2)}) %collective-permute-start.10) | collective-permute-done | bytes 69664 | tf_op jit(solution)/shard_map/ppermute | solution.py:282
  57.0 1.4 %collective-permute-done.11 = bf16[136,256]{1,0:T(8,128)(2,1)S(1)} collective-permute-done((bf16[136,256]{1,0:T(8,128)(2,1)S(1)}, bf16[136,256]{1,0:T(8,128)(2,1)S(1)}, u32[]{:S(2)}, u32[]{:S(2)}) %collective-permute-start.11) | collective-permute-done | bytes 69664 | tf_op jit(solution)/shard_map/ppermute | solution.py:282
  58.5 0.0 collective-permute-done.12
  58.5 0.7 %collective-permute-done.13 = bf16[136,256]{1,0:T(8,128)(2,1)S(1)} collective-permute-done((bf16[136,256]{1,0:T(8,128)(2,1)S(1)}, bf16[136,256]{1,0:T(8,128)(2,1)S(1)}, u32[]{:S(2)}, u32[]{:S(2)}) %collective-permute-start.13) | collective-permute-done | bytes 69664 | tf_op jit(solution)/shard_map/ppermute | solution.py:282
  59.4 0.6 constant_dynamic-slice_fusion
  60.1 0.0 copy-start.1
  60.1 0.8 %copy-done.1 = bf16[128,2048]{1,0:T(8,128)(2,1)} copy-done((bf16[128,2048]{1,0:T(8,128)(2,1)}, bf16[128,2048]{1,0:T(8,128)(2,1)S(1)}, u32[]{:S(2)}) %copy-start.1) | copy-done | bytes 524312
  (46 shorter events, 0.4 us)
Async XLA Ops:
  4.5 11.0 %collective-permute-start = (bf16[1,136,512]{2,1,0:T(8,128)(2,1)S(1)}, bf16[1,136,512]{2,1,0:T(8,128)(2,1)S(1)}, u32[]{:S(2)}, u32[]{:S(2)}) collective-permute-start(bf16[1,136,512]{2,1,0:T(8,128)(2,1)S(1)} %get-tuple-element.10), channel_id=1, source_target_pairs={{0,2},{2,4},{4,6},{6,8},{8,10},{10,12},{12,14},{14,0},{1,3},{3,5},... | collective-permute-start | bytes 417800 | tf_op jit(solution)/shard_map/ppermute | solution.py:242
  7.5 9.6 %collective-permute-start.1 = (bf16[1,136,512]{2,1,0:T(8,128)(2,1)S(1)}, bf16[1,136,512]{2,1,0:T(8,128)(2,1)S(1)}, u32[]{:S(2)}, u32[]{:S(2)}) collective-permute-start(bf16[1,136,512]{2,1,0:T(8,128)(2,1)S(1)} %get-tuple-element.9), channel_id=1, source_target_pairs={{0,4},{2,6},{4,8},{6,10},{8,12},{10,14},{12,0},{14,2},{1,5},{3,7},... | collective-permute-start | bytes 417800 | tf_op jit(solution)/shard_map/ppermute | solution.py:242
  9.1 17.2 %collective-permute-start.2 = (bf16[1,136,512]{2,1,0:T(8,128)(2,1)S(1)}, bf16[1,136,512]{2,1,0:T(8,128)(2,1)S(1)}, u32[]{:S(2)}, u32[]{:S(2)}) collective-permute-start(bf16[1,136,512]{2,1,0:T(8,128)(2,1)S(1)} %get-tuple-element.8), channel_id=1, source_target_pairs={{0,6},{2,8},{4,10},{6,12},{8,14},{10,0},{12,2},{14,4},{1,7},{3,9},... | collective-permute-start | bytes 417800 | tf_op jit(solution)/shard_map/ppermute | solution.py:242
  11.6 14.9 %collective-permute-start.3 = (bf16[1,136,512]{2,1,0:T(8,128)(2,1)S(1)}, bf16[1,136,512]{2,1,0:T(8,128)(2,1)S(1)}, u32[]{:S(2)}, u32[]{:S(2)}) collective-permute-start(bf16[1,136,512]{2,1,0:T(8,128)(2,1)S(1)} %get-tuple-element.7), channel_id=1, source_target_pairs={{0,8},{2,10},{4,12},{6,14},{8,0},{10,2},{12,4},{14,6},{1,9},{3,11}... | collective-permute-start | bytes 417800 | tf_op jit(solution)/shard_map/ppermute | solution.py:242
  12.8 13.7 %collective-permute-start.4 = (bf16[1,136,512]{2,1,0:T(8,128)(2,1)S(1)}, bf16[1,136,512]{2,1,0:T(8,128)(2,1)S(1)}, u32[]{:S(2)}, u32[]{:S(2)}) collective-permute-start(bf16[1,136,512]{2,1,0:T(8,128)(2,1)S(1)} %get-tuple-element.6), channel_id=1, source_target_pairs={{0,10},{2,12},{4,14},{6,0},{8,2},{10,4},{12,6},{14,8},{1,11},{3,13... | collective-permute-start | bytes 417800 | tf_op jit(solution)/shard_map/ppermute | solution.py:242
  15.5 11.1 %collective-permute-start.5 = (bf16[1,136,512]{2,1,0:T(8,128)(2,1)S(1)}, bf16[1,136,512]{2,1,0:T(8,128)(2,1)S(1)}, u32[]{:S(2)}, u32[]{:S(2)}) collective-permute-start(bf16[1,136,512]{2,1,0:T(8,128)(2,1)S(1)} %get-tuple-element.5), channel_id=1, source_target_pairs={{0,12},{2,14},{4,0},{6,2},{8,4},{10,6},{12,8},{14,10},{1,13},{3,15... | collective-permute-start | bytes 417800 | tf_op jit(solution)/shard_map/ppermute | solution.py:242
  17.1 9.6 %collective-permute-start.6 = (bf16[1,136,512]{2,1,0:T(8,128)(2,1)S(1)}, bf16[1,136,512]{2,1,0:T(8,128)(2,1)S(1)}, u32[]{:S(2)}, u32[]{:S(2)}) collective-permute-start(bf16[1,136,512]{2,1,0:T(8,128)(2,1)S(1)} %get-tuple-element.4), channel_id=1, source_target_pairs={{0,14},{2,0},{4,2},{6,4},{8,6},{10,8},{12,10},{14,12},{1,15},{3,1}... | collective-permute-start | bytes 417800 | tf_op jit(solution)/shard_map/ppermute | solution.py:242
  26.7 1.0 %copy-start = (bf16[8,136,512]{2,1,0:T(8,128)(2,1)}, bf16[8,136,512]{2,1,0:T(8,128)(2,1)S(1)}, u32[]{:S(2)}) copy-start(bf16[8,136,512]{2,1,0:T(8,128)(2,1)S(1)} %constant_dynamic-update-slice_fusion.refs_0_) | copy-start | bytes 3342340
  32.9 16.2 %collective-permute-start.7 = (bf16[136,256]{1,0:T(8,128)(2,1)S(1)}, bf16[136,256]{1,0:T(8,128)(2,1)S(1)}, u32[]{:S(2)}, u32[]{:S(2)}) collective-permute-start(bf16[136,256]{1,0:T(8,128)(2,1)S(1)} %get-tuple-element.18), channel_id=1, source_target_pairs={{0,14},{2,0},{4,2},{6,4},{8,6},{10,8},{12,10},{14,12},{1,15},{3,1}... | collective-permute-start | bytes 208904 | tf_op jit(solution)/shard_map/ppermute | solution.py:282
  44.9 7.2 %collective-permute-start.8 = (bf16[136,256]{1,0:T(8,128)(2,1)S(1)}, bf16[136,256]{1,0:T(8,128)(2,1)S(1)}, u32[]{:S(2)}, u32[]{:S(2)}) collective-permute-start(bf16[136,256]{1,0:T(8,128)(2,1)S(1)} %get-tuple-element.17), channel_id=1, source_target_pairs={{0,12},{2,14},{4,0},{6,2},{8,4},{10,6},{12,8},{14,10},{1,13},{3,15... | collective-permute-start | bytes 208904 | tf_op jit(solution)/shard_map/ppermute | solution.py:282
  45.3 7.1 %collective-permute-start.9 = (bf16[136,256]{1,0:T(8,128)(2,1)S(1)}, bf16[136,256]{1,0:T(8,128)(2,1)S(1)}, u32[]{:S(2)}, u32[]{:S(2)}) collective-permute-start(bf16[136,256]{1,0:T(8,128)(2,1)S(1)} %get-tuple-element.16), channel_id=1, source_target_pairs={{0,10},{2,12},{4,14},{6,0},{8,2},{10,4},{12,6},{14,8},{1,11},{3,13... | collective-permute-start | bytes 208904 | tf_op jit(solution)/shard_map/ppermute | solution.py:282
  45.3 11.8 %collective-permute-start.10 = (bf16[136,256]{1,0:T(8,128)(2,1)S(1)}, bf16[136,256]{1,0:T(8,128)(2,1)S(1)}, u32[]{:S(2)}, u32[]{:S(2)}) collective-permute-start(bf16[136,256]{1,0:T(8,128)(2,1)S(1)} %get-tuple-element.15), channel_id=1, source_target_pairs={{0,8},{2,10},{4,12},{6,14},{8,0},{10,2},{12,4},{14,6},{1,9},{3,11}... | collective-permute-start | bytes 208904 | tf_op jit(solution)/shard_map/ppermute | solution.py:282
  47.8 10.6 %collective-permute-start.11 = (bf16[136,256]{1,0:T(8,128)(2,1)S(1)}, bf16[136,256]{1,0:T(8,128)(2,1)S(1)}, u32[]{:S(2)}, u32[]{:S(2)}) collective-permute-start(bf16[136,256]{1,0:T(8,128)(2,1)S(1)} %get-tuple-element.14), channel_id=1, source_target_pairs={{0,6},{2,8},{4,10},{6,12},{8,14},{10,0},{12,2},{14,4},{1,7},{3,9},... | collective-permute-start | bytes 208904 | tf_op jit(solution)/shard_map/ppermute | solution.py:282
  49.1 9.4 %collective-permute-start.12 = (bf16[136,256]{1,0:T(8,128)(2,1)S(1)}, bf16[136,256]{1,0:T(8,128)(2,1)S(1)}, u32[]{:S(2)}, u32[]{:S(2)}) collective-permute-start(bf16[136,256]{1,0:T(8,128)(2,1)S(1)} %get-tuple-element.13), channel_id=1, source_target_pairs={{0,4},{2,6},{4,8},{6,10},{8,12},{10,14},{12,0},{14,2},{1,5},{3,7},... | collective-permute-start | bytes 208904 | tf_op jit(solution)/shard_map/ppermute | solution.py:282
  52.0 7.2 %collective-permute-start.13 = (bf16[136,256]{1,0:T(8,128)(2,1)S(1)}, bf16[136,256]{1,0:T(8,128)(2,1)S(1)}, u32[]{:S(2)}, u32[]{:S(2)}) collective-permute-start(bf16[136,256]{1,0:T(8,128)(2,1)S(1)} %get-tuple-element.12), channel_id=1, source_target_pairs={{0,2},{2,4},{4,6},{6,8},{8,10},{10,12},{12,14},{14,0},{1,3},{3,5},... | collective-permute-start | bytes 208904 | tf_op jit(solution)/shard_map/ppermute | solution.py:282
  60.1 0.8 %copy-start.1 = (bf16[128,2048]{1,0:T(8,128)(2,1)}, bf16[128,2048]{1,0:T(8,128)(2,1)S(1)}, u32[]{:S(2)}) copy-start(bf16[128,2048]{1,0:T(8,128)(2,1)S(1)} %slice_dynamic-update-slice_fusion) | copy-start | bytes 1572868

commit v17 on v16

--- a/solution.py
+++ b/solution.py
@@ -91,20 +91,22 @@
         out_ref[:, br : br + 8, :br] = tile.astype(out_ref.dtype)
 
 
-def pack_kernel(og_ref, gate_ref, x_ref, taps_ref, out_ref, *, br, sw, sf, gw, per_step):
+def pack_kernel(me_ref, *refs, nb, br, sw, sf, gw):
+    og_refs, gate_refs, x_refs = refs[:nb], refs[nb : 2 * nb], refs[2 * nb : 3 * nb]
+    taps_ref, out_refs = refs[3 * nb], refs[3 * nb + 1 :]
     filters = taps_ref.shape[0]
     rows = lax.broadcasted_iota(jnp.int32, (8, filters), 0)
     cols = lax.broadcasted_iota(jnp.int32, (8, filters), 1)
-    for d in range(per_step):
-        j = pl.program_id(0) * per_step + d
-        span = slice(d * sw, (d + 1) * sw)
-        gated = og_ref[:, span].astype(jnp.float32) * gate_ref[:, span].astype(jnp.float32)
-        out_ref[d, :br, :sw] = gated.astype(out_ref.dtype)
-        out_ref[d, :br, sw:] = x_ref[:, span]
+    for k in range(nb):
+        j = (me_ref[0] + k) % nb
+        out_ref = out_refs[k]
+        gated = og_refs[k][...].astype(jnp.float32) * gate_refs[k][...].astype(jnp.float32)
+        out_ref[:br, :sw] = gated.astype(out_ref.dtype)
+        out_ref[:br, sw:] = x_refs[k][...]
         pick = ((cols == (j * sw) // gw + rows) & (rows < sf)).astype(jnp.bfloat16)
         tap_rows = jnp.dot(pick, taps_ref[...], preferred_element_type=jnp.float32)
-        out_ref[d, br:, :br] = tap_rows.astype(out_ref.dtype)
-        out_ref[d, br:, br:] = jnp.zeros((8, 2 * sw - br), out_ref.dtype)
+        out_ref[br:, :br] = tap_rows.astype(out_ref.dtype)
+        out_ref[br:, br:] = jnp.zeros((8, 2 * sw - br), out_ref.dtype)
 
 
 def local_kernel(g_ref, x_ref, t_ref, gain_ref, out_ref, diag_ref, g_scr, xrev_ref, gt_ref, *, nb, br, sf, sg, x_base, t_base, scale, fold_rows):
@@ -190,31 +192,39 @@
         return product.astype(jnp.bfloat16)
 
     if stretch_width % 128 == 0:
-        per_step = seq_count // 2 if seq_count % 2 == 0 else seq_count
-        column_block = pl.BlockSpec((block_rows, per_step * stretch_width), lambda j: (0, j))
-        packed = pl.pallas_call(
+        def column(k):
+            return pl.BlockSpec(
+                (block_rows, stretch_width), lambda i, me, k=k: (0, (me[0] + k) % seq_count)
+            )
+
+        chunk_shape = jax.ShapeDtypeStruct((block_rows + 8, 2 * stretch_width), jnp.bfloat16)
+        chunks = pl.pallas_call(
             functools.partial(
                 pack_kernel,
+                nb=seq_count,
                 br=block_rows,
                 sw=stretch_width,
                 sf=stretch_filters,
                 gw=group_width,
-                per_step=per_step,
             ),
-            grid=(seq_count // per_step,),
-            in_specs=[
-                column_block,
-                column_block,
-                column_block,
-                pl.BlockSpec((filters, block_rows), lambda j: (0, 0)),
-            ],
-            out_specs=pl.BlockSpec(
-                (per_step, block_rows + 8, 2 * stretch_width), lambda j: (j, 0, 0)
+            grid_spec=pltpu.PrefetchScalarGridSpec(
+                num_scalar_prefetch=1,
+                grid=(1,),
+                in_specs=[column(k) for k in range(seq_count)] * 3
+                + [pl.BlockSpec((filters, block_rows), lambda i, me: (0, 0))],
+                out_specs=[
+                    pl.BlockSpec((block_rows + 8, 2 * stretch_width), lambda i, me: (0, 0))
+                ]
+                * seq_count,
             ),
-            out_shape=jax.ShapeDtypeStruct(
-                (seq_count, block_rows + 8, 2 * stretch_width), jnp.bfloat16
-            ),
-        )(out_grad, cached_gate, cached_input, jnp.transpose(filter_taps))
+            out_shape=[chunk_shape] * seq_count,
+        )(
+            seq_index.reshape(1).astype(jnp.int32),
+            *([out_grad] * seq_count),
+            *([cached_gate] * seq_count),
+            *([cached_input] * seq_count),
+            jnp.transpose(filter_taps),
+        )
     else:
         routed_taps = jnp.transpose(filter_taps[:, tap_columns]).reshape(
             seq_count, stretch_filters, block_rows
@@ -234,12 +244,16 @@
     order = []
     for step in range(1, seq_count // 2 + 1):
         order += [step] if step == seq_count - step else [step, seq_count - step]
+    if stretch_width % 128 != 0:
+        chunks = [
+            lax.dynamic_index_in_dim(packed, (seq_index + shift) % seq_count, 0, keepdims=False)
+            for shift in range(seq_count)
+        ]
     arrived = [None] * seq_count
-    arrived[0] = lax.dynamic_index_in_dim(packed, seq_index, 0, keepdims=True)
+    arrived[0] = chunks[0][None]
     for shift in order:
-        chunk = lax.dynamic_index_in_dim(packed, (seq_index + shift) % seq_count, 0, keepdims=True)
         pairs = [(i, (i + shift) % seq_count) for i in range(seq_count)]
-        arrived[shift] = lax.ppermute(chunk, "seq", pairs)
+        arrived[shift] = lax.ppermute(chunks[shift], "seq", pairs)[None]
     moved = jnp.concatenate(arrived, axis=0)
     used_rows = 3 * stretch_filters * block_rows // stretch_width
     extra_rows = -(-used_rows // 8) * 8

time: 61.2 us -> 60.3 us (0.985)
  starting transfers between devices: 32.6 us -> 31.8 us
    dynamic_slice x1 -> x0, local copies, waits for them, and re-layouts: 1.4 us -> none  [per_device(): lax.dynamic_index_in_dim(packed, (seq_index + shift) % seq_count, 0, keep...]
    unnamed x25 -> x26, local copies, waits for them, and re-layouts: 1.99 us -> 2.9 us
    ppermute x7, starting transfers between devices: 14.8 us -> 14 us  [per_device(): arrived[shift] = lax.ppermute(chunks[shift], 'seq', pairs)[None]]
  transfers between devices with their start and end apart: 14 -> 14, of which waited for: 6 -> 6; matrix products, arithmetic and copies ran while one was open for 3% -> 4% of each run, Pallas kernels for 0% -> 0%
where the time goes in v17:
time: 60.3 us; the launch traced here: 59.9 us
  starting transfers between devices  31.8 us (53%)
  waiting for transfers between devices  14.3 us (24%)
  Pallas kernels  6.6 us (11%)
  local copies, waits for them, and re-layouts  5.63 us (9%)
  between operations  0.88 us (1%)
  other arithmetic  0.77 us (1%)
    ppermute x7, starting transfers between devices, per_device(): chunk = lax.ppermute(chunk, 'seq', pairs)  17.7 us
    ppermute x7, starting transfers between devices, per_device(): arrived[shift] = lax.ppermute(chunks[shift], 'seq', pairs)[None]  14 us
    ppermute x7, waiting for transfers between devices, per_device(): arrived[shift] = lax.ppermute(chunks[shift], 'seq', pairs)[None]  7.45 us
    ppermute x7, waiting for transfers between devices, per_device(): chunk = lax.ppermute(chunk, 'seq', pairs)  6.83 us
    pallas_call x1, Pallas kernels, local_grads(): pl.pallas_call(body, out_shape=[jax.ShapeDtypeStruct((nb, out_rows, sw),...  4 us
    unnamed x26, local copies, waits for them, and re-layouts  2.9 us
    pallas_call x1, Pallas kernels, per_device(): pl.pallas_call(functools.partial(pack_kernel, nb=seq_count, br=block_rows...  2.61 us
  transfers between devices with their start and end apart: 14, of which 6 were waited for; matrix products, arithmetic and copies ran while one was open for 4% of the time, Pallas kernels for 0%

profile of v17, /device:TPU:0, one launch (start us, length us, event | category | flops | bytes accessed | tf_op | source)
XLA Modules:
  0.0 59.9 jit_solution(2630155204190629156)
XLA Ops:
  0.6 2.6 %shard_map.68 = (bf16[136,512]{1,0:T(8,128)(2,1)}, bf16[136,512]{1,0:T(8,128)(2,1)}, bf16[136,512]{1,0:T(8,128)(2,1)}, bf16[136,512]{1,0:T(8,128)(2,1)}, bf16[13...) custom-call(s32[1]{0:T(128)} %bitcast.me_ref, ...), custom_call_target="tpu_custom_call" | custom-call | tf_op jit(solution)/shard_map/pallas_call | solution.py:201
  3.2 3.0 %collective-permute-start = (bf16[136,512]{1,0:T(8,128)(2,1)}, bf16[136,512]{1,0:T(8,128)(2,1)S(1)}, u32[]{:S(2)}, u32[]{:S(2)}) collective-permute-start(bf16[136,512]{1,0:T(8,128)(2,1)} %get-tuple-element.12), channel_id=1, source_target_pairs={{0,2},{2,4},{4,6},{6,8},{8,10},{10,12},{12,14},{14,0},{1,3},{3,5},... | collective-permute-start | bytes 417800 | tf_op jit(solution)/shard_map/ppermute | solution.py:256
  6.3 1.6 %collective-permute-start.1 = (bf16[136,512]{1,0:T(8,128)(2,1)}, bf16[136,512]{1,0:T(8,128)(2,1)S(1)}, u32[]{:S(2)}, u32[]{:S(2)}) collective-permute-start(bf16[136,512]{1,0:T(8,128)(2,1)} %get-tuple-element.13), channel_id=1, source_target_pairs={{0,4},{2,6},{4,8},{6,10},{8,12},{10,14},{12,0},{14,2},{1,5},{3,7},... | collective-permute-start | bytes 417800 | tf_op jit(solution)/shard_map/ppermute | solution.py:256
  7.8 2.5 %collective-permute-start.2 = (bf16[136,512]{1,0:T(8,128)(2,1)}, bf16[136,512]{1,0:T(8,128)(2,1)S(1)}, u32[]{:S(2)}, u32[]{:S(2)}) collective-permute-start(bf16[136,512]{1,0:T(8,128)(2,1)} %get-tuple-element.14), channel_id=1, source_target_pairs={{0,6},{2,8},{4,10},{6,12},{8,14},{10,0},{12,2},{14,4},{1,7},{3,9},... | collective-permute-start | bytes 417800 | tf_op jit(solution)/shard_map/ppermute | solution.py:256
  10.4 1.2 %collective-permute-start.3 = (bf16[136,512]{1,0:T(8,128)(2,1)}, bf16[136,512]{1,0:T(8,128)(2,1)S(1)}, u32[]{:S(2)}, u32[]{:S(2)}) collective-permute-start(bf16[136,512]{1,0:T(8,128)(2,1)} %get-tuple-element.15), channel_id=1, source_target_pairs={{0,8},{2,10},{4,12},{6,14},{8,0},{10,2},{12,4},{14,6},{1,9},{3,11}... | collective-permute-start | bytes 417800 | tf_op jit(solution)/shard_map/ppermute | solution.py:256
  11.6 2.6 %collective-permute-start.4 = (bf16[136,512]{1,0:T(8,128)(2,1)}, bf16[136,512]{1,0:T(8,128)(2,1)S(1)}, u32[]{:S(2)}, u32[]{:S(2)}) collective-permute-start(bf16[136,512]{1,0:T(8,128)(2,1)} %get-tuple-element.16), channel_id=1, source_target_pairs={{0,10},{2,12},{4,14},{6,0},{8,2},{10,4},{12,6},{14,8},{1,11},{3,13... | collective-permute-start | bytes 417800 | tf_op jit(solution)/shard_map/ppermute | solution.py:256
  14.3 0.9 %bitcast_dynamic-update-slice_fusion.7 = bf16[8,136,512]{2,1,0:T(8,128)(2,1)S(1)} fusion(bf16[136,512]{1,0:T(8,128)(2,1)} %get-tuple-element.11), kind=kLoop, calls=%fused_computation.7 | loop fusion | bytes 278528
  15.2 0.0 collective-permute-done
  15.2 1.4 %collective-permute-start.5 = (bf16[136,512]{1,0:T(8,128)(2,1)}, bf16[136,512]{1,0:T(8,128)(2,1)S(1)}, u32[]{:S(2)}, u32[]{:S(2)}) collective-permute-start(bf16[136,512]{1,0:T(8,128)(2,1)} %get-tuple-element.17), channel_id=1, source_target_pairs={{0,12},{2,14},{4,0},{6,2},{8,4},{10,6},{12,8},{14,10},{1,13},{3,15... | collective-permute-start | bytes 417800 | tf_op jit(solution)/shard_map/ppermute | solution.py:256
  16.6 0.0 collective-permute-done.1
  16.6 1.6 %collective-permute-start.6 = (bf16[136,512]{1,0:T(8,128)(2,1)}, bf16[136,512]{1,0:T(8,128)(2,1)S(1)}, u32[]{:S(2)}, u32[]{:S(2)}) collective-permute-start(bf16[136,512]{1,0:T(8,128)(2,1)} %get-tuple-element.18), channel_id=1, source_target_pairs={{0,14},{2,0},{4,2},{6,4},{8,6},{10,8},{12,10},{14,12},{1,15},{3,1}... | collective-permute-start | bytes 417800 | tf_op jit(solution)/shard_map/ppermute | solution.py:256
  18.2 7.0 %collective-permute-done.2 = bf16[136,512]{1,0:T(8,128)(2,1)S(1)} collective-permute-done((bf16[136,512]{1,0:T(8,128)(2,1)}, bf16[136,512]{1,0:T(8,128)(2,1)S(1)}, u32[]{:S(2)}, u32[]{:S(2)}) %collective-permute-start.2) | collective-permute-done | bytes 139296 | tf_op jit(solution)/shard_map/ppermute | solution.py:256
  25.2 0.4 collective-permute-done.3
  25.6 0.0 collective-permute-done.4
  25.6 0.0 collective-permute-done.5
  25.7 0.1 collective-permute-done.6
  25.8 0.0 copy-start
  25.8 1.0 %copy-done = bf16[8,136,512]{2,1,0:T(8,128)(2,1)} copy-done((bf16[8,136,512]{2,1,0:T(8,128)(2,1)}, bf16[8,136,512]{2,1,0:T(8,128)(2,1)S(1)}, u32[]{:S(2)}) %copy-start) | copy-done | bytes 1114136
  26.8 4.0 %shard_map.69 = (bf16[8,136,256]{2,1,0:T(8,128)(2,1)}, f32[2,8,256]{2,1,0:T(8,128)}) custom-call(bf16[8,136,512]{2,1,0:T(8,128)(2,1)} %copy-done, f32[8,1,256]{2,1,0:T(1,128)} %bitcast.64), custom_call_target="tpu_custom_call" | custom-call | tf_op jit(solution)/shard_map/pallas_call | solution.py:157
  30.8 1.1 %dynamic-slice_bitcast_fusion = (bf16[136,256]{1,0:T(8,128)(2,1)S(1)}, bf16[136,256]{1,0:T(8,128)(2,1)S(1)}, bf16[136,256]{1,0:T(8,128)(2,1)S(1)}, bf16[136,256]...) fusion(bf16[8,136,256]{2,1,0:T(8,128)(2,1)} %get-tuple-element.19, ...), kind=kLoop, calls=%fused_computation.8 | loop fusion | bytes 974876 | tf_op jit(solution)/shard_map/jit(dynamic_index_in_dim)/squeeze | solution.py:291
  31.9 11.2 %collective-permute-start.7 = (bf16[136,256]{1,0:T(8,128)(2,1)S(1)}, bf16[136,256]{1,0:T(8,128)(2,1)S(1)}, u32[]{:S(2)}, u32[]{:S(2)}) collective-permute-start(bf16[136,256]{1,0:T(8,128)(2,1)S(1)} %get-tuple-element.26), channel_id=1, source_target_pairs={{0,14},{2,0},{4,2},{6,4},{8,6},{10,8},{12,10},{14,12},{1,15},{3,1}... | collective-permute-start | bytes 208904 | tf_op jit(solution)/shard_map/ppermute | solution.py:296
  43.1 0.7 %fusion.1 = f32[1,3,256]{2,1,0:T(4,128)S(1)} fusion(bf16[8,136,256]{2,1,0:T(8,128)(2,1)} %get-tuple-element.19, s32[]{:T(128)S(6)} %select_n.125, s32[]{:T(128)S(6)} %add.388), kind=kLoop, calls=%fused_computation.42 | loop fusion | flops 768 | bytes 4616 | tf_op jit(solution)/shard_map/convert_element_type | solution.py:301
  43.8 0.6 %collective-permute-start.8 = (bf16[136,256]{1,0:T(8,128)(2,1)S(1)}, bf16[136,256]{1,0:T(8,128)(2,1)S(1)}, u32[]{:S(2)}, u32[]{:S(2)}) collective-permute-start(bf16[136,256]{1,0:T(8,128)(2,1)S(1)} %get-tuple-element.25), channel_id=1, source_target_pairs={{0,12},{2,14},{4,0},{6,2},{8,4},{10,6},{12,8},{14,10},{1,13},{3,15... | collective-permute-start | bytes 208904 | tf_op jit(solution)/shard_map/ppermute | solution.py:296
  44.4 0.0 collective-permute-start.9
  44.4 2.3 %collective-permute-start.10 = (bf16[136,256]{1,0:T(8,128)(2,1)S(1)}, bf16[136,256]{1,0:T(8,128)(2,1)S(1)}, u32[]{:S(2)}, u32[]{:S(2)}) collective-permute-start(bf16[136,256]{1,0:T(8,128)(2,1)S(1)} %get-tuple-element.23), channel_id=1, source_target_pairs={{0,8},{2,10},{4,12},{6,14},{8,0},{10,2},{12,4},{14,6},{1,9},{3,11}... | collective-permute-start | bytes 208904 | tf_op jit(solution)/shard_map/ppermute | solution.py:296
  46.8 0.6 collective-permute-start.11
  47.4 0.9 %fusion = bf16[128,2048]{1,0:T(8,128)(2,1)S(1)} fusion(bf16[128,2048]{1,0:T(8,128)(2,1)S(1)} %broadcast_in_dim.27, s32[]{:T(128)S(6)} %select_n.126, bf16[8,136,256]{2,1,0:T(8,128)(2,1)} %get-tuple-element.19, s32[]{:T(128)S(6)} %select_n.125), kind=kLoop, calls=%fused_computation.23 | loop fusion | bytes 131080 | tf_op jit(solution)/shard_map/dynamic_update_slice | solution.py:298
  48.3 0.0 collective-permute-done.7
  48.3 2.8 %collective-permute-start.12 = (bf16[136,256]{1,0:T(8,128)(2,1)S(1)}, bf16[136,256]{1,0:T(8,128)(2,1)S(1)}, u32[]{:S(2)}, u32[]{:S(2)}) collective-permute-start(bf16[136,256]{1,0:T(8,128)(2,1)S(1)} %get-tuple-element.21), channel_id=1, source_target_pairs={{0,4},{2,6},{4,8},{6,10},{8,12},{10,14},{12,0},{14,2},{1,5},{3,7},... | collective-permute-start | bytes 208904 | tf_op jit(solution)/shard_map/ppermute | solution.py:296
  51.1 0.0 collective-permute-done.8
  51.1 0.2 collective-permute-start.13
  51.3 0.0 collective-permute-done.9
  51.3 4.7 %collective-permute-done.10 = bf16[136,256]{1,0:T(8,128)(2,1)S(1)} collective-permute-done((bf16[136,256]{1,0:T(8,128)(2,1)S(1)}, bf16[136,256]{1,0:T(8,128)(2,1)S(1)}, u32[]{:S(2)}, u32[]{:S(2)}) %collective-permute-start.10) | collective-permute-done | bytes 69664 | tf_op jit(solution)/shard_map/ppermute | solution.py:296
  56.1 1.4 %collective-permute-done.11 = bf16[136,256]{1,0:T(8,128)(2,1)S(1)} collective-permute-done((bf16[136,256]{1,0:T(8,128)(2,1)S(1)}, bf16[136,256]{1,0:T(8,128)(2,1)S(1)}, u32[]{:S(2)}, u32[]{:S(2)}) %collective-permute-start.11) | collective-permute-done | bytes 69664 | tf_op jit(solution)/shard_map/ppermute | solution.py:296
  57.5 0.0 collective-permute-done.12
  57.5 0.7 %collective-permute-done.13 = bf16[136,256]{1,0:T(8,128)(2,1)S(1)} collective-permute-done((bf16[136,256]{1,0:T(8,128)(2,1)S(1)}, bf16[136,256]{1,0:T(8,128)(2,1)S(1)}, u32[]{:S(2)}, u32[]{:S(2)}) %collective-permute-start.13) | collective-permute-done | bytes 69664 | tf_op jit(solution)/shard_map/ppermute | solution.py:296
  58.4 0.6 %constant_dynamic-slice_fusion = f32[8,2,128]{2,1,0:T(2,128)} fusion(f32[16,2,128]{2,1,0:T(2,128)S(1)} %constant_dynamic-update-slice_fusion, s32[]{:T(128)S(6)} %select_n.155), kind=kLoop, calls=%fused_computation.40 | loop fusion | bytes 16388 | tf_op jit(solution)/shard_map/jit(_roll_dynamic)/dynamic_slice | solution.py:304
  59.1 0.0 copy-start.1
  59.1 0.8 %copy-done.1 = bf16[128,2048]{1,0:T(8,128)(2,1)} copy-done((bf16[128,2048]{1,0:T(8,128)(2,1)}, bf16[128,2048]{1,0:T(8,128)(2,1)S(1)}, u32[]{:S(2)}) %copy-start.1) | copy-done | bytes 524312
  (46 shorter events, 0.4 us)
Async XLA Ops:
  3.2 11.9 %collective-permute-start = (bf16[136,512]{1,0:T(8,128)(2,1)}, bf16[136,512]{1,0:T(8,128)(2,1)S(1)}, u32[]{:S(2)}, u32[]{:S(2)}) collective-permute-start(bf16[136,512]{1,0:T(8,128)(2,1)} %get-tuple-element.12), channel_id=1, source_target_pairs={{0,2},{2,4},{4,6},{6,8},{8,10},{10,12},{12,14},{14,0},{1,3},{3,5},... | collective-permute-start | bytes 417800 | tf_op jit(solution)/shard_map/ppermute | solution.py:256
  6.3 10.3 %collective-permute-start.1 = (bf16[136,512]{1,0:T(8,128)(2,1)}, bf16[136,512]{1,0:T(8,128)(2,1)S(1)}, u32[]{:S(2)}, u32[]{:S(2)}) collective-permute-start(bf16[136,512]{1,0:T(8,128)(2,1)} %get-tuple-element.13), channel_id=1, source_target_pairs={{0,4},{2,6},{4,8},{6,10},{8,12},{10,14},{12,0},{14,2},{1,5},{3,7},... | collective-permute-start | bytes 417800 | tf_op jit(solution)/shard_map/ppermute | solution.py:256
  7.8 17.4 %collective-permute-start.2 = (bf16[136,512]{1,0:T(8,128)(2,1)}, bf16[136,512]{1,0:T(8,128)(2,1)S(1)}, u32[]{:S(2)}, u32[]{:S(2)}) collective-permute-start(bf16[136,512]{1,0:T(8,128)(2,1)} %get-tuple-element.14), channel_id=1, source_target_pairs={{0,6},{2,8},{4,10},{6,12},{8,14},{10,0},{12,2},{14,4},{1,7},{3,9},... | collective-permute-start | bytes 417800 | tf_op jit(solution)/shard_map/ppermute | solution.py:256
  10.4 15.2 %collective-permute-start.3 = (bf16[136,512]{1,0:T(8,128)(2,1)}, bf16[136,512]{1,0:T(8,128)(2,1)S(1)}, u32[]{:S(2)}, u32[]{:S(2)}) collective-permute-start(bf16[136,512]{1,0:T(8,128)(2,1)} %get-tuple-element.15), channel_id=1, source_target_pairs={{0,8},{2,10},{4,12},{6,14},{8,0},{10,2},{12,4},{14,6},{1,9},{3,11}... | collective-permute-start | bytes 417800 | tf_op jit(solution)/shard_map/ppermute | solution.py:256
  11.6 14.0 %collective-permute-start.4 = (bf16[136,512]{1,0:T(8,128)(2,1)}, bf16[136,512]{1,0:T(8,128)(2,1)S(1)}, u32[]{:S(2)}, u32[]{:S(2)}) collective-permute-start(bf16[136,512]{1,0:T(8,128)(2,1)} %get-tuple-element.16), channel_id=1, source_target_pairs={{0,10},{2,12},{4,14},{6,0},{8,2},{10,4},{12,6},{14,8},{1,11},{3,13... | collective-permute-start | bytes 417800 | tf_op jit(solution)/shard_map/ppermute | solution.py:256
  15.2 10.5 %collective-permute-start.5 = (bf16[136,512]{1,0:T(8,128)(2,1)}, bf16[136,512]{1,0:T(8,128)(2,1)S(1)}, u32[]{:S(2)}, u32[]{:S(2)}) collective-permute-start(bf16[136,512]{1,0:T(8,128)(2,1)} %get-tuple-element.17), channel_id=1, source_target_pairs={{0,12},{2,14},{4,0},{6,2},{8,4},{10,6},{12,8},{14,10},{1,13},{3,15... | collective-permute-start | bytes 417800 | tf_op jit(solution)/shard_map/ppermute | solution.py:256
  16.6 9.2 %collective-permute-start.6 = (bf16[136,512]{1,0:T(8,128)(2,1)}, bf16[136,512]{1,0:T(8,128)(2,1)S(1)}, u32[]{:S(2)}, u32[]{:S(2)}) collective-permute-start(bf16[136,512]{1,0:T(8,128)(2,1)} %get-tuple-element.18), channel_id=1, source_target_pairs={{0,14},{2,0},{4,2},{6,4},{8,6},{10,8},{12,10},{14,12},{1,15},{3,1}... | collective-permute-start | bytes 417800 | tf_op jit(solution)/shard_map/ppermute | solution.py:256
  25.8 1.0 %copy-start = (bf16[8,136,512]{2,1,0:T(8,128)(2,1)}, bf16[8,136,512]{2,1,0:T(8,128)(2,1)S(1)}, u32[]{:S(2)}) copy-start(bf16[8,136,512]{2,1,0:T(8,128)(2,1)S(1)} %bitcast_dynamic-update-slice_fusion.refs_0_) | copy-start | bytes 3342340
  31.9 16.4 %collective-permute-start.7 = (bf16[136,256]{1,0:T(8,128)(2,1)S(1)}, bf16[136,256]{1,0:T(8,128)(2,1)S(1)}, u32[]{:S(2)}, u32[]{:S(2)}) collective-permute-start(bf16[136,256]{1,0:T(8,128)(2,1)S(1)} %get-tuple-element.26), channel_id=1, source_target_pairs={{0,14},{2,0},{4,2},{6,4},{8,6},{10,8},{12,10},{14,12},{1,15},{3,1}... | collective-permute-start | bytes 208904 | tf_op jit(solution)/shard_map/ppermute | solution.py:296
  43.8 7.2 %collective-permute-start.8 = (bf16[136,256]{1,0:T(8,128)(2,1)S(1)}, bf16[136,256]{1,0:T(8,128)(2,1)S(1)}, u32[]{:S(2)}, u32[]{:S(2)}) collective-permute-start(bf16[136,256]{1,0:T(8,128)(2,1)S(1)} %get-tuple-element.25), channel_id=1, source_target_pairs={{0,12},{2,14},{4,0},{6,2},{8,4},{10,6},{12,8},{14,10},{1,13},{3,15... | collective-permute-start | bytes 208904 | tf_op jit(solution)/shard_map/ppermute | solution.py:296
  44.4 6.9 %collective-permute-start.9 = (bf16[136,256]{1,0:T(8,128)(2,1)S(1)}, bf16[136,256]{1,0:T(8,128)(2,1)S(1)}, u32[]{:S(2)}, u32[]{:S(2)}) collective-permute-start(bf16[136,256]{1,0:T(8,128)(2,1)S(1)} %get-tuple-element.24), channel_id=1, source_target_pairs={{0,10},{2,12},{4,14},{6,0},{8,2},{10,4},{12,6},{14,8},{1,11},{3,13... | collective-permute-start | bytes 208904 | tf_op jit(solution)/shard_map/ppermute | solution.py:296
  44.4 11.6 %collective-permute-start.10 = (bf16[136,256]{1,0:T(8,128)(2,1)S(1)}, bf16[136,256]{1,0:T(8,128)(2,1)S(1)}, u32[]{:S(2)}, u32[]{:S(2)}) collective-permute-start(bf16[136,256]{1,0:T(8,128)(2,1)S(1)} %get-tuple-element.23), channel_id=1, source_target_pairs={{0,8},{2,10},{4,12},{6,14},{8,0},{10,2},{12,4},{14,6},{1,9},{3,11}... | collective-permute-start | bytes 208904 | tf_op jit(solution)/shard_map/ppermute | solution.py:296
  46.8 10.7 %collective-permute-start.11 = (bf16[136,256]{1,0:T(8,128)(2,1)S(1)}, bf16[136,256]{1,0:T(8,128)(2,1)S(1)}, u32[]{:S(2)}, u32[]{:S(2)}) collective-permute-start(bf16[136,256]{1,0:T(8,128)(2,1)S(1)} %get-tuple-element.22), channel_id=1, source_target_pairs={{0,6},{2,8},{4,10},{6,12},{8,14},{10,0},{12,2},{14,4},{1,7},{3,9},... | collective-permute-start | bytes 208904 | tf_op jit(solution)/shard_map/ppermute | solution.py:296
  48.3 9.2 %collective-permute-start.12 = (bf16[136,256]{1,0:T(8,128)(2,1)S(1)}, bf16[136,256]{1,0:T(8,128)(2,1)S(1)}, u32[]{:S(2)}, u32[]{:S(2)}) collective-permute-start(bf16[136,256]{1,0:T(8,128)(2,1)S(1)} %get-tuple-element.21), channel_id=1, source_target_pairs={{0,4},{2,6},{4,8},{6,10},{8,12},{10,14},{12,0},{14,2},{1,5},{3,7},... | collective-permute-start | bytes 208904 | tf_op jit(solution)/shard_map/ppermute | solution.py:296
  51.1 7.1 %collective-permute-start.13 = (bf16[136,256]{1,0:T(8,128)(2,1)S(1)}, bf16[136,256]{1,0:T(8,128)(2,1)S(1)}, u32[]{:S(2)}, u32[]{:S(2)}) collective-permute-start(bf16[136,256]{1,0:T(8,128)(2,1)S(1)} %get-tuple-element.20), channel_id=1, source_target_pairs={{0,2},{2,4},{4,6},{6,8},{8,10},{10,12},{12,14},{14,0},{1,3},{3,5},... | collective-permute-start | bytes 208904 | tf_op jit(solution)/shard_map/ppermute | solution.py:296
  59.1 0.8 %copy-start.1 = (bf16[128,2048]{1,0:T(8,128)(2,1)}, bf16[128,2048]{1,0:T(8,128)(2,1)S(1)}, u32[]{:S(2)}) copy-start(bf16[128,2048]{1,0:T(8,128)(2,1)S(1)} %slice_dynamic-update-slice_fusion) | copy-start | bytes 1572868

commit v18 on v17

--- a/solution.py
+++ b/solution.py
@@ -46,7 +46,8 @@
             toeplitz[:, : n - i * br], g_scr[i * br :, :], preferred_element_type=jnp.float32
         )
         own = g_scr[i * br : (i + 1) * br, :].astype(jnp.float32)
-        out_ref[i, :br, :] = (conv * scale + gain * own).astype(out_ref.dtype)
+        dest = slot[i] if fold_rows else i
+        out_ref[dest, :br, :] = (conv * scale + gain * own).astype(out_ref.dtype)
     sums = [None] * nb
     if fold_rows:
         for k in range(nb):
@@ -88,7 +89,9 @@
             high[:, None, :],
             jnp.where(pick == 1, middle[:, None, :], jnp.where(pick == 2, low[:, None, :], 0.0)),
         )
-        out_ref[:, br : br + 8, :br] = tile.astype(out_ref.dtype)
+        tile = tile.astype(out_ref.dtype)
+        for i in range(nb):
+            out_ref[slot[i], br : br + 8, :br] = tile[i]
 
 
 def pack_kernel(me_ref, *refs, nb, br, sw, sf, gw):
@@ -288,9 +291,7 @@
         input_grad = jnp.zeros((block_rows, chan_width), outgoing.dtype)
         lag_slots = []
         for shift in range(seq_count):
-            chunk = lax.dynamic_index_in_dim(
-                outgoing, (seq_index - shift) % seq_count, 0, keepdims=False
-            )
+            chunk = outgoing[shift]
             if shift:
                 pairs = [(i, (i - shift) % seq_count) for i in range(seq_count)]
                 chunk = lax.ppermute(chunk, "seq", pairs)

time: 60.3 us -> 60.3 us (level)
  transfers between devices with their start and end apart: 14 -> 14, of which waited for: 6 -> 6; matrix products, arithmetic and copies ran while one was open for 4% -> 3% of each run, Pallas kernels for 0% -> 0%
where the time goes in v18:
time: 60.3 us; the launch traced here: 59.9 us
  starting transfers between devices  31.7 us (53%)
  waiting for transfers between devices  14.3 us (24%)
  Pallas kernels  6.61 us (11%)
  local copies, waits for them, and re-layouts  5.62 us (9%)
  between operations  0.88 us (1%)
  other arithmetic  0.77 us (1%)
    ppermute x7, starting transfers between devices, per_device(): chunk = lax.ppermute(chunk, 'seq', pairs)  17.7 us
    ppermute x7, starting transfers between devices, per_device(): arrived[shift] = lax.ppermute(chunks[shift], 'seq', pairs)[None]  14 us
    ppermute x7, waiting for transfers between devices, per_device(): arrived[shift] = lax.ppermute(chunks[shift], 'seq', pairs)[None]  7.45 us
    ppermute x7, waiting for transfers between devices, per_device(): chunk = lax.ppermute(chunk, 'seq', pairs)  6.83 us
    pallas_call x1, Pallas kernels, local_grads(): pl.pallas_call(body, out_shape=[jax.ShapeDtypeStruct((nb, out_rows, sw),...  4.01 us
    unnamed x26, local copies, waits for them, and re-layouts  2.9 us
    pallas_call x1, Pallas kernels, per_device(): pl.pallas_call(functools.partial(pack_kernel, nb=seq_count, br=block_rows...  2.61 us
  transfers between devices with their start and end apart: 14, of which 6 were waited for; matrix products, arithmetic and copies ran while one was open for 3% of the time, Pallas kernels for 0%

profile of v18, /device:TPU:0, one launch (start us, length us, event | category | flops | bytes accessed | tf_op | source)
XLA Modules:
  0.0 59.9 jit_solution(8199917347826975993)
XLA Ops:
  0.6 2.6 %shard_map.68 = (bf16[136,512]{1,0:T(8,128)(2,1)}, bf16[136,512]{1,0:T(8,128)(2,1)}, bf16[136,512]{1,0:T(8,128)(2,1)}, bf16[136,512]{1,0:T(8,128)(2,1)}, bf16[13...) custom-call(s32[1]{0:T(128)} %bitcast.me_ref, ...), custom_call_target="tpu_custom_call" | custom-call | tf_op jit(solution)/shard_map/pallas_call | solution.py:204
  3.2 3.0 %collective-permute-start = (bf16[136,512]{1,0:T(8,128)(2,1)}, bf16[136,512]{1,0:T(8,128)(2,1)S(1)}, u32[]{:S(2)}, u32[]{:S(2)}) collective-permute-start(bf16[136,512]{1,0:T(8,128)(2,1)} %get-tuple-element.12), channel_id=1, source_target_pairs={{0,2},{2,4},{4,6},{6,8},{8,10},{10,12},{12,14},{14,0},{1,3},{3,5},... | collective-permute-start | bytes 417800 | tf_op jit(solution)/shard_map/ppermute | solution.py:259
  6.3 1.6 %collective-permute-start.1 = (bf16[136,512]{1,0:T(8,128)(2,1)}, bf16[136,512]{1,0:T(8,128)(2,1)S(1)}, u32[]{:S(2)}, u32[]{:S(2)}) collective-permute-start(bf16[136,512]{1,0:T(8,128)(2,1)} %get-tuple-element.13), channel_id=1, source_target_pairs={{0,4},{2,6},{4,8},{6,10},{8,12},{10,14},{12,0},{14,2},{1,5},{3,7},... | collective-permute-start | bytes 417800 | tf_op jit(solution)/shard_map/ppermute | solution.py:259
  7.8 2.5 %collective-permute-start.2 = (bf16[136,512]{1,0:T(8,128)(2,1)}, bf16[136,512]{1,0:T(8,128)(2,1)S(1)}, u32[]{:S(2)}, u32[]{:S(2)}) collective-permute-start(bf16[136,512]{1,0:T(8,128)(2,1)} %get-tuple-element.14), channel_id=1, source_target_pairs={{0,6},{2,8},{4,10},{6,12},{8,14},{10,0},{12,2},{14,4},{1,7},{3,9},... | collective-permute-start | bytes 417800 | tf_op jit(solution)/shard_map/ppermute | solution.py:259
  10.4 1.2 %collective-permute-start.3 = (bf16[136,512]{1,0:T(8,128)(2,1)}, bf16[136,512]{1,0:T(8,128)(2,1)S(1)}, u32[]{:S(2)}, u32[]{:S(2)}) collective-permute-start(bf16[136,512]{1,0:T(8,128)(2,1)} %get-tuple-element.15), channel_id=1, source_target_pairs={{0,8},{2,10},{4,12},{6,14},{8,0},{10,2},{12,4},{14,6},{1,9},{3,11}... | collective-permute-start | bytes 417800 | tf_op jit(solution)/shard_map/ppermute | solution.py:259
  11.6 2.6 %collective-permute-start.4 = (bf16[136,512]{1,0:T(8,128)(2,1)}, bf16[136,512]{1,0:T(8,128)(2,1)S(1)}, u32[]{:S(2)}, u32[]{:S(2)}) collective-permute-start(bf16[136,512]{1,0:T(8,128)(2,1)} %get-tuple-element.16), channel_id=1, source_target_pairs={{0,10},{2,12},{4,14},{6,0},{8,2},{10,4},{12,6},{14,8},{1,11},{3,13... | collective-permute-start | bytes 417800 | tf_op jit(solution)/shard_map/ppermute | solution.py:259
  14.3 0.9 %bitcast_dynamic-update-slice_fusion.7 = bf16[8,136,512]{2,1,0:T(8,128)(2,1)S(1)} fusion(bf16[136,512]{1,0:T(8,128)(2,1)} %get-tuple-element.11), kind=kLoop, calls=%fused_computation.7 | loop fusion | bytes 278528
  15.2 0.0 collective-permute-done
  15.2 1.4 %collective-permute-start.5 = (bf16[136,512]{1,0:T(8,128)(2,1)}, bf16[136,512]{1,0:T(8,128)(2,1)S(1)}, u32[]{:S(2)}, u32[]{:S(2)}) collective-permute-start(bf16[136,512]{1,0:T(8,128)(2,1)} %get-tuple-element.17), channel_id=1, source_target_pairs={{0,12},{2,14},{4,0},{6,2},{8,4},{10,6},{12,8},{14,10},{1,13},{3,15... | collective-permute-start | bytes 417800 | tf_op jit(solution)/shard_map/ppermute | solution.py:259
  16.6 0.0 collective-permute-done.1
  16.6 1.6 %collective-permute-start.6 = (bf16[136,512]{1,0:T(8,128)(2,1)}, bf16[136,512]{1,0:T(8,128)(2,1)S(1)}, u32[]{:S(2)}, u32[]{:S(2)}) collective-permute-start(bf16[136,512]{1,0:T(8,128)(2,1)} %get-tuple-element.18), channel_id=1, source_target_pairs={{0,14},{2,0},{4,2},{6,4},{8,6},{10,8},{12,10},{14,12},{1,15},{3,1}... | collective-permute-start | bytes 417800 | tf_op jit(solution)/shard_map/ppermute | solution.py:259
  18.2 7.0 %collective-permute-done.2 = bf16[136,512]{1,0:T(8,128)(2,1)S(1)} collective-permute-done((bf16[136,512]{1,0:T(8,128)(2,1)}, bf16[136,512]{1,0:T(8,128)(2,1)S(1)}, u32[]{:S(2)}, u32[]{:S(2)}) %collective-permute-start.2) | collective-permute-done | bytes 139296 | tf_op jit(solution)/shard_map/ppermute | solution.py:259
  25.2 0.4 collective-permute-done.3
  25.6 0.0 collective-permute-done.4
  25.6 0.0 collective-permute-done.5
  25.7 0.1 collective-permute-done.6
  25.8 0.0 copy-start
  25.8 1.0 %copy-done = bf16[8,136,512]{2,1,0:T(8,128)(2,1)} copy-done((bf16[8,136,512]{2,1,0:T(8,128)(2,1)}, bf16[8,136,512]{2,1,0:T(8,128)(2,1)S(1)}, u32[]{:S(2)}) %copy-start) | copy-done | bytes 1114136
  26.8 4.0 %shard_map.69 = (bf16[8,136,256]{2,1,0:T(8,128)(2,1)}, f32[2,8,256]{2,1,0:T(8,128)}) custom-call(bf16[8,136,512]{2,1,0:T(8,128)(2,1)} %copy-done, f32[8,1,256]{2,1,0:T(1,128)} %bitcast.62), custom_call_target="tpu_custom_call" | custom-call | tf_op jit(solution)/shard_map/pallas_call | solution.py:160
  30.8 1.1 %slice_bitcast_fusion = (bf16[136,256]{1,0:T(8,128)(2,1)S(1)}, bf16[136,256]{1,0:T(8,128)(2,1)S(1)}, bf16[136,256]{1,0:T(8,128)(2,1)S(1)}, bf16[136,256]{1,0:T(8...) fusion(bf16[8,136,256]{2,1,0:T(8,128)(2,1)} %get-tuple-element.19), kind=kLoop, calls=%fused_computation.8 | loop fusion | bytes 974848 | tf_op jit(solution)/shard_map/squeeze | solution.py:294
  31.9 0.7 %slice_convert_fusion.7 = f32[1,3,256]{2,1,0:T(4,128)S(1)} fusion(bf16[8,136,256]{2,1,0:T(8,128)(2,1)} %get-tuple-element.19), kind=kLoop, calls=%fused_computation.47 | loop fusion | flops 768 | bytes 4608 | tf_op jit(solution)/shard_map/convert_element_type | solution.py:302
  32.6 11.2 %collective-permute-start.7 = (bf16[136,256]{1,0:T(8,128)(2,1)S(1)}, bf16[136,256]{1,0:T(8,128)(2,1)S(1)}, u32[]{:S(2)}, u32[]{:S(2)}) collective-permute-start(bf16[136,256]{1,0:T(8,128)(2,1)S(1)} %get-tuple-element.26), channel_id=1, source_target_pairs={{0,14},{2,0},{4,2},{6,4},{8,6},{10,8},{12,10},{14,12},{1,15},{3,1}... | collective-permute-start | bytes 208904 | tf_op jit(solution)/shard_map/ppermute | solution.py:297
  43.8 0.6 %collective-permute-start.8 = (bf16[136,256]{1,0:T(8,128)(2,1)S(1)}, bf16[136,256]{1,0:T(8,128)(2,1)S(1)}, u32[]{:S(2)}, u32[]{:S(2)}) collective-permute-start(bf16[136,256]{1,0:T(8,128)(2,1)S(1)} %get-tuple-element.25), channel_id=1, source_target_pairs={{0,12},{2,14},{4,0},{6,2},{8,4},{10,6},{12,8},{14,10},{1,13},{3,15... | collective-permute-start | bytes 208904 | tf_op jit(solution)/shard_map/ppermute | solution.py:297
  44.4 0.0 collective-permute-start.9
  44.4 2.4 %collective-permute-start.10 = (bf16[136,256]{1,0:T(8,128)(2,1)S(1)}, bf16[136,256]{1,0:T(8,128)(2,1)S(1)}, u32[]{:S(2)}, u32[]{:S(2)}) collective-permute-start(bf16[136,256]{1,0:T(8,128)(2,1)S(1)} %get-tuple-element.23), channel_id=1, source_target_pairs={{0,8},{2,10},{4,12},{6,14},{8,0},{10,2},{12,4},{14,6},{1,9},{3,11}... | collective-permute-start | bytes 208904 | tf_op jit(solution)/shard_map/ppermute | solution.py:297
  46.8 0.6 collective-permute-start.11
  47.4 0.9 %bitcast_dynamic-update-slice_fusion.8 = bf16[128,2048]{1,0:T(8,128)(2,1)S(1)} fusion(bf16[128,2048]{1,0:T(8,128)(2,1)S(1)} %broadcast_in_dim.27, s32[]{:T(128)S(6)} %select_n.70, bf16[8,136,256]{2,1,0:T(8,128)(2,1)} %get-tuple-element.19), kind=kLoop, calls=%fused_computation.22 | loop fusion | bytes 131076 | tf_op jit(solution)/shard_map/dynamic_update_slice | solution.py:299
  48.2 0.0 collective-permute-done.7
  48.2 2.7 %collective-permute-start.12 = (bf16[136,256]{1,0:T(8,128)(2,1)S(1)}, bf16[136,256]{1,0:T(8,128)(2,1)S(1)}, u32[]{:S(2)}, u32[]{:S(2)}) collective-permute-start(bf16[136,256]{1,0:T(8,128)(2,1)S(1)} %get-tuple-element.21), channel_id=1, source_target_pairs={{0,4},{2,6},{4,8},{6,10},{8,12},{10,14},{12,0},{14,2},{1,5},{3,7},... | collective-permute-start | bytes 208904 | tf_op jit(solution)/shard_map/ppermute | solution.py:297
  51.0 0.0 collective-permute-done.8
  51.0 0.2 collective-permute-start.13
  51.2 0.0 collective-permute-done.9
  51.3 5.4 %collective-permute-done.10 = bf16[136,256]{1,0:T(8,128)(2,1)S(1)} collective-permute-done((bf16[136,256]{1,0:T(8,128)(2,1)S(1)}, bf16[136,256]{1,0:T(8,128)(2,1)S(1)}, u32[]{:S(2)}, u32[]{:S(2)}) %collective-permute-start.10) | collective-permute-done | bytes 69664 | tf_op jit(solution)/shard_map/ppermute | solution.py:297
  56.7 0.7 %collective-permute-done.11 = bf16[136,256]{1,0:T(8,128)(2,1)S(1)} collective-permute-done((bf16[136,256]{1,0:T(8,128)(2,1)S(1)}, bf16[136,256]{1,0:T(8,128)(2,1)S(1)}, u32[]{:S(2)}, u32[]{:S(2)}) %collective-permute-start.11) | collective-permute-done | bytes 69664 | tf_op jit(solution)/shard_map/ppermute | solution.py:297
  57.4 0.0 collective-permute-done.12
  57.5 0.7 %collective-permute-done.13 = bf16[136,256]{1,0:T(8,128)(2,1)S(1)} collective-permute-done((bf16[136,256]{1,0:T(8,128)(2,1)S(1)}, bf16[136,256]{1,0:T(8,128)(2,1)S(1)}, u32[]{:S(2)}, u32[]{:S(2)}) %collective-permute-start.13) | collective-permute-done | bytes 69664 | tf_op jit(solution)/shard_map/ppermute | solution.py:297
  58.3 0.6 %constant_dynamic-slice_fusion = f32[8,2,128]{2,1,0:T(2,128)} fusion(f32[16,2,128]{2,1,0:T(2,128)S(1)} %constant_dynamic-update-slice_fusion, s32[]{:T(128)S(6)} %select_n.85), kind=kLoop, calls=%fused_computation.39 | loop fusion | bytes 16388 | tf_op jit(solution)/shard_map/jit(_roll_dynamic)/dynamic_slice | solution.py:305
  59.1 0.0 copy-start.1
  59.1 0.8 %copy-done.1 = bf16[128,2048]{1,0:T(8,128)(2,1)} copy-done((bf16[128,2048]{1,0:T(8,128)(2,1)}, bf16[128,2048]{1,0:T(8,128)(2,1)S(1)}, u32[]{:S(2)}) %copy-start.1) | copy-done | bytes 524312
  (46 shorter events, 0.4 us)
Async XLA Ops:
  3.2 11.9 %collective-permute-start = (bf16[136,512]{1,0:T(8,128)(2,1)}, bf16[136,512]{1,0:T(8,128)(2,1)S(1)}, u32[]{:S(2)}, u32[]{:S(2)}) collective-permute-start(bf16[136,512]{1,0:T(8,128)(2,1)} %get-tuple-element.12), channel_id=1, source_target_pairs={{0,2},{2,4},{4,6},{6,8},{8,10},{10,12},{12,14},{14,0},{1,3},{3,5},... | collective-permute-start | bytes 417800 | tf_op jit(solution)/shard_map/ppermute | solution.py:259
  6.3 10.3 %collective-permute-start.1 = (bf16[136,512]{1,0:T(8,128)(2,1)}, bf16[136,512]{1,0:T(8,128)(2,1)S(1)}, u32[]{:S(2)}, u32[]{:S(2)}) collective-permute-start(bf16[136,512]{1,0:T(8,128)(2,1)} %get-tuple-element.13), channel_id=1, source_target_pairs={{0,4},{2,6},{4,8},{6,10},{8,12},{10,14},{12,0},{14,2},{1,5},{3,7},... | collective-permute-start | bytes 417800 | tf_op jit(solution)/shard_map/ppermute | solution.py:259
  7.8 17.4 %collective-permute-start.2 = (bf16[136,512]{1,0:T(8,128)(2,1)}, bf16[136,512]{1,0:T(8,128)(2,1)S(1)}, u32[]{:S(2)}, u32[]{:S(2)}) collective-permute-start(bf16[136,512]{1,0:T(8,128)(2,1)} %get-tuple-element.14), channel_id=1, source_target_pairs={{0,6},{2,8},{4,10},{6,12},{8,14},{10,0},{12,2},{14,4},{1,7},{3,9},... | collective-permute-start | bytes 417800 | tf_op jit(solution)/shard_map/ppermute | solution.py:259
  10.4 15.2 %collective-permute-start.3 = (bf16[136,512]{1,0:T(8,128)(2,1)}, bf16[136,512]{1,0:T(8,128)(2,1)S(1)}, u32[]{:S(2)}, u32[]{:S(2)}) collective-permute-start(bf16[136,512]{1,0:T(8,128)(2,1)} %get-tuple-element.15), channel_id=1, source_target_pairs={{0,8},{2,10},{4,12},{6,14},{8,0},{10,2},{12,4},{14,6},{1,9},{3,11}... | collective-permute-start | bytes 417800 | tf_op jit(solution)/shard_map/ppermute | solution.py:259
  11.6 14.0 %collective-permute-start.4 = (bf16[136,512]{1,0:T(8,128)(2,1)}, bf16[136,512]{1,0:T(8,128)(2,1)S(1)}, u32[]{:S(2)}, u32[]{:S(2)}) collective-permute-start(bf16[136,512]{1,0:T(8,128)(2,1)} %get-tuple-element.16), channel_id=1, source_target_pairs={{0,10},{2,12},{4,14},{6,0},{8,2},{10,4},{12,6},{14,8},{1,11},{3,13... | collective-permute-start | bytes 417800 | tf_op jit(solution)/shard_map/ppermute | solution.py:259
  15.2 10.5 %collective-permute-start.5 = (bf16[136,512]{1,0:T(8,128)(2,1)}, bf16[136,512]{1,0:T(8,128)(2,1)S(1)}, u32[]{:S(2)}, u32[]{:S(2)}) collective-permute-start(bf16[136,512]{1,0:T(8,128)(2,1)} %get-tuple-element.17), channel_id=1, source_target_pairs={{0,12},{2,14},{4,0},{6,2},{8,4},{10,6},{12,8},{14,10},{1,13},{3,15... | collective-permute-start | bytes 417800 | tf_op jit(solution)/shard_map/ppermute | solution.py:259
  16.6 9.2 %collective-permute-start.6 = (bf16[136,512]{1,0:T(8,128)(2,1)}, bf16[136,512]{1,0:T(8,128)(2,1)S(1)}, u32[]{:S(2)}, u32[]{:S(2)}) collective-permute-start(bf16[136,512]{1,0:T(8,128)(2,1)} %get-tuple-element.18), channel_id=1, source_target_pairs={{0,14},{2,0},{4,2},{6,4},{8,6},{10,8},{12,10},{14,12},{1,15},{3,1}... | collective-permute-start | bytes 417800 | tf_op jit(solution)/shard_map/ppermute | solution.py:259
  25.8 1.0 %copy-start = (bf16[8,136,512]{2,1,0:T(8,128)(2,1)}, bf16[8,136,512]{2,1,0:T(8,128)(2,1)S(1)}, u32[]{:S(2)}) copy-start(bf16[8,136,512]{2,1,0:T(8,128)(2,1)S(1)} %bitcast_dynamic-update-slice_fusion.refs_0_) | copy-start | bytes 3342340
  32.6 15.6 %collective-permute-start.7 = (bf16[136,256]{1,0:T(8,128)(2,1)S(1)}, bf16[136,256]{1,0:T(8,128)(2,1)S(1)}, u32[]{:S(2)}, u32[]{:S(2)}) collective-permute-start(bf16[136,256]{1,0:T(8,128)(2,1)S(1)} %get-tuple-element.26), channel_id=1, source_target_pairs={{0,14},{2,0},{4,2},{6,4},{8,6},{10,8},{12,10},{14,12},{1,15},{3,1}... | collective-permute-start | bytes 208904 | tf_op jit(solution)/shard_map/ppermute | solution.py:297
  43.8 7.2 %collective-permute-start.8 = (bf16[136,256]{1,0:T(8,128)(2,1)S(1)}, bf16[136,256]{1,0:T(8,128)(2,1)S(1)}, u32[]{:S(2)}, u32[]{:S(2)}) collective-permute-start(bf16[136,256]{1,0:T(8,128)(2,1)S(1)} %get-tuple-element.25), channel_id=1, source_target_pairs={{0,12},{2,14},{4,0},{6,2},{8,4},{10,6},{12,8},{14,10},{1,13},{3,15... | collective-permute-start | bytes 208904 | tf_op jit(solution)/shard_map/ppermute | solution.py:297
  44.4 6.9 %collective-permute-start.9 = (bf16[136,256]{1,0:T(8,128)(2,1)S(1)}, bf16[136,256]{1,0:T(8,128)(2,1)S(1)}, u32[]{:S(2)}, u32[]{:S(2)}) collective-permute-start(bf16[136,256]{1,0:T(8,128)(2,1)S(1)} %get-tuple-element.24), channel_id=1, source_target_pairs={{0,10},{2,12},{4,14},{6,0},{8,2},{10,4},{12,6},{14,8},{1,11},{3,13... | collective-permute-start | bytes 208904 | tf_op jit(solution)/shard_map/ppermute | solution.py:297
  44.4 12.3 %collective-permute-start.10 = (bf16[136,256]{1,0:T(8,128)(2,1)S(1)}, bf16[136,256]{1,0:T(8,128)(2,1)S(1)}, u32[]{:S(2)}, u32[]{:S(2)}) collective-permute-start(bf16[136,256]{1,0:T(8,128)(2,1)S(1)} %get-tuple-element.23), channel_id=1, source_target_pairs={{0,8},{2,10},{4,12},{6,14},{8,0},{10,2},{12,4},{14,6},{1,9},{3,11}... | collective-permute-start | bytes 208904 | tf_op jit(solution)/shard_map/ppermute | solution.py:297
  46.8 10.7 %collective-permute-start.11 = (bf16[136,256]{1,0:T(8,128)(2,1)S(1)}, bf16[136,256]{1,0:T(8,128)(2,1)S(1)}, u32[]{:S(2)}, u32[]{:S(2)}) collective-permute-start(bf16[136,256]{1,0:T(8,128)(2,1)S(1)} %get-tuple-element.22), channel_id=1, source_target_pairs={{0,6},{2,8},{4,10},{6,12},{8,14},{10,0},{12,2},{14,4},{1,7},{3,9},... | collective-permute-start | bytes 208904 | tf_op jit(solution)/shard_map/ppermute | solution.py:297
  48.2 9.2 %collective-permute-start.12 = (bf16[136,256]{1,0:T(8,128)(2,1)S(1)}, bf16[136,256]{1,0:T(8,128)(2,1)S(1)}, u32[]{:S(2)}, u32[]{:S(2)}) collective-permute-start(bf16[136,256]{1,0:T(8,128)(2,1)S(1)} %get-tuple-element.21), channel_id=1, source_target_pairs={{0,4},{2,6},{4,8},{6,10},{8,12},{10,14},{12,0},{14,2},{1,5},{3,7},... | collective-permute-start | bytes 208904 | tf_op jit(solution)/shard_map/ppermute | solution.py:297
  51.0 7.2 %collective-permute-start.13 = (bf16[136,256]{1,0:T(8,128)(2,1)S(1)}, bf16[136,256]{1,0:T(8,128)(2,1)S(1)}, u32[]{:S(2)}, u32[]{:S(2)}) collective-permute-start(bf16[136,256]{1,0:T(8,128)(2,1)S(1)} %get-tuple-element.20), channel_id=1, source_target_pairs={{0,2},{2,4},{4,6},{6,8},{8,10},{10,12},{12,14},{14,0},{1,3},{3,5},... | collective-permute-start | bytes 208904 | tf_op jit(solution)/shard_map/ppermute | solution.py:297
  59.1 0.8 %copy-start.1 = (bf16[128,2048]{1,0:T(8,128)(2,1)}, bf16[128,2048]{1,0:T(8,128)(2,1)S(1)}, u32[]{:S(2)}) copy-start(bf16[128,2048]{1,0:T(8,128)(2,1)S(1)} %slice_dynamic-update-slice_fusion) | copy-start | bytes 1572868

commit v19 on v17

--- a/solution.py
+++ b/solution.py
@@ -10,7 +10,7 @@
 from jax.sharding import PartitionSpec as P
 
 
-def filter_pass(g_ref, x_ref, t_ref, gain_ref, out_ref, diag_ref, g_scr, xrev_ref, gt_ref, f, nb, br, sg, scale, fold_rows):
+def filter_pass(g_ref, x_ref, t_ref, gain_ref, out_ref, diag_ref, g_scr, xrev_ref, gt_ref, tf_ref, f, nb, br, sg, scale, fold_rows):
     me = lax.axis_index("seq")
     slot = [(me - i + nb) % nb for i in range(nb)]
     n = nb * br
@@ -41,10 +41,19 @@
         else:
             xrev_ref[i * br : (i + 1) * br, :] = flipped.astype(xrev_ref.dtype)
     gain = gain_ref[me, :, f * sg : (f + 1) * sg]
+    if fold_rows:
+        for i in range(nb):
+            if i:
+                tf_ref[i * br : (i + 1) * br, : i * br] = jnp.zeros((br, i * br), tf_ref.dtype)
+            tf_ref[i * br : (i + 1) * br, i * br :] = toeplitz[:, : n - i * br]
+        conv_all = jnp.dot(tf_ref[...], g_scr[...], preferred_element_type=jnp.float32)
     for i in range(nb):
-        conv = jnp.dot(
-            toeplitz[:, : n - i * br], g_scr[i * br :, :], preferred_element_type=jnp.float32
-        )
+        if fold_rows:
+            conv = conv_all[i * br : (i + 1) * br, :]
+        else:
+            conv = jnp.dot(
+                toeplitz[:, : n - i * br], g_scr[i * br :, :], preferred_element_type=jnp.float32
+            )
         own = g_scr[i * br : (i + 1) * br, :].astype(jnp.float32)
         out_ref[i, :br, :] = (conv * scale + gain * own).astype(out_ref.dtype)
     sums = [None] * nb
@@ -109,7 +118,7 @@
         out_ref[br:, br:] = jnp.zeros((8, 2 * sw - br), out_ref.dtype)
 
 
-def local_kernel(g_ref, x_ref, t_ref, gain_ref, out_ref, diag_ref, g_scr, xrev_ref, gt_ref, *, nb, br, sf, sg, x_base, t_base, scale, fold_rows):
+def local_kernel(g_ref, x_ref, t_ref, gain_ref, out_ref, diag_ref, g_scr, xrev_ref, gt_ref, tf_ref, *, nb, br, sf, sg, x_base, t_base, scale, fold_rows):
     for f in range(sf):
         filter_pass(
             g_ref.at[:, :br, f * sg : (f + 1) * sg],
@@ -121,6 +130,7 @@
             g_scr,
             xrev_ref,
             gt_ref,
+            tf_ref,
             f,
             nb,
             br,
@@ -164,6 +174,7 @@
             pltpu.VMEM((nb * br, sg), jnp.bfloat16),
             pltpu.VMEM((br, nb * sg) if fold_rows else (nb * br, sg), jnp.bfloat16),
             pltpu.VMEM((br, nb * sg) if fold_rows else (8, 128), jnp.bfloat16),
+            pltpu.VMEM((nb * br, nb * br) if fold_rows else (8, 128), jnp.bfloat16),
         ],
     )(*operands, gains.reshape(nb, 1, sw))
 

time: 60.3 us -> 61 us (1.012)
  Pallas kernels: 6.6 us -> 7.27 us
    pallas_call x1, Pallas kernels: 4 us -> 4.66 us  [local_grads(): pl.pallas_call(body, out_shape=[jax.ShapeDtypeStruct((nb, out_rows, sw),...]
where the time goes in v19:
time: 61 us; the launch traced here: 60.6 us
  starting transfers between devices  31.8 us (52%)
  waiting for transfers between devices  14.3 us (23%)
  Pallas kernels  7.27 us (12%)
  local copies, waits for them, and re-layouts  5.63 us (9%)
  between operations  0.88 us (1%)
  other arithmetic  0.77 us (1%)
    ppermute x7, starting transfers between devices, per_device(): chunk = lax.ppermute(chunk, 'seq', pairs)  17.7 us
    ppermute x7, starting transfers between devices, per_device(): arrived[shift] = lax.ppermute(chunks[shift], 'seq', pairs)[None]  14 us
    ppermute x7, waiting for transfers between devices, per_device(): arrived[shift] = lax.ppermute(chunks[shift], 'seq', pairs)[None]  7.45 us
    ppermute x7, waiting for transfers between devices, per_device(): chunk = lax.ppermute(chunk, 'seq', pairs)  6.83 us
    pallas_call x1, Pallas kernels, local_grads(): pl.pallas_call(body, out_shape=[jax.ShapeDtypeStruct((nb, out_rows, sw),...  4.66 us
    unnamed x26, local copies, waits for them, and re-layouts  2.9 us
    pallas_call x1, Pallas kernels, per_device(): pl.pallas_call(functools.partial(pack_kernel, nb=seq_count, br=block_rows...  2.61 us
  transfers between devices with their start and end apart: 14, of which 6 were waited for; matrix products, arithmetic and copies ran while one was open for 4% of the time, Pallas kernels for 0%

profile of v19, /device:TPU:0, one launch (start us, length us, event | category | flops | bytes accessed | tf_op | source)
XLA Modules:
  0.0 60.6 jit_solution(17251569655169676667)
XLA Ops:
  0.6 2.6 %shard_map.68 = (bf16[136,512]{1,0:T(8,128)(2,1)}, bf16[136,512]{1,0:T(8,128)(2,1)}, bf16[136,512]{1,0:T(8,128)(2,1)}, bf16[136,512]{1,0:T(8,128)(2,1)}, bf16[13...) custom-call(s32[1]{0:T(128)} %bitcast.me_ref, ...), custom_call_target="tpu_custom_call" | custom-call | tf_op jit(solution)/shard_map/pallas_call | solution.py:212
  3.2 3.0 %collective-permute-start = (bf16[136,512]{1,0:T(8,128)(2,1)}, bf16[136,512]{1,0:T(8,128)(2,1)S(1)}, u32[]{:S(2)}, u32[]{:S(2)}) collective-permute-start(bf16[136,512]{1,0:T(8,128)(2,1)} %get-tuple-element.12), channel_id=1, source_target_pairs={{0,2},{2,4},{4,6},{6,8},{8,10},{10,12},{12,14},{14,0},{1,3},{3,5},... | collective-permute-start | bytes 417800 | tf_op jit(solution)/shard_map/ppermute | solution.py:267
  6.3 1.6 %collective-permute-start.1 = (bf16[136,512]{1,0:T(8,128)(2,1)}, bf16[136,512]{1,0:T(8,128)(2,1)S(1)}, u32[]{:S(2)}, u32[]{:S(2)}) collective-permute-start(bf16[136,512]{1,0:T(8,128)(2,1)} %get-tuple-element.13), channel_id=1, source_target_pairs={{0,4},{2,6},{4,8},{6,10},{8,12},{10,14},{12,0},{14,2},{1,5},{3,7},... | collective-permute-start | bytes 417800 | tf_op jit(solution)/shard_map/ppermute | solution.py:267
  7.8 2.5 %collective-permute-start.2 = (bf16[136,512]{1,0:T(8,128)(2,1)}, bf16[136,512]{1,0:T(8,128)(2,1)S(1)}, u32[]{:S(2)}, u32[]{:S(2)}) collective-permute-start(bf16[136,512]{1,0:T(8,128)(2,1)} %get-tuple-element.14), channel_id=1, source_target_pairs={{0,6},{2,8},{4,10},{6,12},{8,14},{10,0},{12,2},{14,4},{1,7},{3,9},... | collective-permute-start | bytes 417800 | tf_op jit(solution)/shard_map/ppermute | solution.py:267
  10.4 1.2 %collective-permute-start.3 = (bf16[136,512]{1,0:T(8,128)(2,1)}, bf16[136,512]{1,0:T(8,128)(2,1)S(1)}, u32[]{:S(2)}, u32[]{:S(2)}) collective-permute-start(bf16[136,512]{1,0:T(8,128)(2,1)} %get-tuple-element.15), channel_id=1, source_target_pairs={{0,8},{2,10},{4,12},{6,14},{8,0},{10,2},{12,4},{14,6},{1,9},{3,11}... | collective-permute-start | bytes 417800 | tf_op jit(solution)/shard_map/ppermute | solution.py:267
  11.6 2.6 %collective-permute-start.4 = (bf16[136,512]{1,0:T(8,128)(2,1)}, bf16[136,512]{1,0:T(8,128)(2,1)S(1)}, u32[]{:S(2)}, u32[]{:S(2)}) collective-permute-start(bf16[136,512]{1,0:T(8,128)(2,1)} %get-tuple-element.16), channel_id=1, source_target_pairs={{0,10},{2,12},{4,14},{6,0},{8,2},{10,4},{12,6},{14,8},{1,11},{3,13... | collective-permute-start | bytes 417800 | tf_op jit(solution)/shard_map/ppermute | solution.py:267
  14.3 0.9 %bitcast_dynamic-update-slice_fusion.7 = bf16[8,136,512]{2,1,0:T(8,128)(2,1)S(1)} fusion(bf16[136,512]{1,0:T(8,128)(2,1)} %get-tuple-element.11), kind=kLoop, calls=%fused_computation.7 | loop fusion | bytes 278528
  15.2 0.0 collective-permute-done
  15.2 1.4 %collective-permute-start.5 = (bf16[136,512]{1,0:T(8,128)(2,1)}, bf16[136,512]{1,0:T(8,128)(2,1)S(1)}, u32[]{:S(2)}, u32[]{:S(2)}) collective-permute-start(bf16[136,512]{1,0:T(8,128)(2,1)} %get-tuple-element.17), channel_id=1, source_target_pairs={{0,12},{2,14},{4,0},{6,2},{8,4},{10,6},{12,8},{14,10},{1,13},{3,15... | collective-permute-start | bytes 417800 | tf_op jit(solution)/shard_map/ppermute | solution.py:267
  16.6 0.0 collective-permute-done.1
  16.6 1.6 %collective-permute-start.6 = (bf16[136,512]{1,0:T(8,128)(2,1)}, bf16[136,512]{1,0:T(8,128)(2,1)S(1)}, u32[]{:S(2)}, u32[]{:S(2)}) collective-permute-start(bf16[136,512]{1,0:T(8,128)(2,1)} %get-tuple-element.18), channel_id=1, source_target_pairs={{0,14},{2,0},{4,2},{6,4},{8,6},{10,8},{12,10},{14,12},{1,15},{3,1}... | collective-permute-start | bytes 417800 | tf_op jit(solution)/shard_map/ppermute | solution.py:267
  18.2 7.0 %collective-permute-done.2 = bf16[136,512]{1,0:T(8,128)(2,1)S(1)} collective-permute-done((bf16[136,512]{1,0:T(8,128)(2,1)}, bf16[136,512]{1,0:T(8,128)(2,1)S(1)}, u32[]{:S(2)}, u32[]{:S(2)}) %collective-permute-start.2) | collective-permute-done | bytes 139296 | tf_op jit(solution)/shard_map/ppermute | solution.py:267
  25.2 0.4 collective-permute-done.3
  25.6 0.0 collective-permute-done.4
  25.6 0.0 collective-permute-done.5
  25.7 0.1 collective-permute-done.6
  25.8 0.0 copy-start
  25.8 1.0 %copy-done = bf16[8,136,512]{2,1,0:T(8,128)(2,1)} copy-done((bf16[8,136,512]{2,1,0:T(8,128)(2,1)}, bf16[8,136,512]{2,1,0:T(8,128)(2,1)S(1)}, u32[]{:S(2)}) %copy-start) | copy-done | bytes 1114136
  26.8 4.7 %shard_map.69 = (bf16[8,136,256]{2,1,0:T(8,128)(2,1)}, f32[2,8,256]{2,1,0:T(8,128)}) custom-call(bf16[8,136,512]{2,1,0:T(8,128)(2,1)} %copy-done, f32[8,1,256]{2,1,0:T(1,128)} %bitcast.64), custom_call_target="tpu_custom_call" | custom-call | tf_op jit(solution)/shard_map/pallas_call | solution.py:167
  31.5 1.1 %dynamic-slice_bitcast_fusion = (bf16[136,256]{1,0:T(8,128)(2,1)S(1)}, bf16[136,256]{1,0:T(8,128)(2,1)S(1)}, bf16[136,256]{1,0:T(8,128)(2,1)S(1)}, bf16[136,256]...) fusion(bf16[8,136,256]{2,1,0:T(8,128)(2,1)} %get-tuple-element.19, ...), kind=kLoop, calls=%fused_computation.8 | loop fusion | bytes 974876 | tf_op jit(solution)/shard_map/jit(dynamic_index_in_dim)/squeeze | solution.py:302
  32.6 11.2 %collective-permute-start.7 = (bf16[136,256]{1,0:T(8,128)(2,1)S(1)}, bf16[136,256]{1,0:T(8,128)(2,1)S(1)}, u32[]{:S(2)}, u32[]{:S(2)}) collective-permute-start(bf16[136,256]{1,0:T(8,128)(2,1)S(1)} %get-tuple-element.26), channel_id=1, source_target_pairs={{0,14},{2,0},{4,2},{6,4},{8,6},{10,8},{12,10},{14,12},{1,15},{3,1}... | collective-permute-start | bytes 208904 | tf_op jit(solution)/shard_map/ppermute | solution.py:307
  43.8 0.7 %fusion.1 = f32[1,3,256]{2,1,0:T(4,128)S(1)} fusion(bf16[8,136,256]{2,1,0:T(8,128)(2,1)} %get-tuple-element.19, s32[]{:T(128)S(6)} %select_n.125, s32[]{:T(128)S(6)} %add.388), kind=kLoop, calls=%fused_computation.42 | loop fusion | flops 768 | bytes 4616 | tf_op jit(solution)/shard_map/convert_element_type | solution.py:312
  44.5 0.6 %collective-permute-start.8 = (bf16[136,256]{1,0:T(8,128)(2,1)S(1)}, bf16[136,256]{1,0:T(8,128)(2,1)S(1)}, u32[]{:S(2)}, u32[]{:S(2)}) collective-permute-start(bf16[136,256]{1,0:T(8,128)(2,1)S(1)} %get-tuple-element.25), channel_id=1, source_target_pairs={{0,12},{2,14},{4,0},{6,2},{8,4},{10,6},{12,8},{14,10},{1,13},{3,15... | collective-permute-start | bytes 208904 | tf_op jit(solution)/shard_map/ppermute | solution.py:307
  45.1 0.0 collective-permute-start.9
  45.1 2.3 %collective-permute-start.10 = (bf16[136,256]{1,0:T(8,128)(2,1)S(1)}, bf16[136,256]{1,0:T(8,128)(2,1)S(1)}, u32[]{:S(2)}, u32[]{:S(2)}) collective-permute-start(bf16[136,256]{1,0:T(8,128)(2,1)S(1)} %get-tuple-element.23), channel_id=1, source_target_pairs={{0,8},{2,10},{4,12},{6,14},{8,0},{10,2},{12,4},{14,6},{1,9},{3,11}... | collective-permute-start | bytes 208904 | tf_op jit(solution)/shard_map/ppermute | solution.py:307
  47.4 0.6 collective-permute-start.11
  48.1 0.9 %fusion = bf16[128,2048]{1,0:T(8,128)(2,1)S(1)} fusion(bf16[128,2048]{1,0:T(8,128)(2,1)S(1)} %broadcast_in_dim.27, s32[]{:T(128)S(6)} %select_n.126, bf16[8,136,256]{2,1,0:T(8,128)(2,1)} %get-tuple-element.19, s32[]{:T(128)S(6)} %select_n.125), kind=kLoop, calls=%fused_computation.23 | loop fusion | bytes 131080 | tf_op jit(solution)/shard_map/dynamic_update_slice | solution.py:309
  49.0 0.0 collective-permute-done.7
  49.0 2.7 %collective-permute-start.12 = (bf16[136,256]{1,0:T(8,128)(2,1)S(1)}, bf16[136,256]{1,0:T(8,128)(2,1)S(1)}, u32[]{:S(2)}, u32[]{:S(2)}) collective-permute-start(bf16[136,256]{1,0:T(8,128)(2,1)S(1)} %get-tuple-element.21), channel_id=1, source_target_pairs={{0,4},{2,6},{4,8},{6,10},{8,12},{10,14},{12,0},{14,2},{1,5},{3,7},... | collective-permute-start | bytes 208904 | tf_op jit(solution)/shard_map/ppermute | solution.py:307
  51.7 0.0 collective-permute-done.8
  51.7 0.2 collective-permute-start.13
  52.0 0.0 collective-permute-done.9
  52.0 4.7 %collective-permute-done.10 = bf16[136,256]{1,0:T(8,128)(2,1)S(1)} collective-permute-done((bf16[136,256]{1,0:T(8,128)(2,1)S(1)}, bf16[136,256]{1,0:T(8,128)(2,1)S(1)}, u32[]{:S(2)}, u32[]{:S(2)}) %collective-permute-start.10) | collective-permute-done | bytes 69664 | tf_op jit(solution)/shard_map/ppermute | solution.py:307
  56.7 1.4 %collective-permute-done.11 = bf16[136,256]{1,0:T(8,128)(2,1)S(1)} collective-permute-done((bf16[136,256]{1,0:T(8,128)(2,1)S(1)}, bf16[136,256]{1,0:T(8,128)(2,1)S(1)}, u32[]{:S(2)}, u32[]{:S(2)}) %collective-permute-start.11) | collective-permute-done | bytes 69664 | tf_op jit(solution)/shard_map/ppermute | solution.py:307
  58.2 0.0 collective-permute-done.12
  58.2 0.7 %collective-permute-done.13 = bf16[136,256]{1,0:T(8,128)(2,1)S(1)} collective-permute-done((bf16[136,256]{1,0:T(8,128)(2,1)S(1)}, bf16[136,256]{1,0:T(8,128)(2,1)S(1)}, u32[]{:S(2)}, u32[]{:S(2)}) %collective-permute-start.13) | collective-permute-done | bytes 69664 | tf_op jit(solution)/shard_map/ppermute | solution.py:307
  59.1 0.6 %constant_dynamic-slice_fusion = f32[8,2,128]{2,1,0:T(2,128)} fusion(f32[16,2,128]{2,1,0:T(2,128)S(1)} %constant_dynamic-update-slice_fusion, s32[]{:T(128)S(6)} %select_n.155), kind=kLoop, calls=%fused_computation.40 | loop fusion | bytes 16388 | tf_op jit(solution)/shard_map/jit(_roll_dynamic)/dynamic_slice | solution.py:315
  59.8 0.0 copy-start.1
  59.8 0.8 %copy-done.1 = bf16[128,2048]{1,0:T(8,128)(2,1)} copy-done((bf16[128,2048]{1,0:T(8,128)(2,1)}, bf16[128,2048]{1,0:T(8,128)(2,1)S(1)}, u32[]{:S(2)}) %copy-start.1) | copy-done | bytes 524312
  (46 shorter events, 0.4 us)
Async XLA Ops:
  3.2 11.9 %collective-permute-start = (bf16[136,512]{1,0:T(8,128)(2,1)}, bf16[136,512]{1,0:T(8,128)(2,1)S(1)}, u32[]{:S(2)}, u32[]{:S(2)}) collective-permute-start(bf16[136,512]{1,0:T(8,128)(2,1)} %get-tuple-element.12), channel_id=1, source_target_pairs={{0,2},{2,4},{4,6},{6,8},{8,10},{10,12},{12,14},{14,0},{1,3},{3,5},... | collective-permute-start | bytes 417800 | tf_op jit(solution)/shard_map/ppermute | solution.py:267
  6.3 10.3 %collective-permute-start.1 = (bf16[136,512]{1,0:T(8,128)(2,1)}, bf16[136,512]{1,0:T(8,128)(2,1)S(1)}, u32[]{:S(2)}, u32[]{:S(2)}) collective-permute-start(bf16[136,512]{1,0:T(8,128)(2,1)} %get-tuple-element.13), channel_id=1, source_target_pairs={{0,4},{2,6},{4,8},{6,10},{8,12},{10,14},{12,0},{14,2},{1,5},{3,7},... | collective-permute-start | bytes 417800 | tf_op jit(solution)/shard_map/ppermute | solution.py:267
  7.8 17.4 %collective-permute-start.2 = (bf16[136,512]{1,0:T(8,128)(2,1)}, bf16[136,512]{1,0:T(8,128)(2,1)S(1)}, u32[]{:S(2)}, u32[]{:S(2)}) collective-permute-start(bf16[136,512]{1,0:T(8,128)(2,1)} %get-tuple-element.14), channel_id=1, source_target_pairs={{0,6},{2,8},{4,10},{6,12},{8,14},{10,0},{12,2},{14,4},{1,7},{3,9},... | collective-permute-start | bytes 417800 | tf_op jit(solution)/shard_map/ppermute | solution.py:267
  10.4 15.2 %collective-permute-start.3 = (bf16[136,512]{1,0:T(8,128)(2,1)}, bf16[136,512]{1,0:T(8,128)(2,1)S(1)}, u32[]{:S(2)}, u32[]{:S(2)}) collective-permute-start(bf16[136,512]{1,0:T(8,128)(2,1)} %get-tuple-element.15), channel_id=1, source_target_pairs={{0,8},{2,10},{4,12},{6,14},{8,0},{10,2},{12,4},{14,6},{1,9},{3,11}... | collective-permute-start | bytes 417800 | tf_op jit(solution)/shard_map/ppermute | solution.py:267
  11.6 14.0 %collective-permute-start.4 = (bf16[136,512]{1,0:T(8,128)(2,1)}, bf16[136,512]{1,0:T(8,128)(2,1)S(1)}, u32[]{:S(2)}, u32[]{:S(2)}) collective-permute-start(bf16[136,512]{1,0:T(8,128)(2,1)} %get-tuple-element.16), channel_id=1, source_target_pairs={{0,10},{2,12},{4,14},{6,0},{8,2},{10,4},{12,6},{14,8},{1,11},{3,13... | collective-permute-start | bytes 417800 | tf_op jit(solution)/shard_map/ppermute | solution.py:267
  15.2 10.5 %collective-permute-start.5 = (bf16[136,512]{1,0:T(8,128)(2,1)}, bf16[136,512]{1,0:T(8,128)(2,1)S(1)}, u32[]{:S(2)}, u32[]{:S(2)}) collective-permute-start(bf16[136,512]{1,0:T(8,128)(2,1)} %get-tuple-element.17), channel_id=1, source_target_pairs={{0,12},{2,14},{4,0},{6,2},{8,4},{10,6},{12,8},{14,10},{1,13},{3,15... | collective-permute-start | bytes 417800 | tf_op jit(solution)/shard_map/ppermute | solution.py:267
  16.6 9.2 %collective-permute-start.6 = (bf16[136,512]{1,0:T(8,128)(2,1)}, bf16[136,512]{1,0:T(8,128)(2,1)S(1)}, u32[]{:S(2)}, u32[]{:S(2)}) collective-permute-start(bf16[136,512]{1,0:T(8,128)(2,1)} %get-tuple-element.18), channel_id=1, source_target_pairs={{0,14},{2,0},{4,2},{6,4},{8,6},{10,8},{12,10},{14,12},{1,15},{3,1}... | collective-permute-start | bytes 417800 | tf_op jit(solution)/shard_map/ppermute | solution.py:267
  25.8 1.0 %copy-start = (bf16[8,136,512]{2,1,0:T(8,128)(2,1)}, bf16[8,136,512]{2,1,0:T(8,128)(2,1)S(1)}, u32[]{:S(2)}) copy-start(bf16[8,136,512]{2,1,0:T(8,128)(2,1)S(1)} %bitcast_dynamic-update-slice_fusion.refs_0_) | copy-start | bytes 3342340
  32.6 16.4 %collective-permute-start.7 = (bf16[136,256]{1,0:T(8,128)(2,1)S(1)}, bf16[136,256]{1,0:T(8,128)(2,1)S(1)}, u32[]{:S(2)}, u32[]{:S(2)}) collective-permute-start(bf16[136,256]{1,0:T(8,128)(2,1)S(1)} %get-tuple-element.26), channel_id=1, source_target_pairs={{0,14},{2,0},{4,2},{6,4},{8,6},{10,8},{12,10},{14,12},{1,15},{3,1}... | collective-permute-start | bytes 208904 | tf_op jit(solution)/shard_map/ppermute | solution.py:307
  44.5 7.2 %collective-permute-start.8 = (bf16[136,256]{1,0:T(8,128)(2,1)S(1)}, bf16[136,256]{1,0:T(8,128)(2,1)S(1)}, u32[]{:S(2)}, u32[]{:S(2)}) collective-permute-start(bf16[136,256]{1,0:T(8,128)(2,1)S(1)} %get-tuple-element.25), channel_id=1, source_target_pairs={{0,12},{2,14},{4,0},{6,2},{8,4},{10,6},{12,8},{14,10},{1,13},{3,15... | collective-permute-start | bytes 208904 | tf_op jit(solution)/shard_map/ppermute | solution.py:307
  45.1 6.9 %collective-permute-start.9 = (bf16[136,256]{1,0:T(8,128)(2,1)S(1)}, bf16[136,256]{1,0:T(8,128)(2,1)S(1)}, u32[]{:S(2)}, u32[]{:S(2)}) collective-permute-start(bf16[136,256]{1,0:T(8,128)(2,1)S(1)} %get-tuple-element.24), channel_id=1, source_target_pairs={{0,10},{2,12},{4,14},{6,0},{8,2},{10,4},{12,6},{14,8},{1,11},{3,13... | collective-permute-start | bytes 208904 | tf_op jit(solution)/shard_map/ppermute | solution.py:307
  45.1 11.6 %collective-permute-start.10 = (bf16[136,256]{1,0:T(8,128)(2,1)S(1)}, bf16[136,256]{1,0:T(8,128)(2,1)S(1)}, u32[]{:S(2)}, u32[]{:S(2)}) collective-permute-start(bf16[136,256]{1,0:T(8,128)(2,1)S(1)} %get-tuple-element.23), channel_id=1, source_target_pairs={{0,8},{2,10},{4,12},{6,14},{8,0},{10,2},{12,4},{14,6},{1,9},{3,11}... | collective-permute-start | bytes 208904 | tf_op jit(solution)/shard_map/ppermute | solution.py:307
  47.4 10.7 %collective-permute-start.11 = (bf16[136,256]{1,0:T(8,128)(2,1)S(1)}, bf16[136,256]{1,0:T(8,128)(2,1)S(1)}, u32[]{:S(2)}, u32[]{:S(2)}) collective-permute-start(bf16[136,256]{1,0:T(8,128)(2,1)S(1)} %get-tuple-element.22), channel_id=1, source_target_pairs={{0,6},{2,8},{4,10},{6,12},{8,14},{10,0},{12,2},{14,4},{1,7},{3,9},... | collective-permute-start | bytes 208904 | tf_op jit(solution)/shard_map/ppermute | solution.py:307
  49.0 9.2 %collective-permute-start.12 = (bf16[136,256]{1,0:T(8,128)(2,1)S(1)}, bf16[136,256]{1,0:T(8,128)(2,1)S(1)}, u32[]{:S(2)}, u32[]{:S(2)}) collective-permute-start(bf16[136,256]{1,0:T(8,128)(2,1)S(1)} %get-tuple-element.21), channel_id=1, source_target_pairs={{0,4},{2,6},{4,8},{6,10},{8,12},{10,14},{12,0},{14,2},{1,5},{3,7},... | collective-permute-start | bytes 208904 | tf_op jit(solution)/shard_map/ppermute | solution.py:307
  51.7 7.2 %collective-permute-start.13 = (bf16[136,256]{1,0:T(8,128)(2,1)S(1)}, bf16[136,256]{1,0:T(8,128)(2,1)S(1)}, u32[]{:S(2)}, u32[]{:S(2)}) collective-permute-start(bf16[136,256]{1,0:T(8,128)(2,1)S(1)} %get-tuple-element.20), channel_id=1, source_target_pairs={{0,2},{2,4},{4,6},{6,8},{8,10},{10,12},{12,14},{14,0},{1,3},{3,5},... | collective-permute-start | bytes 208904 | tf_op jit(solution)/shard_map/ppermute | solution.py:307
  59.8 0.8 %copy-start.1 = (bf16[128,2048]{1,0:T(8,128)(2,1)}, bf16[128,2048]{1,0:T(8,128)(2,1)S(1)}, u32[]{:S(2)}) copy-start(bf16[128,2048]{1,0:T(8,128)(2,1)S(1)} %slice_dynamic-update-slice_fusion) | copy-start | bytes 1572868

commit v20 on v17

--- a/solution.py
+++ b/solution.py
@@ -287,7 +287,7 @@
     if stretch_group % 128 == 0:
         input_grad = jnp.zeros((block_rows, chan_width), outgoing.dtype)
         lag_slots = []
-        for shift in range(seq_count):
+        for shift in order + [0]:
             chunk = lax.dynamic_index_in_dim(
                 outgoing, (seq_index - shift) % seq_count, 0, keepdims=False
             )
@@ -300,7 +300,8 @@
             )
             rows = chunk[block_rows : block_rows + 3].astype(jnp.float32)
             rows = rows.reshape(3, stretch_filters, stretch_group)[..., :block_rows]
-            lag_slots.append(rows[0] + rows[1] + rows[2])
+            lag_slots.append((shift, rows[0] + rows[1] + rows[2]))
+        lag_slots = [part for _, part in sorted(lag_slots, key=lambda item: item[0])]
         parts = jnp.roll(jnp.stack(lag_slots, axis=0), seq_index, axis=0)
     else:
         returned = lax.all_to_all(outgoing, "seq", split_axis=0, concat_axis=0, tiled=True)

time: 60.3 us -> 61.3 us (1.017)
  waiting for transfers between devices: 14.3 us -> 15.3 us
    ppermute x7, waiting for transfers between devices: 6.83 us -> 7.84 us  [per_device(): chunk = lax.ppermute(chunk, 'seq', pairs)]
  transfers between devices with their start and end apart: 14 -> 14, of which waited for: 6 -> 5; matrix products, arithmetic and copies ran while one was open for 4% -> 3% of each run, Pallas kernels for 0% -> 0%
where the time goes in v20:
time: 61.3 us; the launch traced here: 60.9 us
  starting transfers between devices  31.7 us (52%)
  waiting for transfers between devices  15.3 us (25%)
  Pallas kernels  6.6 us (11%)
  local copies, waits for them, and re-layouts  5.64 us (9%)
  between operations  0.9 us (1%)
  other arithmetic  0.77 us (1%)
    ppermute x7, starting transfers between devices, per_device(): chunk = lax.ppermute(chunk, 'seq', pairs)  17.7 us
    ppermute x7, starting transfers between devices, per_device(): arrived[shift] = lax.ppermute(chunks[shift], 'seq', pairs)[None]  14 us
    ppermute x7, waiting for transfers between devices, per_device(): chunk = lax.ppermute(chunk, 'seq', pairs)  7.84 us
    ppermute x7, waiting for transfers between devices, per_device(): arrived[shift] = lax.ppermute(chunks[shift], 'seq', pairs)[None]  7.45 us
    pallas_call x1, Pallas kernels, local_grads(): pl.pallas_call(body, out_shape=[jax.ShapeDtypeStruct((nb, out_rows, sw),...  4 us
    unnamed x26, local copies, waits for them, and re-layouts  2.91 us
    pallas_call x1, Pallas kernels, per_device(): pl.pallas_call(functools.partial(pack_kernel, nb=seq_count, br=block_rows...  2.61 us
  transfers between devices with their start and end apart: 14, of which 5 were waited for; matrix products, arithmetic and copies ran while one was open for 3% of the time, Pallas kernels for 0%

profile of v20, /device:TPU:0, one launch (start us, length us, event | category | flops | bytes accessed | tf_op | source)
XLA Modules:
  0.0 60.9 jit_solution(11528074701806224865)
XLA Ops:
  0.6 2.6 %shard_map.68 = (bf16[136,512]{1,0:T(8,128)(2,1)}, bf16[136,512]{1,0:T(8,128)(2,1)}, bf16[136,512]{1,0:T(8,128)(2,1)}, bf16[136,512]{1,0:T(8,128)(2,1)}, bf16[13...) custom-call(s32[1]{0:T(128)} %bitcast.me_ref, ...), custom_call_target="tpu_custom_call" | custom-call | tf_op jit(solution)/shard_map/pallas_call | solution.py:201
  3.2 3.0 %collective-permute-start = (bf16[136,512]{1,0:T(8,128)(2,1)}, bf16[136,512]{1,0:T(8,128)(2,1)S(1)}, u32[]{:S(2)}, u32[]{:S(2)}) collective-permute-start(bf16[136,512]{1,0:T(8,128)(2,1)} %get-tuple-element.12), channel_id=1, source_target_pairs={{0,2},{2,4},{4,6},{6,8},{8,10},{10,12},{12,14},{14,0},{1,3},{3,5},... | collective-permute-start | bytes 417800 | tf_op jit(solution)/shard_map/ppermute | solution.py:256
  6.3 1.6 %collective-permute-start.1 = (bf16[136,512]{1,0:T(8,128)(2,1)}, bf16[136,512]{1,0:T(8,128)(2,1)S(1)}, u32[]{:S(2)}, u32[]{:S(2)}) collective-permute-start(bf16[136,512]{1,0:T(8,128)(2,1)} %get-tuple-element.13), channel_id=1, source_target_pairs={{0,4},{2,6},{4,8},{6,10},{8,12},{10,14},{12,0},{14,2},{1,5},{3,7},... | collective-permute-start | bytes 417800 | tf_op jit(solution)/shard_map/ppermute | solution.py:256
  7.8 2.5 %collective-permute-start.2 = (bf16[136,512]{1,0:T(8,128)(2,1)}, bf16[136,512]{1,0:T(8,128)(2,1)S(1)}, u32[]{:S(2)}, u32[]{:S(2)}) collective-permute-start(bf16[136,512]{1,0:T(8,128)(2,1)} %get-tuple-element.14), channel_id=1, source_target_pairs={{0,6},{2,8},{4,10},{6,12},{8,14},{10,0},{12,2},{14,4},{1,7},{3,9},... | collective-permute-start | bytes 417800 | tf_op jit(solution)/shard_map/ppermute | solution.py:256
  10.4 1.2 %collective-permute-start.3 = (bf16[136,512]{1,0:T(8,128)(2,1)}, bf16[136,512]{1,0:T(8,128)(2,1)S(1)}, u32[]{:S(2)}, u32[]{:S(2)}) collective-permute-start(bf16[136,512]{1,0:T(8,128)(2,1)} %get-tuple-element.15), channel_id=1, source_target_pairs={{0,8},{2,10},{4,12},{6,14},{8,0},{10,2},{12,4},{14,6},{1,9},{3,11}... | collective-permute-start | bytes 417800 | tf_op jit(solution)/shard_map/ppermute | solution.py:256
  11.6 2.6 %collective-permute-start.4 = (bf16[136,512]{1,0:T(8,128)(2,1)}, bf16[136,512]{1,0:T(8,128)(2,1)S(1)}, u32[]{:S(2)}, u32[]{:S(2)}) collective-permute-start(bf16[136,512]{1,0:T(8,128)(2,1)} %get-tuple-element.16), channel_id=1, source_target_pairs={{0,10},{2,12},{4,14},{6,0},{8,2},{10,4},{12,6},{14,8},{1,11},{3,13... | collective-permute-start | bytes 417800 | tf_op jit(solution)/shard_map/ppermute | solution.py:256
  14.3 0.9 %bitcast_dynamic-update-slice_fusion.7 = bf16[8,136,512]{2,1,0:T(8,128)(2,1)S(1)} fusion(bf16[136,512]{1,0:T(8,128)(2,1)} %get-tuple-element.11), kind=kLoop, calls=%fused_computation.7 | loop fusion | bytes 278528
  15.2 0.0 collective-permute-done
  15.2 1.4 %collective-permute-start.5 = (bf16[136,512]{1,0:T(8,128)(2,1)}, bf16[136,512]{1,0:T(8,128)(2,1)S(1)}, u32[]{:S(2)}, u32[]{:S(2)}) collective-permute-start(bf16[136,512]{1,0:T(8,128)(2,1)} %get-tuple-element.17), channel_id=1, source_target_pairs={{0,12},{2,14},{4,0},{6,2},{8,4},{10,6},{12,8},{14,10},{1,13},{3,15... | collective-permute-start | bytes 417800 | tf_op jit(solution)/shard_map/ppermute | solution.py:256
  16.6 0.0 collective-permute-done.1
  16.6 1.6 %collective-permute-start.6 = (bf16[136,512]{1,0:T(8,128)(2,1)}, bf16[136,512]{1,0:T(8,128)(2,1)S(1)}, u32[]{:S(2)}, u32[]{:S(2)}) collective-permute-start(bf16[136,512]{1,0:T(8,128)(2,1)} %get-tuple-element.18), channel_id=1, source_target_pairs={{0,14},{2,0},{4,2},{6,4},{8,6},{10,8},{12,10},{14,12},{1,15},{3,1}... | collective-permute-start | bytes 417800 | tf_op jit(solution)/shard_map/ppermute | solution.py:256
  18.2 7.0 %collective-permute-done.2 = bf16[136,512]{1,0:T(8,128)(2,1)S(1)} collective-permute-done((bf16[136,512]{1,0:T(8,128)(2,1)}, bf16[136,512]{1,0:T(8,128)(2,1)S(1)}, u32[]{:S(2)}, u32[]{:S(2)}) %collective-permute-start.2) | collective-permute-done | bytes 139296 | tf_op jit(solution)/shard_map/ppermute | solution.py:256
  25.2 0.4 collective-permute-done.3
  25.6 0.0 collective-permute-done.4
  25.6 0.0 collective-permute-done.5
  25.7 0.1 collective-permute-done.6
  25.8 0.0 copy-start
  25.8 1.0 %copy-done = bf16[8,136,512]{2,1,0:T(8,128)(2,1)} copy-done((bf16[8,136,512]{2,1,0:T(8,128)(2,1)}, bf16[8,136,512]{2,1,0:T(8,128)(2,1)S(1)}, u32[]{:S(2)}) %copy-start) | copy-done | bytes 1114136
  26.8 4.0 %shard_map.69 = (bf16[8,136,256]{2,1,0:T(8,128)(2,1)}, f32[2,8,256]{2,1,0:T(8,128)}) custom-call(bf16[8,136,512]{2,1,0:T(8,128)(2,1)} %copy-done, f32[8,1,256]{2,1,0:T(1,128)} %bitcast.64), custom_call_target="tpu_custom_call" | custom-call | tf_op jit(solution)/shard_map/pallas_call | solution.py:157
  30.8 1.1 %dynamic-slice_bitcast_fusion = (bf16[136,256]{1,0:T(8,128)(2,1)S(1)}, bf16[136,256]{1,0:T(8,128)(2,1)S(1)}, bf16[136,256]{1,0:T(8,128)(2,1)S(1)}, bf16[136,256]...) fusion(bf16[8,136,256]{2,1,0:T(8,128)(2,1)} %get-tuple-element.19, ...), kind=kLoop, calls=%fused_computation.8 | loop fusion | bytes 974876 | tf_op jit(solution)/shard_map/jit(dynamic_index_in_dim)/squeeze | solution.py:291
  31.9 11.2 %collective-permute-start.7 = (bf16[136,256]{1,0:T(8,128)(2,1)S(1)}, bf16[136,256]{1,0:T(8,128)(2,1)S(1)}, u32[]{:S(2)}, u32[]{:S(2)}) collective-permute-start(bf16[136,256]{1,0:T(8,128)(2,1)S(1)} %get-tuple-element.26), channel_id=1, source_target_pairs={{0,14},{2,0},{4,2},{6,4},{8,6},{10,8},{12,10},{14,12},{1,15},{3,1}... | collective-permute-start | bytes 208904 | tf_op jit(solution)/shard_map/ppermute | solution.py:296
  43.1 0.7 %fusion.1 = f32[1,3,256]{2,1,0:T(4,128)S(1)} fusion(bf16[8,136,256]{2,1,0:T(8,128)(2,1)} %get-tuple-element.19, s32[]{:T(128)S(6)} %select_n.153, s32[]{:T(128)S(6)} %add.388), kind=kLoop, calls=%fused_computation.42 | loop fusion | flops 768 | bytes 4616 | tf_op jit(solution)/shard_map/convert_element_type | solution.py:301
  43.8 0.6 %collective-permute-start.9 = (bf16[136,256]{1,0:T(8,128)(2,1)S(1)}, bf16[136,256]{1,0:T(8,128)(2,1)S(1)}, u32[]{:S(2)}, u32[]{:S(2)}) collective-permute-start(bf16[136,256]{1,0:T(8,128)(2,1)S(1)} %get-tuple-element.24), channel_id=1, source_target_pairs={{0,12},{2,14},{4,0},{6,2},{8,4},{10,6},{12,8},{14,10},{1,13},{3,15... | collective-permute-start | bytes 208904 | tf_op jit(solution)/shard_map/ppermute | solution.py:296
  44.4 0.0 collective-permute-start.11
  44.4 2.3 %collective-permute-start.13 = (bf16[136,256]{1,0:T(8,128)(2,1)S(1)}, bf16[136,256]{1,0:T(8,128)(2,1)S(1)}, u32[]{:S(2)}, u32[]{:S(2)}) collective-permute-start(bf16[136,256]{1,0:T(8,128)(2,1)S(1)} %get-tuple-element.20), channel_id=1, source_target_pairs={{0,8},{2,10},{4,12},{6,14},{8,0},{10,2},{12,4},{14,6},{1,9},{3,11}... | collective-permute-start | bytes 208904 | tf_op jit(solution)/shard_map/ppermute | solution.py:296
  46.8 0.6 collective-permute-start.12
  47.4 0.0 collective-permute-done.7
  47.4 2.7 %collective-permute-start.10 = (bf16[136,256]{1,0:T(8,128)(2,1)S(1)}, bf16[136,256]{1,0:T(8,128)(2,1)S(1)}, u32[]{:S(2)}, u32[]{:S(2)}) collective-permute-start(bf16[136,256]{1,0:T(8,128)(2,1)S(1)} %get-tuple-element.23), channel_id=1, source_target_pairs={{0,4},{2,6},{4,8},{6,10},{8,12},{10,14},{12,0},{14,2},{1,5},{3,7},... | collective-permute-start | bytes 208904 | tf_op jit(solution)/shard_map/ppermute | solution.py:296
  50.1 0.0 collective-permute-done.9
  50.1 0.2 collective-permute-start.8
  50.3 0.0 collective-permute-done.11
  50.4 5.7 %collective-permute-done.13 = bf16[136,256]{1,0:T(8,128)(2,1)S(1)} collective-permute-done((bf16[136,256]{1,0:T(8,128)(2,1)S(1)}, bf16[136,256]{1,0:T(8,128)(2,1)S(1)}, u32[]{:S(2)}, u32[]{:S(2)}) %collective-permute-start.13) | collective-permute-done | bytes 69664 | tf_op jit(solution)/shard_map/ppermute | solution.py:296
  56.1 2.1 %collective-permute-done.12 = bf16[136,256]{1,0:T(8,128)(2,1)S(1)} collective-permute-done((bf16[136,256]{1,0:T(8,128)(2,1)S(1)}, bf16[136,256]{1,0:T(8,128)(2,1)S(1)}, u32[]{:S(2)}, u32[]{:S(2)}) %collective-permute-start.12) | collective-permute-done | bytes 69664 | tf_op jit(solution)/shard_map/ppermute | solution.py:296
  58.2 0.0 collective-permute-done.10
  58.2 0.0 collective-permute-done.8
  58.5 0.6 constant_dynamic-slice_fusion
  59.3 0.9 %fusion = bf16[128,2048]{1,0:T(8,128)(2,1)S(1)} fusion(bf16[128,2048]{1,0:T(8,128)(2,1)S(1)} %slice_dynamic-update-slice_fusion, s32[]{:T(128)S(6)} %select_n.154, bf16[8,136,256]{2,1,0:T(8,128)(2,1)} %get-tuple-element.19, s32[]{:T(128)S(6)} %select_n.153), kind=kLoop, calls=%fused_computation.16 | loop fusion | bytes 131080 | tf_op jit(solution)/shard_map/dynamic_update_slice | solution.py:298
  60.1 0.0 copy-start.1
  60.1 0.8 %copy-done.1 = bf16[128,2048]{1,0:T(8,128)(2,1)} copy-done((bf16[128,2048]{1,0:T(8,128)(2,1)}, bf16[128,2048]{1,0:T(8,128)(2,1)S(1)}, u32[]{:S(2)}) %copy-start.1) | copy-done | bytes 524312
  (46 shorter events, 0.4 us)
Async XLA Ops:
  3.2 11.9 %collective-permute-start = (bf16[136,512]{1,0:T(8,128)(2,1)}, bf16[136,512]{1,0:T(8,128)(2,1)S(1)}, u32[]{:S(2)}, u32[]{:S(2)}) collective-permute-start(bf16[136,512]{1,0:T(8,128)(2,1)} %get-tuple-element.12), channel_id=1, source_target_pairs={{0,2},{2,4},{4,6},{6,8},{8,10},{10,12},{12,14},{14,0},{1,3},{3,5},... | collective-permute-start | bytes 417800 | tf_op jit(solution)/shard_map/ppermute | solution.py:256
  6.3 10.3 %collective-permute-start.1 = (bf16[136,512]{1,0:T(8,128)(2,1)}, bf16[136,512]{1,0:T(8,128)(2,1)S(1)}, u32[]{:S(2)}, u32[]{:S(2)}) collective-permute-start(bf16[136,512]{1,0:T(8,128)(2,1)} %get-tuple-element.13), channel_id=1, source_target_pairs={{0,4},{2,6},{4,8},{6,10},{8,12},{10,14},{12,0},{14,2},{1,5},{3,7},... | collective-permute-start | bytes 417800 | tf_op jit(solution)/shard_map/ppermute | solution.py:256
  7.8 17.4 %collective-permute-start.2 = (bf16[136,512]{1,0:T(8,128)(2,1)}, bf16[136,512]{1,0:T(8,128)(2,1)S(1)}, u32[]{:S(2)}, u32[]{:S(2)}) collective-permute-start(bf16[136,512]{1,0:T(8,128)(2,1)} %get-tuple-element.14), channel_id=1, source_target_pairs={{0,6},{2,8},{4,10},{6,12},{8,14},{10,0},{12,2},{14,4},{1,7},{3,9},... | collective-permute-start | bytes 417800 | tf_op jit(solution)/shard_map/ppermute | solution.py:256
  10.4 15.2 %collective-permute-start.3 = (bf16[136,512]{1,0:T(8,128)(2,1)}, bf16[136,512]{1,0:T(8,128)(2,1)S(1)}, u32[]{:S(2)}, u32[]{:S(2)}) collective-permute-start(bf16[136,512]{1,0:T(8,128)(2,1)} %get-tuple-element.15), channel_id=1, source_target_pairs={{0,8},{2,10},{4,12},{6,14},{8,0},{10,2},{12,4},{14,6},{1,9},{3,11}... | collective-permute-start | bytes 417800 | tf_op jit(solution)/shard_map/ppermute | solution.py:256
  11.6 14.0 %collective-permute-start.4 = (bf16[136,512]{1,0:T(8,128)(2,1)}, bf16[136,512]{1,0:T(8,128)(2,1)S(1)}, u32[]{:S(2)}, u32[]{:S(2)}) collective-permute-start(bf16[136,512]{1,0:T(8,128)(2,1)} %get-tuple-element.16), channel_id=1, source_target_pairs={{0,10},{2,12},{4,14},{6,0},{8,2},{10,4},{12,6},{14,8},{1,11},{3,13... | collective-permute-start | bytes 417800 | tf_op jit(solution)/shard_map/ppermute | solution.py:256
  15.2 10.5 %collective-permute-start.5 = (bf16[136,512]{1,0:T(8,128)(2,1)}, bf16[136,512]{1,0:T(8,128)(2,1)S(1)}, u32[]{:S(2)}, u32[]{:S(2)}) collective-permute-start(bf16[136,512]{1,0:T(8,128)(2,1)} %get-tuple-element.17), channel_id=1, source_target_pairs={{0,12},{2,14},{4,0},{6,2},{8,4},{10,6},{12,8},{14,10},{1,13},{3,15... | collective-permute-start | bytes 417800 | tf_op jit(solution)/shard_map/ppermute | solution.py:256
  16.6 9.2 %collective-permute-start.6 = (bf16[136,512]{1,0:T(8,128)(2,1)}, bf16[136,512]{1,0:T(8,128)(2,1)S(1)}, u32[]{:S(2)}, u32[]{:S(2)}) collective-permute-start(bf16[136,512]{1,0:T(8,128)(2,1)} %get-tuple-element.18), channel_id=1, source_target_pairs={{0,14},{2,0},{4,2},{6,4},{8,6},{10,8},{12,10},{14,12},{1,15},{3,1}... | collective-permute-start | bytes 417800 | tf_op jit(solution)/shard_map/ppermute | solution.py:256
  25.8 1.0 %copy-start = (bf16[8,136,512]{2,1,0:T(8,128)(2,1)}, bf16[8,136,512]{2,1,0:T(8,128)(2,1)S(1)}, u32[]{:S(2)}) copy-start(bf16[8,136,512]{2,1,0:T(8,128)(2,1)S(1)} %bitcast_dynamic-update-slice_fusion.refs_0_) | copy-start | bytes 3342340
  31.9 15.4 %collective-permute-start.7 = (bf16[136,256]{1,0:T(8,128)(2,1)S(1)}, bf16[136,256]{1,0:T(8,128)(2,1)S(1)}, u32[]{:S(2)}, u32[]{:S(2)}) collective-permute-start(bf16[136,256]{1,0:T(8,128)(2,1)S(1)} %get-tuple-element.26), channel_id=1, source_target_pairs={{0,14},{2,0},{4,2},{6,4},{8,6},{10,8},{12,10},{14,12},{1,15},{3,1}... | collective-permute-start | bytes 208904 | tf_op jit(solution)/shard_map/ppermute | solution.py:296
  43.8 6.3 %collective-permute-start.9 = (bf16[136,256]{1,0:T(8,128)(2,1)S(1)}, bf16[136,256]{1,0:T(8,128)(2,1)S(1)}, u32[]{:S(2)}, u32[]{:S(2)}) collective-permute-start(bf16[136,256]{1,0:T(8,128)(2,1)S(1)} %get-tuple-element.24), channel_id=1, source_target_pairs={{0,12},{2,14},{4,0},{6,2},{8,4},{10,6},{12,8},{14,10},{1,13},{3,15... | collective-permute-start | bytes 208904 | tf_op jit(solution)/shard_map/ppermute | solution.py:296
  44.4 5.9 %collective-permute-start.11 = (bf16[136,256]{1,0:T(8,128)(2,1)S(1)}, bf16[136,256]{1,0:T(8,128)(2,1)S(1)}, u32[]{:S(2)}, u32[]{:S(2)}) collective-permute-start(bf16[136,256]{1,0:T(8,128)(2,1)S(1)} %get-tuple-element.22), channel_id=1, source_target_pairs={{0,10},{2,12},{4,14},{6,0},{8,2},{10,4},{12,6},{14,8},{1,11},{3,13... | collective-permute-start | bytes 208904 | tf_op jit(solution)/shard_map/ppermute | solution.py:296
  44.4 11.6 %collective-permute-start.13 = (bf16[136,256]{1,0:T(8,128)(2,1)S(1)}, bf16[136,256]{1,0:T(8,128)(2,1)S(1)}, u32[]{:S(2)}, u32[]{:S(2)}) collective-permute-start(bf16[136,256]{1,0:T(8,128)(2,1)S(1)} %get-tuple-element.20), channel_id=1, source_target_pairs={{0,8},{2,10},{4,12},{6,14},{8,0},{10,2},{12,4},{14,6},{1,9},{3,11}... | collective-permute-start | bytes 208904 | tf_op jit(solution)/shard_map/ppermute | solution.py:296
  46.8 11.4 %collective-permute-start.12 = (bf16[136,256]{1,0:T(8,128)(2,1)S(1)}, bf16[136,256]{1,0:T(8,128)(2,1)S(1)}, u32[]{:S(2)}, u32[]{:S(2)}) collective-permute-start(bf16[136,256]{1,0:T(8,128)(2,1)S(1)} %get-tuple-element.21), channel_id=1, source_target_pairs={{0,6},{2,8},{4,10},{6,12},{8,14},{10,0},{12,2},{14,4},{1,7},{3,9},... | collective-permute-start | bytes 208904 | tf_op jit(solution)/shard_map/ppermute | solution.py:296
  47.4 10.8 %collective-permute-start.10 = (bf16[136,256]{1,0:T(8,128)(2,1)S(1)}, bf16[136,256]{1,0:T(8,128)(2,1)S(1)}, u32[]{:S(2)}, u32[]{:S(2)}) collective-permute-start(bf16[136,256]{1,0:T(8,128)(2,1)S(1)} %get-tuple-element.23), channel_id=1, source_target_pairs={{0,4},{2,6},{4,8},{6,10},{8,12},{10,14},{12,0},{14,2},{1,5},{3,7},... | collective-permute-start | bytes 208904 | tf_op jit(solution)/shard_map/ppermute | solution.py:296
  50.1 8.2 %collective-permute-start.8 = (bf16[136,256]{1,0:T(8,128)(2,1)S(1)}, bf16[136,256]{1,0:T(8,128)(2,1)S(1)}, u32[]{:S(2)}, u32[]{:S(2)}) collective-permute-start(bf16[136,256]{1,0:T(8,128)(2,1)S(1)} %get-tuple-element.25), channel_id=1, source_target_pairs={{0,2},{2,4},{4,6},{6,8},{8,10},{10,12},{12,14},{14,0},{1,3},{3,5},... | collective-permute-start | bytes 208904 | tf_op jit(solution)/shard_map/ppermute | solution.py:296
  60.1 0.8 %copy-start.1 = (bf16[128,2048]{1,0:T(8,128)(2,1)}, bf16[128,2048]{1,0:T(8,128)(2,1)S(1)}, u32[]{:S(2)}) copy-start(bf16[128,2048]{1,0:T(8,128)(2,1)S(1)} %fusion) | copy-start | bytes 1572868

commit v21 on v17

--- a/solution.py
+++ b/solution.py
@@ -141,8 +141,15 @@
         x_base, t_base = 0, 0
     def body(*refs):
         if fold_rows:
-            refs = refs[:1] * 3 + refs[1:]
-        local_kernel(*refs, **params)
+            data, gain_ref = refs[0], refs[1]
+            chunk_refs, diag_ref = refs[2 : 2 + nb], refs[2 + nb]
+            scratch, result = refs[3 + nb : -1], refs[-1]
+            local_kernel(data, data, data, gain_ref, result, diag_ref, *scratch, **params)
+            me = lax.axis_index("seq")
+            for k in range(nb):
+                chunk_refs[k][...] = result[(me - k + nb) % nb]
+        else:
+            local_kernel(*refs, **params)
 
     params = dict(
         nb=nb,
@@ -156,15 +163,17 @@
     )
     return pl.pallas_call(
         body,
-        out_shape=[
-            jax.ShapeDtypeStruct((nb, out_rows, sw), jnp.bfloat16),
-            jax.ShapeDtypeStruct((sf, nb, 2 * br), jnp.float32),
-        ],
+        out_shape=(
+            [jax.ShapeDtypeStruct((out_rows, sw), jnp.bfloat16)] * nb if fold_rows
+            else [jax.ShapeDtypeStruct((nb, out_rows, sw), jnp.bfloat16)]
+        )
+        + [jax.ShapeDtypeStruct((sf, nb, 2 * br), jnp.float32)],
         scratch_shapes=[
             pltpu.VMEM((nb * br, sg), jnp.bfloat16),
             pltpu.VMEM((br, nb * sg) if fold_rows else (nb * br, sg), jnp.bfloat16),
             pltpu.VMEM((br, nb * sg) if fold_rows else (8, 128), jnp.bfloat16),
-        ],
+        ]
+        + ([pltpu.VMEM((nb, out_rows, sw), jnp.bfloat16)] if fold_rows else []),
     )(*operands, gains.reshape(nb, 1, sw))
 
 
@@ -257,7 +266,7 @@
     moved = jnp.concatenate(arrived, axis=0)
     used_rows = 3 * stretch_filters * block_rows // stretch_width
     extra_rows = -(-used_rows // 8) * 8
-    local_grad, diag = local_grads(
+    *local_grad, diag = local_grads(
         moved,
         skip_gain,
         seq_count,
@@ -270,6 +279,7 @@
     if stretch_group % 128 == 0:
         outgoing = local_grad
     else:
+        local_grad = local_grad[0]
         front = jnp.pad(diag[:, :, :block_rows], ((0, 0), (0, 1), (0, 0)))
         back = jnp.pad(diag[:, :, block_rows:], ((0, 0), (1, 0), (0, 0)))
         lag_sums = (front + back).reshape(stretch_filters, (seq_count + 1) * block_rows)
@@ -285,12 +295,10 @@
         outgoing = lax.dynamic_update_slice_in_dim(local_grad, split, block_rows, 1)
     sharers = seq_count * stretch_filters // filters
     if stretch_group % 128 == 0:
-        input_grad = jnp.zeros((block_rows, chan_width), outgoing.dtype)
+        input_grad = jnp.zeros((block_rows, chan_width), jnp.bfloat16)
         lag_slots = []
         for shift in range(seq_count):
-            chunk = lax.dynamic_index_in_dim(
-                outgoing, (seq_index - shift) % seq_count, 0, keepdims=False
-            )
+            chunk = outgoing[shift]
             if shift:
                 pairs = [(i, (i - shift) % seq_count) for i in range(seq_count)]
                 chunk = lax.ppermute(chunk, "seq", pairs)

time: 60.3 us -> 59.3 us (0.983)
  local copies, waits for them, and re-layouts: 5.63 us -> 4.49 us
    squeeze x1 -> x0, local copies, waits for them, and re-layouts: 1.12 us -> none  [per_device(): lax.dynamic_index_in_dim(outgoing, (seq_index - shift) % seq_count, 0, ke...]
where the time goes in v21:
time: 59.3 us; the launch traced here: 59 us
  starting transfers between devices  31.7 us (53%)
  waiting for transfers between devices  14.5 us (24%)
  Pallas kernels  6.61 us (11%)
  local copies, waits for them, and re-layouts  4.49 us (8%)
  between operations  0.88 us (1%)
  other arithmetic  0.78 us (1%)
    ppermute x7, starting transfers between devices, per_device(): chunk = lax.ppermute(chunk, 'seq', pairs)  17.7 us
    ppermute x7, starting transfers between devices, per_device(): arrived[shift] = lax.ppermute(chunks[shift], 'seq', pairs)[None]  14 us
    ppermute x7, waiting for transfers between devices, per_device(): arrived[shift] = lax.ppermute(chunks[shift], 'seq', pairs)[None]  7.45 us
    ppermute x7, waiting for transfers between devices, per_device(): chunk = lax.ppermute(chunk, 'seq', pairs)  7.04 us
    pallas_call x1, Pallas kernels, local_grads(): pl.pallas_call(body, out_shape=([jax.ShapeDtypeStruct((out_rows, sw), jnp...  4 us
    unnamed x26, local copies, waits for them, and re-layouts  2.89 us
    pallas_call x1, Pallas kernels, per_device(): pl.pallas_call(functools.partial(pack_kernel, nb=seq_count, br=block_rows...  2.61 us
  transfers between devices with their start and end apart: 14, of which 6 were waited for; matrix products, arithmetic and copies ran while one was open for 4% of the time, Pallas kernels for 0%

profile of v21, /device:TPU:0, one launch (start us, length us, event | category | flops | bytes accessed | tf_op | source)
XLA Modules:
  0.0 59.0 jit_solution(5658407315899200413)
XLA Ops:
  0.6 2.6 %shard_map.68 = (bf16[136,512]{1,0:T(8,128)(2,1)}, bf16[136,512]{1,0:T(8,128)(2,1)}, bf16[136,512]{1,0:T(8,128)(2,1)}, bf16[136,512]{1,0:T(8,128)(2,1)}, bf16[13...) custom-call(s32[1]{0:T(128)} %bitcast.me_ref, ...), custom_call_target="tpu_custom_call" | custom-call | tf_op jit(solution)/shard_map/pallas_call | solution.py:210
  3.2 3.0 %collective-permute-start = (bf16[136,512]{1,0:T(8,128)(2,1)}, bf16[136,512]{1,0:T(8,128)(2,1)S(1)}, u32[]{:S(2)}, u32[]{:S(2)}) collective-permute-start(bf16[136,512]{1,0:T(8,128)(2,1)} %get-tuple-element.19), channel_id=1, source_target_pairs={{0,2},{2,4},{4,6},{6,8},{8,10},{10,12},{12,14},{14,0},{1,3},{3,5},... | collective-permute-start | bytes 417800 | tf_op jit(solution)/shard_map/ppermute | solution.py:265
  6.3 1.6 %collective-permute-start.1 = (bf16[136,512]{1,0:T(8,128)(2,1)}, bf16[136,512]{1,0:T(8,128)(2,1)S(1)}, u32[]{:S(2)}, u32[]{:S(2)}) collective-permute-start(bf16[136,512]{1,0:T(8,128)(2,1)} %get-tuple-element.20), channel_id=1, source_target_pairs={{0,4},{2,6},{4,8},{6,10},{8,12},{10,14},{12,0},{14,2},{1,5},{3,7},... | collective-permute-start | bytes 417800 | tf_op jit(solution)/shard_map/ppermute | solution.py:265
  7.8 2.5 %collective-permute-start.2 = (bf16[136,512]{1,0:T(8,128)(2,1)}, bf16[136,512]{1,0:T(8,128)(2,1)S(1)}, u32[]{:S(2)}, u32[]{:S(2)}) collective-permute-start(bf16[136,512]{1,0:T(8,128)(2,1)} %get-tuple-element.21), channel_id=1, source_target_pairs={{0,6},{2,8},{4,10},{6,12},{8,14},{10,0},{12,2},{14,4},{1,7},{3,9},... | collective-permute-start | bytes 417800 | tf_op jit(solution)/shard_map/ppermute | solution.py:265
  10.4 1.2 %collective-permute-start.3 = (bf16[136,512]{1,0:T(8,128)(2,1)}, bf16[136,512]{1,0:T(8,128)(2,1)S(1)}, u32[]{:S(2)}, u32[]{:S(2)}) collective-permute-start(bf16[136,512]{1,0:T(8,128)(2,1)} %get-tuple-element.22), channel_id=1, source_target_pairs={{0,8},{2,10},{4,12},{6,14},{8,0},{10,2},{12,4},{14,6},{1,9},{3,11}... | collective-permute-start | bytes 417800 | tf_op jit(solution)/shard_map/ppermute | solution.py:265
  11.6 2.6 %collective-permute-start.4 = (bf16[136,512]{1,0:T(8,128)(2,1)}, bf16[136,512]{1,0:T(8,128)(2,1)S(1)}, u32[]{:S(2)}, u32[]{:S(2)}) collective-permute-start(bf16[136,512]{1,0:T(8,128)(2,1)} %get-tuple-element.23), channel_id=1, source_target_pairs={{0,10},{2,12},{4,14},{6,0},{8,2},{10,4},{12,6},{14,8},{1,11},{3,13... | collective-permute-start | bytes 417800 | tf_op jit(solution)/shard_map/ppermute | solution.py:265
  14.3 0.9 %bitcast_dynamic-update-slice_fusion.7 = bf16[8,136,512]{2,1,0:T(8,128)(2,1)S(1)} fusion(bf16[136,512]{1,0:T(8,128)(2,1)} %get-tuple-element.18), kind=kLoop, calls=%fused_computation.7 | loop fusion | bytes 278528
  15.2 0.0 collective-permute-done
  15.2 1.4 %collective-permute-start.5 = (bf16[136,512]{1,0:T(8,128)(2,1)}, bf16[136,512]{1,0:T(8,128)(2,1)S(1)}, u32[]{:S(2)}, u32[]{:S(2)}) collective-permute-start(bf16[136,512]{1,0:T(8,128)(2,1)} %get-tuple-element.24), channel_id=1, source_target_pairs={{0,12},{2,14},{4,0},{6,2},{8,4},{10,6},{12,8},{14,10},{1,13},{3,15... | collective-permute-start | bytes 417800 | tf_op jit(solution)/shard_map/ppermute | solution.py:265
  16.6 0.0 collective-permute-done.1
  16.6 1.6 %collective-permute-start.6 = (bf16[136,512]{1,0:T(8,128)(2,1)}, bf16[136,512]{1,0:T(8,128)(2,1)S(1)}, u32[]{:S(2)}, u32[]{:S(2)}) collective-permute-start(bf16[136,512]{1,0:T(8,128)(2,1)} %get-tuple-element.25), channel_id=1, source_target_pairs={{0,14},{2,0},{4,2},{6,4},{8,6},{10,8},{12,10},{14,12},{1,15},{3,1}... | collective-permute-start | bytes 417800 | tf_op jit(solution)/shard_map/ppermute | solution.py:265
  18.3 7.0 %collective-permute-done.2 = bf16[136,512]{1,0:T(8,128)(2,1)S(1)} collective-permute-done((bf16[136,512]{1,0:T(8,128)(2,1)}, bf16[136,512]{1,0:T(8,128)(2,1)S(1)}, u32[]{:S(2)}, u32[]{:S(2)}) %collective-permute-start.2) | collective-permute-done | bytes 139296 | tf_op jit(solution)/shard_map/ppermute | solution.py:265
  25.2 0.4 collective-permute-done.3
  25.6 0.0 collective-permute-done.4
  25.6 0.0 collective-permute-done.5
  25.7 0.1 collective-permute-done.6
  25.8 0.0 copy-start
  25.8 1.0 %copy-done = bf16[8,136,512]{2,1,0:T(8,128)(2,1)} copy-done((bf16[8,136,512]{2,1,0:T(8,128)(2,1)}, bf16[8,136,512]{2,1,0:T(8,128)(2,1)S(1)}, u32[]{:S(2)}) %copy-start) | copy-done | bytes 1114136
  26.8 4.0 %shard_map.69 = (bf16[136,256]{1,0:T(8,128)(2,1)}, bf16[136,256]{1,0:T(8,128)(2,1)}, bf16[136,256]{1,0:T(8,128)(2,1)}, bf16[136,256]{1,0:T(8,128)(2,1)}, bf16[13...) custom-call(bf16[8,136,512]{2,1,0:T(8,128)(2,1)} %copy-done, ...), custom_call_target="tpu_custom_call" | custom-call | tf_op jit(solution)/shard_map/pallas_call | solution.py:164
  30.8 11.2 %collective-permute-start.7 = (bf16[136,256]{1,0:T(8,128)(2,1)}, bf16[136,256]{1,0:T(8,128)(2,1)S(1)}, u32[]{:S(2)}, u32[]{:S(2)}) collective-permute-start(bf16[136,256]{1,0:T(8,128)(2,1)} %get-tuple-element.27), channel_id=1, source_target_pairs={{0,14},{2,0},{4,2},{6,4},{8,6},{10,8},{12,10},{14,12},{1,15},{3,1}... | collective-permute-start | bytes 208904 | tf_op jit(solution)/shard_map/ppermute | solution.py:304
  42.0 0.7 %slice_convert_fusion.7 = f32[3,256]{1,0:T(4,128)S(1)} fusion(bf16[136,256]{1,0:T(8,128)(2,1)} %get-tuple-element.26), kind=kLoop, calls=%fused_computation.40 | loop fusion | flops 768 | bytes 4608 | tf_op jit(solution)/shard_map/convert_element_type | solution.py:309
  42.7 0.6 %collective-permute-start.8 = (bf16[136,256]{1,0:T(8,128)(2,1)}, bf16[136,256]{1,0:T(8,128)(2,1)S(1)}, u32[]{:S(2)}, u32[]{:S(2)}) collective-permute-start(bf16[136,256]{1,0:T(8,128)(2,1)} %get-tuple-element.28), channel_id=1, source_target_pairs={{0,12},{2,14},{4,0},{6,2},{8,4},{10,6},{12,8},{14,10},{1,13},{3,15... | collective-permute-start | bytes 208904 | tf_op jit(solution)/shard_map/ppermute | solution.py:304
  43.3 0.0 collective-permute-start.9
  43.3 2.3 %collective-permute-start.10 = (bf16[136,256]{1,0:T(8,128)(2,1)}, bf16[136,256]{1,0:T(8,128)(2,1)S(1)}, u32[]{:S(2)}, u32[]{:S(2)}) collective-permute-start(bf16[136,256]{1,0:T(8,128)(2,1)} %get-tuple-element.30), channel_id=1, source_target_pairs={{0,8},{2,10},{4,12},{6,14},{8,0},{10,2},{12,4},{14,6},{1,9},{3,11}... | collective-permute-start | bytes 208904 | tf_op jit(solution)/shard_map/ppermute | solution.py:304
  45.6 0.6 %collective-permute-start.11 = (bf16[136,256]{1,0:T(8,128)(2,1)}, bf16[136,256]{1,0:T(8,128)(2,1)S(1)}, u32[]{:S(2)}, u32[]{:S(2)}) collective-permute-start(bf16[136,256]{1,0:T(8,128)(2,1)} %get-tuple-element.31), channel_id=1, source_target_pairs={{0,6},{2,8},{4,10},{6,12},{8,14},{10,0},{12,2},{14,4},{1,7},{3,9},... | collective-permute-start | bytes 208904 | tf_op jit(solution)/shard_map/ppermute | solution.py:304
  46.2 0.9 %slice_dynamic-update-slice_fusion.7 = bf16[128,2048]{1,0:T(8,128)(2,1)S(1)} fusion(bf16[128,2048]{1,0:T(8,128)(2,1)S(1)} %broadcast_in_dim.27, s32[]{:T(128)S(6)} %select_n.70, bf16[136,256]{1,0:T(8,128)(2,1)} %get-tuple-element.26), kind=kLoop, calls=%fused_computation.15 | loop fusion | bytes 131076 | tf_op jit(solution)/shard_map/dynamic_update_slice | solution.py:306
  47.1 0.0 collective-permute-done.7
  47.1 2.8 %collective-permute-start.12 = (bf16[136,256]{1,0:T(8,128)(2,1)}, bf16[136,256]{1,0:T(8,128)(2,1)S(1)}, u32[]{:S(2)}, u32[]{:S(2)}) collective-permute-start(bf16[136,256]{1,0:T(8,128)(2,1)} %get-tuple-element.32), channel_id=1, source_target_pairs={{0,4},{2,6},{4,8},{6,10},{8,12},{10,14},{12,0},{14,2},{1,5},{3,7},... | collective-permute-start | bytes 208904 | tf_op jit(solution)/shard_map/ppermute | solution.py:304
  49.9 0.0 collective-permute-done.8
  49.9 0.2 collective-permute-start.13
  50.1 0.0 collective-permute-done.9
  50.1 4.9 %collective-permute-done.10 = bf16[136,256]{1,0:T(8,128)(2,1)S(1)} collective-permute-done((bf16[136,256]{1,0:T(8,128)(2,1)}, bf16[136,256]{1,0:T(8,128)(2,1)S(1)}, u32[]{:S(2)}, u32[]{:S(2)}) %collective-permute-start.10) | collective-permute-done | bytes 69664 | tf_op jit(solution)/shard_map/ppermute | solution.py:304
  55.1 1.4 %collective-permute-done.11 = bf16[136,256]{1,0:T(8,128)(2,1)S(1)} collective-permute-done((bf16[136,256]{1,0:T(8,128)(2,1)}, bf16[136,256]{1,0:T(8,128)(2,1)S(1)}, u32[]{:S(2)}, u32[]{:S(2)}) %collective-permute-start.11) | collective-permute-done | bytes 69664 | tf_op jit(solution)/shard_map/ppermute | solution.py:304
  56.5 0.0 collective-permute-done.12
  56.5 0.7 %collective-permute-done.13 = bf16[136,256]{1,0:T(8,128)(2,1)S(1)} collective-permute-done((bf16[136,256]{1,0:T(8,128)(2,1)}, bf16[136,256]{1,0:T(8,128)(2,1)S(1)}, u32[]{:S(2)}, u32[]{:S(2)}) %collective-permute-start.13) | collective-permute-done | bytes 69664 | tf_op jit(solution)/shard_map/ppermute | solution.py:304
  57.4 0.6 %constant_dynamic-slice_fusion = f32[8,2,128]{2,1,0:T(2,128)} fusion(f32[16,2,128]{2,1,0:T(2,128)S(1)} %constant_dynamic-update-slice_fusion, s32[]{:T(128)S(6)} %select_n.85), kind=kLoop, calls=%fused_computation.32 | loop fusion | bytes 16388 | tf_op jit(solution)/shard_map/jit(_roll_dynamic)/dynamic_slice | solution.py:312
  58.2 0.0 copy-start.1
  58.2 0.8 %copy-done.1 = bf16[128,2048]{1,0:T(8,128)(2,1)} copy-done((bf16[128,2048]{1,0:T(8,128)(2,1)}, bf16[128,2048]{1,0:T(8,128)(2,1)S(1)}, u32[]{:S(2)}) %copy-start.1) | copy-done | bytes 524312
  (46 shorter events, 0.4 us)
Async XLA Ops:
  3.2 11.9 %collective-permute-start = (bf16[136,512]{1,0:T(8,128)(2,1)}, bf16[136,512]{1,0:T(8,128)(2,1)S(1)}, u32[]{:S(2)}, u32[]{:S(2)}) collective-permute-start(bf16[136,512]{1,0:T(8,128)(2,1)} %get-tuple-element.19), channel_id=1, source_target_pairs={{0,2},{2,4},{4,6},{6,8},{8,10},{10,12},{12,14},{14,0},{1,3},{3,5},... | collective-permute-start | bytes 417800 | tf_op jit(solution)/shard_map/ppermute | solution.py:265
  6.3 10.3 %collective-permute-start.1 = (bf16[136,512]{1,0:T(8,128)(2,1)}, bf16[136,512]{1,0:T(8,128)(2,1)S(1)}, u32[]{:S(2)}, u32[]{:S(2)}) collective-permute-start(bf16[136,512]{1,0:T(8,128)(2,1)} %get-tuple-element.20), channel_id=1, source_target_pairs={{0,4},{2,6},{4,8},{6,10},{8,12},{10,14},{12,0},{14,2},{1,5},{3,7},... | collective-permute-start | bytes 417800 | tf_op jit(solution)/shard_map/ppermute | solution.py:265
  7.8 17.4 %collective-permute-start.2 = (bf16[136,512]{1,0:T(8,128)(2,1)}, bf16[136,512]{1,0:T(8,128)(2,1)S(1)}, u32[]{:S(2)}, u32[]{:S(2)}) collective-permute-start(bf16[136,512]{1,0:T(8,128)(2,1)} %get-tuple-element.21), channel_id=1, source_target_pairs={{0,6},{2,8},{4,10},{6,12},{8,14},{10,0},{12,2},{14,4},{1,7},{3,9},... | collective-permute-start | bytes 417800 | tf_op jit(solution)/shard_map/ppermute | solution.py:265
  10.4 15.2 %collective-permute-start.3 = (bf16[136,512]{1,0:T(8,128)(2,1)}, bf16[136,512]{1,0:T(8,128)(2,1)S(1)}, u32[]{:S(2)}, u32[]{:S(2)}) collective-permute-start(bf16[136,512]{1,0:T(8,128)(2,1)} %get-tuple-element.22), channel_id=1, source_target_pairs={{0,8},{2,10},{4,12},{6,14},{8,0},{10,2},{12,4},{14,6},{1,9},{3,11}... | collective-permute-start | bytes 417800 | tf_op jit(solution)/shard_map/ppermute | solution.py:265
  11.6 14.0 %collective-permute-start.4 = (bf16[136,512]{1,0:T(8,128)(2,1)}, bf16[136,512]{1,0:T(8,128)(2,1)S(1)}, u32[]{:S(2)}, u32[]{:S(2)}) collective-permute-start(bf16[136,512]{1,0:T(8,128)(2,1)} %get-tuple-element.23), channel_id=1, source_target_pairs={{0,10},{2,12},{4,14},{6,0},{8,2},{10,4},{12,6},{14,8},{1,11},{3,13... | collective-permute-start | bytes 417800 | tf_op jit(solution)/shard_map/ppermute | solution.py:265
  15.2 10.5 %collective-permute-start.5 = (bf16[136,512]{1,0:T(8,128)(2,1)}, bf16[136,512]{1,0:T(8,128)(2,1)S(1)}, u32[]{:S(2)}, u32[]{:S(2)}) collective-permute-start(bf16[136,512]{1,0:T(8,128)(2,1)} %get-tuple-element.24), channel_id=1, source_target_pairs={{0,12},{2,14},{4,0},{6,2},{8,4},{10,6},{12,8},{14,10},{1,13},{3,15... | collective-permute-start | bytes 417800 | tf_op jit(solution)/shard_map/ppermute | solution.py:265
  16.6 9.2 %collective-permute-start.6 = (bf16[136,512]{1,0:T(8,128)(2,1)}, bf16[136,512]{1,0:T(8,128)(2,1)S(1)}, u32[]{:S(2)}, u32[]{:S(2)}) collective-permute-start(bf16[136,512]{1,0:T(8,128)(2,1)} %get-tuple-element.25), channel_id=1, source_target_pairs={{0,14},{2,0},{4,2},{6,4},{8,6},{10,8},{12,10},{14,12},{1,15},{3,1}... | collective-permute-start | bytes 417800 | tf_op jit(solution)/shard_map/ppermute | solution.py:265
  25.8 1.0 %copy-start = (bf16[8,136,512]{2,1,0:T(8,128)(2,1)}, bf16[8,136,512]{2,1,0:T(8,128)(2,1)S(1)}, u32[]{:S(2)}) copy-start(bf16[8,136,512]{2,1,0:T(8,128)(2,1)S(1)} %bitcast_dynamic-update-slice_fusion.refs_0_) | copy-start | bytes 3342340
  30.8 16.3 %collective-permute-start.7 = (bf16[136,256]{1,0:T(8,128)(2,1)}, bf16[136,256]{1,0:T(8,128)(2,1)S(1)}, u32[]{:S(2)}, u32[]{:S(2)}) collective-permute-start(bf16[136,256]{1,0:T(8,128)(2,1)} %get-tuple-element.27), channel_id=1, source_target_pairs={{0,14},{2,0},{4,2},{6,4},{8,6},{10,8},{12,10},{14,12},{1,15},{3,1}... | collective-permute-start | bytes 208904 | tf_op jit(solution)/shard_map/ppermute | solution.py:304
  42.7 7.2 %collective-permute-start.8 = (bf16[136,256]{1,0:T(8,128)(2,1)}, bf16[136,256]{1,0:T(8,128)(2,1)S(1)}, u32[]{:S(2)}, u32[]{:S(2)}) collective-permute-start(bf16[136,256]{1,0:T(8,128)(2,1)} %get-tuple-element.28), channel_id=1, source_target_pairs={{0,12},{2,14},{4,0},{6,2},{8,4},{10,6},{12,8},{14,10},{1,13},{3,15... | collective-permute-start | bytes 208904 | tf_op jit(solution)/shard_map/ppermute | solution.py:304
  43.3 6.9 %collective-permute-start.9 = (bf16[136,256]{1,0:T(8,128)(2,1)}, bf16[136,256]{1,0:T(8,128)(2,1)S(1)}, u32[]{:S(2)}, u32[]{:S(2)}) collective-permute-start(bf16[136,256]{1,0:T(8,128)(2,1)} %get-tuple-element.29), channel_id=1, source_target_pairs={{0,10},{2,12},{4,14},{6,0},{8,2},{10,4},{12,6},{14,8},{1,11},{3,13... | collective-permute-start | bytes 208904 | tf_op jit(solution)/shard_map/ppermute | solution.py:304
  43.3 11.8 %collective-permute-start.10 = (bf16[136,256]{1,0:T(8,128)(2,1)}, bf16[136,256]{1,0:T(8,128)(2,1)S(1)}, u32[]{:S(2)}, u32[]{:S(2)}) collective-permute-start(bf16[136,256]{1,0:T(8,128)(2,1)} %get-tuple-element.30), channel_id=1, source_target_pairs={{0,8},{2,10},{4,12},{6,14},{8,0},{10,2},{12,4},{14,6},{1,9},{3,11}... | collective-permute-start | bytes 208904 | tf_op jit(solution)/shard_map/ppermute | solution.py:304
  45.6 10.9 %collective-permute-start.11 = (bf16[136,256]{1,0:T(8,128)(2,1)}, bf16[136,256]{1,0:T(8,128)(2,1)S(1)}, u32[]{:S(2)}, u32[]{:S(2)}) collective-permute-start(bf16[136,256]{1,0:T(8,128)(2,1)} %get-tuple-element.31), channel_id=1, source_target_pairs={{0,6},{2,8},{4,10},{6,12},{8,14},{10,0},{12,2},{14,4},{1,7},{3,9},... | collective-permute-start | bytes 208904 | tf_op jit(solution)/shard_map/ppermute | solution.py:304
  47.1 9.4 %collective-permute-start.12 = (bf16[136,256]{1,0:T(8,128)(2,1)}, bf16[136,256]{1,0:T(8,128)(2,1)S(1)}, u32[]{:S(2)}, u32[]{:S(2)}) collective-permute-start(bf16[136,256]{1,0:T(8,128)(2,1)} %get-tuple-element.32), channel_id=1, source_target_pairs={{0,4},{2,6},{4,8},{6,10},{8,12},{10,14},{12,0},{14,2},{1,5},{3,7},... | collective-permute-start | bytes 208904 | tf_op jit(solution)/shard_map/ppermute | solution.py:304
  49.9 7.4 %collective-permute-start.13 = (bf16[136,256]{1,0:T(8,128)(2,1)}, bf16[136,256]{1,0:T(8,128)(2,1)S(1)}, u32[]{:S(2)}, u32[]{:S(2)}) collective-permute-start(bf16[136,256]{1,0:T(8,128)(2,1)} %get-tuple-element.33), channel_id=1, source_target_pairs={{0,2},{2,4},{4,6},{6,8},{8,10},{10,12},{12,14},{14,0},{1,3},{3,5},... | collective-permute-start | bytes 208904 | tf_op jit(solution)/shard_map/ppermute | solution.py:304
  58.2 0.8 %copy-start.1 = (bf16[128,2048]{1,0:T(8,128)(2,1)}, bf16[128,2048]{1,0:T(8,128)(2,1)S(1)}, u32[]{:S(2)}) copy-start(bf16[128,2048]{1,0:T(8,128)(2,1)S(1)} %slice_dynamic-update-slice_fusion) | copy-start | bytes 1572868
